TPU v7x, 32 devices: a whole 2x2x4 slice. The times are simulated.
32 devices in a mesh: leaf: 8 (over z, x), couple: 4 (over y, core).
Axes of the slice: x: 2, y: 2, z: 4, core: 2. Of those that a mesh axis runs over, the one named last changes fastest.
Arguments:
- charges: bfloat16 [2048, 64, 128], P(('leaf', 'couple')), may hold values from -6 to 6
- leaf_basis: bfloat16 [131072, 64], P(('leaf', 'couple')), may hold values from -0.75 to 0.75
- transfer: bfloat16 [131072, 64], P(('leaf', 'couple')), may hold values from -0.75 to 0.75
- near_blocks: bfloat16 [131072, 768], P(('leaf', 'couple')), may hold values from -0.21875 to 0.21875
- near_source: int32 [24576], P(('leaf', 'couple')), may hold values from 0 to 71, as said below
- couple_fine: bfloat16 [131072, 1024], P(('leaf', 'couple')), may hold values from -0.1875 to 0.1875
- source_fine: int32 [32768], P(('leaf', 'couple')), may hold values from 0 to 255, as said below
- couple_coarse: bfloat16 [65536, 1024], P(('leaf', 'couple')), may hold values from -0.1875 to 0.1875
- source_coarse: int32 [16384], P(('leaf', 'couple')), may hold values from 0 to 127, as said below
- send_fine: int32 [32, 192], P(('leaf', 'couple')), may hold values from 0 to 63
- send_coarse: int32 [32, 96], P(('leaf', 'couple')), may hold values from 0 to 31
Outputs:
- product: bfloat16 [2048, 64, 128], P(('leaf', 'couple'))
Inputs may be any that keep to these rules, and one draw needn't show every extreme that they name: `source_fine`: entry k of a device's part belongs to leaf cluster k // 16 of that device. A value 64 + q * 32 + m appears only where the owner d - o_q exists, and on every device each such value appears at least once. `source_coarse`: entry k of a device's part belongs to parent cluster k // 16 of that device. A value 64 / 2 + q * 16 + m appears only where the owner d - o_q exists, and on every device each such value appears at least once. `near_source`: entry k of a device's part belongs to leaf k // 12 of that device and names a place in the device's leaves extended by 4 leaves on each side (own leaf t at place t + 4), at most 4 places from its own leaf; the first three entries of each leaf name the leaf itself and the leaves 4 before and 4 after it.
All inputs are finite; a program needn't handle non-finite values.
Results may differ from a plain program's by a relative error of at most 0.0063.
Values may be sent and summed in bfloat16 or wider, within the bound.
No kernel may reach another device: no remote copies, remote signals or barrier semaphores. Data moves between devices by JAX's collectives and lax.ppermute only.
A program may use at most 128 MiB of HBM per device.

v0:
```python
import jax
import jax.numpy as jnp
from jax import lax
from jax.sharding import PartitionSpec as P

LEAF = 64
RANK = 64
RHS = 128
HALO = 4
REACH = 3


def from_behind(value, axis, steps):
    count = lax.axis_size(axis)
    first, last = (max(0, -steps), min(count, count - steps))
    return lax.ppermute(value, axis, [(source, source + steps) for source in range(first, last)])


def extended_2(block, sides, width):
    for axis, dim in sides:
        count = lax.axis_size(axis)
        forward = [(i, i + 1) for i in range(count - 1)]
        backward = [(target, source) for source, target in forward]
        low = lax.ppermute(
            lax.slice_in_dim(block, block.shape[dim] - width, None, axis=dim), axis, forward
        )
        high = lax.ppermute(lax.slice_in_dim(block, 0, width, axis=dim), axis, backward)
        block = jnp.concatenate([low, block, high], axis=dim)
    return block


def offset_list():
    values = []
    for step in range(REACH):
        values.append(step + 1)
        values.append(-(step + 1))
    return values


def couple_sum(blocks, sources, source_pool, clusters):
    matrices = blocks.reshape(clusters, RANK, -1)
    picked = source_pool[sources].reshape(clusters, -1, RHS)
    return jnp.einsum("tak,tkr->tar", matrices, picked, preferred_element_type=jnp.float32)


def on_device(
    charges,
    leaf_basis,
    transfer,
    near_blocks,
    near_source,
    couple_fine,
    source_fine,
    couple_coarse,
    source_coarse,
    send_fine,
    send_coarse,
):
    leaves = charges.shape[0]
    parents = leaves // 2
    fine_each = send_fine.shape[1] // (2 * REACH)
    coarse_each = send_coarse.shape[1] // (2 * REACH)
    leaf_bases = leaf_basis.reshape(leaves, LEAF, RANK)
    fine_coeffs = jnp.einsum(
        "nlr,nlc->nrc", leaf_bases, charges, preferred_element_type=jnp.float32
    ).astype(jnp.bfloat16)
    stacked = transfer.reshape(parents, 2 * RANK, RANK)
    coarse_coeffs = jnp.einsum(
        "pab,par->pbr",
        stacked,
        fine_coeffs.reshape(parents, 2 * RANK, RHS),
        preferred_element_type=jnp.float32,
    ).astype(jnp.bfloat16)
    fine_out = fine_coeffs[send_fine[0]].reshape(2 * REACH, fine_each, RANK, RHS)
    coarse_out = coarse_coeffs[send_coarse[0]].reshape(2 * REACH, coarse_each, RANK, RHS)
    packets = jnp.concatenate([fine_out, coarse_out], 1)
    offsets = offset_list()
    arrived = {}
    for slot, offset in enumerate(offsets):
        arrived[offset] = from_behind(packets[slot], ("leaf", "couple"), offset)
    incoming = jnp.stack([arrived[offset] for offset in offsets], 0)
    fine_in = incoming[:, :fine_each].reshape(2 * REACH * fine_each, RANK, RHS)
    coarse_in = incoming[:, fine_each:].reshape(2 * REACH * coarse_each, RANK, RHS)
    fine_target = couple_sum(
        couple_fine, source_fine, jnp.concatenate([fine_coeffs, fine_in], 0), leaves
    )
    coarse_target = couple_sum(
        couple_coarse, source_coarse, jnp.concatenate([coarse_coeffs, coarse_in], 0), parents
    )
    coarse_round = coarse_target.astype(jnp.bfloat16)
    downward_terms = jnp.einsum(
        "pab,pbr->par", stacked, coarse_round, preferred_element_type=jnp.float32
    )
    fine_total = fine_target + downward_terms.reshape(leaves, RANK, RHS)
    far_field = jnp.einsum(
        "nlr,nrc->nlc",
        leaf_bases,
        fine_total.astype(jnp.bfloat16),
        preferred_element_type=jnp.float32,
    )
    extended = extended_2(charges, ((("leaf", "couple"), 0),), HALO)
    nearby = extended[near_source].reshape(leaves, -1, RHS)
    near_mats = near_blocks.reshape(leaves, LEAF, -1)
    near_field = jnp.einsum("nik,nkr->nir", near_mats, nearby, preferred_element_type=jnp.float32)
    return (far_field + near_field).astype(jnp.bfloat16)


def solution(mesh):
    return jax.shard_map(
        on_device,
        mesh=mesh,
        in_specs=(
            P(("leaf", "couple"), None, None),
            P(("leaf", "couple"), None),
            P(("leaf", "couple"), None),
            P(("leaf", "couple"), None),
            P(("leaf", "couple")),
            P(("leaf", "couple"), None),
            P(("leaf", "couple")),
            P(("leaf", "couple"), None),
            P(("leaf", "couple")),
            P(("leaf", "couple"), None),
            P(("leaf", "couple"), None),
        ),
        out_specs=P(("leaf", "couple"), None, None),
        check_vma=False,
    )
```

profile of v0, /device:TPU:4, one launch (start us, length us, event | category | flops | bytes accessed | tf_op | source)
XLA Modules:
  0.0 178.9 jit_solution(9525292159095045105)
XLA Ops:
  0.0 0.0 copy-start
  0.0 1.6 copy.20
  1.6 0.0 copy-start.4
  1.6 0.7 fusion.21
  2.3 0.7 compare_select_fusion.2
  3.0 1.7 convolution_convert_fusion
  4.7 0.0 copy-start.2
  4.7 2.7 %gather_fusion = bf16[192,64,128]{2,1,0:T(8,128)(2,1)} fusion(bf16[64,64,128]{2,1,0:T(8,128)(2,1)S(1)} %convolution_convert_fusion, s32[1024]{0:T(1024)S(1)} %get-tuple-element.16), kind=kCustom, calls=%fused_computation | custom fusion | bytes 6292224 | tf_op jit(solution)/shard_map/gather | solution.py:74
  7.4 0.0 copy-done
  7.4 0.4 fusion.3
  7.9 2.0 %gather_fusion.1 = bf16[96,64,128]{2,1,0:T(8,128)(2,1)} fusion(bf16[32,64,128]{2,1,0:T(8,128)(2,1)S(1)} %fusion.3, s32[1024]{0:T(1024)S(1)} %get-tuple-element.15), kind=kCustom, calls=%fused_computation.1 | custom fusion | bytes 3146112 | tf_op jit(solution)/shard_map/gather | solution.py:75
  9.8 0.0 copy-start.7
  9.8 4.1 %fusion.15 = (bf16[48,64,128]{2,1,0:T(8,128)(2,1)S(1)}, bf16[48,64,128]{2,1,0:T(8,128)(2,1)}, bf16[48,64,128]{2,1,0:T(8,128)(2,1)}, bf16[48,64,128]{2,1,0:T(8,12...) fusion(bf16[6,16,64,128]{3,2,1,0:T(8,128)(2,1)} %bitcast.89, bf16[6,32,64,128]{3,2,1,0:T(8,128)(2,1)} %bitcast.84), kind=kLoop, calls=%fused_computation.39 | loop fusion | flops 2359296 | bytes 9437184 | tf_op jit(solution)/shard_map/squeeze | solution.py:80
  13.9 1.9 %collective-permute-start = (bf16[48,64,128]{2,1,0:T(8,128)(2,1)}, bf16[48,64,128]{2,1,0:T(8,128)(2,1)}, u32[]{:S(2)}, u32[]{:S(2)}) collective-permute-start(bf16[48,64,128]{2,1,0:T(8,128)(2,1)} %get-tuple-element.6), channel_id=1, source_target_pairs={{0,1},{1,2},{2,3},{3,4},{4,5},{5,6},{6,7},{7,8},{8,9},{9,10},{10,1... | collective-permute-start | bytes 2359304 | tf_op jit(solution)/shard_map/ppermute | solution.py:16
  15.9 3.6 %collective-permute-start.1 = (bf16[48,64,128]{2,1,0:T(8,128)(2,1)}, bf16[48,64,128]{2,1,0:T(8,128)(2,1)}, u32[]{:S(2)}, u32[]{:S(2)}) collective-permute-start(bf16[48,64,128]{2,1,0:T(8,128)(2,1)} %get-tuple-element.7), channel_id=1, source_target_pairs={{1,0},{2,1},{3,2},{4,3},{5,4},{6,5},{7,6},{8,7},{9,8},{10,9},{11,1... | collective-permute-start | bytes 2359304 | tf_op jit(solution)/shard_map/ppermute | solution.py:16
  19.5 4.2 %collective-permute-start.2 = (bf16[48,64,128]{2,1,0:T(8,128)(2,1)}, bf16[48,64,128]{2,1,0:T(8,128)(2,1)}, u32[]{:S(2)}, u32[]{:S(2)}) collective-permute-start(bf16[48,64,128]{2,1,0:T(8,128)(2,1)} %get-tuple-element.8), channel_id=1, source_target_pairs={{0,2},{1,3},{2,4},{3,5},{4,6},{5,7},{6,8},{7,9},{8,10},{9,11},{10,... | collective-permute-start | bytes 2359304 | tf_op jit(solution)/shard_map/ppermute | solution.py:16
  23.8 1.9 %collective-permute-start.7 = (bf16[4,64,128]{2,1,0:T(8,128)(2,1)S(1)}, bf16[4,64,128]{2,1,0:T(8,128)(2,1)S(1)}, u32[]{:S(2)}, u32[]{:S(2)}) collective-permute-start(bf16[4,64,128]{2,1,0:T(8,128)(2,1)S(1)} %get-tuple-element.12), channel_id=1, source_target_pairs={{1,0},{2,1},{3,2},{4,3},{5,4},{6,5},{7,6},{8,7},{9,8},{10,9},{11,1... | collective-permute-start | bytes 196616 | tf_op jit(solution)/shard_map/ppermute | solution.py:27
  25.7 2.4 %collective-permute-start.6 = (bf16[4,64,128]{2,1,0:T(8,128)(2,1)S(1)}, bf16[4,64,128]{2,1,0:T(8,128)(2,1)S(1)}, u32[]{:S(2)}, u32[]{:S(2)}) collective-permute-start(bf16[4,64,128]{2,1,0:T(8,128)(2,1)S(1)} %get-tuple-element.11), channel_id=1, source_target_pairs={{0,1},{1,2},{2,3},{3,4},{4,5},{5,6},{6,7},{7,8},{8,9},{9,10},{10,1... | collective-permute-start | bytes 196616 | tf_op jit(solution)/shard_map/ppermute | solution.py:24
  28.2 1.7 collective-permute-done.7
  29.9 1.9 %collective-permute-start.3 = (bf16[48,64,128]{2,1,0:T(8,128)(2,1)}, bf16[48,64,128]{2,1,0:T(8,128)(2,1)}, u32[]{:S(2)}, u32[]{:S(2)}) collective-permute-start(bf16[48,64,128]{2,1,0:T(8,128)(2,1)} %get-tuple-element.9), channel_id=1, source_target_pairs={{2,0},{3,1},{4,2},{5,3},{6,4},{7,5},{8,6},{9,7},{10,8},{11,9},{12,... | collective-permute-start | bytes 2359304 | tf_op jit(solution)/shard_map/ppermute | solution.py:16
  31.8 43.6 %collective-permute-done.6 = bf16[4,64,128]{2,1,0:T(8,128)(2,1)S(1)} collective-permute-done((bf16[4,64,128]{2,1,0:T(8,128)(2,1)S(1)}, bf16[4,64,128]{2,1,0:T(8,128)(2,1)S(1)}, u32[]{:S(2)}, u32[]{:S(2)}) %collective-permute-start.6) | collective-permute-done | bytes 65568 | tf_op jit(solution)/shard_map/ppermute | solution.py:24
  75.4 2.2 %collective-permute-start.4 = (bf16[48,64,128]{2,1,0:T(8,128)(2,1)}, bf16[48,64,128]{2,1,0:T(8,128)(2,1)}, u32[]{:S(2)}, u32[]{:S(2)}) collective-permute-start(bf16[48,64,128]{2,1,0:T(8,128)(2,1)} %get-tuple-element.10), channel_id=1, source_target_pairs={{0,3},{1,4},{2,5},{3,6},{4,7},{5,8},{6,9},{7,10},{8,11},{9,12},{10... | collective-permute-start | bytes 2359304 | tf_op jit(solution)/shard_map/ppermute | solution.py:16
  77.6 0.2 pad_maximum_fusion.2
  77.7 18.2 %gather_fusion.4 = bf16[768,64,128]{2,1,0:T(8,128)(2,1)} fusion(bf16[72,64,128]{2,1,0:T(8,128)(2,1)S(1)} %pad_maximum_fusion.2, s32[1024]{0:T(1024)S(1)} %pad_clamp_fusion), kind=kCustom, calls=%fused_computation.4 | custom fusion | bytes 25168896 | tf_op jit(solution)/shard_map/gather | solution.py:102
  95.9 0.0 collective-permute-done
  95.9 1.3 collective-permute-start.5
  97.2 1.2 bitcast_dynamic-update-slice_fusion.5
  98.4 0.0 collective-permute-done.1
  98.4 1.2 bitcast_dynamic-update-slice_fusion.4
  99.7 0.0 collective-permute-done.2
  99.7 1.2 bitcast_dynamic-update-slice_fusion.3
  100.9 0.0 collective-permute-done.3
  100.9 1.2 bitcast_dynamic-update-slice_fusion.2
  102.2 0.0 collective-permute-done.4
  102.2 1.2 bitcast_dynamic-update-slice_fusion.1
  103.4 13.5 %collective-permute-done.5 = bf16[48,64,128]{2,1,0:T(8,128)(2,1)S(1)} collective-permute-done((bf16[48,64,128]{2,1,0:T(8,128)(2,1)S(1)}, bf16[48,64,128]{2,1,0:T(8,128)(2,1)S(1)}, u32[]{:S(2)}, u32[]{:S(2)}) %collective-permute-start.5) | collective-permute-done | bytes 786464 | tf_op jit(solution)/shard_map/ppermute | solution.py:16
  116.9 0.1 bitcast_dynamic-update-slice_fusion
  117.1 0.2 slice.61
  117.3 0.7 slice.60
  118.0 0.2 pad_maximum_fusion.1
  118.2 0.3 copy-done.3
  118.5 2.3 %pad_maximum_fusion = bf16[256,64,128]{2,1,0:T(8,128)(2,1)} fusion(bf16[192,64,128]{2,1,0:T(8,128)(2,1)S(1)} %bitcast.83, bf16[64,64,128]{2,1,0:T(8,128)(2,1)S(1)} %copy-done.3), kind=kLoop, calls=%fused_computation.15 | loop fusion | flops 2097152 | bytes 8388608 | tf_op jit(solution)/shard_map/concatenate | solution.py:85
  120.8 13.7 %gather_fusion.3 = bf16[512,64,128]{2,1,0:T(8,128)(2,1)} fusion(bf16[128,64,128]{2,1,0:T(8,128)(2,1)S(1)} %pad_maximum_fusion.1, s32[1024]{0:T(1024)S(1)} %get-tuple-element.14), kind=kCustom, calls=%fused_computation.3 | custom fusion | bytes 16779264 | tf_op jit(solution)/shard_map/gather | solution.py:42
  134.5 7.9 %fusion.4 = f32[32,128,128]{1,2,0:T(8,128)} fusion(bf16[32,64,1024]{2,1,0:T(8,128)(2,1)} %bitcast.91, bf16[32,1024,128]{2,1,0:T(8,128)(2,1)} %bitcast.81, bf16[4096,64]{0,1:T(8,128)(2,1)S(1)} %copy-done), kind=kOutput, calls=%fused_computation.26 | convolution fusion | flops 604241920 | bytes 15204352 | tf_op jit(solution)/shard_map/pab,pbr->par/dot_general | solution.py:91
  142.3 15.7 %gather_fusion.2 = bf16[1024,64,128]{2,1,0:T(8,128)(2,1)} fusion(bf16[256,64,128]{2,1,0:T(8,128)(2,1)} %pad_maximum_fusion, s32[1024]{0:T(1024)S(1)} %get-tuple-element.13), kind=kCustom, calls=%fused_computation.2 | custom fusion | bytes 33558528 | tf_op jit(solution)/shard_map/gather | solution.py:42
  158.0 10.8 %fusion.1 = f32[64,128,64]{1,2,0:T(8,128)S(1)} fusion(bf16[64,64,64]{2,1,0:T(8,128)(2,1)} %bitcast.86, f32[64,64,128]{2,1,0:T(8,128)} %bitcast.88, bf16[64,64,1024]{2,1,0:T(8,128)(2,1)} %bitcast.87, bf16[64,1024,128]{2,1,0:T(8,128)(2,1)} %bitcast.79), kind=kOutput, calls=%fused_computation.20 | convolution fusion | flops 1141899264 | bytes 29884416 | tf_op jit(solution)/shard_map/nlr,nrc->nlc/dot_general | solution.py:95
  168.9 0.0 copy-start.1
  168.9 10.0 %fusion.2 = bf16[64,64,128]{2,1,0:T(8,128)(2,1)} fusion(f32[64,128,64]{1,2,0:T(8,128)S(1)} %fusion.1, bf16[64,64,768]{2,1,0:T(8,128)(2,1)} %bitcast.82, bf16[64,768,128]{2,1,0:T(8,128)(2,1)} %bitcast.78), kind=kOutput, calls=%fused_computation.22 | convolution fusion | flops 806354944 | bytes 22020096 | tf_op jit(solution)/shard_map/nik,nkr->nir/dot_general | solution.py:104
  (17 shorter events, 0.1 us)
Async XLA Ops:
  0.0 7.4 %copy-start = (bf16[4096,64]{0,1:T(8,128)(2,1)S(1)}, bf16[4096,64]{0,1:T(8,128)(2,1)}, u32[]{:S(2)}) copy-start(bf16[4096,64]{0,1:T(8,128)(2,1)} %param.13) | copy-start | bytes 1572868
  1.6 5.9 %copy-start.4 = (bf16[4096,64]{1,0:T(8,128)(2,1)}, bf16[4096,64]{1,0:T(8,128)(2,1)S(1)}, u32[]{:S(2)}) copy-start(bf16[4096,64]{1,0:T(8,128)(2,1)S(1)} %copy.20) | copy-start | bytes 1572868
  4.7 5.1 %copy-start.2 = (bf16[64,64,128]{2,1,0:T(8,128)(2,1)}, bf16[64,64,128]{2,1,0:T(8,128)(2,1)S(1)}, u32[]{:S(2)}) copy-start(bf16[64,64,128]{2,1,0:T(8,128)(2,1)S(1)} %convolution_convert_fusion) | copy-start | bytes 3145732
  9.8 14.0 %copy-start.5 = (bf16[64,64,128]{2,1,0:T(8,128)(2,1)S(1)}, bf16[64,64,128]{2,1,0:T(8,128)(2,1)}, u32[]{:S(2)}) copy-start(bf16[64,64,128]{2,1,0:T(8,128)(2,1)} %param.11) | copy-start | bytes 3145732
  9.8 18.3 %copy-start.8 = (s32[512]{0:T(512)S(1)}, s32[512]{0:T(512)}, u32[]{:S(2)}) copy-start(s32[512]{0:T(512)} %param.19) | copy-start | bytes 6148
  9.8 18.4 %copy-start.6 = (s32[1024]{0:T(1024)S(1)}, s32[1024]{0:T(1024)}, u32[]{:S(2)}) copy-start(s32[1024]{0:T(1024)} %param.17) | copy-start | bytes 12292
  9.8 18.4 %copy-start.7 = (s32[768]{0:T(1024)S(1)}, s32[768]{0:T(1024)}, u32[]{:S(2)}) copy-start(s32[768]{0:T(1024)} %param.15) | copy-start | bytes 9220
  13.9 82.0 %collective-permute-start = (bf16[48,64,128]{2,1,0:T(8,128)(2,1)}, bf16[48,64,128]{2,1,0:T(8,128)(2,1)}, u32[]{:S(2)}, u32[]{:S(2)}) collective-permute-start(bf16[48,64,128]{2,1,0:T(8,128)(2,1)} %get-tuple-element.6), channel_id=1, source_target_pairs={{0,1},{1,2},{2,3},{3,4},{4,5},{5,6},{6,7},{7,8},{8,9},{9,10},{10,1... | collective-permute-start | bytes 2359304 | tf_op jit(solution)/shard_map/ppermute | solution.py:16
  15.9 82.5 %collective-permute-start.1 = (bf16[48,64,128]{2,1,0:T(8,128)(2,1)}, bf16[48,64,128]{2,1,0:T(8,128)(2,1)}, u32[]{:S(2)}, u32[]{:S(2)}) collective-permute-start(bf16[48,64,128]{2,1,0:T(8,128)(2,1)} %get-tuple-element.7), channel_id=1, source_target_pairs={{1,0},{2,1},{3,2},{4,3},{5,4},{6,5},{7,6},{8,7},{9,8},{10,9},{11,1... | collective-permute-start | bytes 2359304 | tf_op jit(solution)/shard_map/ppermute | solution.py:16
  19.5 80.1 %collective-permute-start.2 = (bf16[48,64,128]{2,1,0:T(8,128)(2,1)}, bf16[48,64,128]{2,1,0:T(8,128)(2,1)}, u32[]{:S(2)}, u32[]{:S(2)}) collective-permute-start(bf16[48,64,128]{2,1,0:T(8,128)(2,1)} %get-tuple-element.8), channel_id=1, source_target_pairs={{0,2},{1,3},{2,4},{3,5},{4,6},{5,7},{6,8},{7,9},{8,10},{9,11},{10,... | collective-permute-start | bytes 2359304 | tf_op jit(solution)/shard_map/ppermute | solution.py:16
  23.8 6.1 %collective-permute-start.7 = (bf16[4,64,128]{2,1,0:T(8,128)(2,1)S(1)}, bf16[4,64,128]{2,1,0:T(8,128)(2,1)S(1)}, u32[]{:S(2)}, u32[]{:S(2)}) collective-permute-start(bf16[4,64,128]{2,1,0:T(8,128)(2,1)S(1)} %get-tuple-element.12), channel_id=1, source_target_pairs={{1,0},{2,1},{3,2},{4,3},{5,4},{6,5},{7,6},{8,7},{9,8},{10,9},{11,1... | collective-permute-start | bytes 196616 | tf_op jit(solution)/shard_map/ppermute | solution.py:27
  25.7 49.7 %collective-permute-start.6 = (bf16[4,64,128]{2,1,0:T(8,128)(2,1)S(1)}, bf16[4,64,128]{2,1,0:T(8,128)(2,1)S(1)}, u32[]{:S(2)}, u32[]{:S(2)}) collective-permute-start(bf16[4,64,128]{2,1,0:T(8,128)(2,1)S(1)} %get-tuple-element.11), channel_id=1, source_target_pairs={{0,1},{1,2},{2,3},{3,4},{4,5},{5,6},{6,7},{7,8},{8,9},{9,10},{10,1... | collective-permute-start | bytes 196616 | tf_op jit(solution)/shard_map/ppermute | solution.py:24
  29.9 71.0 %collective-permute-start.3 = (bf16[48,64,128]{2,1,0:T(8,128)(2,1)}, bf16[48,64,128]{2,1,0:T(8,128)(2,1)}, u32[]{:S(2)}, u32[]{:S(2)}) collective-permute-start(bf16[48,64,128]{2,1,0:T(8,128)(2,1)} %get-tuple-element.9), channel_id=1, source_target_pairs={{2,0},{3,1},{4,2},{5,3},{6,4},{7,5},{8,6},{9,7},{10,8},{11,9},{12,... | collective-permute-start | bytes 2359304 | tf_op jit(solution)/shard_map/ppermute | solution.py:16
  75.4 26.8 %collective-permute-start.4 = (bf16[48,64,128]{2,1,0:T(8,128)(2,1)}, bf16[48,64,128]{2,1,0:T(8,128)(2,1)}, u32[]{:S(2)}, u32[]{:S(2)}) collective-permute-start(bf16[48,64,128]{2,1,0:T(8,128)(2,1)} %get-tuple-element.10), channel_id=1, source_target_pairs={{0,3},{1,4},{2,5},{3,6},{4,7},{5,8},{6,9},{7,10},{8,11},{9,12},{10... | collective-permute-start | bytes 2359304 | tf_op jit(solution)/shard_map/ppermute | solution.py:16
  95.9 21.0 %collective-permute-start.5 = (bf16[48,64,128]{2,1,0:T(8,128)(2,1)S(1)}, bf16[48,64,128]{2,1,0:T(8,128)(2,1)S(1)}, u32[]{:S(2)}, u32[]{:S(2)}) collective-permute-start(bf16[48,64,128]{2,1,0:T(8,128)(2,1)S(1)} %get-tuple-element.5), channel_id=1, source_target_pairs={{3,0},{4,1},{5,2},{6,3},{7,4},{8,5},{9,6},{10,7},{11,8},{12,9},{13... | collective-permute-start | bytes 2359304 | tf_op jit(solution)/shard_map/ppermute | solution.py:16
  117.3 1.2 copy-start.3
  168.9 10.0 %copy-start.1 = (bf16[4096,64]{0,1:T(8,128)(2,1)S(1)}, bf16[4096,64]{0,1:T(8,128)(2,1)}, u32[]{:S(2)}) copy-start(bf16[4096,64]{0,1:T(8,128)(2,1)} %param.13) | copy-start | bytes 1572868
where the time goes:
time: 180 us; the launch traced here: 179 us
  local copies, waits for them, and re-layouts  61.3 us (34%)
  waiting for transfers between devices  58.8 us (33%)
  matrix products  30.8 us (17%)
  starting transfers between devices  19.5 us (11%)
  other arithmetic  8.14 us (5%)
    ppermute x1, waiting for transfers between devices, extended_2(): lax.ppermute(lax.slice_in_dim(block, block.shape[dim] - width, None, axis...  43.6 us
    gather x2, local copies, waits for them, and re-layouts, couple_sum(): picked = source_pool[sources].reshape(clusters, -1, RHS)  29.4 us
    gather x1, local copies, waits for them, and re-layouts, on_device(): nearby = extended[near_source].reshape(leaves, -1, RHS)  18.2 us
    ppermute x6, starting transfers between devices, from_behind(): lax.ppermute(value, axis, [(source, source + steps) for source in range(f...  15.2 us
    ppermute x6, waiting for transfers between devices, from_behind(): lax.ppermute(value, axis, [(source, source + steps) for source in range(f...  13.5 us
    dot_general x1, matrix products, on_device(): jnp.einsum('nlr,nrc->nlc', leaf_bases, fine_total.astype(jnp.bfloat16), p...  10.8 us
    dot_general x1, matrix products, on_device(): jnp.einsum('nik,nkr->nir', near_mats, nearby, preferred_element_type=jnp....  9.97 us
    dot_general x1, matrix products, on_device(): jnp.einsum('pab,pbr->par', stacked, coarse_round, preferred_element_type=...  7.87 us
  transfers between devices with their start and end apart: 8, of which 3 were waited for; matrix products, arithmetic and copies ran while one was open for 14% of the time, Pallas kernels for 0%

commit v1 on v0

v1 whole, which is shorter than its diff:
```python
import functools

import jax
import jax.numpy as jnp
from jax import lax
from jax.experimental import pallas as pl
from jax.experimental.pallas import tpu as pltpu
from jax.sharding import PartitionSpec as P

LEAF = 64
RANK = 64
RHS = 128
HALO = 4
REACH = 3
BLOCK_TARGETS = 8


def from_behind(value, axis, steps):
    count = lax.axis_size(axis)
    first, last = (max(0, -steps), min(count, count - steps))
    return lax.ppermute(value, axis, [(source, source + steps) for source in range(first, last)])


def halo_pieces(block, axis, width):
    count = lax.axis_size(axis)
    forward = [(i, i + 1) for i in range(count - 1)]
    backward = [(target, source) for source, target in forward]
    low = lax.ppermute(lax.slice_in_dim(block, block.shape[0] - width, None, axis=0), axis, forward)
    high = lax.ppermute(lax.slice_in_dim(block, 0, width, axis=0), axis, backward)
    return low, high


def offset_list():
    values = []
    for step in range(REACH):
        values.append(step + 1)
        values.append(-(step + 1))
    return values


def gather_dot(idx, mats, segments, pairs, epilogue=None):
    rows = mats.shape[0]
    width = mats.shape[1] // pairs
    targets = rows // LEAF
    tb = min(BLOCK_TARGETS, targets)
    steps = targets // tb
    n_seg = len(segments)
    seg_arrays = [s[0] for s in segments]
    seg_meta = [(s[1], s[2], s[3]) for s in segments]

    in_specs = [pl.BlockSpec((tb * LEAF, pairs * width), lambda i, ix: (i, 0))]
    for arr in seg_arrays:
        in_specs.append(pl.BlockSpec(arr.shape, lambda i, ix: (0, 0, 0)))
    extra = []
    if epilogue is not None:
        extra, extra_specs, _, out_dtype = epilogue
        in_specs.extend(extra_specs)
    else:
        out_dtype = jnp.float32

    def kernel(idx_ref, mats_ref, *refs):
        seg_refs = refs[:n_seg]
        extra_refs = refs[n_seg:len(refs) - 2]
        out_ref = refs[len(refs) - 2]
        g_ref = refs[len(refs) - 1]
        blk = pl.program_id(0)

        def per_target(tt, carry):
            base = (blk * tb + tt) * pairs

            def per_pair(k, c):
                s = idx_ref[base + k]
                dst = pl.multiple_of(k * width, width)
                for ref, (lo, cnt, row) in zip(seg_refs, seg_meta):
                    @pl.when(jnp.logical_and(s >= lo, s < lo + cnt))
                    def _():
                        at = jnp.clip(s - lo, 0, cnt - 1) + row
                        g_ref[pl.ds(dst, width), :] = ref[at]
                return c

            lax.fori_loop(0, pairs, per_pair, 0)
            r0 = pl.multiple_of(tt * LEAF, LEAF)
            acc = jnp.dot(mats_ref[pl.ds(r0, LEAF), :], g_ref[...], preferred_element_type=jnp.float32)
            if epilogue is None:
                out_ref[tt] = acc
            else:
                out_ref[tt] = epilogue[2](tt, acc, extra_refs)
            return carry

        lax.fori_loop(0, tb, per_target, 0)

    grid_spec = pltpu.PrefetchScalarGridSpec(
        num_scalar_prefetch=1,
        grid=(steps,),
        in_specs=in_specs,
        out_specs=pl.BlockSpec((tb, LEAF, RHS), lambda i, ix: (i, 0, 0)),
        scratch_shapes=[pltpu.VMEM((pairs * width, RHS), jnp.bfloat16)],
    )
    flops = 2 * rows * pairs * width * RHS
    bytes_accessed = mats.size * 2 + sum(a.size * 2 for a in seg_arrays) + targets * LEAF * RHS * 4
    return pl.pallas_call(
        kernel,
        grid_spec=grid_spec,
        out_shape=jax.ShapeDtypeStruct((targets, LEAF, RHS), out_dtype),
        compiler_params=pltpu.CompilerParams(dimension_semantics=("arbitrary",)),
        cost_estimate=pl.CostEstimate(flops=flops, transcendentals=0, bytes_accessed=bytes_accessed),
    )(idx, mats, *seg_arrays, *extra)


def on_device(
    charges,
    leaf_basis,
    transfer,
    near_blocks,
    near_source,
    couple_fine,
    source_fine,
    couple_coarse,
    source_coarse,
    send_fine,
    send_coarse,
):
    leaves = charges.shape[0]
    parents = leaves // 2
    fine_each = send_fine.shape[1] // (2 * REACH)
    coarse_each = send_coarse.shape[1] // (2 * REACH)
    axis = ("leaf", "couple")
    leaf_bases = leaf_basis.reshape(leaves, LEAF, RANK)
    fine_coeffs = jnp.einsum(
        "nlr,nlc->nrc", leaf_bases, charges, preferred_element_type=jnp.float32
    ).astype(jnp.bfloat16)
    stacked = transfer.reshape(parents, 2 * RANK, RANK)
    coarse_coeffs = jnp.einsum(
        "pab,par->pbr",
        stacked,
        fine_coeffs.reshape(parents, 2 * RANK, RHS),
        preferred_element_type=jnp.float32,
    ).astype(jnp.bfloat16)
    fine_out = fine_coeffs[send_fine[0]].reshape(2 * REACH, fine_each, RANK, RHS)
    coarse_out = coarse_coeffs[send_coarse[0]].reshape(2 * REACH, coarse_each, RANK, RHS)
    packets = jnp.concatenate([fine_out, coarse_out], 1)
    incoming = []
    for slot, offset in enumerate(offset_list()):
        incoming.append(from_behind(packets[slot], axis, offset))

    low, high = halo_pieces(charges, axis, HALO)
    near_field = gather_dot(
        near_source,
        near_blocks,
        [(low, 0, HALO, 0), (charges, HALO, leaves, 0), (high, HALO + leaves, HALO, 0)],
        near_source.shape[0] // leaves,
    )

    coarse_segments = [(coarse_coeffs, 0, parents, 0)]
    for slot in range(2 * REACH):
        coarse_segments.append((incoming[slot], parents + slot * coarse_each, coarse_each, fine_each))
    coarse_target = gather_dot(
        source_coarse, couple_coarse, coarse_segments, source_coarse.shape[0] // parents
    )
    coarse_round = coarse_target.astype(jnp.bfloat16)

    fine_segments = [(fine_coeffs, 0, leaves, 0)]
    for slot in range(2 * REACH):
        fine_segments.append((incoming[slot], leaves + slot * fine_each, fine_each, 0))

    tb = min(BLOCK_TARGETS, leaves)

    def finish(tt, acc, refs):
        cr_ref, e_ref, v_ref, near_ref = refs
        r0 = pl.multiple_of(tt * LEAF, LEAF)
        down = jnp.dot(e_ref[pl.ds(r0, RANK), :], cr_ref[tt // 2], preferred_element_type=jnp.float32)
        fine_round = (acc + down).astype(jnp.bfloat16)
        far = jnp.dot(v_ref[pl.ds(r0, LEAF), :], fine_round, preferred_element_type=jnp.float32)
        return (far + near_ref[tt]).astype(jnp.bfloat16)

    epilogue = (
        [coarse_round, transfer, leaf_basis, near_field],
        [
            pl.BlockSpec((tb // 2, RANK, RHS), lambda i, ix: (i, 0, 0)),
            pl.BlockSpec((tb * RANK, RANK), lambda i, ix: (i, 0)),
            pl.BlockSpec((tb * LEAF, RANK), lambda i, ix: (i, 0)),
            pl.BlockSpec((tb, LEAF, RHS), lambda i, ix: (i, 0, 0)),
        ],
        finish,
        jnp.bfloat16,
    )
    return gather_dot(
        source_fine, couple_fine, fine_segments, source_fine.shape[0] // leaves, epilogue
    )


def solution(mesh):
    return jax.shard_map(
        on_device,
        mesh=mesh,
        in_specs=(
            P(("leaf", "couple"), None, None),
            P(("leaf", "couple"), None),
            P(("leaf", "couple"), None),
            P(("leaf", "couple"), None),
            P(("leaf", "couple")),
            P(("leaf", "couple"), None),
            P(("leaf", "couple")),
            P(("leaf", "couple"), None),
            P(("leaf", "couple")),
            P(("leaf", "couple"), None),
            P(("leaf", "couple"), None),
        ),
        out_specs=P(("leaf", "couple"), None, None),
        check_vma=False,
    )
```

time: 180 us -> 205 us (1.14)
  the two profiles are of different devices: /device:TPU:4 before, /device:TPU:24 now
where the time goes in v1:
time: 205 us; the launch traced here: 204 us
  Pallas kernels  149 us (73%)
  starting transfers between devices  24.4 us (12%)
  local copies, waits for them, and re-layouts  11.3 us (6%)
  waiting for transfers between devices  9.54 us (5%)
  other arithmetic  7.03 us (3%)
  matrix products  2.56 us (1%)
    pallas_call x3, Pallas kernels, gather_dot(): pl.pallas_call(kernel, grid_spec=grid_spec, out_shape=jax.ShapeDtypeStruc...  149 us
    ppermute x6, starting transfers between devices, from_behind(): lax.ppermute(value, axis, [(source, source + steps) for source in range(f...  17.1 us
    ppermute x6, waiting for transfers between devices, from_behind(): lax.ppermute(value, axis, [(source, source + steps) for source in range(f...  8.16 us
    unnamed x20, local copies, waits for them, and re-layouts  4.76 us
  transfers between devices with their start and end apart: 8, of which 4 were waited for; matrix products, arithmetic and copies ran while one was open for 3% of the time, Pallas kernels for 18%

profile of v1, /device:TPU:24, one launch (start us, length us, event | category | flops | bytes accessed | tf_op | source)
XLA Modules:
  0.0 204.1 jit_solution(14235085523532988474)
XLA Ops:
  0.0 2.1 %reshape.71 = bf16[64,64,64]{1,0,2:T(8,128)(2,1)S(1)} reshape(bf16[4096,64]{0,1:T(8,128)(2,1)} %param.12) | data formatting | bytes 1048576 | tf_op jit(solution)/shard_map/reshape | solution.py:128
  2.1 0.7 fusion.15
  2.7 0.7 compare_select_fusion
  3.4 0.0 copy-start.6
  3.4 2.2 %convolution_convert_fusion.refs_0_ = bf16[64,64,128]{2,1,0:T(8,128)(2,1)S(1)} fusion(bf16[64,64,128]{2,1,0:T(8,128)(2,1)} %refs_1_.1, bf16[64,64,64]{1,0,2:T(8,128)(2,1)S(1)} %reshape.71), kind=kOutput, calls=%fused_computation.12 | convolution fusion | flops 67633152 | bytes 2621440 | tf_op jit(solution)/shard_map/nlr,nlc->nrc/dot_general | solution.py:129
  5.6 0.0 copy-start
  5.6 2.7 %gather_fusion = bf16[192,64,128]{2,1,0:T(8,128)(2,1)} fusion(bf16[64,64,128]{2,1,0:T(8,128)(2,1)S(1)} %convolution_convert_fusion.refs_0_, s32[1024]{0:T(1024)S(1)} %pad_clamp_fusion.1), kind=kCustom, calls=%fused_computation | custom fusion | bytes 6292224 | tf_op jit(solution)/shard_map/gather | solution.py:139
  8.3 0.0 copy-done.6
  8.3 0.4 fusion.refs_0_
  8.7 0.0 copy-done
  8.7 0.0 copy-start.1
  8.7 0.8 gather_fusion.1
  9.6 3.5 %fusion.12 = (bf16[48,64,128]{2,1,0:T(8,128)(2,1)}, bf16[48,64,128]{2,1,0:T(8,128)(2,1)S(1)}, bf16[48,64,128]{2,1,0:T(8,128)(2,1)}, bf16[48,64,128]{2,1,0:T(8,12...) fusion(bf16[6,16,64,128]{3,2,1,0:T(8,128)(2,1)S(1)} %bitcast.37, bf16[6,32,64,128]{3,2,1,0:T(8,128)(2,1)} %bitcast.36), kind=kLoop, calls=%fused_computation.27 | loop fusion | flops 2359296 | bytes 9437184 | tf_op jit(solution)/shard_map/squeeze | solution.py:144
  13.1 0.0 copy-done.1
  13.1 1.9 collective-permute-start
  15.1 0.9 fusion.16
  16.0 3.5 %collective-permute-start.6 = (bf16[4,64,128]{2,1,0:T(8,128)(2,1)S(1)}, bf16[4,64,128]{2,1,0:T(8,128)(2,1)S(1)}, u32[]{:S(2)}, u32[]{:S(2)}) collective-permute-start(bf16[4,64,128]{2,1,0:T(8,128)(2,1)S(1)} %get-tuple-element.12), channel_id=1, source_target_pairs={{0,1},{1,2},{2,3},{3,4},{4,5},{5,6},{6,7},{7,8},{8,9},{9,10},{10,1... | collective-permute-start | bytes 196616 | tf_op jit(solution)/shard_map/ppermute | solution.py:28
  19.5 3.8 %collective-permute-start.7 = (bf16[4,64,128]{2,1,0:T(8,128)(2,1)S(1)}, bf16[4,64,128]{2,1,0:T(8,128)(2,1)S(1)}, u32[]{:S(2)}, u32[]{:S(2)}) collective-permute-start(bf16[4,64,128]{2,1,0:T(8,128)(2,1)S(1)} %get-tuple-element.11), channel_id=1, source_target_pairs={{1,0},{2,1},{3,2},{4,3},{5,4},{6,5},{7,6},{8,7},{9,8},{10,9},{11,1... | collective-permute-start | bytes 196616 | tf_op jit(solution)/shard_map/ppermute | solution.py:29
  23.3 2.4 %collective-permute-start.1 = (bf16[48,64,128]{2,1,0:T(8,128)(2,1)}, bf16[48,64,128]{2,1,0:T(8,128)(2,1)S(1)}, u32[]{:S(2)}, u32[]{:S(2)}) collective-permute-start(bf16[48,64,128]{2,1,0:T(8,128)(2,1)} %get-tuple-element.7), channel_id=1, source_target_pairs={{1,0},{2,1},{3,2},{4,3},{5,4},{6,5},{7,6},{8,7},{9,8},{10,9},{11,1... | collective-permute-start | bytes 2359304 | tf_op jit(solution)/shard_map/ppermute | solution.py:21
  25.7 1.9 collective-permute-start.2
  27.7 1.4 collective-permute-done.6.refs_0_
  29.1 0.0 copy-start.7
  29.1 4.4 %collective-permute-start.3 = (bf16[48,64,128]{2,1,0:T(8,128)(2,1)}, bf16[48,64,128]{2,1,0:T(8,128)(2,1)S(1)}, u32[]{:S(2)}, u32[]{:S(2)}) collective-permute-start(bf16[48,64,128]{2,1,0:T(8,128)(2,1)} %get-tuple-element.9), channel_id=1, source_target_pairs={{2,0},{3,1},{4,2},{5,3},{6,4},{7,5},{8,6},{9,7},{10,8},{11,9},{12,... | collective-permute-start | bytes 2359304 | tf_op jit(solution)/shard_map/ppermute | solution.py:21
  33.4 0.0 collective-permute-done.7.refs_2_
  33.4 0.0 copy-start.8
  33.4 1.9 collective-permute-start.4
  35.4 0.0 collective-permute-done.refs_1_
  35.4 0.0 copy-start.2
  35.4 4.5 %collective-permute-start.5 = (bf16[48,64,128]{2,1,0:T(8,128)(2,1)}, bf16[48,64,128]{2,1,0:T(8,128)(2,1)}, u32[]{:S(2)}, u32[]{:S(2)}) collective-permute-start(bf16[48,64,128]{2,1,0:T(8,128)(2,1)} %get-tuple-element.5), channel_id=1, source_target_pairs={{3,0},{4,1},{5,2},{6,3},{7,4},{8,5},{9,6},{10,7},{11,8},{12,9},{13... | collective-permute-start | bytes 2359304 | tf_op jit(solution)/shard_map/ppermute | solution.py:21
  39.9 2.4 %copy.18.refs_8_ = bf16[4096,64]{1,0:T(8,128)(2,1)} copy(bf16[4096,64]{0,1:T(8,128)(2,1)} %param.13) | data formatting | bytes 1048576 | tf_op args[2]
  42.3 2.4 %copy.19.refs_9_ = bf16[4096,64]{1,0:T(8,128)(2,1)} copy(bf16[4096,64]{0,1:T(8,128)(2,1)} %param.12) | data formatting | bytes 1048576 | tf_op args[1]
  44.7 0.0 copy-done.7
  44.7 0.0 copy-done.8
  44.7 35.9 %shard_map.110.refs_10_ = f32[64,64,128]{2,1,0:T(8,128)} custom-call(s32[768]{0:T(1024)} %idx_ref.4, bf16[4096,768]{1,0:T(8,128)(2,1)} %mats_ref.4, bf16[4,64,128]{2,1,0:T(8,128)(2,1)} %copy-done.7, bf16[64,64,128]{2,1,0:T(8,128)(2,1)} %refs_1_.1, bf16[4,64,128]{2,1,0:T(8,128)(2,1)} %copy-done.8), custom_call_target="tpu_custom_call" | custom-call | flops 805306368 | bytes 9568256 | tf_op jit(solution)/shard_map/pallas_call | solution.py:101
  80.6 0.0 copy-done.2
  80.6 0.0 collective-permute-done.1.refs_2_
  80.6 0.0 copy-start.3
  80.6 0.0 collective-permute-done.2.refs_3_
  80.6 0.0 copy-start.4
  80.6 5.3 %collective-permute-done.3.refs_4_ = bf16[48,64,128]{2,1,0:T(8,128)(2,1)S(1)} collective-permute-done((bf16[48,64,128]{2,1,0:T(8,128)(2,1)}, bf16[48,64,128]{2,1,0:T(8,128)(2,1)S(1)}, u32[]{:S(2)}, u32[]{:S(2)}) %collective-permute-start.3) | collective-permute-done | bytes 786464 | tf_op jit(solution)/shard_map/ppermute | solution.py:21
  85.9 0.3 collective-permute-done.4.refs_5_
  86.1 2.6 %collective-permute-done.5.refs_6_ = bf16[48,64,128]{2,1,0:T(8,128)(2,1)} collective-permute-done((bf16[48,64,128]{2,1,0:T(8,128)(2,1)}, bf16[48,64,128]{2,1,0:T(8,128)(2,1)}, u32[]{:S(2)}, u32[]{:S(2)}) %collective-permute-start.5) | collective-permute-done | bytes 786464 | tf_op jit(solution)/shard_map/ppermute | solution.py:21
  88.7 0.0 copy-done.3
  88.7 0.0 copy-done.4
  88.8 0.0 copy-done.5
  88.8 36.5 %shard_map.109 = f32[32,64,128]{2,1,0:T(8,128)} custom-call(s32[512]{0:T(512)} %idx_ref.3, bf16[2048,1024]{1,0:T(8,128)(2,1)} %mats_ref.3, bf16[32,64,128]{2,1,0:T(8,128)(2,1)} %copy-done.1, bf16[48,64,128]{2,1,0:T(8,128)(2,1)} %copy-done.2, bf16[48,64,128]{2,1,0:T(8,128)(2,1)} %copy-done.3, bf16[48,64,128]{2,1,0:T(8,128)(2,1)} %copy-done.4, ...), custom_call_target="tpu_custom_call" | custom-call | flops 536870912 | bytes 10485760 | tf_op jit(solution)/shard_map/pallas_call | solution.py:101
  125.2 2.1 %convert_element_type.14.refs_7_ = bf16[32,64,128]{2,1,0:T(8,128)(2,1)} convert(f32[32,64,128]{2,1,0:T(8,128)} %shard_map.109) | non-fusion elementwise | flops 262144 | bytes 1572864 | tf_op jit(solution)/shard_map/convert_element_type | solution.py:160
  127.4 76.7 %shard_map.111 = bf16[64,64,128]{2,1,0:T(8,128)(2,1)} custom-call(s32[1024]{0:T(1024)} %idx_ref.5, bf16[4096,1024]{1,0:T(8,128)(2,1)} %mats_ref.5, bf16[64,64,128]{2,1,0:T(8,128)(2,1)} %copy-done, bf16[48,64,128]{2,1,0:T(8,128)(2,1)} %copy-done.2, bf16[48,64,128]{2,1,0:T(8,128)(2,1)} %copy-done.3, bf16[48,64,128]{2,1,0:T(8,128)(2,1)} %copy-done.4, ...), custom_call_target="tpu_custom_call" | custom-call | flops 1073741824 | bytes 16252928 | tf_op jit(solution)/shard_map/pallas_call | solution.py:101
  (3 shorter events, 0.0 us)
Async XLA Ops:
  3.4 4.9 %copy-start.6 = (bf16[4096,64]{0,1:T(8,128)(2,1)S(1)}, bf16[4096,64]{0,1:T(8,128)(2,1)}, u32[]{:S(2)}) copy-start(bf16[4096,64]{0,1:T(8,128)(2,1)} %param.13) | copy-start | bytes 1572868
  5.6 3.1 %copy-start = (bf16[64,64,128]{2,1,0:T(8,128)(2,1)}, bf16[64,64,128]{2,1,0:T(8,128)(2,1)S(1)}, u32[]{:S(2)}) copy-start(bf16[64,64,128]{2,1,0:T(8,128)(2,1)S(1)} %convolution_convert_fusion.refs_0_) | copy-start | bytes 3145732
  8.7 4.4 %copy-start.1 = (bf16[32,64,128]{2,1,0:T(8,128)(2,1)}, bf16[32,64,128]{2,1,0:T(8,128)(2,1)S(1)}, u32[]{:S(2)}) copy-start(bf16[32,64,128]{2,1,0:T(8,128)(2,1)S(1)} %fusion.refs_0_) | copy-start | bytes 1572868
  13.1 22.2 %collective-permute-start = (bf16[48,64,128]{2,1,0:T(8,128)(2,1)S(1)}, bf16[48,64,128]{2,1,0:T(8,128)(2,1)S(1)}, u32[]{:S(2)}, u32[]{:S(2)}) collective-permute-start(bf16[48,64,128]{2,1,0:T(8,128)(2,1)S(1)} %get-tuple-element.6), channel_id=1, source_target_pairs={{0,1},{1,2},{2,3},{3,4},{4,5},{5,6},{6,7},{7,8},{8,9},{9,10},{10,1... | collective-permute-start | bytes 2359304 | tf_op jit(solution)/shard_map/ppermute | solution.py:21
  16.0 13.1 %collective-permute-start.6 = (bf16[4,64,128]{2,1,0:T(8,128)(2,1)S(1)}, bf16[4,64,128]{2,1,0:T(8,128)(2,1)S(1)}, u32[]{:S(2)}, u32[]{:S(2)}) collective-permute-start(bf16[4,64,128]{2,1,0:T(8,128)(2,1)S(1)} %get-tuple-element.12), channel_id=1, source_target_pairs={{0,1},{1,2},{2,3},{3,4},{4,5},{5,6},{6,7},{7,8},{8,9},{9,10},{10,1... | collective-permute-start | bytes 196616 | tf_op jit(solution)/shard_map/ppermute | solution.py:28
  19.5 13.9 %collective-permute-start.7 = (bf16[4,64,128]{2,1,0:T(8,128)(2,1)S(1)}, bf16[4,64,128]{2,1,0:T(8,128)(2,1)S(1)}, u32[]{:S(2)}, u32[]{:S(2)}) collective-permute-start(bf16[4,64,128]{2,1,0:T(8,128)(2,1)S(1)} %get-tuple-element.11), channel_id=1, source_target_pairs={{1,0},{2,1},{3,2},{4,3},{5,4},{6,5},{7,6},{8,7},{9,8},{10,9},{11,1... | collective-permute-start | bytes 196616 | tf_op jit(solution)/shard_map/ppermute | solution.py:29
  23.3 57.2 %collective-permute-start.1 = (bf16[48,64,128]{2,1,0:T(8,128)(2,1)}, bf16[48,64,128]{2,1,0:T(8,128)(2,1)S(1)}, u32[]{:S(2)}, u32[]{:S(2)}) collective-permute-start(bf16[48,64,128]{2,1,0:T(8,128)(2,1)} %get-tuple-element.7), channel_id=1, source_target_pairs={{1,0},{2,1},{3,2},{4,3},{5,4},{6,5},{7,6},{8,7},{9,8},{10,9},{11,1... | collective-permute-start | bytes 2359304 | tf_op jit(solution)/shard_map/ppermute | solution.py:21
  25.7 54.8 %collective-permute-start.2 = (bf16[48,64,128]{2,1,0:T(8,128)(2,1)}, bf16[48,64,128]{2,1,0:T(8,128)(2,1)S(1)}, u32[]{:S(2)}, u32[]{:S(2)}) collective-permute-start(bf16[48,64,128]{2,1,0:T(8,128)(2,1)} %get-tuple-element.8), channel_id=1, source_target_pairs={{0,2},{1,3},{2,4},{3,5},{4,6},{5,7},{6,8},{7,9},{8,10},{9,11},{10,... | collective-permute-start | bytes 2359304 | tf_op jit(solution)/shard_map/ppermute | solution.py:21
  29.1 15.6 %copy-start.7 = (bf16[4,64,128]{2,1,0:T(8,128)(2,1)}, bf16[4,64,128]{2,1,0:T(8,128)(2,1)S(1)}, u32[]{:S(2)}) copy-start(bf16[4,64,128]{2,1,0:T(8,128)(2,1)S(1)} %collective-permute-done.6.refs_0_) | copy-start | bytes 196612
  29.1 56.8 %collective-permute-start.3 = (bf16[48,64,128]{2,1,0:T(8,128)(2,1)}, bf16[48,64,128]{2,1,0:T(8,128)(2,1)S(1)}, u32[]{:S(2)}, u32[]{:S(2)}) collective-permute-start(bf16[48,64,128]{2,1,0:T(8,128)(2,1)} %get-tuple-element.9), channel_id=1, source_target_pairs={{2,0},{3,1},{4,2},{5,3},{6,4},{7,5},{8,6},{9,7},{10,8},{11,9},{12,... | collective-permute-start | bytes 2359304 | tf_op jit(solution)/shard_map/ppermute | solution.py:21
  33.4 11.2 %copy-start.8 = (bf16[4,64,128]{2,1,0:T(8,128)(2,1)}, bf16[4,64,128]{2,1,0:T(8,128)(2,1)S(1)}, u32[]{:S(2)}) copy-start(bf16[4,64,128]{2,1,0:T(8,128)(2,1)S(1)} %collective-permute-done.7.refs_2_) | copy-start | bytes 196612
  33.4 52.7 %collective-permute-start.4 = (bf16[48,64,128]{2,1,0:T(8,128)(2,1)}, bf16[48,64,128]{2,1,0:T(8,128)(2,1)}, u32[]{:S(2)}, u32[]{:S(2)}) collective-permute-start(bf16[48,64,128]{2,1,0:T(8,128)(2,1)} %get-tuple-element.10), channel_id=1, source_target_pairs={{0,3},{1,4},{2,5},{3,6},{4,7},{5,8},{6,9},{7,10},{8,11},{9,12},{10... | collective-permute-start | bytes 2359304 | tf_op jit(solution)/shard_map/ppermute | solution.py:21
  35.4 45.2 %copy-start.2 = (bf16[48,64,128]{2,1,0:T(8,128)(2,1)}, bf16[48,64,128]{2,1,0:T(8,128)(2,1)S(1)}, u32[]{:S(2)}) copy-start(bf16[48,64,128]{2,1,0:T(8,128)(2,1)S(1)} %collective-permute-done.refs_1_) | copy-start | bytes 2359300
  35.4 53.4 %collective-permute-start.5 = (bf16[48,64,128]{2,1,0:T(8,128)(2,1)}, bf16[48,64,128]{2,1,0:T(8,128)(2,1)}, u32[]{:S(2)}, u32[]{:S(2)}) collective-permute-start(bf16[48,64,128]{2,1,0:T(8,128)(2,1)} %get-tuple-element.5), channel_id=1, source_target_pairs={{3,0},{4,1},{5,2},{6,3},{7,4},{8,5},{9,6},{10,7},{11,8},{12,9},{13... | collective-permute-start | bytes 2359304 | tf_op jit(solution)/shard_map/ppermute | solution.py:21
  80.6 8.2 %copy-start.3 = (bf16[48,64,128]{2,1,0:T(8,128)(2,1)}, bf16[48,64,128]{2,1,0:T(8,128)(2,1)S(1)}, u32[]{:S(2)}) copy-start(bf16[48,64,128]{2,1,0:T(8,128)(2,1)S(1)} %collective-permute-done.1.refs_2_) | copy-start | bytes 2359300
  80.6 8.2 %copy-start.4 = (bf16[48,64,128]{2,1,0:T(8,128)(2,1)}, bf16[48,64,128]{2,1,0:T(8,128)(2,1)S(1)}, u32[]{:S(2)}) copy-start(bf16[48,64,128]{2,1,0:T(8,128)(2,1)S(1)} %collective-permute-done.2.refs_3_) | copy-start | bytes 2359300
  85.9 2.9 %copy-start.5 = (bf16[48,64,128]{2,1,0:T(8,128)(2,1)}, bf16[48,64,128]{2,1,0:T(8,128)(2,1)S(1)}, u32[]{:S(2)}) copy-start(bf16[48,64,128]{2,1,0:T(8,128)(2,1)S(1)} %collective-permute-done.3.refs_4_) | copy-start | bytes 2359300

commit v2 on v1

--- a/solution.py
+++ b/solution.py
@@ -47,10 +47,11 @@
     n_seg = len(segments)
     seg_arrays = [s[0] for s in segments]
     seg_meta = [(s[1], s[2], s[3]) for s in segments]
+    total = sum(s[2] for s in segments)
 
     in_specs = [pl.BlockSpec((tb * LEAF, pairs * width), lambda i, ix: (i, 0))]
     for arr in seg_arrays:
-        in_specs.append(pl.BlockSpec(arr.shape, lambda i, ix: (0, 0, 0)))
+        in_specs.append(pl.BlockSpec(memory_space=pl.ANY))
     extra = []
     if epilogue is not None:
         extra, extra_specs, _, out_dtype = epilogue
@@ -60,25 +61,25 @@
 
     def kernel(idx_ref, mats_ref, *refs):
         seg_refs = refs[:n_seg]
-        extra_refs = refs[n_seg:len(refs) - 2]
-        out_ref = refs[len(refs) - 2]
-        g_ref = refs[len(refs) - 1]
+        extra_refs = refs[n_seg:len(refs) - 4]
+        out_ref, g_ref, pool_ref, sem = refs[len(refs) - 4:]
         blk = pl.program_id(0)
+
+        @pl.when(blk == 0)
+        def _():
+            copies = []
+            for j, (ref, (lo, cnt, row)) in enumerate(zip(seg_refs, seg_meta)):
+                cp = pltpu.make_async_copy(ref.at[pl.ds(row, cnt)], pool_ref.at[pl.ds(lo, cnt)], sem.at[j])
+                cp.start()
+                copies.append(cp)
+            for cp in copies:
+                cp.wait()
 
         def per_target(tt, carry):
             base = (blk * tb + tt) * pairs
-
-            def per_pair(k, c):
-                s = idx_ref[base + k]
-                dst = pl.multiple_of(k * width, width)
-                for ref, (lo, cnt, row) in zip(seg_refs, seg_meta):
-                    @pl.when(jnp.logical_and(s >= lo, s < lo + cnt))
-                    def _():
-                        at = jnp.clip(s - lo, 0, cnt - 1) + row
-                        g_ref[pl.ds(dst, width), :] = ref[at]
-                return c
-
-            lax.fori_loop(0, pairs, per_pair, 0)
+            for k in range(pairs):
+                s = jnp.clip(idx_ref[base + k], 0, total - 1)
+                g_ref[k * width:(k + 1) * width, :] = pool_ref[s]
             r0 = pl.multiple_of(tt * LEAF, LEAF)
             acc = jnp.dot(mats_ref[pl.ds(r0, LEAF), :], g_ref[...], preferred_element_type=jnp.float32)
             if epilogue is None:
@@ -94,10 +95,14 @@
         grid=(steps,),
         in_specs=in_specs,
         out_specs=pl.BlockSpec((tb, LEAF, RHS), lambda i, ix: (i, 0, 0)),
-        scratch_shapes=[pltpu.VMEM((pairs * width, RHS), jnp.bfloat16)],
+        scratch_shapes=[
+            pltpu.VMEM((pairs * width, RHS), jnp.bfloat16),
+            pltpu.VMEM((total, width, RHS), jnp.bfloat16),
+            pltpu.SemaphoreType.DMA((n_seg,)),
+        ],
     )
     flops = 2 * rows * pairs * width * RHS
-    bytes_accessed = mats.size * 2 + sum(a.size * 2 for a in seg_arrays) + targets * LEAF * RHS * 4
+    bytes_accessed = mats.size * 2 + total * width * RHS * 2 + targets * LEAF * RHS * 4
     return pl.pallas_call(
         kernel,
         grid_spec=grid_spec,

time: 205 us -> 129 us (0.63)
  Pallas kernels: 149 us -> 53.9 us
  waiting for transfers between devices: 9.54 us -> 29 us
    pallas_call x3, Pallas kernels: 149 us -> 53.9 us  [gather_dot(): pl.pallas_call(kernel, grid_spec=grid_spec, out_shape=jax.ShapeDtypeStruc...]
    ppermute x6, waiting for transfers between devices: 8.16 us -> 27.6 us  [from_behind(): lax.ppermute(value, axis, [(source, source + steps) for source in range(f...]
  transfers between devices with their start and end apart: 8 -> 8, of which waited for: 4 -> 5; matrix products, arithmetic and copies ran while one was open for 3% -> 4% of each run, Pallas kernels for 18% -> 13%
where the time goes in v2:
time: 129 us; the launch traced here: 128 us
  Pallas kernels  53.9 us (42%)
  waiting for transfers between devices  29 us (22%)
  starting transfers between devices  24.4 us (19%)
  local copies, waits for them, and re-layouts  11.3 us (9%)
  other arithmetic  7.03 us (5%)
  matrix products  2.56 us (2%)
    pallas_call x3, Pallas kernels, gather_dot(): pl.pallas_call(kernel, grid_spec=grid_spec, out_shape=jax.ShapeDtypeStruc...  53.9 us
    ppermute x6, waiting for transfers between devices, from_behind(): lax.ppermute(value, axis, [(source, source + steps) for source in range(f...  27.6 us
    ppermute x6, starting transfers between devices, from_behind(): lax.ppermute(value, axis, [(source, source + steps) for source in range(f...  17.1 us
    unnamed x20, local copies, waits for them, and re-layouts  4.76 us
    ppermute x1, starting transfers between devices, halo_pieces(): lax.ppermute(lax.slice_in_dim(block, 0, width, axis=0), axis, backward)  3.83 us
    squeeze x1, other arithmetic, on_device(): incoming.append(from_behind(packets[slot], axis, offset))  3.53 us
    ppermute x1, starting transfers between devices, halo_pieces(): lax.ppermute(lax.slice_in_dim(block, block.shape[0] - width, None, axis=0...  3.53 us
    gather x1, local copies, waits for them, and re-layouts, on_device(): fine_coeffs[send_fine[0]].reshape(2 * REACH, fine_each, RANK, RHS)  2.71 us
  transfers between devices with their start and end apart: 8, of which 5 were waited for; matrix products, arithmetic and copies ran while one was open for 4% of the time, Pallas kernels for 13%

profile of v2, /device:TPU:24, one launch (start us, length us, event | category | flops | bytes accessed | tf_op | source)
XLA Modules:
  0.0 128.3 jit_solution(3524625049804827912)
XLA Ops:
  0.0 2.1 %reshape.71 = bf16[64,64,64]{1,0,2:T(8,128)(2,1)S(1)} reshape(bf16[4096,64]{0,1:T(8,128)(2,1)} %param.12) | data formatting | bytes 1048576 | tf_op jit(solution)/shard_map/reshape | solution.py:133
  2.1 0.7 fusion.15
  2.7 0.7 compare_select_fusion
  3.4 0.0 copy-start.6
  3.4 2.2 %convolution_convert_fusion.refs_0_ = bf16[64,64,128]{2,1,0:T(8,128)(2,1)S(1)} fusion(bf16[64,64,128]{2,1,0:T(8,128)(2,1)} %refs_1_.1, bf16[64,64,64]{1,0,2:T(8,128)(2,1)S(1)} %reshape.71), kind=kOutput, calls=%fused_computation.12 | convolution fusion | flops 67633152 | bytes 2621440 | tf_op jit(solution)/shard_map/nlr,nlc->nrc/dot_general | solution.py:134
  5.6 0.0 copy-start
  5.6 2.7 %gather_fusion = bf16[192,64,128]{2,1,0:T(8,128)(2,1)} fusion(bf16[64,64,128]{2,1,0:T(8,128)(2,1)S(1)} %convolution_convert_fusion.refs_0_, s32[1024]{0:T(1024)S(1)} %pad_clamp_fusion.1), kind=kCustom, calls=%fused_computation | custom fusion | bytes 6292224 | tf_op jit(solution)/shard_map/gather | solution.py:144
  8.3 0.0 copy-done.6
  8.3 0.4 fusion.refs_0_
  8.7 0.0 copy-done
  8.7 0.0 copy-start.1
  8.7 0.8 gather_fusion.1
  9.6 3.5 %fusion.12 = (bf16[48,64,128]{2,1,0:T(8,128)(2,1)}, bf16[48,64,128]{2,1,0:T(8,128)(2,1)S(1)}, bf16[48,64,128]{2,1,0:T(8,128)(2,1)}, bf16[48,64,128]{2,1,0:T(8,12...) fusion(bf16[6,16,64,128]{3,2,1,0:T(8,128)(2,1)S(1)} %bitcast.37, bf16[6,32,64,128]{3,2,1,0:T(8,128)(2,1)} %bitcast.36), kind=kLoop, calls=%fused_computation.27 | loop fusion | flops 2359296 | bytes 9437184 | tf_op jit(solution)/shard_map/squeeze | solution.py:149
  13.1 0.0 copy-done.1
  13.1 1.9 %collective-permute-start = (bf16[48,64,128]{2,1,0:T(8,128)(2,1)S(1)}, bf16[48,64,128]{2,1,0:T(8,128)(2,1)S(1)}, u32[]{:S(2)}, u32[]{:S(2)}) collective-permute-start(bf16[48,64,128]{2,1,0:T(8,128)(2,1)S(1)} %get-tuple-element.6), channel_id=1, source_target_pairs={{0,1},{1,2},{2,3},{3,4},{4,5},{5,6},{6,7},{7,8},{8,9},{9,10},{10,1... | collective-permute-start | bytes 2359304 | tf_op jit(solution)/shard_map/ppermute | solution.py:21
  15.1 0.9 fusion.16
  16.0 3.5 %collective-permute-start.6 = (bf16[4,64,128]{2,1,0:T(8,128)(2,1)S(1)}, bf16[4,64,128]{2,1,0:T(8,128)(2,1)S(1)}, u32[]{:S(2)}, u32[]{:S(2)}) collective-permute-start(bf16[4,64,128]{2,1,0:T(8,128)(2,1)S(1)} %get-tuple-element.12), channel_id=1, source_target_pairs={{0,1},{1,2},{2,3},{3,4},{4,5},{5,6},{6,7},{7,8},{8,9},{9,10},{10,1... | collective-permute-start | bytes 196616 | tf_op jit(solution)/shard_map/ppermute | solution.py:28
  19.5 3.8 %collective-permute-start.7 = (bf16[4,64,128]{2,1,0:T(8,128)(2,1)S(1)}, bf16[4,64,128]{2,1,0:T(8,128)(2,1)S(1)}, u32[]{:S(2)}, u32[]{:S(2)}) collective-permute-start(bf16[4,64,128]{2,1,0:T(8,128)(2,1)S(1)} %get-tuple-element.11), channel_id=1, source_target_pairs={{1,0},{2,1},{3,2},{4,3},{5,4},{6,5},{7,6},{8,7},{9,8},{10,9},{11,1... | collective-permute-start | bytes 196616 | tf_op jit(solution)/shard_map/ppermute | solution.py:29
  23.3 2.4 %collective-permute-start.1 = (bf16[48,64,128]{2,1,0:T(8,128)(2,1)}, bf16[48,64,128]{2,1,0:T(8,128)(2,1)S(1)}, u32[]{:S(2)}, u32[]{:S(2)}) collective-permute-start(bf16[48,64,128]{2,1,0:T(8,128)(2,1)} %get-tuple-element.7), channel_id=1, source_target_pairs={{1,0},{2,1},{3,2},{4,3},{5,4},{6,5},{7,6},{8,7},{9,8},{10,9},{11,1... | collective-permute-start | bytes 2359304 | tf_op jit(solution)/shard_map/ppermute | solution.py:21
  25.7 1.9 %collective-permute-start.2 = (bf16[48,64,128]{2,1,0:T(8,128)(2,1)}, bf16[48,64,128]{2,1,0:T(8,128)(2,1)S(1)}, u32[]{:S(2)}, u32[]{:S(2)}) collective-permute-start(bf16[48,64,128]{2,1,0:T(8,128)(2,1)} %get-tuple-element.8), channel_id=1, source_target_pairs={{0,2},{1,3},{2,4},{3,5},{4,6},{5,7},{6,8},{7,9},{8,10},{9,11},{10,... | collective-permute-start | bytes 2359304 | tf_op jit(solution)/shard_map/ppermute | solution.py:21
  27.7 1.4 %collective-permute-done.6.refs_0_ = bf16[4,64,128]{2,1,0:T(8,128)(2,1)S(1)} collective-permute-done((bf16[4,64,128]{2,1,0:T(8,128)(2,1)S(1)}, bf16[4,64,128]{2,1,0:T(8,128)(2,1)S(1)}, u32[]{:S(2)}, u32[]{:S(2)}) %collective-permute-start.6) | collective-permute-done | bytes 65568 | tf_op jit(solution)/shard_map/ppermute | solution.py:28
  29.1 0.0 copy-start.7
  29.1 4.4 %collective-permute-start.3 = (bf16[48,64,128]{2,1,0:T(8,128)(2,1)}, bf16[48,64,128]{2,1,0:T(8,128)(2,1)S(1)}, u32[]{:S(2)}, u32[]{:S(2)}) collective-permute-start(bf16[48,64,128]{2,1,0:T(8,128)(2,1)} %get-tuple-element.9), channel_id=1, source_target_pairs={{2,0},{3,1},{4,2},{5,3},{6,4},{7,5},{8,6},{9,7},{10,8},{11,9},{12,... | collective-permute-start | bytes 2359304 | tf_op jit(solution)/shard_map/ppermute | solution.py:21
  33.4 0.0 collective-permute-done.7.refs_2_
  33.4 0.0 copy-start.8
  33.4 1.9 %collective-permute-start.4 = (bf16[48,64,128]{2,1,0:T(8,128)(2,1)}, bf16[48,64,128]{2,1,0:T(8,128)(2,1)}, u32[]{:S(2)}, u32[]{:S(2)}) collective-permute-start(bf16[48,64,128]{2,1,0:T(8,128)(2,1)} %get-tuple-element.10), channel_id=1, source_target_pairs={{0,3},{1,4},{2,5},{3,6},{4,7},{5,8},{6,9},{7,10},{8,11},{9,12},{10... | collective-permute-start | bytes 2359304 | tf_op jit(solution)/shard_map/ppermute | solution.py:21
  35.4 0.0 collective-permute-done.refs_1_
  35.4 0.0 copy-start.2
  35.4 4.5 %collective-permute-start.5 = (bf16[48,64,128]{2,1,0:T(8,128)(2,1)}, bf16[48,64,128]{2,1,0:T(8,128)(2,1)}, u32[]{:S(2)}, u32[]{:S(2)}) collective-permute-start(bf16[48,64,128]{2,1,0:T(8,128)(2,1)} %get-tuple-element.5), channel_id=1, source_target_pairs={{3,0},{4,1},{5,2},{6,3},{7,4},{8,5},{9,6},{10,7},{11,8},{12,9},{13... | collective-permute-start | bytes 2359304 | tf_op jit(solution)/shard_map/ppermute | solution.py:21
  39.9 2.4 %copy.18.refs_8_ = bf16[4096,64]{1,0:T(8,128)(2,1)} copy(bf16[4096,64]{0,1:T(8,128)(2,1)} %param.13) | data formatting | bytes 1048576 | tf_op args[2]
  42.3 2.4 %copy.19.refs_9_ = bf16[4096,64]{1,0:T(8,128)(2,1)} copy(bf16[4096,64]{0,1:T(8,128)(2,1)} %param.12) | data formatting | bytes 1048576 | tf_op args[1]
  44.7 0.0 copy-done.7
  44.7 0.0 copy-done.8
  44.7 16.5 %shard_map.110.refs_10_ = f32[64,64,128]{2,1,0:T(8,128)} custom-call(s32[768]{0:T(1024)} %idx_ref.4, bf16[4096,768]{1,0:T(8,128)(2,1)} %mats_ref.4, bf16[4,64,128]{2,1,0:T(8,128)(2,1)} %copy-done.7, bf16[64,64,128]{2,1,0:T(8,128)(2,1)} %refs_1_.1, bf16[4,64,128]{2,1,0:T(8,128)(2,1)} %copy-done.8), custom_call_target="tpu_custom_call" | custom-call | flops 805306368 | bytes 9568256 | tf_op jit(solution)/shard_map/pallas_call | solution.py:106
  61.1 0.0 copy-done.2
  61.1 0.0 collective-permute-done.1.refs_2_
  61.2 0.0 copy-start.3
  61.2 16.5 %collective-permute-done.2.refs_3_ = bf16[48,64,128]{2,1,0:T(8,128)(2,1)S(1)} collective-permute-done((bf16[48,64,128]{2,1,0:T(8,128)(2,1)}, bf16[48,64,128]{2,1,0:T(8,128)(2,1)S(1)}, u32[]{:S(2)}, u32[]{:S(2)}) %collective-permute-start.2) | collective-permute-done | bytes 786464 | tf_op jit(solution)/shard_map/ppermute | solution.py:21
  77.7 0.0 copy-start.4
  77.7 8.2 %collective-permute-done.3.refs_4_ = bf16[48,64,128]{2,1,0:T(8,128)(2,1)S(1)} collective-permute-done((bf16[48,64,128]{2,1,0:T(8,128)(2,1)}, bf16[48,64,128]{2,1,0:T(8,128)(2,1)S(1)}, u32[]{:S(2)}, u32[]{:S(2)}) %collective-permute-start.3) | collective-permute-done | bytes 786464 | tf_op jit(solution)/shard_map/ppermute | solution.py:21
  85.9 0.3 collective-permute-done.4.refs_5_
  86.1 2.6 %collective-permute-done.5.refs_6_ = bf16[48,64,128]{2,1,0:T(8,128)(2,1)} collective-permute-done((bf16[48,64,128]{2,1,0:T(8,128)(2,1)}, bf16[48,64,128]{2,1,0:T(8,128)(2,1)}, u32[]{:S(2)}, u32[]{:S(2)}) %collective-permute-start.5) | collective-permute-done | bytes 786464 | tf_op jit(solution)/shard_map/ppermute | solution.py:21
  88.7 0.0 copy-done.3
  88.7 0.0 copy-done.4
  88.8 0.0 copy-done.5
  88.8 11.0 %shard_map.109 = f32[32,64,128]{2,1,0:T(8,128)} custom-call(s32[512]{0:T(512)} %idx_ref.3, bf16[2048,1024]{1,0:T(8,128)(2,1)} %mats_ref.3, bf16[32,64,128]{2,1,0:T(8,128)(2,1)} %copy-done.1, bf16[48,64,128]{2,1,0:T(8,128)(2,1)} %copy-done.2, bf16[48,64,128]{2,1,0:T(8,128)(2,1)} %copy-done.3, bf16[48,64,128]{2,1,0:T(8,128)(2,1)} %copy-done.4, ...), custom_call_target="tpu_custom_call" | custom-call | flops 536870912 | bytes 7340032 | tf_op jit(solution)/shard_map/pallas_call | solution.py:106
  99.7 2.1 %convert_element_type.14.refs_7_ = bf16[32,64,128]{2,1,0:T(8,128)(2,1)} convert(f32[32,64,128]{2,1,0:T(8,128)} %shard_map.109) | non-fusion elementwise | flops 262144 | bytes 1572864 | tf_op jit(solution)/shard_map/convert_element_type | solution.py:165
  101.9 26.5 %shard_map.111 = bf16[64,64,128]{2,1,0:T(8,128)(2,1)} custom-call(s32[1024]{0:T(1024)} %idx_ref.5, bf16[4096,1024]{1,0:T(8,128)(2,1)} %mats_ref.5, bf16[64,64,128]{2,1,0:T(8,128)(2,1)} %copy-done, bf16[48,64,128]{2,1,0:T(8,128)(2,1)} %copy-done.2, bf16[48,64,128]{2,1,0:T(8,128)(2,1)} %copy-done.3, bf16[48,64,128]{2,1,0:T(8,128)(2,1)} %copy-done.4, ...), custom_call_target="tpu_custom_call" | custom-call | flops 1073741824 | bytes 14680064 | tf_op jit(solution)/shard_map/pallas_call | solution.py:106
  (3 shorter events, 0.0 us)
Async XLA Ops:
  3.4 4.9 %copy-start.6 = (bf16[4096,64]{0,1:T(8,128)(2,1)S(1)}, bf16[4096,64]{0,1:T(8,128)(2,1)}, u32[]{:S(2)}) copy-start(bf16[4096,64]{0,1:T(8,128)(2,1)} %param.13) | copy-start | bytes 1572868
  5.6 3.1 %copy-start = (bf16[64,64,128]{2,1,0:T(8,128)(2,1)}, bf16[64,64,128]{2,1,0:T(8,128)(2,1)S(1)}, u32[]{:S(2)}) copy-start(bf16[64,64,128]{2,1,0:T(8,128)(2,1)S(1)} %convolution_convert_fusion.refs_0_) | copy-start | bytes 3145732
  8.7 4.4 %copy-start.1 = (bf16[32,64,128]{2,1,0:T(8,128)(2,1)}, bf16[32,64,128]{2,1,0:T(8,128)(2,1)S(1)}, u32[]{:S(2)}) copy-start(bf16[32,64,128]{2,1,0:T(8,128)(2,1)S(1)} %fusion.refs_0_) | copy-start | bytes 1572868
  13.1 22.2 %collective-permute-start = (bf16[48,64,128]{2,1,0:T(8,128)(2,1)S(1)}, bf16[48,64,128]{2,1,0:T(8,128)(2,1)S(1)}, u32[]{:S(2)}, u32[]{:S(2)}) collective-permute-start(bf16[48,64,128]{2,1,0:T(8,128)(2,1)S(1)} %get-tuple-element.6), channel_id=1, source_target_pairs={{0,1},{1,2},{2,3},{3,4},{4,5},{5,6},{6,7},{7,8},{8,9},{9,10},{10,1... | collective-permute-start | bytes 2359304 | tf_op jit(solution)/shard_map/ppermute | solution.py:21
  16.0 13.1 %collective-permute-start.6 = (bf16[4,64,128]{2,1,0:T(8,128)(2,1)S(1)}, bf16[4,64,128]{2,1,0:T(8,128)(2,1)S(1)}, u32[]{:S(2)}, u32[]{:S(2)}) collective-permute-start(bf16[4,64,128]{2,1,0:T(8,128)(2,1)S(1)} %get-tuple-element.12), channel_id=1, source_target_pairs={{0,1},{1,2},{2,3},{3,4},{4,5},{5,6},{6,7},{7,8},{8,9},{9,10},{10,1... | collective-permute-start | bytes 196616 | tf_op jit(solution)/shard_map/ppermute | solution.py:28
  19.5 13.9 %collective-permute-start.7 = (bf16[4,64,128]{2,1,0:T(8,128)(2,1)S(1)}, bf16[4,64,128]{2,1,0:T(8,128)(2,1)S(1)}, u32[]{:S(2)}, u32[]{:S(2)}) collective-permute-start(bf16[4,64,128]{2,1,0:T(8,128)(2,1)S(1)} %get-tuple-element.11), channel_id=1, source_target_pairs={{1,0},{2,1},{3,2},{4,3},{5,4},{6,5},{7,6},{8,7},{9,8},{10,9},{11,1... | collective-permute-start | bytes 196616 | tf_op jit(solution)/shard_map/ppermute | solution.py:29
  23.3 37.8 %collective-permute-start.1 = (bf16[48,64,128]{2,1,0:T(8,128)(2,1)}, bf16[48,64,128]{2,1,0:T(8,128)(2,1)S(1)}, u32[]{:S(2)}, u32[]{:S(2)}) collective-permute-start(bf16[48,64,128]{2,1,0:T(8,128)(2,1)} %get-tuple-element.7), channel_id=1, source_target_pairs={{1,0},{2,1},{3,2},{4,3},{5,4},{6,5},{7,6},{8,7},{9,8},{10,9},{11,1... | collective-permute-start | bytes 2359304 | tf_op jit(solution)/shard_map/ppermute | solution.py:21
  25.7 52.0 %collective-permute-start.2 = (bf16[48,64,128]{2,1,0:T(8,128)(2,1)}, bf16[48,64,128]{2,1,0:T(8,128)(2,1)S(1)}, u32[]{:S(2)}, u32[]{:S(2)}) collective-permute-start(bf16[48,64,128]{2,1,0:T(8,128)(2,1)} %get-tuple-element.8), channel_id=1, source_target_pairs={{0,2},{1,3},{2,4},{3,5},{4,6},{5,7},{6,8},{7,9},{8,10},{9,11},{10,... | collective-permute-start | bytes 2359304 | tf_op jit(solution)/shard_map/ppermute | solution.py:21
  29.1 15.6 %copy-start.7 = (bf16[4,64,128]{2,1,0:T(8,128)(2,1)}, bf16[4,64,128]{2,1,0:T(8,128)(2,1)S(1)}, u32[]{:S(2)}) copy-start(bf16[4,64,128]{2,1,0:T(8,128)(2,1)S(1)} %collective-permute-done.6.refs_0_) | copy-start | bytes 196612
  29.1 56.8 %collective-permute-start.3 = (bf16[48,64,128]{2,1,0:T(8,128)(2,1)}, bf16[48,64,128]{2,1,0:T(8,128)(2,1)S(1)}, u32[]{:S(2)}, u32[]{:S(2)}) collective-permute-start(bf16[48,64,128]{2,1,0:T(8,128)(2,1)} %get-tuple-element.9), channel_id=1, source_target_pairs={{2,0},{3,1},{4,2},{5,3},{6,4},{7,5},{8,6},{9,7},{10,8},{11,9},{12,... | collective-permute-start | bytes 2359304 | tf_op jit(solution)/shard_map/ppermute | solution.py:21
  33.4 11.2 %copy-start.8 = (bf16[4,64,128]{2,1,0:T(8,128)(2,1)}, bf16[4,64,128]{2,1,0:T(8,128)(2,1)S(1)}, u32[]{:S(2)}) copy-start(bf16[4,64,128]{2,1,0:T(8,128)(2,1)S(1)} %collective-permute-done.7.refs_2_) | copy-start | bytes 196612
  33.4 52.7 %collective-permute-start.4 = (bf16[48,64,128]{2,1,0:T(8,128)(2,1)}, bf16[48,64,128]{2,1,0:T(8,128)(2,1)}, u32[]{:S(2)}, u32[]{:S(2)}) collective-permute-start(bf16[48,64,128]{2,1,0:T(8,128)(2,1)} %get-tuple-element.10), channel_id=1, source_target_pairs={{0,3},{1,4},{2,5},{3,6},{4,7},{5,8},{6,9},{7,10},{8,11},{9,12},{10... | collective-permute-start | bytes 2359304 | tf_op jit(solution)/shard_map/ppermute | solution.py:21
  35.4 25.8 %copy-start.2 = (bf16[48,64,128]{2,1,0:T(8,128)(2,1)}, bf16[48,64,128]{2,1,0:T(8,128)(2,1)S(1)}, u32[]{:S(2)}) copy-start(bf16[48,64,128]{2,1,0:T(8,128)(2,1)S(1)} %collective-permute-done.refs_1_) | copy-start | bytes 2359300
  35.4 53.4 %collective-permute-start.5 = (bf16[48,64,128]{2,1,0:T(8,128)(2,1)}, bf16[48,64,128]{2,1,0:T(8,128)(2,1)}, u32[]{:S(2)}, u32[]{:S(2)}) collective-permute-start(bf16[48,64,128]{2,1,0:T(8,128)(2,1)} %get-tuple-element.5), channel_id=1, source_target_pairs={{3,0},{4,1},{5,2},{6,3},{7,4},{8,5},{9,6},{10,7},{11,8},{12,9},{13... | collective-permute-start | bytes 2359304 | tf_op jit(solution)/shard_map/ppermute | solution.py:21
  61.2 27.6 %copy-start.3 = (bf16[48,64,128]{2,1,0:T(8,128)(2,1)}, bf16[48,64,128]{2,1,0:T(8,128)(2,1)S(1)}, u32[]{:S(2)}) copy-start(bf16[48,64,128]{2,1,0:T(8,128)(2,1)S(1)} %collective-permute-done.1.refs_2_) | copy-start | bytes 2359300
  77.7 11.0 %copy-start.4 = (bf16[48,64,128]{2,1,0:T(8,128)(2,1)}, bf16[48,64,128]{2,1,0:T(8,128)(2,1)S(1)}, u32[]{:S(2)}) copy-start(bf16[48,64,128]{2,1,0:T(8,128)(2,1)S(1)} %collective-permute-done.2.refs_3_) | copy-start | bytes 2359300
  85.9 2.9 %copy-start.5 = (bf16[48,64,128]{2,1,0:T(8,128)(2,1)}, bf16[48,64,128]{2,1,0:T(8,128)(2,1)S(1)}, u32[]{:S(2)}) copy-start(bf16[48,64,128]{2,1,0:T(8,128)(2,1)S(1)} %collective-permute-done.3.refs_4_) | copy-start | bytes 2359300

commit v3 on v2

--- a/solution.py
+++ b/solution.py
@@ -75,20 +75,16 @@
             for cp in copies:
                 cp.wait()
 
-        def per_target(tt, carry):
+        for tt in range(tb):
             base = (blk * tb + tt) * pairs
             for k in range(pairs):
                 s = jnp.clip(idx_ref[base + k], 0, total - 1)
-                g_ref[k * width:(k + 1) * width, :] = pool_ref[s]
-            r0 = pl.multiple_of(tt * LEAF, LEAF)
-            acc = jnp.dot(mats_ref[pl.ds(r0, LEAF), :], g_ref[...], preferred_element_type=jnp.float32)
+                g_ref[tt, k * width:(k + 1) * width, :] = pool_ref[s]
+            acc = jnp.dot(mats_ref[tt * LEAF:(tt + 1) * LEAF, :], g_ref[tt], preferred_element_type=jnp.float32)
             if epilogue is None:
                 out_ref[tt] = acc
             else:
                 out_ref[tt] = epilogue[2](tt, acc, extra_refs)
-            return carry
-
-        lax.fori_loop(0, tb, per_target, 0)
 
     grid_spec = pltpu.PrefetchScalarGridSpec(
         num_scalar_prefetch=1,
@@ -96,7 +92,7 @@
         in_specs=in_specs,
         out_specs=pl.BlockSpec((tb, LEAF, RHS), lambda i, ix: (i, 0, 0)),
         scratch_shapes=[
-            pltpu.VMEM((pairs * width, RHS), jnp.bfloat16),
+            pltpu.VMEM((tb, pairs * width, RHS), jnp.bfloat16),
             pltpu.VMEM((total, width, RHS), jnp.bfloat16),
             pltpu.SemaphoreType.DMA((n_seg,)),
         ],
@@ -110,6 +106,57 @@
         compiler_params=pltpu.CompilerParams(dimension_semantics=("arbitrary",)),
         cost_estimate=pl.CostEstimate(flops=flops, transcendentals=0, bytes_accessed=bytes_accessed),
     )(idx, mats, *seg_arrays, *extra)
+
+
+def upward(charges, basis_t, transfer_t, send_fine, send_coarse, fine_each, coarse_each):
+    leaves = charges.shape[0]
+    parents = leaves // 2
+    slots = 2 * REACH
+    each = fine_each + coarse_each
+
+    def kernel(sf_ref, sc_ref, x_ref, v_ref, e_ref, fine_ref, coarse_ref, *packet_refs):
+        def per_parent(j, c):
+            col = pl.multiple_of(j * 2 * RANK, 2 * RANK)
+            v = v_ref[:, pl.ds(col, 2 * RANK)]
+            f0 = jnp.dot(v[:, :RANK], x_ref[2 * j], preferred_element_type=jnp.float32).astype(jnp.bfloat16)
+            f1 = jnp.dot(v[:, RANK:], x_ref[2 * j + 1], preferred_element_type=jnp.float32).astype(jnp.bfloat16)
+            fine_ref[2 * j] = f0
+            fine_ref[2 * j + 1] = f1
+            e = e_ref[:, pl.ds(col, 2 * RANK)]
+            pair = jnp.concatenate([f0, f1], axis=0)
+            coarse_ref[j] = jnp.dot(e, pair, preferred_element_type=jnp.float32).astype(jnp.bfloat16)
+            return c
+
+        lax.fori_loop(0, parents, per_parent, 0)
+
+        for q in range(slots):
+            out = packet_refs[q]
+
+            def fine_pick(m, c):
+                out[m] = fine_ref[jnp.clip(sf_ref[q * fine_each + m], 0, leaves - 1)]
+                return c
+
+            def coarse_pick(m, c):
+                out[fine_each + m] = coarse_ref[jnp.clip(sc_ref[q * coarse_each + m], 0, parents - 1)]
+                return c
+
+            lax.fori_loop(0, fine_each, fine_pick, 0)
+            lax.fori_loop(0, coarse_each, coarse_pick, 0)
+
+    smem = pl.BlockSpec(memory_space=pltpu.SMEM)
+    vmem = pl.BlockSpec(memory_space=pltpu.VMEM)
+    block = jax.ShapeDtypeStruct
+    outs = pl.pallas_call(
+        kernel,
+        in_specs=[smem, smem, vmem, vmem, vmem],
+        out_specs=[vmem] * (2 + slots),
+        out_shape=[block((leaves, RANK, RHS), jnp.bfloat16), block((parents, RANK, RHS), jnp.bfloat16)]
+        + [block((each, RANK, RHS), jnp.bfloat16)] * slots,
+        cost_estimate=pl.CostEstimate(
+            flops=2 * leaves * LEAF * RANK * RHS * 2, transcendentals=0, bytes_accessed=16 * 2 ** 20
+        ),
+    )(send_fine, send_coarse, charges, basis_t, transfer_t)
+    return outs[0], outs[1], outs[2:]
 
 
 def on_device(
@@ -130,20 +177,11 @@
     fine_each = send_fine.shape[1] // (2 * REACH)
     coarse_each = send_coarse.shape[1] // (2 * REACH)
     axis = ("leaf", "couple")
-    leaf_bases = leaf_basis.reshape(leaves, LEAF, RANK)
-    fine_coeffs = jnp.einsum(
-        "nlr,nlc->nrc", leaf_bases, charges, preferred_element_type=jnp.float32
-    ).astype(jnp.bfloat16)
-    stacked = transfer.reshape(parents, 2 * RANK, RANK)
-    coarse_coeffs = jnp.einsum(
-        "pab,par->pbr",
-        stacked,
-        fine_coeffs.reshape(parents, 2 * RANK, RHS),
-        preferred_element_type=jnp.float32,
-    ).astype(jnp.bfloat16)
-    fine_out = fine_coeffs[send_fine[0]].reshape(2 * REACH, fine_each, RANK, RHS)
-    coarse_out = coarse_coeffs[send_coarse[0]].reshape(2 * REACH, coarse_each, RANK, RHS)
-    packets = jnp.concatenate([fine_out, coarse_out], 1)
+    basis_t = leaf_basis.T
+    transfer_t = transfer.T
+    fine_coeffs, coarse_coeffs, packets = upward(
+        charges, basis_t, transfer_t, send_fine[0], send_coarse[0], fine_each, coarse_each
+    )
     incoming = []
     for slot, offset in enumerate(offset_list()):
         incoming.append(from_behind(packets[slot], axis, offset))
@@ -172,18 +210,20 @@
 
     def finish(tt, acc, refs):
         cr_ref, e_ref, v_ref, near_ref = refs
-        r0 = pl.multiple_of(tt * LEAF, LEAF)
-        down = jnp.dot(e_ref[pl.ds(r0, RANK), :], cr_ref[tt // 2], preferred_element_type=jnp.float32)
+        lhs_t = (((0,), (0,)), ((), ()))
+        e_t = e_ref[:, tt * RANK:(tt + 1) * RANK]
+        down = lax.dot_general(e_t, cr_ref[tt // 2], lhs_t, preferred_element_type=jnp.float32)
         fine_round = (acc + down).astype(jnp.bfloat16)
-        far = jnp.dot(v_ref[pl.ds(r0, LEAF), :], fine_round, preferred_element_type=jnp.float32)
+        v_t = v_ref[:, tt * LEAF:(tt + 1) * LEAF]
+        far = lax.dot_general(v_t, fine_round, lhs_t, preferred_element_type=jnp.float32)
         return (far + near_ref[tt]).astype(jnp.bfloat16)
 
     epilogue = (
-        [coarse_round, transfer, leaf_basis, near_field],
+        [coarse_round, transfer_t, basis_t, near_field],
         [
             pl.BlockSpec((tb // 2, RANK, RHS), lambda i, ix: (i, 0, 0)),
-            pl.BlockSpec((tb * RANK, RANK), lambda i, ix: (i, 0)),
-            pl.BlockSpec((tb * LEAF, RANK), lambda i, ix: (i, 0)),
+            pl.BlockSpec((RANK, tb * RANK), lambda i, ix: (0, i)),
+            pl.BlockSpec((RANK, tb * LEAF), lambda i, ix: (0, i)),
             pl.BlockSpec((tb, LEAF, RHS), lambda i, ix: (i, 0, 0)),
         ],
         finish,

time: 129 us -> 123 us (0.953); the launches traced: 128 us -> 121 us
  local copies, waits for them, and re-layouts: 11.3 us -> 0.91 us
  waiting for transfers between devices: 29 us -> 35.5 us
  other arithmetic: 7.03 us -> 2.11 us
  starting transfers between devices: 24.4 us -> 28.8 us
  matrix products: 2.56 us -> 0 us
    pallas_call x3, Pallas kernels: 53.9 us -> 36.3 us  [gather_dot(): pl.pallas_call(kernel, grid_spec=grid_spec, out_shape=jax.ShapeDtypeStruc...]
    pallas_call x0 -> x1, Pallas kernels: none -> 16.8 us  [upward(): pl.pallas_call(kernel, in_specs=[smem, smem, vmem, vmem, vmem], out_specs...]
    ppermute x6, waiting for transfers between devices: 27.6 us -> 35.5 us  [from_behind(): lax.ppermute(value, axis, [(source, source + steps) for source in range(f...]
    unnamed x20 -> x12, local copies, waits for them, and re-layouts: 4.76 us -> 0.02 us
    ppermute x6, starting transfers between devices: 17.1 us -> 21.5 us  [from_behind(): lax.ppermute(value, axis, [(source, source + steps) for source in range(f...]
    gather x2 -> x0, local copies, waits for them, and re-layouts: 3.56 us -> none  [the longest x1 2.71 us: on_device(): fine_coeffs[send_fine[0]].reshape(2 * REACH, fine_each, RANK, RHS)]
    squeeze x1 -> x0, other arithmetic: 3.53 us -> none  [on_device(): incoming.append(from_behind(packets[slot], axis, offset))]
    dot_general x2 -> x0, matrix products: 2.56 us -> none  [the longest x1 2.16 us: on_device(): jnp.einsum('nlr,nlc->nrc', leaf_bases, charges, preferred_element_type=jn...]
  transfers between devices with their start and end apart: 8 -> 8, of which waited for: 5 -> 4; matrix products, arithmetic and copies ran while one was open for 4% -> 1% of each run, Pallas kernels for 13% -> 9%
where the time goes in v3:
time: 123 us; the launch traced here: 121 us
  Pallas kernels  53.1 us (43%)
  waiting for transfers between devices  35.5 us (29%)
  starting transfers between devices  28.8 us (23%)
  other arithmetic  2.11 us (2%)
    pallas_call x3, Pallas kernels, gather_dot(): pl.pallas_call(kernel, grid_spec=grid_spec, out_shape=jax.ShapeDtypeStruc...  36.3 us
    ppermute x6, waiting for transfers between devices, from_behind(): lax.ppermute(value, axis, [(source, source + steps) for source in range(f...  35.5 us
    ppermute x6, starting transfers between devices, from_behind(): lax.ppermute(value, axis, [(source, source + steps) for source in range(f...  21.5 us
    pallas_call x1, Pallas kernels, upward(): pl.pallas_call(kernel, in_specs=[smem, smem, vmem, vmem, vmem], out_specs...  16.8 us
    ppermute x1, starting transfers between devices, halo_pieces(): lax.ppermute(lax.slice_in_dim(block, 0, width, axis=0), axis, backward)  5.44 us
  transfers between devices with their start and end apart: 8, of which 4 were waited for; matrix products, arithmetic and copies ran while one was open for 1% of the time, Pallas kernels for 9%

profile of v3, /device:TPU:24, one launch (start us, length us, event | category | flops | bytes accessed | tf_op | source)
XLA Modules:
  0.0 120.6 jit_solution(13845072164093365885)
XLA Ops:
  0.0 16.8 %shard_map.109 = (bf16[64,64,128]{2,1,0:T(8,128)(2,1)}, bf16[32,64,128]{2,1,0:T(8,128)(2,1)}, bf16[48,64,128]{2,1,0:T(8,128)(2,1)}, bf16[48,64,128]{2,1,0:T(8,12...) custom-call(s32[192]{0:T(256)} %bitcast.8, ...), custom_call_target="tpu_custom_call" | custom-call | flops 134217728 | bytes 16777216 | tf_op jit(solution)/shard_map/pallas_call | solution.py:149
  16.8 1.9 %collective-permute-start = (bf16[48,64,128]{2,1,0:T(8,128)(2,1)}, bf16[48,64,128]{2,1,0:T(8,128)(2,1)S(1)}, u32[]{:S(2)}, u32[]{:S(2)}) collective-permute-start(bf16[48,64,128]{2,1,0:T(8,128)(2,1)} %get-tuple-element.14), channel_id=1, source_target_pairs={{0,1},{1,2},{2,3},{3,4},{4,5},{5,6},{6,7},{7,8},{8,9},{9,10},{10,1... | collective-permute-start | bytes 2359304 | tf_op jit(solution)/shard_map/ppermute | solution.py:21
  18.7 0.9 fusion
  19.6 5.4 %collective-permute-start.7 = (bf16[4,64,128]{2,1,0:T(8,128)(2,1)S(1)}, bf16[4,64,128]{2,1,0:T(8,128)(2,1)S(1)}, u32[]{:S(2)}, u32[]{:S(2)}) collective-permute-start(bf16[4,64,128]{2,1,0:T(8,128)(2,1)S(1)} %get-tuple-element.21), channel_id=1, source_target_pairs={{1,0},{2,1},{3,2},{4,3},{5,4},{6,5},{7,6},{8,7},{9,8},{10,9},{11,1... | collective-permute-start | bytes 196616 | tf_op jit(solution)/shard_map/ppermute | solution.py:29
  25.0 1.9 %collective-permute-start.6 = (bf16[4,64,128]{2,1,0:T(8,128)(2,1)S(1)}, bf16[4,64,128]{2,1,0:T(8,128)(2,1)S(1)}, u32[]{:S(2)}, u32[]{:S(2)}) collective-permute-start(bf16[4,64,128]{2,1,0:T(8,128)(2,1)S(1)} %get-tuple-element.22), channel_id=1, source_target_pairs={{0,1},{1,2},{2,3},{3,4},{4,5},{5,6},{6,7},{7,8},{8,9},{9,10},{10,1... | collective-permute-start | bytes 196616 | tf_op jit(solution)/shard_map/ppermute | solution.py:28
  26.9 5.4 %collective-permute-start.1 = (bf16[48,64,128]{2,1,0:T(8,128)(2,1)}, bf16[48,64,128]{2,1,0:T(8,128)(2,1)S(1)}, u32[]{:S(2)}, u32[]{:S(2)}) collective-permute-start(bf16[48,64,128]{2,1,0:T(8,128)(2,1)} %get-tuple-element.15), channel_id=1, source_target_pairs={{1,0},{2,1},{3,2},{4,3},{5,4},{6,5},{7,6},{8,7},{9,8},{10,9},{11,1... | collective-permute-start | bytes 2359304 | tf_op jit(solution)/shard_map/ppermute | solution.py:21
  32.4 1.9 %collective-permute-start.2 = (bf16[48,64,128]{2,1,0:T(8,128)(2,1)}, bf16[48,64,128]{2,1,0:T(8,128)(2,1)S(1)}, u32[]{:S(2)}, u32[]{:S(2)}) collective-permute-start(bf16[48,64,128]{2,1,0:T(8,128)(2,1)} %get-tuple-element.16), channel_id=1, source_target_pairs={{0,2},{1,3},{2,4},{3,5},{4,6},{5,7},{6,8},{7,9},{8,10},{9,11},{10,... | collective-permute-start | bytes 2359304 | tf_op jit(solution)/shard_map/ppermute | solution.py:21
  34.3 0.0 collective-permute-done.7.refs_2_
  34.3 0.0 copy-start.4
  34.3 5.7 %collective-permute-start.3 = (bf16[48,64,128]{2,1,0:T(8,128)(2,1)}, bf16[48,64,128]{2,1,0:T(8,128)(2,1)S(1)}, u32[]{:S(2)}, u32[]{:S(2)}) collective-permute-start(bf16[48,64,128]{2,1,0:T(8,128)(2,1)} %get-tuple-element.17), channel_id=1, source_target_pairs={{2,0},{3,1},{4,2},{5,3},{6,4},{7,5},{8,6},{9,7},{10,8},{11,9},{12,... | collective-permute-start | bytes 2359304 | tf_op jit(solution)/shard_map/ppermute | solution.py:21
  40.1 0.0 collective-permute-done.6.refs_0_
  40.1 0.0 copy-start.5
  40.1 1.9 %collective-permute-start.4 = (bf16[48,64,128]{2,1,0:T(8,128)(2,1)}, bf16[48,64,128]{2,1,0:T(8,128)(2,1)}, u32[]{:S(2)}, u32[]{:S(2)}) collective-permute-start(bf16[48,64,128]{2,1,0:T(8,128)(2,1)} %get-tuple-element.18), channel_id=1, source_target_pairs={{0,3},{1,4},{2,5},{3,6},{4,7},{5,8},{6,9},{7,10},{8,11},{9,12},{10... | collective-permute-start | bytes 2359304 | tf_op jit(solution)/shard_map/ppermute | solution.py:21
  42.0 0.0 collective-permute-done.refs_1_
  42.0 0.0 copy-start
  42.0 4.5 %collective-permute-start.5 = (bf16[48,64,128]{2,1,0:T(8,128)(2,1)}, bf16[48,64,128]{2,1,0:T(8,128)(2,1)}, u32[]{:S(2)}, u32[]{:S(2)}) collective-permute-start(bf16[48,64,128]{2,1,0:T(8,128)(2,1)} %get-tuple-element.19), channel_id=1, source_target_pairs={{3,0},{4,1},{5,2},{6,3},{7,4},{8,5},{9,6},{10,7},{11,8},{12,9},{13... | collective-permute-start | bytes 2359304 | tf_op jit(solution)/shard_map/ppermute | solution.py:21
  46.6 0.0 copy-done.4
  46.6 0.0 copy-done.5
  46.6 10.4 %shard_map.111.refs_10_ = f32[64,64,128]{2,1,0:T(8,128)} custom-call(s32[768]{0:T(1024)} %idx_ref.4, bf16[4096,768]{1,0:T(8,128)(2,1)} %mats_ref.4, bf16[4,64,128]{2,1,0:T(8,128)(2,1)} %copy-done.5, bf16[64,64,128]{2,1,0:T(8,128)(2,1)} %refs_1_.1, bf16[4,64,128]{2,1,0:T(8,128)(2,1)} %copy-done.4), custom_call_target="tpu_custom_call" | custom-call | flops 805306368 | bytes 9568256 | tf_op jit(solution)/shard_map/pallas_call | solution.py:102
  57.1 0.0 collective-permute-done.1.refs_2_
  57.1 0.0 copy-start.1
  57.1 26.4 %collective-permute-done.2.refs_3_ = bf16[48,64,128]{2,1,0:T(8,128)(2,1)S(1)} collective-permute-done((bf16[48,64,128]{2,1,0:T(8,128)(2,1)}, bf16[48,64,128]{2,1,0:T(8,128)(2,1)S(1)}, u32[]{:S(2)}, u32[]{:S(2)}) %collective-permute-start.2) | collective-permute-done | bytes 786464 | tf_op jit(solution)/shard_map/ppermute | solution.py:21
  83.5 0.0 copy-start.2
  83.5 6.4 %collective-permute-done.3.refs_4_ = bf16[48,64,128]{2,1,0:T(8,128)(2,1)S(1)} collective-permute-done((bf16[48,64,128]{2,1,0:T(8,128)(2,1)}, bf16[48,64,128]{2,1,0:T(8,128)(2,1)S(1)}, u32[]{:S(2)}, u32[]{:S(2)}) %collective-permute-start.3) | collective-permute-done | bytes 786464 | tf_op jit(solution)/shard_map/ppermute | solution.py:21
  89.9 0.0 copy-start.3
  89.9 2.0 %collective-permute-done.4.refs_5_ = bf16[48,64,128]{2,1,0:T(8,128)(2,1)} collective-permute-done((bf16[48,64,128]{2,1,0:T(8,128)(2,1)}, bf16[48,64,128]{2,1,0:T(8,128)(2,1)}, u32[]{:S(2)}, u32[]{:S(2)}) %collective-permute-start.4) | collective-permute-done | bytes 786464 | tf_op jit(solution)/shard_map/ppermute | solution.py:21
  91.9 0.7 collective-permute-done.5.refs_6_
  92.6 0.0 copy-done
  92.6 0.0 copy-done.1
  92.6 0.0 copy-done.2
  92.6 0.0 copy-done.3
  92.6 7.6 %shard_map.110 = f32[32,64,128]{2,1,0:T(8,128)} custom-call(s32[512]{0:T(512)} %idx_ref.3, bf16[2048,1024]{1,0:T(8,128)(2,1)} %mats_ref.3, bf16[32,64,128]{2,1,0:T(8,128)(2,1)} %get-tuple-element.20.refs_0_, bf16[48,64,128]{2,1,0:T(8,128)(2,1)} %copy-done, bf16[48,64,128]{2,1,0:T(8,128)(2,1)} %copy-done.1, bf16[48,64,128]{2,1,0:T(8,128)(2,1)} %copy-done.2, ...), custom_call_target="tpu_custom_call" | custom-call | flops 536870912 | bytes 7340032 | tf_op jit(solution)/shard_map/pallas_call | solution.py:102
  100.2 2.1 %convert_element_type.3.refs_7_ = bf16[32,64,128]{2,1,0:T(8,128)(2,1)} convert(f32[32,64,128]{2,1,0:T(8,128)} %shard_map.110) | non-fusion elementwise | flops 262144 | bytes 1572864 | tf_op jit(solution)/shard_map/convert_element_type | solution.py:203
  102.4 18.2 %shard_map.112 = bf16[64,64,128]{2,1,0:T(8,128)(2,1)} custom-call(s32[1024]{0:T(1024)} %idx_ref.5, bf16[4096,1024]{1,0:T(8,128)(2,1)} %mats_ref.5, bf16[64,64,128]{2,1,0:T(8,128)(2,1)} %get-tuple-element.13.refs_0_, bf16[48,64,128]{2,1,0:T(8,128)(2,1)} %copy-done, bf16[48,64,128]{2,1,0:T(8,128)(2,1)} %copy-done.1, bf16[48,64,128]{2,1,0:T(8,128)(2,1)} %copy-done.2, ...), custom_call_target="tpu_custom_call" | custom-call | flops 1073741824 | bytes 14680064 | tf_op jit(solution)/shard_map/pallas_call | solution.py:102
Async XLA Ops:
  16.8 25.3 %collective-permute-start = (bf16[48,64,128]{2,1,0:T(8,128)(2,1)}, bf16[48,64,128]{2,1,0:T(8,128)(2,1)S(1)}, u32[]{:S(2)}, u32[]{:S(2)}) collective-permute-start(bf16[48,64,128]{2,1,0:T(8,128)(2,1)} %get-tuple-element.14), channel_id=1, source_target_pairs={{0,1},{1,2},{2,3},{3,4},{4,5},{5,6},{6,7},{7,8},{8,9},{9,10},{10,1... | collective-permute-start | bytes 2359304 | tf_op jit(solution)/shard_map/ppermute | solution.py:21
  19.6 14.8 %collective-permute-start.7 = (bf16[4,64,128]{2,1,0:T(8,128)(2,1)S(1)}, bf16[4,64,128]{2,1,0:T(8,128)(2,1)S(1)}, u32[]{:S(2)}, u32[]{:S(2)}) collective-permute-start(bf16[4,64,128]{2,1,0:T(8,128)(2,1)S(1)} %get-tuple-element.21), channel_id=1, source_target_pairs={{1,0},{2,1},{3,2},{4,3},{5,4},{6,5},{7,6},{8,7},{9,8},{10,9},{11,1... | collective-permute-start | bytes 196616 | tf_op jit(solution)/shard_map/ppermute | solution.py:29
  25.0 15.1 %collective-permute-start.6 = (bf16[4,64,128]{2,1,0:T(8,128)(2,1)S(1)}, bf16[4,64,128]{2,1,0:T(8,128)(2,1)S(1)}, u32[]{:S(2)}, u32[]{:S(2)}) collective-permute-start(bf16[4,64,128]{2,1,0:T(8,128)(2,1)S(1)} %get-tuple-element.22), channel_id=1, source_target_pairs={{0,1},{1,2},{2,3},{3,4},{4,5},{5,6},{6,7},{7,8},{8,9},{9,10},{10,1... | collective-permute-start | bytes 196616 | tf_op jit(solution)/shard_map/ppermute | solution.py:28
  26.9 30.1 %collective-permute-start.1 = (bf16[48,64,128]{2,1,0:T(8,128)(2,1)}, bf16[48,64,128]{2,1,0:T(8,128)(2,1)S(1)}, u32[]{:S(2)}, u32[]{:S(2)}) collective-permute-start(bf16[48,64,128]{2,1,0:T(8,128)(2,1)} %get-tuple-element.15), channel_id=1, source_target_pairs={{1,0},{2,1},{3,2},{4,3},{5,4},{6,5},{7,6},{8,7},{9,8},{10,9},{11,1... | collective-permute-start | bytes 2359304 | tf_op jit(solution)/shard_map/ppermute | solution.py:21
  32.4 51.1 %collective-permute-start.2 = (bf16[48,64,128]{2,1,0:T(8,128)(2,1)}, bf16[48,64,128]{2,1,0:T(8,128)(2,1)S(1)}, u32[]{:S(2)}, u32[]{:S(2)}) collective-permute-start(bf16[48,64,128]{2,1,0:T(8,128)(2,1)} %get-tuple-element.16), channel_id=1, source_target_pairs={{0,2},{1,3},{2,4},{3,5},{4,6},{5,7},{6,8},{7,9},{8,10},{9,11},{10,... | collective-permute-start | bytes 2359304 | tf_op jit(solution)/shard_map/ppermute | solution.py:21
  34.3 12.3 %copy-start.4 = (bf16[4,64,128]{2,1,0:T(8,128)(2,1)}, bf16[4,64,128]{2,1,0:T(8,128)(2,1)S(1)}, u32[]{:S(2)}) copy-start(bf16[4,64,128]{2,1,0:T(8,128)(2,1)S(1)} %collective-permute-done.7.refs_2_) | copy-start | bytes 196612
  34.3 55.6 %collective-permute-start.3 = (bf16[48,64,128]{2,1,0:T(8,128)(2,1)}, bf16[48,64,128]{2,1,0:T(8,128)(2,1)S(1)}, u32[]{:S(2)}, u32[]{:S(2)}) collective-permute-start(bf16[48,64,128]{2,1,0:T(8,128)(2,1)} %get-tuple-element.17), channel_id=1, source_target_pairs={{2,0},{3,1},{4,2},{5,3},{6,4},{7,5},{8,6},{9,7},{10,8},{11,9},{12,... | collective-permute-start | bytes 2359304 | tf_op jit(solution)/shard_map/ppermute | solution.py:21
  40.1 6.5 %copy-start.5 = (bf16[4,64,128]{2,1,0:T(8,128)(2,1)}, bf16[4,64,128]{2,1,0:T(8,128)(2,1)S(1)}, u32[]{:S(2)}) copy-start(bf16[4,64,128]{2,1,0:T(8,128)(2,1)S(1)} %collective-permute-done.6.refs_0_) | copy-start | bytes 196612
  40.1 51.8 %collective-permute-start.4 = (bf16[48,64,128]{2,1,0:T(8,128)(2,1)}, bf16[48,64,128]{2,1,0:T(8,128)(2,1)}, u32[]{:S(2)}, u32[]{:S(2)}) collective-permute-start(bf16[48,64,128]{2,1,0:T(8,128)(2,1)} %get-tuple-element.18), channel_id=1, source_target_pairs={{0,3},{1,4},{2,5},{3,6},{4,7},{5,8},{6,9},{7,10},{8,11},{9,12},{10... | collective-permute-start | bytes 2359304 | tf_op jit(solution)/shard_map/ppermute | solution.py:21
  42.0 50.5 %copy-start = (bf16[48,64,128]{2,1,0:T(8,128)(2,1)}, bf16[48,64,128]{2,1,0:T(8,128)(2,1)S(1)}, u32[]{:S(2)}) copy-start(bf16[48,64,128]{2,1,0:T(8,128)(2,1)S(1)} %collective-permute-done.refs_1_) | copy-start | bytes 2359300
  42.0 50.5 %collective-permute-start.5 = (bf16[48,64,128]{2,1,0:T(8,128)(2,1)}, bf16[48,64,128]{2,1,0:T(8,128)(2,1)}, u32[]{:S(2)}, u32[]{:S(2)}) collective-permute-start(bf16[48,64,128]{2,1,0:T(8,128)(2,1)} %get-tuple-element.19), channel_id=1, source_target_pairs={{3,0},{4,1},{5,2},{6,3},{7,4},{8,5},{9,6},{10,7},{11,8},{12,9},{13... | collective-permute-start | bytes 2359304 | tf_op jit(solution)/shard_map/ppermute | solution.py:21
  57.1 35.5 %copy-start.1 = (bf16[48,64,128]{2,1,0:T(8,128)(2,1)}, bf16[48,64,128]{2,1,0:T(8,128)(2,1)S(1)}, u32[]{:S(2)}) copy-start(bf16[48,64,128]{2,1,0:T(8,128)(2,1)S(1)} %collective-permute-done.1.refs_2_) | copy-start | bytes 2359300
  83.5 9.1 %copy-start.2 = (bf16[48,64,128]{2,1,0:T(8,128)(2,1)}, bf16[48,64,128]{2,1,0:T(8,128)(2,1)S(1)}, u32[]{:S(2)}) copy-start(bf16[48,64,128]{2,1,0:T(8,128)(2,1)S(1)} %collective-permute-done.2.refs_3_) | copy-start | bytes 2359300
  89.9 2.7 %copy-start.3 = (bf16[48,64,128]{2,1,0:T(8,128)(2,1)}, bf16[48,64,128]{2,1,0:T(8,128)(2,1)S(1)}, u32[]{:S(2)}) copy-start(bf16[48,64,128]{2,1,0:T(8,128)(2,1)S(1)} %collective-permute-done.3.refs_4_) | copy-start | bytes 2359300

commit v4 on v3

--- a/solution.py
+++ b/solution.py
@@ -38,7 +38,7 @@
     return values
 
 
-def gather_dot(idx, mats, segments, pairs, epilogue=None):
+def gather_dot(idx, mats, segments, pairs, epilogue=None, out_dtype=jnp.float32):
     rows = mats.shape[0]
     width = mats.shape[1] // pairs
     targets = rows // LEAF
@@ -56,8 +56,6 @@
     if epilogue is not None:
         extra, extra_specs, _, out_dtype = epilogue
         in_specs.extend(extra_specs)
-    else:
-        out_dtype = jnp.float32
 
     def kernel(idx_ref, mats_ref, *refs):
         seg_refs = refs[:n_seg]
@@ -82,7 +80,7 @@
                 g_ref[tt, k * width:(k + 1) * width, :] = pool_ref[s]
             acc = jnp.dot(mats_ref[tt * LEAF:(tt + 1) * LEAF, :], g_ref[tt], preferred_element_type=jnp.float32)
             if epilogue is None:
-                out_ref[tt] = acc
+                out_ref[tt] = acc.astype(out_dtype)
             else:
                 out_ref[tt] = epilogue[2](tt, acc, extra_refs)
 
@@ -114,44 +112,63 @@
     slots = 2 * REACH
     each = fine_each + coarse_each
 
-    def kernel(sf_ref, sc_ref, x_ref, v_ref, e_ref, fine_ref, coarse_ref, *packet_refs):
-        def per_parent(j, c):
-            col = pl.multiple_of(j * 2 * RANK, 2 * RANK)
-            v = v_ref[:, pl.ds(col, 2 * RANK)]
-            f0 = jnp.dot(v[:, :RANK], x_ref[2 * j], preferred_element_type=jnp.float32).astype(jnp.bfloat16)
-            f1 = jnp.dot(v[:, RANK:], x_ref[2 * j + 1], preferred_element_type=jnp.float32).astype(jnp.bfloat16)
-            fine_ref[2 * j] = f0
-            fine_ref[2 * j + 1] = f1
-            e = e_ref[:, pl.ds(col, 2 * RANK)]
-            pair = jnp.concatenate([f0, f1], axis=0)
-            coarse_ref[j] = jnp.dot(e, pair, preferred_element_type=jnp.float32).astype(jnp.bfloat16)
-            return c
-
-        lax.fori_loop(0, parents, per_parent, 0)
+    def kernel(sf_ref, sc_ref, x_ref, v_ref, e_ref, fine_out, coarse_out, *rest):
+        packet_refs = rest[:slots]
+        fine_v, coarse_v, sem = rest[slots:]
+        for j in range(parents):
+            col = j * 2 * RANK
+            f0 = jnp.dot(v_ref[:, col:col + RANK], x_ref[2 * j], preferred_element_type=jnp.float32)
+            f1 = jnp.dot(v_ref[:, col + RANK:col + 2 * RANK], x_ref[2 * j + 1], preferred_element_type=jnp.float32)
+            pair = jnp.concatenate([f0.astype(jnp.bfloat16), f1.astype(jnp.bfloat16)], axis=0)
+            fine_v[2 * j] = pair[:RANK]
+            fine_v[2 * j + 1] = pair[RANK:]
+            e = e_ref[:, col:col + 2 * RANK]
+            coarse_v[j] = jnp.dot(e, pair, preferred_element_type=jnp.float32).astype(jnp.bfloat16)
+
+        whole = [
+            pltpu.make_async_copy(fine_v, fine_out, sem.at[0]),
+            pltpu.make_async_copy(coarse_v, coarse_out, sem.at[1]),
+        ]
+        for cp in whole:
+            cp.start()
+
+        def picks(q, m, start):
+            base = 2 + q * each + m
+            if start:
+                if m < fine_each:
+                    s = jnp.clip(sf_ref[q * fine_each + m], 0, leaves - 1)
+                    src = fine_v.at[s]
+                else:
+                    s = jnp.clip(sc_ref[q * coarse_each + m - fine_each], 0, parents - 1)
+                    src = coarse_v.at[s]
+            else:
+                src = fine_v.at[0]
+            return pltpu.make_async_copy(src, packet_refs[q].at[m], sem.at[base])
 
         for q in range(slots):
-            out = packet_refs[q]
-
-            def fine_pick(m, c):
-                out[m] = fine_ref[jnp.clip(sf_ref[q * fine_each + m], 0, leaves - 1)]
-                return c
-
-            def coarse_pick(m, c):
-                out[fine_each + m] = coarse_ref[jnp.clip(sc_ref[q * coarse_each + m], 0, parents - 1)]
-                return c
-
-            lax.fori_loop(0, fine_each, fine_pick, 0)
-            lax.fori_loop(0, coarse_each, coarse_pick, 0)
+            for m in range(each):
+                picks(q, m, True).start()
+        for cp in whole:
+            cp.wait()
+        for q in range(slots):
+            for m in range(each):
+                picks(q, m, False).wait()
 
     smem = pl.BlockSpec(memory_space=pltpu.SMEM)
     vmem = pl.BlockSpec(memory_space=pltpu.VMEM)
+    hbm = pl.BlockSpec(memory_space=pl.ANY)
     block = jax.ShapeDtypeStruct
     outs = pl.pallas_call(
         kernel,
         in_specs=[smem, smem, vmem, vmem, vmem],
-        out_specs=[vmem] * (2 + slots),
+        out_specs=[hbm] * (2 + slots),
         out_shape=[block((leaves, RANK, RHS), jnp.bfloat16), block((parents, RANK, RHS), jnp.bfloat16)]
         + [block((each, RANK, RHS), jnp.bfloat16)] * slots,
+        scratch_shapes=[
+            pltpu.VMEM((leaves, RANK, RHS), jnp.bfloat16),
+            pltpu.VMEM((parents, RANK, RHS), jnp.bfloat16),
+            pltpu.SemaphoreType.DMA((2 + slots * each,)),
+        ],
         cost_estimate=pl.CostEstimate(
             flops=2 * leaves * LEAF * RANK * RHS * 2, transcendentals=0, bytes_accessed=16 * 2 ** 20
         ),
@@ -197,10 +214,10 @@
     coarse_segments = [(coarse_coeffs, 0, parents, 0)]
     for slot in range(2 * REACH):
         coarse_segments.append((incoming[slot], parents + slot * coarse_each, coarse_each, fine_each))
-    coarse_target = gather_dot(
-        source_coarse, couple_coarse, coarse_segments, source_coarse.shape[0] // parents
-    )
-    coarse_round = coarse_target.astype(jnp.bfloat16)
+    coarse_round = gather_dot(
+        source_coarse, couple_coarse, coarse_segments, source_coarse.shape[0] // parents,
+        out_dtype=jnp.bfloat16,
+    )
 
     fine_segments = [(fine_coeffs, 0, leaves, 0)]
     for slot in range(2 * REACH):

time: 123 us -> 111 us (0.902)
  Pallas kernels: 53.1 us -> 43.6 us
  other arithmetic: 2.11 us -> 0 us
    pallas_call x1, Pallas kernels: 16.8 us -> 7.4 us  [upward(): pl.pallas_call(kernel, in_specs=[smem, smem, vmem, vmem, vmem], out_specs...]
    convert_element_type x1 -> x0, other arithmetic: 2.11 us -> none  [on_device(): coarse_round = coarse_target.astype(jnp.bfloat16)]
  transfers between devices with their start and end apart: 8 -> 8, of which waited for: 4 -> 4; matrix products, arithmetic and copies ran while one was open for 1% -> 1% of each run, Pallas kernels for 9% -> 10%
where the time goes in v4:
time: 111 us; the launch traced here: 109 us
  Pallas kernels  43.6 us (39%)
  waiting for transfers between devices  35.5 us (32%)
  starting transfers between devices  28.8 us (26%)
    pallas_call x3, Pallas kernels, gather_dot(): pl.pallas_call(kernel, grid_spec=grid_spec, out_shape=jax.ShapeDtypeStruc...  36.2 us
    ppermute x6, waiting for transfers between devices, from_behind(): lax.ppermute(value, axis, [(source, source + steps) for source in range(f...  35.5 us
    ppermute x6, starting transfers between devices, from_behind(): lax.ppermute(value, axis, [(source, source + steps) for source in range(f...  21.5 us
    pallas_call x1, Pallas kernels, upward(): pl.pallas_call(kernel, in_specs=[smem, smem, vmem, vmem, vmem], out_specs...  7.4 us
    ppermute x1, starting transfers between devices, halo_pieces(): lax.ppermute(lax.slice_in_dim(block, 0, width, axis=0), axis, backward)  5.44 us
  transfers between devices with their start and end apart: 8, of which 4 were waited for; matrix products, arithmetic and copies ran while one was open for 1% of the time, Pallas kernels for 10%

profile of v4, /device:TPU:24, one launch (start us, length us, event | category | flops | bytes accessed | tf_op | source)
XLA Modules:
  0.0 109.0 jit_solution(16546606824231597013)
XLA Ops:
  0.0 7.4 %shard_map.109 = (bf16[64,64,128]{2,1,0:T(8,128)(2,1)}, bf16[32,64,128]{2,1,0:T(8,128)(2,1)}, bf16[48,64,128]{2,1,0:T(8,128)(2,1)}, bf16[48,64,128]{2,1,0:T(8,12...) custom-call(s32[192]{0:T(256)} %bitcast.8, ...), custom_call_target="tpu_custom_call" | custom-call | flops 134217728 | bytes 16777216 | tf_op jit(solution)/shard_map/pallas_call | solution.py:161
  7.4 1.9 %collective-permute-start = (bf16[48,64,128]{2,1,0:T(8,128)(2,1)}, bf16[48,64,128]{2,1,0:T(8,128)(2,1)S(1)}, u32[]{:S(2)}, u32[]{:S(2)}) collective-permute-start(bf16[48,64,128]{2,1,0:T(8,128)(2,1)} %get-tuple-element.14), channel_id=1, source_target_pairs={{0,1},{1,2},{2,3},{3,4},{4,5},{5,6},{6,7},{7,8},{8,9},{9,10},{10,1... | collective-permute-start | bytes 2359304 | tf_op jit(solution)/shard_map/ppermute | solution.py:21
  9.3 0.9 fusion
  10.2 5.4 %collective-permute-start.7 = (bf16[4,64,128]{2,1,0:T(8,128)(2,1)S(1)}, bf16[4,64,128]{2,1,0:T(8,128)(2,1)S(1)}, u32[]{:S(2)}, u32[]{:S(2)}) collective-permute-start(bf16[4,64,128]{2,1,0:T(8,128)(2,1)S(1)} %get-tuple-element.21), channel_id=1, source_target_pairs={{1,0},{2,1},{3,2},{4,3},{5,4},{6,5},{7,6},{8,7},{9,8},{10,9},{11,1... | collective-permute-start | bytes 196616 | tf_op jit(solution)/shard_map/ppermute | solution.py:29
  15.7 1.9 %collective-permute-start.6 = (bf16[4,64,128]{2,1,0:T(8,128)(2,1)S(1)}, bf16[4,64,128]{2,1,0:T(8,128)(2,1)S(1)}, u32[]{:S(2)}, u32[]{:S(2)}) collective-permute-start(bf16[4,64,128]{2,1,0:T(8,128)(2,1)S(1)} %get-tuple-element.22), channel_id=1, source_target_pairs={{0,1},{1,2},{2,3},{3,4},{4,5},{5,6},{6,7},{7,8},{8,9},{9,10},{10,1... | collective-permute-start | bytes 196616 | tf_op jit(solution)/shard_map/ppermute | solution.py:28
  17.6 5.4 %collective-permute-start.1 = (bf16[48,64,128]{2,1,0:T(8,128)(2,1)}, bf16[48,64,128]{2,1,0:T(8,128)(2,1)S(1)}, u32[]{:S(2)}, u32[]{:S(2)}) collective-permute-start(bf16[48,64,128]{2,1,0:T(8,128)(2,1)} %get-tuple-element.15), channel_id=1, source_target_pairs={{1,0},{2,1},{3,2},{4,3},{5,4},{6,5},{7,6},{8,7},{9,8},{10,9},{11,1... | collective-permute-start | bytes 2359304 | tf_op jit(solution)/shard_map/ppermute | solution.py:21
  23.1 1.9 %collective-permute-start.2 = (bf16[48,64,128]{2,1,0:T(8,128)(2,1)}, bf16[48,64,128]{2,1,0:T(8,128)(2,1)S(1)}, u32[]{:S(2)}, u32[]{:S(2)}) collective-permute-start(bf16[48,64,128]{2,1,0:T(8,128)(2,1)} %get-tuple-element.16), channel_id=1, source_target_pairs={{0,2},{1,3},{2,4},{3,5},{4,6},{5,7},{6,8},{7,9},{8,10},{9,11},{10,... | collective-permute-start | bytes 2359304 | tf_op jit(solution)/shard_map/ppermute | solution.py:21
  25.0 0.0 collective-permute-done.7.refs_2_
  25.0 0.0 copy-start.4
  25.0 5.7 %collective-permute-start.3 = (bf16[48,64,128]{2,1,0:T(8,128)(2,1)}, bf16[48,64,128]{2,1,0:T(8,128)(2,1)S(1)}, u32[]{:S(2)}, u32[]{:S(2)}) collective-permute-start(bf16[48,64,128]{2,1,0:T(8,128)(2,1)} %get-tuple-element.17), channel_id=1, source_target_pairs={{2,0},{3,1},{4,2},{5,3},{6,4},{7,5},{8,6},{9,7},{10,8},{11,9},{12,... | collective-permute-start | bytes 2359304 | tf_op jit(solution)/shard_map/ppermute | solution.py:21
  30.7 0.0 collective-permute-done.6.refs_0_
  30.7 0.0 copy-start.5
  30.7 1.9 %collective-permute-start.4 = (bf16[48,64,128]{2,1,0:T(8,128)(2,1)}, bf16[48,64,128]{2,1,0:T(8,128)(2,1)}, u32[]{:S(2)}, u32[]{:S(2)}) collective-permute-start(bf16[48,64,128]{2,1,0:T(8,128)(2,1)} %get-tuple-element.18), channel_id=1, source_target_pairs={{0,3},{1,4},{2,5},{3,6},{4,7},{5,8},{6,9},{7,10},{8,11},{9,12},{10... | collective-permute-start | bytes 2359304 | tf_op jit(solution)/shard_map/ppermute | solution.py:21
  32.7 0.0 collective-permute-done.refs_1_
  32.7 0.0 copy-start
  32.7 4.5 %collective-permute-start.5 = (bf16[48,64,128]{2,1,0:T(8,128)(2,1)}, bf16[48,64,128]{2,1,0:T(8,128)(2,1)}, u32[]{:S(2)}, u32[]{:S(2)}) collective-permute-start(bf16[48,64,128]{2,1,0:T(8,128)(2,1)} %get-tuple-element.19), channel_id=1, source_target_pairs={{3,0},{4,1},{5,2},{6,3},{7,4},{8,5},{9,6},{10,7},{11,8},{12,9},{13... | collective-permute-start | bytes 2359304 | tf_op jit(solution)/shard_map/ppermute | solution.py:21
  37.2 0.0 copy-done.4
  37.3 0.0 copy-done.5
  37.3 10.4 %shard_map.111.refs_10_ = f32[64,64,128]{2,1,0:T(8,128)} custom-call(s32[768]{0:T(1024)} %idx_ref.4, bf16[4096,768]{1,0:T(8,128)(2,1)} %mats_ref.4, bf16[4,64,128]{2,1,0:T(8,128)(2,1)} %copy-done.5, bf16[64,64,128]{2,1,0:T(8,128)(2,1)} %refs_1_.1, bf16[4,64,128]{2,1,0:T(8,128)(2,1)} %copy-done.4), custom_call_target="tpu_custom_call" | custom-call | flops 805306368 | bytes 9568256 | tf_op jit(solution)/shard_map/pallas_call | solution.py:100
  47.7 0.0 collective-permute-done.1.refs_2_
  47.7 0.0 copy-start.1
  47.7 26.4 %collective-permute-done.2.refs_3_ = bf16[48,64,128]{2,1,0:T(8,128)(2,1)S(1)} collective-permute-done((bf16[48,64,128]{2,1,0:T(8,128)(2,1)}, bf16[48,64,128]{2,1,0:T(8,128)(2,1)S(1)}, u32[]{:S(2)}, u32[]{:S(2)}) %collective-permute-start.2) | collective-permute-done | bytes 786464 | tf_op jit(solution)/shard_map/ppermute | solution.py:21
  74.1 0.0 copy-start.2
  74.1 6.4 %collective-permute-done.3.refs_4_ = bf16[48,64,128]{2,1,0:T(8,128)(2,1)S(1)} collective-permute-done((bf16[48,64,128]{2,1,0:T(8,128)(2,1)}, bf16[48,64,128]{2,1,0:T(8,128)(2,1)S(1)}, u32[]{:S(2)}, u32[]{:S(2)}) %collective-permute-start.3) | collective-permute-done | bytes 786464 | tf_op jit(solution)/shard_map/ppermute | solution.py:21
  80.6 0.0 copy-start.3
  80.6 2.0 %collective-permute-done.4.refs_5_ = bf16[48,64,128]{2,1,0:T(8,128)(2,1)} collective-permute-done((bf16[48,64,128]{2,1,0:T(8,128)(2,1)}, bf16[48,64,128]{2,1,0:T(8,128)(2,1)}, u32[]{:S(2)}, u32[]{:S(2)}) %collective-permute-start.4) | collective-permute-done | bytes 786464 | tf_op jit(solution)/shard_map/ppermute | solution.py:21
  82.5 0.7 collective-permute-done.5.refs_6_
  83.2 0.0 copy-done
  83.2 0.0 copy-done.1
  83.2 0.0 copy-done.2
  83.2 0.0 copy-done.3
  83.2 7.5 %shard_map.110.refs_7_ = bf16[32,64,128]{2,1,0:T(8,128)(2,1)} custom-call(s32[512]{0:T(512)} %idx_ref.3, bf16[2048,1024]{1,0:T(8,128)(2,1)} %mats_ref.3, bf16[32,64,128]{2,1,0:T(8,128)(2,1)} %get-tuple-element.20.refs_0_, bf16[48,64,128]{2,1,0:T(8,128)(2,1)} %copy-done, bf16[48,64,128]{2,1,0:T(8,128)(2,1)} %copy-done.1, bf16[48,64,128]{2,1,0:T(8,128)(2,1)} %copy-done.2, ...), custom_call_target="tpu_custom_call" | custom-call | flops 536870912 | bytes 7340032 | tf_op jit(solution)/shard_map/pallas_call | solution.py:100
  90.8 18.2 %shard_map.112 = bf16[64,64,128]{2,1,0:T(8,128)(2,1)} custom-call(s32[1024]{0:T(1024)} %idx_ref.5, bf16[4096,1024]{1,0:T(8,128)(2,1)} %mats_ref.5, bf16[64,64,128]{2,1,0:T(8,128)(2,1)} %get-tuple-element.13.refs_0_, bf16[48,64,128]{2,1,0:T(8,128)(2,1)} %copy-done, bf16[48,64,128]{2,1,0:T(8,128)(2,1)} %copy-done.1, bf16[48,64,128]{2,1,0:T(8,128)(2,1)} %copy-done.2, ...), custom_call_target="tpu_custom_call" | custom-call | flops 1073741824 | bytes 14680064 | tf_op jit(solution)/shard_map/pallas_call | solution.py:100
Async XLA Ops:
  7.4 25.3 %collective-permute-start = (bf16[48,64,128]{2,1,0:T(8,128)(2,1)}, bf16[48,64,128]{2,1,0:T(8,128)(2,1)S(1)}, u32[]{:S(2)}, u32[]{:S(2)}) collective-permute-start(bf16[48,64,128]{2,1,0:T(8,128)(2,1)} %get-tuple-element.14), channel_id=1, source_target_pairs={{0,1},{1,2},{2,3},{3,4},{4,5},{5,6},{6,7},{7,8},{8,9},{9,10},{10,1... | collective-permute-start | bytes 2359304 | tf_op jit(solution)/shard_map/ppermute | solution.py:21
  10.2 14.8 %collective-permute-start.7 = (bf16[4,64,128]{2,1,0:T(8,128)(2,1)S(1)}, bf16[4,64,128]{2,1,0:T(8,128)(2,1)S(1)}, u32[]{:S(2)}, u32[]{:S(2)}) collective-permute-start(bf16[4,64,128]{2,1,0:T(8,128)(2,1)S(1)} %get-tuple-element.21), channel_id=1, source_target_pairs={{1,0},{2,1},{3,2},{4,3},{5,4},{6,5},{7,6},{8,7},{9,8},{10,9},{11,1... | collective-permute-start | bytes 196616 | tf_op jit(solution)/shard_map/ppermute | solution.py:29
  15.7 15.1 %collective-permute-start.6 = (bf16[4,64,128]{2,1,0:T(8,128)(2,1)S(1)}, bf16[4,64,128]{2,1,0:T(8,128)(2,1)S(1)}, u32[]{:S(2)}, u32[]{:S(2)}) collective-permute-start(bf16[4,64,128]{2,1,0:T(8,128)(2,1)S(1)} %get-tuple-element.22), channel_id=1, source_target_pairs={{0,1},{1,2},{2,3},{3,4},{4,5},{5,6},{6,7},{7,8},{8,9},{9,10},{10,1... | collective-permute-start | bytes 196616 | tf_op jit(solution)/shard_map/ppermute | solution.py:28
  17.6 30.1 %collective-permute-start.1 = (bf16[48,64,128]{2,1,0:T(8,128)(2,1)}, bf16[48,64,128]{2,1,0:T(8,128)(2,1)S(1)}, u32[]{:S(2)}, u32[]{:S(2)}) collective-permute-start(bf16[48,64,128]{2,1,0:T(8,128)(2,1)} %get-tuple-element.15), channel_id=1, source_target_pairs={{1,0},{2,1},{3,2},{4,3},{5,4},{6,5},{7,6},{8,7},{9,8},{10,9},{11,1... | collective-permute-start | bytes 2359304 | tf_op jit(solution)/shard_map/ppermute | solution.py:21
  23.1 51.1 %collective-permute-start.2 = (bf16[48,64,128]{2,1,0:T(8,128)(2,1)}, bf16[48,64,128]{2,1,0:T(8,128)(2,1)S(1)}, u32[]{:S(2)}, u32[]{:S(2)}) collective-permute-start(bf16[48,64,128]{2,1,0:T(8,128)(2,1)} %get-tuple-element.16), channel_id=1, source_target_pairs={{0,2},{1,3},{2,4},{3,5},{4,6},{5,7},{6,8},{7,9},{8,10},{9,11},{10,... | collective-permute-start | bytes 2359304 | tf_op jit(solution)/shard_map/ppermute | solution.py:21
  25.0 12.3 %copy-start.4 = (bf16[4,64,128]{2,1,0:T(8,128)(2,1)}, bf16[4,64,128]{2,1,0:T(8,128)(2,1)S(1)}, u32[]{:S(2)}) copy-start(bf16[4,64,128]{2,1,0:T(8,128)(2,1)S(1)} %collective-permute-done.7.refs_2_) | copy-start | bytes 196612
  25.0 55.6 %collective-permute-start.3 = (bf16[48,64,128]{2,1,0:T(8,128)(2,1)}, bf16[48,64,128]{2,1,0:T(8,128)(2,1)S(1)}, u32[]{:S(2)}, u32[]{:S(2)}) collective-permute-start(bf16[48,64,128]{2,1,0:T(8,128)(2,1)} %get-tuple-element.17), channel_id=1, source_target_pairs={{2,0},{3,1},{4,2},{5,3},{6,4},{7,5},{8,6},{9,7},{10,8},{11,9},{12,... | collective-permute-start | bytes 2359304 | tf_op jit(solution)/shard_map/ppermute | solution.py:21
  30.7 6.5 %copy-start.5 = (bf16[4,64,128]{2,1,0:T(8,128)(2,1)}, bf16[4,64,128]{2,1,0:T(8,128)(2,1)S(1)}, u32[]{:S(2)}) copy-start(bf16[4,64,128]{2,1,0:T(8,128)(2,1)S(1)} %collective-permute-done.6.refs_0_) | copy-start | bytes 196612
  30.7 51.8 %collective-permute-start.4 = (bf16[48,64,128]{2,1,0:T(8,128)(2,1)}, bf16[48,64,128]{2,1,0:T(8,128)(2,1)}, u32[]{:S(2)}, u32[]{:S(2)}) collective-permute-start(bf16[48,64,128]{2,1,0:T(8,128)(2,1)} %get-tuple-element.18), channel_id=1, source_target_pairs={{0,3},{1,4},{2,5},{3,6},{4,7},{5,8},{6,9},{7,10},{8,11},{9,12},{10... | collective-permute-start | bytes 2359304 | tf_op jit(solution)/shard_map/ppermute | solution.py:21
  32.7 50.5 %copy-start = (bf16[48,64,128]{2,1,0:T(8,128)(2,1)}, bf16[48,64,128]{2,1,0:T(8,128)(2,1)S(1)}, u32[]{:S(2)}) copy-start(bf16[48,64,128]{2,1,0:T(8,128)(2,1)S(1)} %collective-permute-done.refs_1_) | copy-start | bytes 2359300
  32.7 50.5 %collective-permute-start.5 = (bf16[48,64,128]{2,1,0:T(8,128)(2,1)}, bf16[48,64,128]{2,1,0:T(8,128)(2,1)}, u32[]{:S(2)}, u32[]{:S(2)}) collective-permute-start(bf16[48,64,128]{2,1,0:T(8,128)(2,1)} %get-tuple-element.19), channel_id=1, source_target_pairs={{3,0},{4,1},{5,2},{6,3},{7,4},{8,5},{9,6},{10,7},{11,8},{12,9},{13... | collective-permute-start | bytes 2359304 | tf_op jit(solution)/shard_map/ppermute | solution.py:21
  47.7 35.5 %copy-start.1 = (bf16[48,64,128]{2,1,0:T(8,128)(2,1)}, bf16[48,64,128]{2,1,0:T(8,128)(2,1)S(1)}, u32[]{:S(2)}) copy-start(bf16[48,64,128]{2,1,0:T(8,128)(2,1)S(1)} %collective-permute-done.1.refs_2_) | copy-start | bytes 2359300
  74.1 9.1 %copy-start.2 = (bf16[48,64,128]{2,1,0:T(8,128)(2,1)}, bf16[48,64,128]{2,1,0:T(8,128)(2,1)S(1)}, u32[]{:S(2)}) copy-start(bf16[48,64,128]{2,1,0:T(8,128)(2,1)S(1)} %collective-permute-done.2.refs_3_) | copy-start | bytes 2359300
  80.6 2.7 %copy-start.3 = (bf16[48,64,128]{2,1,0:T(8,128)(2,1)}, bf16[48,64,128]{2,1,0:T(8,128)(2,1)S(1)}, u32[]{:S(2)}) copy-start(bf16[48,64,128]{2,1,0:T(8,128)(2,1)S(1)} %collective-permute-done.3.refs_4_) | copy-start | bytes 2359300

commit v5 on v4

--- a/solution.py
+++ b/solution.py
@@ -59,8 +59,8 @@
 
     def kernel(idx_ref, mats_ref, *refs):
         seg_refs = refs[:n_seg]
-        extra_refs = refs[n_seg:len(refs) - 4]
-        out_ref, g_ref, pool_ref, sem = refs[len(refs) - 4:]
+        extra_refs = refs[n_seg:len(refs) - 3]
+        out_ref, pool_ref, sem = refs[len(refs) - 3:]
         blk = pl.program_id(0)
 
         @pl.when(blk == 0)
@@ -75,10 +75,9 @@
 
         for tt in range(tb):
             base = (blk * tb + tt) * pairs
-            for k in range(pairs):
-                s = jnp.clip(idx_ref[base + k], 0, total - 1)
-                g_ref[tt, k * width:(k + 1) * width, :] = pool_ref[s]
-            acc = jnp.dot(mats_ref[tt * LEAF:(tt + 1) * LEAF, :], g_ref[tt], preferred_element_type=jnp.float32)
+            blocks = [pool_ref[jnp.clip(idx_ref[base + k], 0, total - 1)] for k in range(pairs)]
+            rhs = jnp.concatenate(blocks, axis=0)
+            acc = jnp.dot(mats_ref[tt * LEAF:(tt + 1) * LEAF, :], rhs, preferred_element_type=jnp.float32)
             if epilogue is None:
                 out_ref[tt] = acc.astype(out_dtype)
             else:
@@ -90,7 +89,6 @@
         in_specs=in_specs,
         out_specs=pl.BlockSpec((tb, LEAF, RHS), lambda i, ix: (i, 0, 0)),
         scratch_shapes=[
-            pltpu.VMEM((tb, pairs * width, RHS), jnp.bfloat16),
             pltpu.VMEM((total, width, RHS), jnp.bfloat16),
             pltpu.SemaphoreType.DMA((n_seg,)),
         ],
@@ -227,20 +225,19 @@
 
     def finish(tt, acc, refs):
         cr_ref, e_ref, v_ref, near_ref = refs
-        lhs_t = (((0,), (0,)), ((), ()))
-        e_t = e_ref[:, tt * RANK:(tt + 1) * RANK]
-        down = lax.dot_general(e_t, cr_ref[tt // 2], lhs_t, preferred_element_type=jnp.float32)
+        e = e_ref[tt * RANK:(tt + 1) * RANK, :]
+        down = jnp.dot(e, cr_ref[tt // 2], preferred_element_type=jnp.float32)
         fine_round = (acc + down).astype(jnp.bfloat16)
-        v_t = v_ref[:, tt * LEAF:(tt + 1) * LEAF]
-        far = lax.dot_general(v_t, fine_round, lhs_t, preferred_element_type=jnp.float32)
+        v = v_ref[tt * LEAF:(tt + 1) * LEAF, :]
+        far = jnp.dot(v, fine_round, preferred_element_type=jnp.float32)
         return (far + near_ref[tt]).astype(jnp.bfloat16)
 
     epilogue = (
-        [coarse_round, transfer_t, basis_t, near_field],
+        [coarse_round, transfer, leaf_basis, near_field],
         [
             pl.BlockSpec((tb // 2, RANK, RHS), lambda i, ix: (i, 0, 0)),
-            pl.BlockSpec((RANK, tb * RANK), lambda i, ix: (0, i)),
-            pl.BlockSpec((RANK, tb * LEAF), lambda i, ix: (0, i)),
+            pl.BlockSpec((tb * RANK, RANK), lambda i, ix: (i, 0)),
+            pl.BlockSpec((tb * LEAF, RANK), lambda i, ix: (i, 0)),
             pl.BlockSpec((tb, LEAF, RHS), lambda i, ix: (i, 0, 0)),
         ],
         finish,

time: 111 us -> 110 us (level)
  local copies, waits for them, and re-layouts: 0.91 us -> 5.65 us
  waiting for transfers between devices: 35.5 us -> 31 us
  Pallas kernels: 43.6 us -> 42.3 us
    unnamed x12 -> x14, local copies, waits for them, and re-layouts: 0.02 us -> 4.77 us
    ppermute x6, waiting for transfers between devices: 35.5 us -> 31 us  [from_behind(): lax.ppermute(value, axis, [(source, source + steps) for source in range(f...]
    pallas_call x3, Pallas kernels: 36.2 us -> 34.9 us  [gather_dot(): pl.pallas_call(kernel, grid_spec=grid_spec, out_shape=jax.ShapeDtypeStruc...]
  transfers between devices with their start and end apart: 8 -> 8, of which waited for: 4 -> 4; matrix products, arithmetic and copies ran while one was open for 1% -> 5% of each run, Pallas kernels for 10% -> 9%
where the time goes in v5:
time: 110 us; the launch traced here: 108 us
  Pallas kernels  42.3 us (38%)
  waiting for transfers between devices  31 us (28%)
  starting transfers between devices  28.8 us (26%)
  local copies, waits for them, and re-layouts  5.65 us (5%)
    pallas_call x3, Pallas kernels, gather_dot(): pl.pallas_call(kernel, grid_spec=grid_spec, out_shape=jax.ShapeDtypeStruc...  34.9 us
    ppermute x6, waiting for transfers between devices, from_behind(): lax.ppermute(value, axis, [(source, source + steps) for source in range(f...  31 us
    ppermute x6, starting transfers between devices, from_behind(): lax.ppermute(value, axis, [(source, source + steps) for source in range(f...  21.5 us
    pallas_call x1, Pallas kernels, upward(): pl.pallas_call(kernel, in_specs=[smem, smem, vmem, vmem, vmem], out_specs...  7.4 us
    ppermute x1, starting transfers between devices, halo_pieces(): lax.ppermute(lax.slice_in_dim(block, 0, width, axis=0), axis, backward)  5.44 us
    unnamed x14, local copies, waits for them, and re-layouts  4.77 us
  transfers between devices with their start and end apart: 8, of which 4 were waited for; matrix products, arithmetic and copies ran while one was open for 5% of the time, Pallas kernels for 9%

profile of v5, /device:TPU:24, one launch (start us, length us, event | category | flops | bytes accessed | tf_op | source)
XLA Modules:
  0.0 108.0 jit_solution(187978593131747474)
XLA Ops:
  0.0 7.4 %shard_map.109 = (bf16[64,64,128]{2,1,0:T(8,128)(2,1)}, bf16[32,64,128]{2,1,0:T(8,128)(2,1)}, bf16[48,64,128]{2,1,0:T(8,128)(2,1)}, bf16[48,64,128]{2,1,0:T(8,12...) custom-call(s32[192]{0:T(256)} %bitcast.6, ...), custom_call_target="tpu_custom_call" | custom-call | flops 134217728 | bytes 16777216 | tf_op jit(solution)/shard_map/pallas_call | solution.py:159
  7.4 1.9 %collective-permute-start = (bf16[48,64,128]{2,1,0:T(8,128)(2,1)}, bf16[48,64,128]{2,1,0:T(8,128)(2,1)S(1)}, u32[]{:S(2)}, u32[]{:S(2)}) collective-permute-start(bf16[48,64,128]{2,1,0:T(8,128)(2,1)} %get-tuple-element.14), channel_id=1, source_target_pairs={{0,1},{1,2},{2,3},{3,4},{4,5},{5,6},{6,7},{7,8},{8,9},{9,10},{10,1... | collective-permute-start | bytes 2359304 | tf_op jit(solution)/shard_map/ppermute | solution.py:21
  9.3 0.9 fusion
  10.2 5.4 %collective-permute-start.7 = (bf16[4,64,128]{2,1,0:T(8,128)(2,1)S(1)}, bf16[4,64,128]{2,1,0:T(8,128)(2,1)S(1)}, u32[]{:S(2)}, u32[]{:S(2)}) collective-permute-start(bf16[4,64,128]{2,1,0:T(8,128)(2,1)S(1)} %get-tuple-element.21), channel_id=1, source_target_pairs={{1,0},{2,1},{3,2},{4,3},{5,4},{6,5},{7,6},{8,7},{9,8},{10,9},{11,1... | collective-permute-start | bytes 196616 | tf_op jit(solution)/shard_map/ppermute | solution.py:29
  15.7 1.9 %collective-permute-start.6 = (bf16[4,64,128]{2,1,0:T(8,128)(2,1)S(1)}, bf16[4,64,128]{2,1,0:T(8,128)(2,1)S(1)}, u32[]{:S(2)}, u32[]{:S(2)}) collective-permute-start(bf16[4,64,128]{2,1,0:T(8,128)(2,1)S(1)} %get-tuple-element.22), channel_id=1, source_target_pairs={{0,1},{1,2},{2,3},{3,4},{4,5},{5,6},{6,7},{7,8},{8,9},{9,10},{10,1... | collective-permute-start | bytes 196616 | tf_op jit(solution)/shard_map/ppermute | solution.py:28
  17.6 5.4 %collective-permute-start.1 = (bf16[48,64,128]{2,1,0:T(8,128)(2,1)}, bf16[48,64,128]{2,1,0:T(8,128)(2,1)S(1)}, u32[]{:S(2)}, u32[]{:S(2)}) collective-permute-start(bf16[48,64,128]{2,1,0:T(8,128)(2,1)} %get-tuple-element.15), channel_id=1, source_target_pairs={{1,0},{2,1},{3,2},{4,3},{5,4},{6,5},{7,6},{8,7},{9,8},{10,9},{11,1... | collective-permute-start | bytes 2359304 | tf_op jit(solution)/shard_map/ppermute | solution.py:21
  23.0 1.9 %collective-permute-start.2 = (bf16[48,64,128]{2,1,0:T(8,128)(2,1)}, bf16[48,64,128]{2,1,0:T(8,128)(2,1)S(1)}, u32[]{:S(2)}, u32[]{:S(2)}) collective-permute-start(bf16[48,64,128]{2,1,0:T(8,128)(2,1)} %get-tuple-element.16), channel_id=1, source_target_pairs={{0,2},{1,3},{2,4},{3,5},{4,6},{5,7},{6,8},{7,9},{8,10},{9,11},{10,... | collective-permute-start | bytes 2359304 | tf_op jit(solution)/shard_map/ppermute | solution.py:21
  25.0 0.0 collective-permute-done.7.refs_2_
  25.0 0.0 copy-start.4
  25.0 5.7 %collective-permute-start.3 = (bf16[48,64,128]{2,1,0:T(8,128)(2,1)}, bf16[48,64,128]{2,1,0:T(8,128)(2,1)S(1)}, u32[]{:S(2)}, u32[]{:S(2)}) collective-permute-start(bf16[48,64,128]{2,1,0:T(8,128)(2,1)} %get-tuple-element.17), channel_id=1, source_target_pairs={{2,0},{3,1},{4,2},{5,3},{6,4},{7,5},{8,6},{9,7},{10,8},{11,9},{12,... | collective-permute-start | bytes 2359304 | tf_op jit(solution)/shard_map/ppermute | solution.py:21
  30.7 0.0 collective-permute-done.6.refs_0_
  30.7 0.0 copy-start.5
  30.7 1.9 %collective-permute-start.4 = (bf16[48,64,128]{2,1,0:T(8,128)(2,1)}, bf16[48,64,128]{2,1,0:T(8,128)(2,1)}, u32[]{:S(2)}, u32[]{:S(2)}) collective-permute-start(bf16[48,64,128]{2,1,0:T(8,128)(2,1)} %get-tuple-element.18), channel_id=1, source_target_pairs={{0,3},{1,4},{2,5},{3,6},{4,7},{5,8},{6,9},{7,10},{8,11},{9,12},{10... | collective-permute-start | bytes 2359304 | tf_op jit(solution)/shard_map/ppermute | solution.py:21
  32.7 0.0 collective-permute-done.refs_1_
  32.7 0.0 copy-start
  32.7 4.5 %collective-permute-start.5 = (bf16[48,64,128]{2,1,0:T(8,128)(2,1)}, bf16[48,64,128]{2,1,0:T(8,128)(2,1)}, u32[]{:S(2)}, u32[]{:S(2)}) collective-permute-start(bf16[48,64,128]{2,1,0:T(8,128)(2,1)} %get-tuple-element.19), channel_id=1, source_target_pairs={{3,0},{4,1},{5,2},{6,3},{7,4},{8,5},{9,6},{10,7},{11,8},{12,9},{13... | collective-permute-start | bytes 2359304 | tf_op jit(solution)/shard_map/ppermute | solution.py:21
  37.2 2.4 %copy.13.refs_9_ = bf16[4096,64]{1,0:T(8,128)(2,1)} copy(bf16[4096,64]{0,1:T(8,128)(2,1)} %param.12) | data formatting | bytes 1048576 | tf_op args[1]
  39.6 2.4 %copy.12.refs_8_ = bf16[4096,64]{1,0:T(8,128)(2,1)} copy(bf16[4096,64]{0,1:T(8,128)(2,1)} %param.13) | data formatting | bytes 1048576 | tf_op args[2]
  42.0 0.0 copy-done.4
  42.0 0.0 copy-done.5
  42.0 10.2 %shard_map.111.refs_10_ = f32[64,64,128]{2,1,0:T(8,128)} custom-call(s32[768]{0:T(1024)} %idx_ref.4, bf16[4096,768]{1,0:T(8,128)(2,1)} %mats_ref.4, bf16[4,64,128]{2,1,0:T(8,128)(2,1)} %copy-done.5, bf16[64,64,128]{2,1,0:T(8,128)(2,1)} %refs_1_.1, bf16[4,64,128]{2,1,0:T(8,128)(2,1)} %copy-done.4), custom_call_target="tpu_custom_call" | custom-call | flops 805306368 | bytes 9568256 | tf_op jit(solution)/shard_map/pallas_call | solution.py:98
  52.2 0.0 copy-done
  52.2 0.0 collective-permute-done.1.refs_2_
  52.2 0.0 copy-start.1
  52.2 21.9 %collective-permute-done.2.refs_3_ = bf16[48,64,128]{2,1,0:T(8,128)(2,1)S(1)} collective-permute-done((bf16[48,64,128]{2,1,0:T(8,128)(2,1)}, bf16[48,64,128]{2,1,0:T(8,128)(2,1)S(1)}, u32[]{:S(2)}, u32[]{:S(2)}) %collective-permute-start.2) | collective-permute-done | bytes 786464 | tf_op jit(solution)/shard_map/ppermute | solution.py:21
  74.1 0.0 copy-start.2
  74.1 6.4 %collective-permute-done.3.refs_4_ = bf16[48,64,128]{2,1,0:T(8,128)(2,1)S(1)} collective-permute-done((bf16[48,64,128]{2,1,0:T(8,128)(2,1)}, bf16[48,64,128]{2,1,0:T(8,128)(2,1)S(1)}, u32[]{:S(2)}, u32[]{:S(2)}) %collective-permute-start.3) | collective-permute-done | bytes 786464 | tf_op jit(solution)/shard_map/ppermute | solution.py:21
  80.6 0.0 copy-start.3
  80.6 2.0 %collective-permute-done.4.refs_5_ = bf16[48,64,128]{2,1,0:T(8,128)(2,1)} collective-permute-done((bf16[48,64,128]{2,1,0:T(8,128)(2,1)}, bf16[48,64,128]{2,1,0:T(8,128)(2,1)}, u32[]{:S(2)}, u32[]{:S(2)}) %collective-permute-start.4) | collective-permute-done | bytes 786464 | tf_op jit(solution)/shard_map/ppermute | solution.py:21
  82.5 0.7 collective-permute-done.5.refs_6_
  83.2 0.0 copy-done.1
  83.2 0.0 copy-done.2
  83.2 0.0 copy-done.3
  83.2 7.3 %shard_map.110.refs_7_ = bf16[32,64,128]{2,1,0:T(8,128)(2,1)} custom-call(s32[512]{0:T(512)} %idx_ref.3, bf16[2048,1024]{1,0:T(8,128)(2,1)} %mats_ref.3, bf16[32,64,128]{2,1,0:T(8,128)(2,1)} %get-tuple-element.20.refs_0_, bf16[48,64,128]{2,1,0:T(8,128)(2,1)} %copy-done, bf16[48,64,128]{2,1,0:T(8,128)(2,1)} %copy-done.1, bf16[48,64,128]{2,1,0:T(8,128)(2,1)} %copy-done.2, ...), custom_call_target="tpu_custom_call" | custom-call | flops 536870912 | bytes 7340032 | tf_op jit(solution)/shard_map/pallas_call | solution.py:98
  90.5 17.5 %shard_map.112 = bf16[64,64,128]{2,1,0:T(8,128)(2,1)} custom-call(s32[1024]{0:T(1024)} %idx_ref.5, bf16[4096,1024]{1,0:T(8,128)(2,1)} %mats_ref.5, bf16[64,64,128]{2,1,0:T(8,128)(2,1)} %get-tuple-element.13.refs_0_, bf16[48,64,128]{2,1,0:T(8,128)(2,1)} %copy-done, bf16[48,64,128]{2,1,0:T(8,128)(2,1)} %copy-done.1, bf16[48,64,128]{2,1,0:T(8,128)(2,1)} %copy-done.2, ...), custom_call_target="tpu_custom_call" | custom-call | flops 1073741824 | bytes 14680064 | tf_op jit(solution)/shard_map/pallas_call | solution.py:98
Async XLA Ops:
  7.4 25.3 %collective-permute-start = (bf16[48,64,128]{2,1,0:T(8,128)(2,1)}, bf16[48,64,128]{2,1,0:T(8,128)(2,1)S(1)}, u32[]{:S(2)}, u32[]{:S(2)}) collective-permute-start(bf16[48,64,128]{2,1,0:T(8,128)(2,1)} %get-tuple-element.14), channel_id=1, source_target_pairs={{0,1},{1,2},{2,3},{3,4},{4,5},{5,6},{6,7},{7,8},{8,9},{9,10},{10,1... | collective-permute-start | bytes 2359304 | tf_op jit(solution)/shard_map/ppermute | solution.py:21
  10.2 14.8 %collective-permute-start.7 = (bf16[4,64,128]{2,1,0:T(8,128)(2,1)S(1)}, bf16[4,64,128]{2,1,0:T(8,128)(2,1)S(1)}, u32[]{:S(2)}, u32[]{:S(2)}) collective-permute-start(bf16[4,64,128]{2,1,0:T(8,128)(2,1)S(1)} %get-tuple-element.21), channel_id=1, source_target_pairs={{1,0},{2,1},{3,2},{4,3},{5,4},{6,5},{7,6},{8,7},{9,8},{10,9},{11,1... | collective-permute-start | bytes 196616 | tf_op jit(solution)/shard_map/ppermute | solution.py:29
  15.7 15.1 %collective-permute-start.6 = (bf16[4,64,128]{2,1,0:T(8,128)(2,1)S(1)}, bf16[4,64,128]{2,1,0:T(8,128)(2,1)S(1)}, u32[]{:S(2)}, u32[]{:S(2)}) collective-permute-start(bf16[4,64,128]{2,1,0:T(8,128)(2,1)S(1)} %get-tuple-element.22), channel_id=1, source_target_pairs={{0,1},{1,2},{2,3},{3,4},{4,5},{5,6},{6,7},{7,8},{8,9},{9,10},{10,1... | collective-permute-start | bytes 196616 | tf_op jit(solution)/shard_map/ppermute | solution.py:28
  17.6 34.6 %collective-permute-start.1 = (bf16[48,64,128]{2,1,0:T(8,128)(2,1)}, bf16[48,64,128]{2,1,0:T(8,128)(2,1)S(1)}, u32[]{:S(2)}, u32[]{:S(2)}) collective-permute-start(bf16[48,64,128]{2,1,0:T(8,128)(2,1)} %get-tuple-element.15), channel_id=1, source_target_pairs={{1,0},{2,1},{3,2},{4,3},{5,4},{6,5},{7,6},{8,7},{9,8},{10,9},{11,1... | collective-permute-start | bytes 2359304 | tf_op jit(solution)/shard_map/ppermute | solution.py:21
  23.0 51.1 %collective-permute-start.2 = (bf16[48,64,128]{2,1,0:T(8,128)(2,1)}, bf16[48,64,128]{2,1,0:T(8,128)(2,1)S(1)}, u32[]{:S(2)}, u32[]{:S(2)}) collective-permute-start(bf16[48,64,128]{2,1,0:T(8,128)(2,1)} %get-tuple-element.16), channel_id=1, source_target_pairs={{0,2},{1,3},{2,4},{3,5},{4,6},{5,7},{6,8},{7,9},{8,10},{9,11},{10,... | collective-permute-start | bytes 2359304 | tf_op jit(solution)/shard_map/ppermute | solution.py:21
  25.0 17.0 %copy-start.4 = (bf16[4,64,128]{2,1,0:T(8,128)(2,1)}, bf16[4,64,128]{2,1,0:T(8,128)(2,1)S(1)}, u32[]{:S(2)}) copy-start(bf16[4,64,128]{2,1,0:T(8,128)(2,1)S(1)} %collective-permute-done.7.refs_2_) | copy-start | bytes 196612
  25.0 55.6 %collective-permute-start.3 = (bf16[48,64,128]{2,1,0:T(8,128)(2,1)}, bf16[48,64,128]{2,1,0:T(8,128)(2,1)S(1)}, u32[]{:S(2)}, u32[]{:S(2)}) collective-permute-start(bf16[48,64,128]{2,1,0:T(8,128)(2,1)} %get-tuple-element.17), channel_id=1, source_target_pairs={{2,0},{3,1},{4,2},{5,3},{6,4},{7,5},{8,6},{9,7},{10,8},{11,9},{12,... | collective-permute-start | bytes 2359304 | tf_op jit(solution)/shard_map/ppermute | solution.py:21
  30.7 11.3 %copy-start.5 = (bf16[4,64,128]{2,1,0:T(8,128)(2,1)}, bf16[4,64,128]{2,1,0:T(8,128)(2,1)S(1)}, u32[]{:S(2)}) copy-start(bf16[4,64,128]{2,1,0:T(8,128)(2,1)S(1)} %collective-permute-done.6.refs_0_) | copy-start | bytes 196612
  30.7 51.8 %collective-permute-start.4 = (bf16[48,64,128]{2,1,0:T(8,128)(2,1)}, bf16[48,64,128]{2,1,0:T(8,128)(2,1)}, u32[]{:S(2)}, u32[]{:S(2)}) collective-permute-start(bf16[48,64,128]{2,1,0:T(8,128)(2,1)} %get-tuple-element.18), channel_id=1, source_target_pairs={{0,3},{1,4},{2,5},{3,6},{4,7},{5,8},{6,9},{7,10},{8,11},{9,12},{10... | collective-permute-start | bytes 2359304 | tf_op jit(solution)/shard_map/ppermute | solution.py:21
  32.7 19.5 %copy-start = (bf16[48,64,128]{2,1,0:T(8,128)(2,1)}, bf16[48,64,128]{2,1,0:T(8,128)(2,1)S(1)}, u32[]{:S(2)}) copy-start(bf16[48,64,128]{2,1,0:T(8,128)(2,1)S(1)} %collective-permute-done.refs_1_) | copy-start | bytes 2359300
  32.7 50.5 %collective-permute-start.5 = (bf16[48,64,128]{2,1,0:T(8,128)(2,1)}, bf16[48,64,128]{2,1,0:T(8,128)(2,1)}, u32[]{:S(2)}, u32[]{:S(2)}) collective-permute-start(bf16[48,64,128]{2,1,0:T(8,128)(2,1)} %get-tuple-element.19), channel_id=1, source_target_pairs={{3,0},{4,1},{5,2},{6,3},{7,4},{8,5},{9,6},{10,7},{11,8},{12,9},{13... | collective-permute-start | bytes 2359304 | tf_op jit(solution)/shard_map/ppermute | solution.py:21
  52.2 31.0 %copy-start.1 = (bf16[48,64,128]{2,1,0:T(8,128)(2,1)}, bf16[48,64,128]{2,1,0:T(8,128)(2,1)S(1)}, u32[]{:S(2)}) copy-start(bf16[48,64,128]{2,1,0:T(8,128)(2,1)S(1)} %collective-permute-done.1.refs_2_) | copy-start | bytes 2359300
  74.1 9.1 %copy-start.2 = (bf16[48,64,128]{2,1,0:T(8,128)(2,1)}, bf16[48,64,128]{2,1,0:T(8,128)(2,1)S(1)}, u32[]{:S(2)}) copy-start(bf16[48,64,128]{2,1,0:T(8,128)(2,1)S(1)} %collective-permute-done.2.refs_3_) | copy-start | bytes 2359300
  80.6 2.7 %copy-start.3 = (bf16[48,64,128]{2,1,0:T(8,128)(2,1)}, bf16[48,64,128]{2,1,0:T(8,128)(2,1)S(1)}, u32[]{:S(2)}) copy-start(bf16[48,64,128]{2,1,0:T(8,128)(2,1)S(1)} %collective-permute-done.3.refs_4_) | copy-start | bytes 2359300

commit v6 on v5

--- a/solution.py
+++ b/solution.py
@@ -111,8 +111,9 @@
     each = fine_each + coarse_each
 
     def kernel(sf_ref, sc_ref, x_ref, v_ref, e_ref, fine_out, coarse_out, *rest):
-        packet_refs = rest[:slots]
-        fine_v, coarse_v, sem = rest[slots:]
+        fine_refs = rest[:slots]
+        coarse_refs = rest[slots:2 * slots]
+        fine_v, coarse_v, sem = rest[2 * slots:]
         for j in range(parents):
             col = j * 2 * RANK
             f0 = jnp.dot(v_ref[:, col:col + RANK], x_ref[2 * j], preferred_element_type=jnp.float32)
@@ -132,19 +133,21 @@
 
         def picks(q, m, start):
             base = 2 + q * each + m
-            if start:
-                if m < fine_each:
-                    s = jnp.clip(sf_ref[q * fine_each + m], 0, leaves - 1)
-                    src = fine_v.at[s]
-                else:
-                    s = jnp.clip(sc_ref[q * coarse_each + m - fine_each], 0, parents - 1)
-                    src = coarse_v.at[s]
+            if m < fine_each:
+                dst = fine_refs[q].at[m]
+                s = jnp.clip(sf_ref[q * fine_each + m], 0, leaves - 1) if start else 0
+                src = fine_v.at[s]
             else:
-                src = fine_v.at[0]
-            return pltpu.make_async_copy(src, packet_refs[q].at[m], sem.at[base])
+                dst = coarse_refs[q].at[m - fine_each]
+                s = jnp.clip(sc_ref[q * coarse_each + m - fine_each], 0, parents - 1) if start else 0
+                src = coarse_v.at[s]
+            return pltpu.make_async_copy(src, dst, sem.at[base])
 
         for q in range(slots):
-            for m in range(each):
+            for m in range(fine_each, each):
+                picks(q, m, True).start()
+        for q in range(slots):
+            for m in range(fine_each):
                 picks(q, m, True).start()
         for cp in whole:
             cp.wait()
@@ -159,9 +162,10 @@
     outs = pl.pallas_call(
         kernel,
         in_specs=[smem, smem, vmem, vmem, vmem],
-        out_specs=[hbm] * (2 + slots),
+        out_specs=[hbm] * (2 + 2 * slots),
         out_shape=[block((leaves, RANK, RHS), jnp.bfloat16), block((parents, RANK, RHS), jnp.bfloat16)]
-        + [block((each, RANK, RHS), jnp.bfloat16)] * slots,
+        + [block((fine_each, RANK, RHS), jnp.bfloat16)] * slots
+        + [block((coarse_each, RANK, RHS), jnp.bfloat16)] * slots,
         scratch_shapes=[
             pltpu.VMEM((leaves, RANK, RHS), jnp.bfloat16),
             pltpu.VMEM((parents, RANK, RHS), jnp.bfloat16),
@@ -171,7 +175,7 @@
             flops=2 * leaves * LEAF * RANK * RHS * 2, transcendentals=0, bytes_accessed=16 * 2 ** 20
         ),
     )(send_fine, send_coarse, charges, basis_t, transfer_t)
-    return outs[0], outs[1], outs[2:]
+    return outs[0], outs[1], outs[2:2 + slots], outs[2 + slots:]
 
 
 def on_device(
@@ -194,12 +198,15 @@
     axis = ("leaf", "couple")
     basis_t = leaf_basis.T
     transfer_t = transfer.T
-    fine_coeffs, coarse_coeffs, packets = upward(
+    fine_coeffs, coarse_coeffs, fine_packets, coarse_packets = upward(
         charges, basis_t, transfer_t, send_fine[0], send_coarse[0], fine_each, coarse_each
     )
-    incoming = []
+    coarse_in = []
     for slot, offset in enumerate(offset_list()):
-        incoming.append(from_behind(packets[slot], axis, offset))
+        coarse_in.append(from_behind(coarse_packets[slot], axis, offset))
+    fine_in = []
+    for slot, offset in enumerate(offset_list()):
+        fine_in.append(from_behind(fine_packets[slot], axis, offset))
 
     low, high = halo_pieces(charges, axis, HALO)
     near_field = gather_dot(
@@ -211,7 +218,7 @@
 
     coarse_segments = [(coarse_coeffs, 0, parents, 0)]
     for slot in range(2 * REACH):
-        coarse_segments.append((incoming[slot], parents + slot * coarse_each, coarse_each, fine_each))
+        coarse_segments.append((coarse_in[slot], parents + slot * coarse_each, coarse_each, 0))
     coarse_round = gather_dot(
         source_coarse, couple_coarse, coarse_segments, source_coarse.shape[0] // parents,
         out_dtype=jnp.bfloat16,
@@ -219,7 +226,7 @@
 
     fine_segments = [(fine_coeffs, 0, leaves, 0)]
     for slot in range(2 * REACH):
-        fine_segments.append((incoming[slot], leaves + slot * fine_each, fine_each, 0))
+        fine_segments.append((fine_in[slot], leaves + slot * fine_each, fine_each, 0))
 
     tb = min(BLOCK_TARGETS, leaves)
 

time: 110 us -> 112 us (1.018)
  waiting for transfers between devices: 31 us -> 9.72 us
  starting transfers between devices: 28.8 us -> 48.8 us
  local copies, waits for them, and re-layouts: 5.65 us -> 9.88 us
    ppermute x6 -> x12, waiting for transfers between devices: 31 us -> 7.21 us  [from_behind(): lax.ppermute(value, axis, [(source, source + steps) for source in range(f...]
    ppermute x6 -> x12, starting transfers between devices: 21.5 us -> 41.5 us  [from_behind(): lax.ppermute(value, axis, [(source, source + steps) for source in range(f...]
    unnamed x14 -> x30, local copies, waits for them, and re-layouts: 4.77 us -> 8.99 us
    ppermute x1, waiting for transfers between devices: 0.01 us -> 2.5 us  [halo_pieces(): lax.ppermute(lax.slice_in_dim(block, block.shape[0] - width, None, axis=0...]
  transfers between devices with their start and end apart: 8 -> 14, of which waited for: 4 -> 2; matrix products, arithmetic and copies ran while one was open for 5% -> 5% of each run, Pallas kernels for 9% -> 16%
where the time goes in v6:
time: 112 us; the launch traced here: 111 us
  starting transfers between devices  48.8 us (44%)
  Pallas kernels  42.3 us (38%)
  local copies, waits for them, and re-layouts  9.88 us (9%)
  waiting for transfers between devices  9.72 us (9%)
    ppermute x12, starting transfers between devices, from_behind(): lax.ppermute(value, axis, [(source, source + steps) for source in range(f...  41.5 us
    pallas_call x3, Pallas kernels, gather_dot(): pl.pallas_call(kernel, grid_spec=grid_spec, out_shape=jax.ShapeDtypeStruc...  34.9 us
    unnamed x30, local copies, waits for them, and re-layouts  8.99 us
    pallas_call x1, Pallas kernels, upward(): pl.pallas_call(kernel, in_specs=[smem, smem, vmem, vmem, vmem], out_specs...  7.45 us
    ppermute x12, waiting for transfers between devices, from_behind(): lax.ppermute(value, axis, [(source, source + steps) for source in range(f...  7.21 us
    ppermute x1, starting transfers between devices, halo_pieces(): lax.ppermute(lax.slice_in_dim(block, 0, width, axis=0), axis, backward)  4.55 us
    ppermute x1, starting transfers between devices, halo_pieces(): lax.ppermute(lax.slice_in_dim(block, block.shape[0] - width, None, axis=0...  2.81 us
    ppermute x1, waiting for transfers between devices, halo_pieces(): lax.ppermute(lax.slice_in_dim(block, block.shape[0] - width, None, axis=0...  2.5 us
  transfers between devices with their start and end apart: 14, of which 2 were waited for; matrix products, arithmetic and copies ran while one was open for 5% of the time, Pallas kernels for 16%

profile of v6, /device:TPU:24, one launch (start us, length us, event | category | flops | bytes accessed | tf_op | source)
XLA Modules:
  0.0 111.1 jit_solution(16671548559587546197)
XLA Ops:
  0.0 7.5 %shard_map.109 = (bf16[64,64,128]{2,1,0:T(8,128)(2,1)}, bf16[32,64,128]{2,1,0:T(8,128)(2,1)}, bf16[32,64,128]{2,1,0:T(8,128)(2,1)}, bf16[32,64,128]{2,1,0:T(8,12...) custom-call(s32[192]{0:T(256)} %bitcast.6, ...), custom_call_target="tpu_custom_call" | custom-call | flops 134217728 | bytes 16777216 | tf_op jit(solution)/shard_map/pallas_call | solution.py:162
  7.5 2.9 %collective-permute-start.10 = (bf16[16,64,128]{2,1,0:T(8,128)(2,1)}, bf16[16,64,128]{2,1,0:T(8,128)(2,1)S(1)}, u32[]{:S(2)}, u32[]{:S(2)}) collective-permute-start(bf16[16,64,128]{2,1,0:T(8,128)(2,1)} %get-tuple-element.31), channel_id=1, source_target_pairs={{0,3},{1,4},{2,5},{3,6},{4,7},{5,8},{6,9},{7,10},{8,11},{9,12},{10... | collective-permute-start | bytes 786440 | tf_op jit(solution)/shard_map/ppermute | solution.py:21
  10.3 3.6 %collective-permute-start.11 = (bf16[16,64,128]{2,1,0:T(8,128)(2,1)}, bf16[16,64,128]{2,1,0:T(8,128)(2,1)S(1)}, u32[]{:S(2)}, u32[]{:S(2)}) collective-permute-start(bf16[16,64,128]{2,1,0:T(8,128)(2,1)} %get-tuple-element.32), channel_id=1, source_target_pairs={{3,0},{4,1},{5,2},{6,3},{7,4},{8,5},{9,6},{10,7},{11,8},{12,9},{13... | collective-permute-start | bytes 786440 | tf_op jit(solution)/shard_map/ppermute | solution.py:21
  13.9 2.6 %collective-permute-start = (bf16[32,64,128]{2,1,0:T(8,128)(2,1)}, bf16[32,64,128]{2,1,0:T(8,128)(2,1)S(1)}, u32[]{:S(2)}, u32[]{:S(2)}) collective-permute-start(bf16[32,64,128]{2,1,0:T(8,128)(2,1)} %get-tuple-element.20), channel_id=1, source_target_pairs={{0,1},{1,2},{2,3},{3,4},{4,5},{5,6},{6,7},{7,8},{8,9},{9,10},{10,1... | collective-permute-start | bytes 1572872 | tf_op jit(solution)/shard_map/ppermute | solution.py:21
  16.6 0.9 fusion
  17.5 2.8 %collective-permute-start.12 = (bf16[4,64,128]{2,1,0:T(8,128)(2,1)S(1)}, bf16[4,64,128]{2,1,0:T(8,128)(2,1)S(1)}, u32[]{:S(2)}, u32[]{:S(2)}) collective-permute-start(bf16[4,64,128]{2,1,0:T(8,128)(2,1)S(1)} %get-tuple-element.34), channel_id=1, source_target_pairs={{0,1},{1,2},{2,3},{3,4},{4,5},{5,6},{6,7},{7,8},{8,9},{9,10},{10,1... | collective-permute-start | bytes 196616 | tf_op jit(solution)/shard_map/ppermute | solution.py:28
  20.3 4.6 %collective-permute-start.13 = (bf16[4,64,128]{2,1,0:T(8,128)(2,1)S(1)}, bf16[4,64,128]{2,1,0:T(8,128)(2,1)S(1)}, u32[]{:S(2)}, u32[]{:S(2)}) collective-permute-start(bf16[4,64,128]{2,1,0:T(8,128)(2,1)S(1)} %get-tuple-element.33), channel_id=1, source_target_pairs={{1,0},{2,1},{3,2},{4,3},{5,4},{6,5},{7,6},{8,7},{9,8},{10,9},{11,1... | collective-permute-start | bytes 196616 | tf_op jit(solution)/shard_map/ppermute | solution.py:29
  24.9 2.5 %collective-permute-done.12.refs_0_ = bf16[4,64,128]{2,1,0:T(8,128)(2,1)S(1)} collective-permute-done((bf16[4,64,128]{2,1,0:T(8,128)(2,1)S(1)}, bf16[4,64,128]{2,1,0:T(8,128)(2,1)S(1)}, u32[]{:S(2)}, u32[]{:S(2)}) %collective-permute-start.12) | collective-permute-done | bytes 65568 | tf_op jit(solution)/shard_map/ppermute | solution.py:28
  27.4 1.9 %collective-permute-start.6 = (bf16[16,64,128]{2,1,0:T(8,128)(2,1)}, bf16[16,64,128]{2,1,0:T(8,128)(2,1)S(1)}, u32[]{:S(2)}, u32[]{:S(2)}) collective-permute-start(bf16[16,64,128]{2,1,0:T(8,128)(2,1)} %get-tuple-element.27), channel_id=1, source_target_pairs={{0,1},{1,2},{2,3},{3,4},{4,5},{5,6},{6,7},{7,8},{8,9},{9,10},{10,1... | collective-permute-start | bytes 786440 | tf_op jit(solution)/shard_map/ppermute | solution.py:21
  29.3 0.0 collective-permute-done.13.refs_2_
  29.3 5.4 %collective-permute-start.7 = (bf16[16,64,128]{2,1,0:T(8,128)(2,1)}, bf16[16,64,128]{2,1,0:T(8,128)(2,1)S(1)}, u32[]{:S(2)}, u32[]{:S(2)}) collective-permute-start(bf16[16,64,128]{2,1,0:T(8,128)(2,1)} %get-tuple-element.28), channel_id=1, source_target_pairs={{1,0},{2,1},{3,2},{4,3},{5,4},{6,5},{7,6},{8,7},{9,8},{10,9},{11,1... | collective-permute-start | bytes 786440 | tf_op jit(solution)/shard_map/ppermute | solution.py:21
  34.7 0.0 collective-permute-done.10.refs_5_
  34.8 0.0 copy-start.6
  34.8 1.9 %collective-permute-start.8 = (bf16[16,64,128]{2,1,0:T(8,128)(2,1)}, bf16[16,64,128]{2,1,0:T(8,128)(2,1)S(1)}, u32[]{:S(2)}, u32[]{:S(2)}) collective-permute-start(bf16[16,64,128]{2,1,0:T(8,128)(2,1)} %get-tuple-element.29), channel_id=1, source_target_pairs={{0,2},{1,3},{2,4},{3,5},{4,6},{5,7},{6,8},{7,9},{8,10},{9,11},{10,... | collective-permute-start | bytes 786440 | tf_op jit(solution)/shard_map/ppermute | solution.py:21
  36.7 0.0 collective-permute-done.11.refs_6_
  36.7 0.0 copy-start.7
  36.7 5.7 %collective-permute-start.9 = (bf16[16,64,128]{2,1,0:T(8,128)(2,1)}, bf16[16,64,128]{2,1,0:T(8,128)(2,1)S(1)}, u32[]{:S(2)}, u32[]{:S(2)}) collective-permute-start(bf16[16,64,128]{2,1,0:T(8,128)(2,1)} %get-tuple-element.30), channel_id=1, source_target_pairs={{2,0},{3,1},{4,2},{5,3},{6,4},{7,5},{8,6},{9,7},{10,8},{11,9},{12,... | collective-permute-start | bytes 786440 | tf_op jit(solution)/shard_map/ppermute | solution.py:21
  42.4 0.0 collective-permute-done.6.refs_1_
  42.5 0.7 copy-done.8
  43.2 1.9 %collective-permute-start.1 = (bf16[32,64,128]{2,1,0:T(8,128)(2,1)}, bf16[32,64,128]{2,1,0:T(8,128)(2,1)S(1)}, u32[]{:S(2)}, u32[]{:S(2)}) collective-permute-start(bf16[32,64,128]{2,1,0:T(8,128)(2,1)} %get-tuple-element.21), channel_id=1, source_target_pairs={{1,0},{2,1},{3,2},{4,3},{5,4},{6,5},{7,6},{8,7},{9,8},{10,9},{11,1... | collective-permute-start | bytes 1572872 | tf_op jit(solution)/shard_map/ppermute | solution.py:21
  45.1 0.0 collective-permute-done.7.refs_2_
  45.1 0.0 copy-start.9
  45.1 0.7 copy-done.9
  45.8 2.0 %collective-permute-start.2 = (bf16[32,64,128]{2,1,0:T(8,128)(2,1)}, bf16[32,64,128]{2,1,0:T(8,128)(2,1)S(1)}, u32[]{:S(2)}, u32[]{:S(2)}) collective-permute-start(bf16[32,64,128]{2,1,0:T(8,128)(2,1)} %get-tuple-element.22), channel_id=1, source_target_pairs={{0,2},{1,3},{2,4},{3,5},{4,6},{5,7},{6,8},{7,9},{8,10},{9,11},{10,... | collective-permute-start | bytes 1572872 | tf_op jit(solution)/shard_map/ppermute | solution.py:21
  47.8 7.2 %collective-permute-done.8.refs_3_ = bf16[16,64,128]{2,1,0:T(8,128)(2,1)S(1)} collective-permute-done((bf16[16,64,128]{2,1,0:T(8,128)(2,1)}, bf16[16,64,128]{2,1,0:T(8,128)(2,1)S(1)}, u32[]{:S(2)}, u32[]{:S(2)}) %collective-permute-start.8) | collective-permute-done | bytes 262176 | tf_op jit(solution)/shard_map/ppermute | solution.py:21
  55.0 0.7 copy-done.10
  55.7 7.0 %collective-permute-start.3 = (bf16[32,64,128]{2,1,0:T(8,128)(2,1)}, bf16[32,64,128]{2,1,0:T(8,128)(2,1)S(1)}, u32[]{:S(2)}, u32[]{:S(2)}) collective-permute-start(bf16[32,64,128]{2,1,0:T(8,128)(2,1)} %get-tuple-element.23), channel_id=1, source_target_pairs={{2,0},{3,1},{4,2},{5,3},{6,4},{7,5},{8,6},{9,7},{10,8},{11,9},{12,... | collective-permute-start | bytes 1572872 | tf_op jit(solution)/shard_map/ppermute | solution.py:21
  62.7 0.0 collective-permute-done.9.refs_4_
  62.7 0.0 copy-start.11
  62.7 0.7 copy-done.11
  63.5 1.9 %collective-permute-start.4 = (bf16[32,64,128]{2,1,0:T(8,128)(2,1)}, bf16[32,64,128]{2,1,0:T(8,128)(2,1)S(1)}, u32[]{:S(2)}, u32[]{:S(2)}) collective-permute-start(bf16[32,64,128]{2,1,0:T(8,128)(2,1)} %get-tuple-element.24), channel_id=1, source_target_pairs={{0,3},{1,4},{2,5},{3,6},{4,7},{5,8},{6,9},{7,10},{8,11},{9,12},{10... | collective-permute-start | bytes 1572872 | tf_op jit(solution)/shard_map/ppermute | solution.py:21
  65.4 0.0 collective-permute-done.refs_1_
  65.4 4.5 %collective-permute-start.5 = (bf16[32,64,128]{2,1,0:T(8,128)(2,1)}, bf16[32,64,128]{2,1,0:T(8,128)(2,1)S(1)}, u32[]{:S(2)}, u32[]{:S(2)}) collective-permute-start(bf16[32,64,128]{2,1,0:T(8,128)(2,1)} %get-tuple-element.25), channel_id=1, source_target_pairs={{3,0},{4,1},{5,2},{6,3},{7,4},{8,5},{9,6},{10,7},{11,8},{12,9},{13... | collective-permute-start | bytes 1572872 | tf_op jit(solution)/shard_map/ppermute | solution.py:21
  69.9 2.3 %copy.12.refs_8_ = bf16[4096,64]{1,0:T(8,128)(2,1)} copy(bf16[4096,64]{0,1:T(8,128)(2,1)} %param.13) | data formatting | bytes 1048576 | tf_op args[2]
  72.3 2.4 %copy.13.refs_9_ = bf16[4096,64]{1,0:T(8,128)(2,1)} copy(bf16[4096,64]{0,1:T(8,128)(2,1)} %param.12) | data formatting | bytes 1048576 | tf_op args[1]
  74.7 10.2 %shard_map.111.refs_10_ = f32[64,64,128]{2,1,0:T(8,128)} custom-call(s32[768]{0:T(1024)} %idx_ref.4, bf16[4096,768]{1,0:T(8,128)(2,1)} %mats_ref.4, bf16[4,64,128]{2,1,0:T(8,128)(2,1)} %copy-done.12, bf16[64,64,128]{2,1,0:T(8,128)(2,1)} %refs_1_.1, bf16[4,64,128]{2,1,0:T(8,128)(2,1)} %copy-done.13), custom_call_target="tpu_custom_call" | custom-call | flops 805306368 | bytes 9568256 | tf_op jit(solution)/shard_map/pallas_call | solution.py:98
  84.9 7.3 %shard_map.110.refs_7_ = bf16[32,64,128]{2,1,0:T(8,128)(2,1)} custom-call(s32[512]{0:T(512)} %idx_ref.3, bf16[2048,1024]{1,0:T(8,128)(2,1)} %mats_ref.3, bf16[32,64,128]{2,1,0:T(8,128)(2,1)} %get-tuple-element.26.refs_0_, bf16[16,64,128]{2,1,0:T(8,128)(2,1)} %copy-done.8, bf16[16,64,128]{2,1,0:T(8,128)(2,1)} %copy-done.9, bf16[16,64,128]{2,1,0:T(8,128)(2,1)} %copy-done.10, ...), custom_call_target="tpu_custom_call" | custom-call | flops 536870912 | bytes 7340032 | tf_op jit(solution)/shard_map/pallas_call | solution.py:98
  92.1 0.0 collective-permute-done.1.refs_2_
  92.2 0.0 collective-permute-done.2.refs_3_
  92.2 0.0 collective-permute-done.3.refs_4_
  92.2 0.0 collective-permute-done.4.refs_5_
  92.2 0.0 collective-permute-done.5.refs_6_
  92.2 0.7 copy-done.1
  93.0 0.2 copy-done.2
  93.1 0.2 copy-done.3
  93.3 0.2 copy-done.4
  93.5 0.2 copy-done.5
  93.7 17.4 %shard_map.112 = bf16[64,64,128]{2,1,0:T(8,128)(2,1)} custom-call(s32[1024]{0:T(1024)} %idx_ref.5, bf16[4096,1024]{1,0:T(8,128)(2,1)} %mats_ref.5, bf16[64,64,128]{2,1,0:T(8,128)(2,1)} %get-tuple-element.19.refs_0_, bf16[32,64,128]{2,1,0:T(8,128)(2,1)} %copy-done, bf16[32,64,128]{2,1,0:T(8,128)(2,1)} %copy-done.1, bf16[32,64,128]{2,1,0:T(8,128)(2,1)} %copy-done.2, ...), custom_call_target="tpu_custom_call" | custom-call | flops 1073741824 | bytes 14680064 | tf_op jit(solution)/shard_map/pallas_call | solution.py:98
  (15 shorter events, 0.0 us)
Async XLA Ops:
  7.5 27.3 %collective-permute-start.10 = (bf16[16,64,128]{2,1,0:T(8,128)(2,1)}, bf16[16,64,128]{2,1,0:T(8,128)(2,1)S(1)}, u32[]{:S(2)}, u32[]{:S(2)}) collective-permute-start(bf16[16,64,128]{2,1,0:T(8,128)(2,1)} %get-tuple-element.31), channel_id=1, source_target_pairs={{0,3},{1,4},{2,5},{3,6},{4,7},{5,8},{6,9},{7,10},{8,11},{9,12},{10... | collective-permute-start | bytes 786440 | tf_op jit(solution)/shard_map/ppermute | solution.py:21
  10.3 26.4 %collective-permute-start.11 = (bf16[16,64,128]{2,1,0:T(8,128)(2,1)}, bf16[16,64,128]{2,1,0:T(8,128)(2,1)S(1)}, u32[]{:S(2)}, u32[]{:S(2)}) collective-permute-start(bf16[16,64,128]{2,1,0:T(8,128)(2,1)} %get-tuple-element.32), channel_id=1, source_target_pairs={{3,0},{4,1},{5,2},{6,3},{7,4},{8,5},{9,6},{10,7},{11,8},{12,9},{13... | collective-permute-start | bytes 786440 | tf_op jit(solution)/shard_map/ppermute | solution.py:21
  13.9 51.4 %collective-permute-start = (bf16[32,64,128]{2,1,0:T(8,128)(2,1)}, bf16[32,64,128]{2,1,0:T(8,128)(2,1)S(1)}, u32[]{:S(2)}, u32[]{:S(2)}) collective-permute-start(bf16[32,64,128]{2,1,0:T(8,128)(2,1)} %get-tuple-element.20), channel_id=1, source_target_pairs={{0,1},{1,2},{2,3},{3,4},{4,5},{5,6},{6,7},{7,8},{8,9},{9,10},{10,1... | collective-permute-start | bytes 1572872 | tf_op jit(solution)/shard_map/ppermute | solution.py:21
  17.5 9.9 %collective-permute-start.12 = (bf16[4,64,128]{2,1,0:T(8,128)(2,1)S(1)}, bf16[4,64,128]{2,1,0:T(8,128)(2,1)S(1)}, u32[]{:S(2)}, u32[]{:S(2)}) collective-permute-start(bf16[4,64,128]{2,1,0:T(8,128)(2,1)S(1)} %get-tuple-element.34), channel_id=1, source_target_pairs={{0,1},{1,2},{2,3},{3,4},{4,5},{5,6},{6,7},{7,8},{8,9},{9,10},{10,1... | collective-permute-start | bytes 196616 | tf_op jit(solution)/shard_map/ppermute | solution.py:28
  20.3 9.0 %collective-permute-start.13 = (bf16[4,64,128]{2,1,0:T(8,128)(2,1)S(1)}, bf16[4,64,128]{2,1,0:T(8,128)(2,1)S(1)}, u32[]{:S(2)}, u32[]{:S(2)}) collective-permute-start(bf16[4,64,128]{2,1,0:T(8,128)(2,1)S(1)} %get-tuple-element.33), channel_id=1, source_target_pairs={{1,0},{2,1},{3,2},{4,3},{5,4},{6,5},{7,6},{8,7},{9,8},{10,9},{11,1... | collective-permute-start | bytes 196616 | tf_op jit(solution)/shard_map/ppermute | solution.py:29
  27.4 47.3 %copy-start.12 = (bf16[4,64,128]{2,1,0:T(8,128)(2,1)}, bf16[4,64,128]{2,1,0:T(8,128)(2,1)S(1)}, u32[]{:S(2)}) copy-start(bf16[4,64,128]{2,1,0:T(8,128)(2,1)S(1)} %collective-permute-done.12.refs_0_) | copy-start | bytes 196612
  27.4 15.1 %collective-permute-start.6 = (bf16[16,64,128]{2,1,0:T(8,128)(2,1)}, bf16[16,64,128]{2,1,0:T(8,128)(2,1)S(1)}, u32[]{:S(2)}, u32[]{:S(2)}) collective-permute-start(bf16[16,64,128]{2,1,0:T(8,128)(2,1)} %get-tuple-element.27), channel_id=1, source_target_pairs={{0,1},{1,2},{2,3},{3,4},{4,5},{5,6},{6,7},{7,8},{8,9},{9,10},{10,1... | collective-permute-start | bytes 786440 | tf_op jit(solution)/shard_map/ppermute | solution.py:21
  29.3 45.4 %copy-start.13 = (bf16[4,64,128]{2,1,0:T(8,128)(2,1)}, bf16[4,64,128]{2,1,0:T(8,128)(2,1)S(1)}, u32[]{:S(2)}) copy-start(bf16[4,64,128]{2,1,0:T(8,128)(2,1)S(1)} %collective-permute-done.13.refs_2_) | copy-start | bytes 196612
  29.3 15.8 %collective-permute-start.7 = (bf16[16,64,128]{2,1,0:T(8,128)(2,1)}, bf16[16,64,128]{2,1,0:T(8,128)(2,1)S(1)}, u32[]{:S(2)}, u32[]{:S(2)}) collective-permute-start(bf16[16,64,128]{2,1,0:T(8,128)(2,1)} %get-tuple-element.28), channel_id=1, source_target_pairs={{1,0},{2,1},{3,2},{4,3},{5,4},{6,5},{7,6},{8,7},{9,8},{10,9},{11,1... | collective-permute-start | bytes 786440 | tf_op jit(solution)/shard_map/ppermute | solution.py:21
  34.8 50.1 %copy-start.6 = (bf16[16,64,128]{2,1,0:T(8,128)(2,1)}, bf16[16,64,128]{2,1,0:T(8,128)(2,1)S(1)}, u32[]{:S(2)}) copy-start(bf16[16,64,128]{2,1,0:T(8,128)(2,1)S(1)} %collective-permute-done.10.refs_5_) | copy-start | bytes 786436
  34.8 20.2 %collective-permute-start.8 = (bf16[16,64,128]{2,1,0:T(8,128)(2,1)}, bf16[16,64,128]{2,1,0:T(8,128)(2,1)S(1)}, u32[]{:S(2)}, u32[]{:S(2)}) collective-permute-start(bf16[16,64,128]{2,1,0:T(8,128)(2,1)} %get-tuple-element.29), channel_id=1, source_target_pairs={{0,2},{1,3},{2,4},{3,5},{4,6},{5,7},{6,8},{7,9},{8,10},{9,11},{10,... | collective-permute-start | bytes 786440 | tf_op jit(solution)/shard_map/ppermute | solution.py:21
  36.7 5.8 %copy-start.7 = (bf16[16,64,128]{2,1,0:T(8,128)(2,1)}, bf16[16,64,128]{2,1,0:T(8,128)(2,1)S(1)}, u32[]{:S(2)}) copy-start(bf16[16,64,128]{2,1,0:T(8,128)(2,1)S(1)} %collective-permute-done.11.refs_6_) | copy-start | bytes 786436
  36.7 26.0 %collective-permute-start.9 = (bf16[16,64,128]{2,1,0:T(8,128)(2,1)}, bf16[16,64,128]{2,1,0:T(8,128)(2,1)S(1)}, u32[]{:S(2)}, u32[]{:S(2)}) collective-permute-start(bf16[16,64,128]{2,1,0:T(8,128)(2,1)} %get-tuple-element.30), channel_id=1, source_target_pairs={{2,0},{3,1},{4,2},{5,3},{6,4},{7,5},{8,6},{9,7},{10,8},{11,9},{12,... | collective-permute-start | bytes 786440 | tf_op jit(solution)/shard_map/ppermute | solution.py:21
  42.5 0.7 copy-start.8
  43.2 49.0 %collective-permute-start.1 = (bf16[32,64,128]{2,1,0:T(8,128)(2,1)}, bf16[32,64,128]{2,1,0:T(8,128)(2,1)S(1)}, u32[]{:S(2)}, u32[]{:S(2)}) collective-permute-start(bf16[32,64,128]{2,1,0:T(8,128)(2,1)} %get-tuple-element.21), channel_id=1, source_target_pairs={{1,0},{2,1},{3,2},{4,3},{5,4},{6,5},{7,6},{8,7},{9,8},{10,9},{11,1... | collective-permute-start | bytes 1572872 | tf_op jit(solution)/shard_map/ppermute | solution.py:21
  45.1 0.7 copy-start.9
  45.8 46.4 %collective-permute-start.2 = (bf16[32,64,128]{2,1,0:T(8,128)(2,1)}, bf16[32,64,128]{2,1,0:T(8,128)(2,1)S(1)}, u32[]{:S(2)}, u32[]{:S(2)}) collective-permute-start(bf16[32,64,128]{2,1,0:T(8,128)(2,1)} %get-tuple-element.22), channel_id=1, source_target_pairs={{0,2},{1,3},{2,4},{3,5},{4,6},{5,7},{6,8},{7,9},{8,10},{9,11},{10,... | collective-permute-start | bytes 1572872 | tf_op jit(solution)/shard_map/ppermute | solution.py:21
  55.0 0.7 copy-start.10
  55.7 36.5 %collective-permute-start.3 = (bf16[32,64,128]{2,1,0:T(8,128)(2,1)}, bf16[32,64,128]{2,1,0:T(8,128)(2,1)S(1)}, u32[]{:S(2)}, u32[]{:S(2)}) collective-permute-start(bf16[32,64,128]{2,1,0:T(8,128)(2,1)} %get-tuple-element.23), channel_id=1, source_target_pairs={{2,0},{3,1},{4,2},{5,3},{6,4},{7,5},{8,6},{9,7},{10,8},{11,9},{12,... | collective-permute-start | bytes 1572872 | tf_op jit(solution)/shard_map/ppermute | solution.py:21
  62.7 0.7 copy-start.11
  63.5 28.8 %collective-permute-start.4 = (bf16[32,64,128]{2,1,0:T(8,128)(2,1)}, bf16[32,64,128]{2,1,0:T(8,128)(2,1)S(1)}, u32[]{:S(2)}, u32[]{:S(2)}) collective-permute-start(bf16[32,64,128]{2,1,0:T(8,128)(2,1)} %get-tuple-element.24), channel_id=1, source_target_pairs={{0,3},{1,4},{2,5},{3,6},{4,7},{5,8},{6,9},{7,10},{8,11},{9,12},{10... | collective-permute-start | bytes 1572872 | tf_op jit(solution)/shard_map/ppermute | solution.py:21
  65.4 19.5 %copy-start = (bf16[32,64,128]{2,1,0:T(8,128)(2,1)}, bf16[32,64,128]{2,1,0:T(8,128)(2,1)S(1)}, u32[]{:S(2)}) copy-start(bf16[32,64,128]{2,1,0:T(8,128)(2,1)S(1)} %collective-permute-done.refs_1_) | copy-start | bytes 1572868
  65.4 26.8 %collective-permute-start.5 = (bf16[32,64,128]{2,1,0:T(8,128)(2,1)}, bf16[32,64,128]{2,1,0:T(8,128)(2,1)S(1)}, u32[]{:S(2)}, u32[]{:S(2)}) collective-permute-start(bf16[32,64,128]{2,1,0:T(8,128)(2,1)} %get-tuple-element.25), channel_id=1, source_target_pairs={{3,0},{4,1},{5,2},{6,3},{7,4},{8,5},{9,6},{10,7},{11,8},{12,9},{13... | collective-permute-start | bytes 1572872 | tf_op jit(solution)/shard_map/ppermute | solution.py:21
  92.2 0.8 copy-start.1
  92.2 1.0 copy-start.2
  92.2 1.1 copy-start.3
  92.2 1.3 %copy-start.4 = (bf16[32,64,128]{2,1,0:T(8,128)(2,1)}, bf16[32,64,128]{2,1,0:T(8,128)(2,1)S(1)}, u32[]{:S(2)}) copy-start(bf16[32,64,128]{2,1,0:T(8,128)(2,1)S(1)} %collective-permute-done.4.refs_5_) | copy-start | bytes 1572868
  92.2 1.4 %copy-start.5 = (bf16[32,64,128]{2,1,0:T(8,128)(2,1)}, bf16[32,64,128]{2,1,0:T(8,128)(2,1)S(1)}, u32[]{:S(2)}) copy-start(bf16[32,64,128]{2,1,0:T(8,128)(2,1)S(1)} %collective-permute-done.5.refs_6_) | copy-start | bytes 1572868

commit v7 on v5

--- a/solution.py
+++ b/solution.py
@@ -109,10 +109,13 @@
     parents = leaves // 2
     slots = 2 * REACH
     each = fine_each + coarse_each
+    sizes = [each + (HALO if q < 2 else 0) for q in range(slots)]
 
     def kernel(sf_ref, sc_ref, x_ref, v_ref, e_ref, fine_out, coarse_out, *rest):
         packet_refs = rest[:slots]
-        fine_v, coarse_v, sem = rest[slots:]
+        fine_v, coarse_v = rest[slots:slots + 2]
+        bufs = rest[slots + 2:2 * slots + 2]
+        sem = rest[2 * slots + 2]
         for j in range(parents):
             col = j * 2 * RANK
             f0 = jnp.dot(v_ref[:, col:col + RANK], x_ref[2 * j], preferred_element_type=jnp.float32)
@@ -123,34 +126,27 @@
             e = e_ref[:, col:col + 2 * RANK]
             coarse_v[j] = jnp.dot(e, pair, preferred_element_type=jnp.float32).astype(jnp.bfloat16)
 
-        whole = [
+        copies = [
             pltpu.make_async_copy(fine_v, fine_out, sem.at[0]),
             pltpu.make_async_copy(coarse_v, coarse_out, sem.at[1]),
         ]
-        for cp in whole:
+        for cp in copies:
             cp.start()
-
-        def picks(q, m, start):
-            base = 2 + q * each + m
-            if start:
-                if m < fine_each:
-                    s = jnp.clip(sf_ref[q * fine_each + m], 0, leaves - 1)
-                    src = fine_v.at[s]
-                else:
-                    s = jnp.clip(sc_ref[q * coarse_each + m - fine_each], 0, parents - 1)
-                    src = coarse_v.at[s]
-            else:
-                src = fine_v.at[0]
-            return pltpu.make_async_copy(src, packet_refs[q].at[m], sem.at[base])
-
         for q in range(slots):
-            for m in range(each):
-                picks(q, m, True).start()
-        for cp in whole:
+            buf = bufs[q]
+            for m in range(fine_each):
+                buf[m] = fine_v[jnp.clip(sf_ref[q * fine_each + m], 0, leaves - 1)]
+            for m in range(coarse_each):
+                buf[fine_each + m] = coarse_v[jnp.clip(sc_ref[q * coarse_each + m], 0, parents - 1)]
+            if q == 0:
+                buf[each:each + HALO] = x_ref[leaves - HALO:leaves]
+            elif q == 1:
+                buf[each:each + HALO] = x_ref[0:HALO]
+            cp = pltpu.make_async_copy(buf, packet_refs[q], sem.at[2 + q])
+            cp.start()
+            copies.append(cp)
+        for cp in copies:
             cp.wait()
-        for q in range(slots):
-            for m in range(each):
-                picks(q, m, False).wait()
 
     smem = pl.BlockSpec(memory_space=pltpu.SMEM)
     vmem = pl.BlockSpec(memory_space=pltpu.VMEM)
@@ -161,12 +157,13 @@
         in_specs=[smem, smem, vmem, vmem, vmem],
         out_specs=[hbm] * (2 + slots),
         out_shape=[block((leaves, RANK, RHS), jnp.bfloat16), block((parents, RANK, RHS), jnp.bfloat16)]
-        + [block((each, RANK, RHS), jnp.bfloat16)] * slots,
+        + [block((n, RANK, RHS), jnp.bfloat16) for n in sizes],
         scratch_shapes=[
             pltpu.VMEM((leaves, RANK, RHS), jnp.bfloat16),
             pltpu.VMEM((parents, RANK, RHS), jnp.bfloat16),
-            pltpu.SemaphoreType.DMA((2 + slots * each,)),
-        ],
+        ]
+        + [pltpu.VMEM((n, RANK, RHS), jnp.bfloat16) for n in sizes]
+        + [pltpu.SemaphoreType.DMA((2 + slots,))],
         cost_estimate=pl.CostEstimate(
             flops=2 * leaves * LEAF * RANK * RHS * 2, transcendentals=0, bytes_accessed=16 * 2 ** 20
         ),
@@ -201,11 +198,11 @@
     for slot, offset in enumerate(offset_list()):
         incoming.append(from_behind(packets[slot], axis, offset))
 
-    low, high = halo_pieces(charges, axis, HALO)
+    each = fine_each + coarse_each
     near_field = gather_dot(
         near_source,
         near_blocks,
-        [(low, 0, HALO, 0), (charges, HALO, leaves, 0), (high, HALO + leaves, HALO, 0)],
+        [(incoming[0], 0, HALO, each), (charges, HALO, leaves, 0), (incoming[1], HALO + leaves, HALO, each)],
         near_source.shape[0] // leaves,
     )
 

time: 110 us -> 107 us (0.973); the launches traced: 108 us -> 106 us
  starting transfers between devices: 28.8 us -> 45.5 us
  waiting for transfers between devices: 31 us -> 14.3 us
  Pallas kernels: 42.3 us -> 40 us
    ppermute x6, starting transfers between devices: 21.5 us -> 45.5 us  [from_behind(): lax.ppermute(value, axis, [(source, source + steps) for source in range(f...]
    ppermute x6, waiting for transfers between devices: 31 us -> 14.3 us  [from_behind(): lax.ppermute(value, axis, [(source, source + steps) for source in range(f...]
    ppermute x2 -> x0, starting transfers between devices: 7.36 us -> none  [the longest x1 5.44 us: halo_pieces(): lax.ppermute(lax.slice_in_dim(block, 0, width, axis=0), axis, backward)]
    pallas_call x1, Pallas kernels: 7.4 us -> 5.1 us  [upward(): pl.pallas_call(kernel, in_specs=[smem, smem, vmem, vmem, vmem], out_specs...]
    unnamed x14 -> x10, local copies, waits for them, and re-layouts: 4.77 us -> 6.51 us
  transfers between devices with their start and end apart: 8 -> 6, of which waited for: 4 -> 2; matrix products, arithmetic and copies ran while one was open for 5% -> 4% of each run, Pallas kernels for 9% -> 10%
where the time goes in v7:
time: 107 us; the launch traced here: 106 us
  starting transfers between devices  45.5 us (43%)
  Pallas kernels  40 us (37%)
  waiting for transfers between devices  14.3 us (13%)
  local copies, waits for them, and re-layouts  6.51 us (6%)
    ppermute x6, starting transfers between devices, from_behind(): lax.ppermute(value, axis, [(source, source + steps) for source in range(f...  45.5 us
    pallas_call x3, Pallas kernels, gather_dot(): pl.pallas_call(kernel, grid_spec=grid_spec, out_shape=jax.ShapeDtypeStruc...  34.9 us
    ppermute x6, waiting for transfers between devices, from_behind(): lax.ppermute(value, axis, [(source, source + steps) for source in range(f...  14.3 us
    unnamed x10, local copies, waits for them, and re-layouts  6.51 us
    pallas_call x1, Pallas kernels, upward(): pl.pallas_call(kernel, in_specs=[smem, smem, vmem, vmem, vmem], out_specs...  5.1 us
  transfers between devices with their start and end apart: 6, of which 2 were waited for; matrix products, arithmetic and copies ran while one was open for 4% of the time, Pallas kernels for 10%

profile of v7, /device:TPU:24, one launch (start us, length us, event | category | flops | bytes accessed | tf_op | source)
XLA Modules:
  0.0 106.4 jit_solution(11328132145210140320)
XLA Ops:
  0.0 5.1 %shard_map.109 = (bf16[64,64,128]{2,1,0:T(8,128)(2,1)}, bf16[32,64,128]{2,1,0:T(8,128)(2,1)}, bf16[52,64,128]{2,1,0:T(8,128)(2,1)}, bf16[52,64,128]{2,1,0:T(8,12...) custom-call(s32[192]{0:T(256)} %bitcast.6, ...), custom_call_target="tpu_custom_call" | custom-call | flops 134217728 | bytes 16777216 | tf_op jit(solution)/shard_map/pallas_call | solution.py:155
  5.1 1.9 %collective-permute-start = (bf16[52,64,128]{2,1,0:T(8,128)(2,1)}, bf16[52,64,128]{2,1,0:T(8,128)(2,1)S(1)}, u32[]{:S(2)}, u32[]{:S(2)}) collective-permute-start(bf16[52,64,128]{2,1,0:T(8,128)(2,1)} %get-tuple-element.14), channel_id=1, source_target_pairs={{0,1},{1,2},{2,3},{3,4},{4,5},{5,6},{6,7},{7,8},{8,9},{9,10},{10,1... | collective-permute-start | bytes 2555912 | tf_op jit(solution)/shard_map/ppermute | solution.py:21
  7.0 5.4 %collective-permute-start.1 = (bf16[52,64,128]{2,1,0:T(8,128)(2,1)}, bf16[52,64,128]{2,1,0:T(8,128)(2,1)S(1)}, u32[]{:S(2)}, u32[]{:S(2)}) collective-permute-start(bf16[52,64,128]{2,1,0:T(8,128)(2,1)} %get-tuple-element.15), channel_id=1, source_target_pairs={{1,0},{2,1},{3,2},{4,3},{5,4},{6,5},{7,6},{8,7},{9,8},{10,9},{11,1... | collective-permute-start | bytes 2555912 | tf_op jit(solution)/shard_map/ppermute | solution.py:21
  12.5 1.9 %collective-permute-start.2 = (bf16[48,64,128]{2,1,0:T(8,128)(2,1)}, bf16[48,64,128]{2,1,0:T(8,128)(2,1)S(1)}, u32[]{:S(2)}, u32[]{:S(2)}) collective-permute-start(bf16[48,64,128]{2,1,0:T(8,128)(2,1)} %get-tuple-element.16), channel_id=1, source_target_pairs={{0,2},{1,3},{2,4},{3,5},{4,6},{5,7},{6,8},{7,9},{8,10},{9,11},{10,... | collective-permute-start | bytes 2359304 | tf_op jit(solution)/shard_map/ppermute | solution.py:21
  14.4 5.7 %collective-permute-start.3 = (bf16[48,64,128]{2,1,0:T(8,128)(2,1)}, bf16[48,64,128]{2,1,0:T(8,128)(2,1)S(1)}, u32[]{:S(2)}, u32[]{:S(2)}) collective-permute-start(bf16[48,64,128]{2,1,0:T(8,128)(2,1)} %get-tuple-element.17), channel_id=1, source_target_pairs={{2,0},{3,1},{4,2},{5,3},{6,4},{7,5},{8,6},{9,7},{10,8},{11,9},{12,... | collective-permute-start | bytes 2359304 | tf_op jit(solution)/shard_map/ppermute | solution.py:21
  20.1 1.9 %collective-permute-start.4 = (bf16[48,64,128]{2,1,0:T(8,128)(2,1)}, bf16[48,64,128]{2,1,0:T(8,128)(2,1)}, u32[]{:S(2)}, u32[]{:S(2)}) collective-permute-start(bf16[48,64,128]{2,1,0:T(8,128)(2,1)} %get-tuple-element.18), channel_id=1, source_target_pairs={{0,3},{1,4},{2,5},{3,6},{4,7},{5,8},{6,9},{7,10},{8,11},{9,12},{10... | collective-permute-start | bytes 2359304 | tf_op jit(solution)/shard_map/ppermute | solution.py:21
  22.1 0.3 collective-permute-done.refs_1_.refs_0_
  22.3 0.0 copy-start
  22.3 28.6 %collective-permute-start.5 = (bf16[48,64,128]{2,1,0:T(8,128)(2,1)}, bf16[48,64,128]{2,1,0:T(8,128)(2,1)}, u32[]{:S(2)}, u32[]{:S(2)}) collective-permute-start(bf16[48,64,128]{2,1,0:T(8,128)(2,1)} %get-tuple-element.19), channel_id=1, source_target_pairs={{3,0},{4,1},{5,2},{6,3},{7,4},{8,5},{9,6},{10,7},{11,8},{12,9},{13... | collective-permute-start | bytes 2359304 | tf_op jit(solution)/shard_map/ppermute | solution.py:21
  50.9 2.3 %copy.13.refs_9_ = bf16[4096,64]{1,0:T(8,128)(2,1)} copy(bf16[4096,64]{0,1:T(8,128)(2,1)} %param.12) | data formatting | bytes 1048576 | tf_op args[1]
  53.3 2.4 %copy.12.refs_8_ = bf16[4096,64]{1,0:T(8,128)(2,1)} copy(bf16[4096,64]{0,1:T(8,128)(2,1)} %param.13) | data formatting | bytes 1048576 | tf_op args[2]
  55.6 0.0 collective-permute-done.1.refs_2_
  55.6 0.0 copy-done
  55.7 0.0 copy-start.1
  55.7 0.9 copy-done.1
  56.6 10.2 %shard_map.111.refs_10_ = f32[64,64,128]{2,1,0:T(8,128)} custom-call(s32[768]{0:T(1024)} %idx_ref.4, bf16[4096,768]{1,0:T(8,128)(2,1)} %mats_ref.4, bf16[52,64,128]{2,1,0:T(8,128)(2,1)} %copy-done, bf16[64,64,128]{2,1,0:T(8,128)(2,1)} %refs_1_.1, bf16[52,64,128]{2,1,0:T(8,128)(2,1)} %copy-done.1), custom_call_target="tpu_custom_call" | custom-call | flops 805306368 | bytes 9568256 | tf_op jit(solution)/shard_map/pallas_call | solution.py:98
  66.8 0.0 collective-permute-done.2.refs_3_
  66.8 0.0 copy-start.2
  66.8 14.0 %collective-permute-done.3.refs_4_ = bf16[48,64,128]{2,1,0:T(8,128)(2,1)S(1)} collective-permute-done((bf16[48,64,128]{2,1,0:T(8,128)(2,1)}, bf16[48,64,128]{2,1,0:T(8,128)(2,1)S(1)}, u32[]{:S(2)}, u32[]{:S(2)}) %collective-permute-start.3) | collective-permute-done | bytes 786464 | tf_op jit(solution)/shard_map/ppermute | solution.py:21
  80.8 0.0 copy-start.3
  80.8 0.0 collective-permute-done.4.refs_5_
  80.8 0.0 collective-permute-done.5.refs_6_
  80.8 0.0 copy-done.2
  80.8 0.9 copy-done.3
  81.7 7.2 %shard_map.110.refs_7_ = bf16[32,64,128]{2,1,0:T(8,128)(2,1)} custom-call(s32[512]{0:T(512)} %idx_ref.3, bf16[2048,1024]{1,0:T(8,128)(2,1)} %mats_ref.3, bf16[32,64,128]{2,1,0:T(8,128)(2,1)} %get-tuple-element.20.refs_0_, bf16[52,64,128]{2,1,0:T(8,128)(2,1)} %copy-done, bf16[52,64,128]{2,1,0:T(8,128)(2,1)} %copy-done.1, bf16[48,64,128]{2,1,0:T(8,128)(2,1)} %copy-done.2, ...), custom_call_target="tpu_custom_call" | custom-call | flops 536870912 | bytes 7340032 | tf_op jit(solution)/shard_map/pallas_call | solution.py:98
  89.0 17.4 %shard_map.112 = bf16[64,64,128]{2,1,0:T(8,128)(2,1)} custom-call(s32[1024]{0:T(1024)} %idx_ref.5, bf16[4096,1024]{1,0:T(8,128)(2,1)} %mats_ref.5, bf16[64,64,128]{2,1,0:T(8,128)(2,1)} %get-tuple-element.13.refs_0_, bf16[52,64,128]{2,1,0:T(8,128)(2,1)} %copy-done, bf16[52,64,128]{2,1,0:T(8,128)(2,1)} %copy-done.1, bf16[48,64,128]{2,1,0:T(8,128)(2,1)} %copy-done.2, ...), custom_call_target="tpu_custom_call" | custom-call | flops 1073741824 | bytes 14680064 | tf_op jit(solution)/shard_map/pallas_call | solution.py:98
Async XLA Ops:
  5.1 17.2 %collective-permute-start = (bf16[52,64,128]{2,1,0:T(8,128)(2,1)}, bf16[52,64,128]{2,1,0:T(8,128)(2,1)S(1)}, u32[]{:S(2)}, u32[]{:S(2)}) collective-permute-start(bf16[52,64,128]{2,1,0:T(8,128)(2,1)} %get-tuple-element.14), channel_id=1, source_target_pairs={{0,1},{1,2},{2,3},{3,4},{4,5},{5,6},{6,7},{7,8},{8,9},{9,10},{10,1... | collective-permute-start | bytes 2555912 | tf_op jit(solution)/shard_map/ppermute | solution.py:21
  7.0 48.6 %collective-permute-start.1 = (bf16[52,64,128]{2,1,0:T(8,128)(2,1)}, bf16[52,64,128]{2,1,0:T(8,128)(2,1)S(1)}, u32[]{:S(2)}, u32[]{:S(2)}) collective-permute-start(bf16[52,64,128]{2,1,0:T(8,128)(2,1)} %get-tuple-element.15), channel_id=1, source_target_pairs={{1,0},{2,1},{3,2},{4,3},{5,4},{6,5},{7,6},{8,7},{9,8},{10,9},{11,1... | collective-permute-start | bytes 2555912 | tf_op jit(solution)/shard_map/ppermute | solution.py:21
  12.5 54.3 %collective-permute-start.2 = (bf16[48,64,128]{2,1,0:T(8,128)(2,1)}, bf16[48,64,128]{2,1,0:T(8,128)(2,1)S(1)}, u32[]{:S(2)}, u32[]{:S(2)}) collective-permute-start(bf16[48,64,128]{2,1,0:T(8,128)(2,1)} %get-tuple-element.16), channel_id=1, source_target_pairs={{0,2},{1,3},{2,4},{3,5},{4,6},{5,7},{6,8},{7,9},{8,10},{9,11},{10,... | collective-permute-start | bytes 2359304 | tf_op jit(solution)/shard_map/ppermute | solution.py:21
  14.4 66.4 %collective-permute-start.3 = (bf16[48,64,128]{2,1,0:T(8,128)(2,1)}, bf16[48,64,128]{2,1,0:T(8,128)(2,1)S(1)}, u32[]{:S(2)}, u32[]{:S(2)}) collective-permute-start(bf16[48,64,128]{2,1,0:T(8,128)(2,1)} %get-tuple-element.17), channel_id=1, source_target_pairs={{2,0},{3,1},{4,2},{5,3},{6,4},{7,5},{8,6},{9,7},{10,8},{11,9},{12,... | collective-permute-start | bytes 2359304 | tf_op jit(solution)/shard_map/ppermute | solution.py:21
  20.1 60.7 %collective-permute-start.4 = (bf16[48,64,128]{2,1,0:T(8,128)(2,1)}, bf16[48,64,128]{2,1,0:T(8,128)(2,1)}, u32[]{:S(2)}, u32[]{:S(2)}) collective-permute-start(bf16[48,64,128]{2,1,0:T(8,128)(2,1)} %get-tuple-element.18), channel_id=1, source_target_pairs={{0,3},{1,4},{2,5},{3,6},{4,7},{5,8},{6,9},{7,10},{8,11},{9,12},{10... | collective-permute-start | bytes 2359304 | tf_op jit(solution)/shard_map/ppermute | solution.py:21
  22.3 33.3 %copy-start = (bf16[52,64,128]{2,1,0:T(8,128)(2,1)}, bf16[52,64,128]{2,1,0:T(8,128)(2,1)S(1)}, u32[]{:S(2)}) copy-start(bf16[52,64,128]{2,1,0:T(8,128)(2,1)S(1)} %collective-permute-done.refs_1_.refs_0_) | copy-start | bytes 2555908
  22.3 58.5 %collective-permute-start.5 = (bf16[48,64,128]{2,1,0:T(8,128)(2,1)}, bf16[48,64,128]{2,1,0:T(8,128)(2,1)}, u32[]{:S(2)}, u32[]{:S(2)}) collective-permute-start(bf16[48,64,128]{2,1,0:T(8,128)(2,1)} %get-tuple-element.19), channel_id=1, source_target_pairs={{3,0},{4,1},{5,2},{6,3},{7,4},{8,5},{9,6},{10,7},{11,8},{12,9},{13... | collective-permute-start | bytes 2359304 | tf_op jit(solution)/shard_map/ppermute | solution.py:21
  55.7 0.9 copy-start.1
  66.8 14.1 %copy-start.2 = (bf16[48,64,128]{2,1,0:T(8,128)(2,1)}, bf16[48,64,128]{2,1,0:T(8,128)(2,1)S(1)}, u32[]{:S(2)}) copy-start(bf16[48,64,128]{2,1,0:T(8,128)(2,1)S(1)} %collective-permute-done.2.refs_3_) | copy-start | bytes 2359300
  80.8 0.9 copy-start.3

commit v8 on v7

--- a/solution.py
+++ b/solution.py
@@ -12,7 +12,7 @@
 RHS = 128
 HALO = 4
 REACH = 3
-BLOCK_TARGETS = 8
+BLOCK_TARGETS = 16
 
 
 def from_behind(value, axis, steps):

time: 107 us -> 106 us (level)
  Pallas kernels: 40 us -> 37.5 us
  waiting for transfers between devices: 14.3 us -> 16.2 us
    pallas_call x3, Pallas kernels: 34.9 us -> 32.4 us  [gather_dot(): pl.pallas_call(kernel, grid_spec=grid_spec, out_shape=jax.ShapeDtypeStruc...]
    ppermute x6, waiting for transfers between devices: 14.3 us -> 16.2 us  [from_behind(): lax.ppermute(value, axis, [(source, source + steps) for source in range(f...]
  transfers between devices with their start and end apart: 6 -> 6, of which waited for: 2 -> 2; matrix products, arithmetic and copies ran while one was open for 4% -> 4% of each run, Pallas kernels for 10% -> 8%
where the time goes in v8:
time: 106 us
  starting transfers between devices  45.5 us (43%)
  Pallas kernels  37.5 us (35%)
  waiting for transfers between devices  16.2 us (15%)
  local copies, waits for them, and re-layouts  6.51 us (6%)
    ppermute x6, starting transfers between devices, from_behind(): lax.ppermute(value, axis, [(source, source + steps) for source in range(f...  45.5 us
    pallas_call x3, Pallas kernels, gather_dot(): pl.pallas_call(kernel, grid_spec=grid_spec, out_shape=jax.ShapeDtypeStruc...  32.4 us
    ppermute x6, waiting for transfers between devices, from_behind(): lax.ppermute(value, axis, [(source, source + steps) for source in range(f...  16.2 us
    unnamed x10, local copies, waits for them, and re-layouts  6.51 us
    pallas_call x1, Pallas kernels, upward(): pl.pallas_call(kernel, in_specs=[smem, smem, vmem, vmem, vmem], out_specs...  5.1 us
  transfers between devices with their start and end apart: 6, of which 2 were waited for; matrix products, arithmetic and copies ran while one was open for 4% of the time, Pallas kernels for 8%

profile of v8, /device:TPU:24, one launch (start us, length us, event | category | flops | bytes accessed | tf_op | source)
XLA Modules:
  0.0 105.8 jit_solution(284039318744272721)
XLA Ops:
  0.0 5.1 %shard_map.109 = (bf16[64,64,128]{2,1,0:T(8,128)(2,1)}, bf16[32,64,128]{2,1,0:T(8,128)(2,1)}, bf16[52,64,128]{2,1,0:T(8,128)(2,1)}, bf16[52,64,128]{2,1,0:T(8,12...) custom-call(s32[192]{0:T(256)} %bitcast.6, ...), custom_call_target="tpu_custom_call" | custom-call | flops 134217728 | bytes 16777216 | tf_op jit(solution)/shard_map/pallas_call | solution.py:155
  5.1 1.9 %collective-permute-start = (bf16[52,64,128]{2,1,0:T(8,128)(2,1)}, bf16[52,64,128]{2,1,0:T(8,128)(2,1)S(1)}, u32[]{:S(2)}, u32[]{:S(2)}) collective-permute-start(bf16[52,64,128]{2,1,0:T(8,128)(2,1)} %get-tuple-element.14), channel_id=1, source_target_pairs={{0,1},{1,2},{2,3},{3,4},{4,5},{5,6},{6,7},{7,8},{8,9},{9,10},{10,1... | collective-permute-start | bytes 2555912 | tf_op jit(solution)/shard_map/ppermute | solution.py:21
  7.0 5.4 %collective-permute-start.1 = (bf16[52,64,128]{2,1,0:T(8,128)(2,1)}, bf16[52,64,128]{2,1,0:T(8,128)(2,1)S(1)}, u32[]{:S(2)}, u32[]{:S(2)}) collective-permute-start(bf16[52,64,128]{2,1,0:T(8,128)(2,1)} %get-tuple-element.15), channel_id=1, source_target_pairs={{1,0},{2,1},{3,2},{4,3},{5,4},{6,5},{7,6},{8,7},{9,8},{10,9},{11,1... | collective-permute-start | bytes 2555912 | tf_op jit(solution)/shard_map/ppermute | solution.py:21
  12.5 1.9 %collective-permute-start.2 = (bf16[48,64,128]{2,1,0:T(8,128)(2,1)}, bf16[48,64,128]{2,1,0:T(8,128)(2,1)S(1)}, u32[]{:S(2)}, u32[]{:S(2)}) collective-permute-start(bf16[48,64,128]{2,1,0:T(8,128)(2,1)} %get-tuple-element.16), channel_id=1, source_target_pairs={{0,2},{1,3},{2,4},{3,5},{4,6},{5,7},{6,8},{7,9},{8,10},{9,11},{10,... | collective-permute-start | bytes 2359304 | tf_op jit(solution)/shard_map/ppermute | solution.py:21
  14.4 5.7 %collective-permute-start.3 = (bf16[48,64,128]{2,1,0:T(8,128)(2,1)}, bf16[48,64,128]{2,1,0:T(8,128)(2,1)S(1)}, u32[]{:S(2)}, u32[]{:S(2)}) collective-permute-start(bf16[48,64,128]{2,1,0:T(8,128)(2,1)} %get-tuple-element.17), channel_id=1, source_target_pairs={{2,0},{3,1},{4,2},{5,3},{6,4},{7,5},{8,6},{9,7},{10,8},{11,9},{12,... | collective-permute-start | bytes 2359304 | tf_op jit(solution)/shard_map/ppermute | solution.py:21
  20.1 1.9 %collective-permute-start.4 = (bf16[48,64,128]{2,1,0:T(8,128)(2,1)}, bf16[48,64,128]{2,1,0:T(8,128)(2,1)}, u32[]{:S(2)}, u32[]{:S(2)}) collective-permute-start(bf16[48,64,128]{2,1,0:T(8,128)(2,1)} %get-tuple-element.18), channel_id=1, source_target_pairs={{0,3},{1,4},{2,5},{3,6},{4,7},{5,8},{6,9},{7,10},{8,11},{9,12},{10... | collective-permute-start | bytes 2359304 | tf_op jit(solution)/shard_map/ppermute | solution.py:21
  22.1 0.3 collective-permute-done.refs_1_.refs_0_
  22.3 0.0 copy-start
  22.3 28.6 %collective-permute-start.5 = (bf16[48,64,128]{2,1,0:T(8,128)(2,1)}, bf16[48,64,128]{2,1,0:T(8,128)(2,1)}, u32[]{:S(2)}, u32[]{:S(2)}) collective-permute-start(bf16[48,64,128]{2,1,0:T(8,128)(2,1)} %get-tuple-element.19), channel_id=1, source_target_pairs={{3,0},{4,1},{5,2},{6,3},{7,4},{8,5},{9,6},{10,7},{11,8},{12,9},{13... | collective-permute-start | bytes 2359304 | tf_op jit(solution)/shard_map/ppermute | solution.py:21
  50.9 2.3 %copy.13.refs_9_ = bf16[4096,64]{1,0:T(8,128)(2,1)} copy(bf16[4096,64]{0,1:T(8,128)(2,1)} %param.12) | data formatting | bytes 1048576 | tf_op args[1]
  53.3 2.4 %copy.12.refs_8_ = bf16[4096,64]{1,0:T(8,128)(2,1)} copy(bf16[4096,64]{0,1:T(8,128)(2,1)} %param.13) | data formatting | bytes 1048576 | tf_op args[2]
  55.6 0.0 collective-permute-done.1.refs_2_
  55.6 0.0 copy-done
  55.7 0.0 copy-start.1
  55.7 0.9 copy-done.1
  56.6 8.4 %shard_map.111.refs_10_ = f32[64,64,128]{2,1,0:T(8,128)} custom-call(s32[768]{0:T(1024)} %idx_ref.4, bf16[4096,768]{1,0:T(8,128)(2,1)} %mats_ref.4, bf16[52,64,128]{2,1,0:T(8,128)(2,1)} %copy-done, bf16[64,64,128]{2,1,0:T(8,128)(2,1)} %refs_1_.1, bf16[52,64,128]{2,1,0:T(8,128)(2,1)} %copy-done.1), custom_call_target="tpu_custom_call" | custom-call | flops 805306368 | bytes 9568256 | tf_op jit(solution)/shard_map/pallas_call | solution.py:98
  64.9 0.0 collective-permute-done.2.refs_3_
  64.9 0.0 copy-start.2
  64.9 15.9 %collective-permute-done.3.refs_4_ = bf16[48,64,128]{2,1,0:T(8,128)(2,1)S(1)} collective-permute-done((bf16[48,64,128]{2,1,0:T(8,128)(2,1)}, bf16[48,64,128]{2,1,0:T(8,128)(2,1)S(1)}, u32[]{:S(2)}, u32[]{:S(2)}) %collective-permute-start.3) | collective-permute-done | bytes 786464 | tf_op jit(solution)/shard_map/ppermute | solution.py:21
  80.8 0.0 copy-start.3
  80.8 0.0 collective-permute-done.4.refs_5_
  80.8 0.0 collective-permute-done.5.refs_6_
  80.8 0.0 copy-done.2
  80.8 0.9 copy-done.3
  81.7 6.6 %shard_map.110.refs_7_ = bf16[32,64,128]{2,1,0:T(8,128)(2,1)} custom-call(s32[512]{0:T(512)} %idx_ref.3, bf16[2048,1024]{1,0:T(8,128)(2,1)} %mats_ref.3, bf16[32,64,128]{2,1,0:T(8,128)(2,1)} %get-tuple-element.20.refs_0_, bf16[52,64,128]{2,1,0:T(8,128)(2,1)} %copy-done, bf16[52,64,128]{2,1,0:T(8,128)(2,1)} %copy-done.1, bf16[48,64,128]{2,1,0:T(8,128)(2,1)} %copy-done.2, ...), custom_call_target="tpu_custom_call" | custom-call | flops 536870912 | bytes 7340032 | tf_op jit(solution)/shard_map/pallas_call | solution.py:98
  88.4 17.4 %shard_map.112 = bf16[64,64,128]{2,1,0:T(8,128)(2,1)} custom-call(s32[1024]{0:T(1024)} %idx_ref.5, bf16[4096,1024]{1,0:T(8,128)(2,1)} %mats_ref.5, bf16[64,64,128]{2,1,0:T(8,128)(2,1)} %get-tuple-element.13.refs_0_, bf16[52,64,128]{2,1,0:T(8,128)(2,1)} %copy-done, bf16[52,64,128]{2,1,0:T(8,128)(2,1)} %copy-done.1, bf16[48,64,128]{2,1,0:T(8,128)(2,1)} %copy-done.2, ...), custom_call_target="tpu_custom_call" | custom-call | flops 1073741824 | bytes 14680064 | tf_op jit(solution)/shard_map/pallas_call | solution.py:98
Async XLA Ops:
  5.1 17.2 %collective-permute-start = (bf16[52,64,128]{2,1,0:T(8,128)(2,1)}, bf16[52,64,128]{2,1,0:T(8,128)(2,1)S(1)}, u32[]{:S(2)}, u32[]{:S(2)}) collective-permute-start(bf16[52,64,128]{2,1,0:T(8,128)(2,1)} %get-tuple-element.14), channel_id=1, source_target_pairs={{0,1},{1,2},{2,3},{3,4},{4,5},{5,6},{6,7},{7,8},{8,9},{9,10},{10,1... | collective-permute-start | bytes 2555912 | tf_op jit(solution)/shard_map/ppermute | solution.py:21
  7.0 48.6 %collective-permute-start.1 = (bf16[52,64,128]{2,1,0:T(8,128)(2,1)}, bf16[52,64,128]{2,1,0:T(8,128)(2,1)S(1)}, u32[]{:S(2)}, u32[]{:S(2)}) collective-permute-start(bf16[52,64,128]{2,1,0:T(8,128)(2,1)} %get-tuple-element.15), channel_id=1, source_target_pairs={{1,0},{2,1},{3,2},{4,3},{5,4},{6,5},{7,6},{8,7},{9,8},{10,9},{11,1... | collective-permute-start | bytes 2555912 | tf_op jit(solution)/shard_map/ppermute | solution.py:21
  12.5 52.4 %collective-permute-start.2 = (bf16[48,64,128]{2,1,0:T(8,128)(2,1)}, bf16[48,64,128]{2,1,0:T(8,128)(2,1)S(1)}, u32[]{:S(2)}, u32[]{:S(2)}) collective-permute-start(bf16[48,64,128]{2,1,0:T(8,128)(2,1)} %get-tuple-element.16), channel_id=1, source_target_pairs={{0,2},{1,3},{2,4},{3,5},{4,6},{5,7},{6,8},{7,9},{8,10},{9,11},{10,... | collective-permute-start | bytes 2359304 | tf_op jit(solution)/shard_map/ppermute | solution.py:21
  14.4 66.4 %collective-permute-start.3 = (bf16[48,64,128]{2,1,0:T(8,128)(2,1)}, bf16[48,64,128]{2,1,0:T(8,128)(2,1)S(1)}, u32[]{:S(2)}, u32[]{:S(2)}) collective-permute-start(bf16[48,64,128]{2,1,0:T(8,128)(2,1)} %get-tuple-element.17), channel_id=1, source_target_pairs={{2,0},{3,1},{4,2},{5,3},{6,4},{7,5},{8,6},{9,7},{10,8},{11,9},{12,... | collective-permute-start | bytes 2359304 | tf_op jit(solution)/shard_map/ppermute | solution.py:21
  20.1 60.7 %collective-permute-start.4 = (bf16[48,64,128]{2,1,0:T(8,128)(2,1)}, bf16[48,64,128]{2,1,0:T(8,128)(2,1)}, u32[]{:S(2)}, u32[]{:S(2)}) collective-permute-start(bf16[48,64,128]{2,1,0:T(8,128)(2,1)} %get-tuple-element.18), channel_id=1, source_target_pairs={{0,3},{1,4},{2,5},{3,6},{4,7},{5,8},{6,9},{7,10},{8,11},{9,12},{10... | collective-permute-start | bytes 2359304 | tf_op jit(solution)/shard_map/ppermute | solution.py:21
  22.3 33.3 %copy-start = (bf16[52,64,128]{2,1,0:T(8,128)(2,1)}, bf16[52,64,128]{2,1,0:T(8,128)(2,1)S(1)}, u32[]{:S(2)}) copy-start(bf16[52,64,128]{2,1,0:T(8,128)(2,1)S(1)} %collective-permute-done.refs_1_.refs_0_) | copy-start | bytes 2555908
  22.3 58.5 %collective-permute-start.5 = (bf16[48,64,128]{2,1,0:T(8,128)(2,1)}, bf16[48,64,128]{2,1,0:T(8,128)(2,1)}, u32[]{:S(2)}, u32[]{:S(2)}) collective-permute-start(bf16[48,64,128]{2,1,0:T(8,128)(2,1)} %get-tuple-element.19), channel_id=1, source_target_pairs={{3,0},{4,1},{5,2},{6,3},{7,4},{8,5},{9,6},{10,7},{11,8},{12,9},{13... | collective-permute-start | bytes 2359304 | tf_op jit(solution)/shard_map/ppermute | solution.py:21
  55.7 0.9 copy-start.1
  64.9 15.9 %copy-start.2 = (bf16[48,64,128]{2,1,0:T(8,128)(2,1)}, bf16[48,64,128]{2,1,0:T(8,128)(2,1)S(1)}, u32[]{:S(2)}) copy-start(bf16[48,64,128]{2,1,0:T(8,128)(2,1)S(1)} %collective-permute-done.2.refs_3_) | copy-start | bytes 2359300
  80.8 0.9 copy-start.3

commit v9 on v8

--- a/solution.py
+++ b/solution.py
@@ -59,8 +59,8 @@
 
     def kernel(idx_ref, mats_ref, *refs):
         seg_refs = refs[:n_seg]
-        extra_refs = refs[n_seg:len(refs) - 3]
-        out_ref, pool_ref, sem = refs[len(refs) - 3:]
+        extra_refs = refs[n_seg:len(refs) - 4]
+        out_ref, pool_ref, sem, acc_ref = refs[len(refs) - 4:]
         blk = pl.program_id(0)
 
         @pl.when(blk == 0)
@@ -81,7 +81,9 @@
             if epilogue is None:
                 out_ref[tt] = acc.astype(out_dtype)
             else:
-                out_ref[tt] = epilogue[2](tt, acc, extra_refs)
+                acc_ref[tt] = acc
+        if epilogue is not None:
+            epilogue[2](tb, acc_ref, extra_refs, out_ref)
 
     grid_spec = pltpu.PrefetchScalarGridSpec(
         num_scalar_prefetch=1,
@@ -91,6 +93,7 @@
         scratch_shapes=[
             pltpu.VMEM((total, width, RHS), jnp.bfloat16),
             pltpu.SemaphoreType.DMA((n_seg,)),
+            pltpu.VMEM((tb if epilogue is not None else 1, LEAF, RHS), jnp.float32),
         ],
     )
     flops = 2 * rows * pairs * width * RHS
@@ -220,14 +223,17 @@
 
     tb = min(BLOCK_TARGETS, leaves)
 
-    def finish(tt, acc, refs):
+    def finish(count, acc_ref, refs, out_ref):
         cr_ref, e_ref, v_ref, near_ref = refs
-        e = e_ref[tt * RANK:(tt + 1) * RANK, :]
-        down = jnp.dot(e, cr_ref[tt // 2], preferred_element_type=jnp.float32)
-        fine_round = (acc + down).astype(jnp.bfloat16)
-        v = v_ref[tt * LEAF:(tt + 1) * LEAF, :]
-        far = jnp.dot(v, fine_round, preferred_element_type=jnp.float32)
-        return (far + near_ref[tt]).astype(jnp.bfloat16)
+        rounded = []
+        for tt in range(count):
+            e = e_ref[tt * RANK:(tt + 1) * RANK, :]
+            down = jnp.dot(e, cr_ref[tt // 2], preferred_element_type=jnp.float32)
+            rounded.append((acc_ref[tt] + down).astype(jnp.bfloat16))
+        for tt in range(count):
+            v = v_ref[tt * LEAF:(tt + 1) * LEAF, :]
+            far = jnp.dot(v, rounded[tt], preferred_element_type=jnp.float32)
+            out_ref[tt] = (far + near_ref[tt]).astype(jnp.bfloat16)
 
     epilogue = (
         [coarse_round, transfer, leaf_basis, near_field],

time: 106 us -> 101 us (0.953)
  Pallas kernels: 37.5 us -> 31.9 us
    pallas_call x3, Pallas kernels: 32.4 us -> 26.8 us  [gather_dot(): pl.pallas_call(kernel, grid_spec=grid_spec, out_shape=jax.ShapeDtypeStruc...]
  transfers between devices with their start and end apart: 6 -> 6, of which waited for: 2 -> 2; matrix products, arithmetic and copies ran while one was open for 4% -> 5% of each run, Pallas kernels for 8% -> 8%
where the time goes in v9:
time: 101 us; the launch traced here: 100 us
  starting transfers between devices  45.5 us (45%)
  Pallas kernels  31.9 us (32%)
  waiting for transfers between devices  16.2 us (16%)
  local copies, waits for them, and re-layouts  6.51 us (6%)
    ppermute x6, starting transfers between devices, from_behind(): lax.ppermute(value, axis, [(source, source + steps) for source in range(f...  45.5 us
    pallas_call x3, Pallas kernels, gather_dot(): pl.pallas_call(kernel, grid_spec=grid_spec, out_shape=jax.ShapeDtypeStruc...  26.8 us
    ppermute x6, waiting for transfers between devices, from_behind(): lax.ppermute(value, axis, [(source, source + steps) for source in range(f...  16.2 us
    unnamed x10, local copies, waits for them, and re-layouts  6.51 us
    pallas_call x1, Pallas kernels, upward(): pl.pallas_call(kernel, in_specs=[smem, smem, vmem, vmem, vmem], out_specs...  5.1 us
  transfers between devices with their start and end apart: 6, of which 2 were waited for; matrix products, arithmetic and copies ran while one was open for 5% of the time, Pallas kernels for 8%

profile of v9, /device:TPU:24, one launch (start us, length us, event | category | flops | bytes accessed | tf_op | source)
XLA Modules:
  0.0 100.2 jit_solution(9793607444108428591)
XLA Ops:
  0.0 5.1 %shard_map.109 = (bf16[64,64,128]{2,1,0:T(8,128)(2,1)}, bf16[32,64,128]{2,1,0:T(8,128)(2,1)}, bf16[52,64,128]{2,1,0:T(8,128)(2,1)}, bf16[52,64,128]{2,1,0:T(8,12...) custom-call(s32[192]{0:T(256)} %bitcast.6, ...), custom_call_target="tpu_custom_call" | custom-call | flops 134217728 | bytes 16777216 | tf_op jit(solution)/shard_map/pallas_call | solution.py:158
  5.1 1.9 %collective-permute-start = (bf16[52,64,128]{2,1,0:T(8,128)(2,1)}, bf16[52,64,128]{2,1,0:T(8,128)(2,1)S(1)}, u32[]{:S(2)}, u32[]{:S(2)}) collective-permute-start(bf16[52,64,128]{2,1,0:T(8,128)(2,1)} %get-tuple-element.14), channel_id=1, source_target_pairs={{0,1},{1,2},{2,3},{3,4},{4,5},{5,6},{6,7},{7,8},{8,9},{9,10},{10,1... | collective-permute-start | bytes 2555912 | tf_op jit(solution)/shard_map/ppermute | solution.py:21
  7.0 5.4 %collective-permute-start.1 = (bf16[52,64,128]{2,1,0:T(8,128)(2,1)}, bf16[52,64,128]{2,1,0:T(8,128)(2,1)S(1)}, u32[]{:S(2)}, u32[]{:S(2)}) collective-permute-start(bf16[52,64,128]{2,1,0:T(8,128)(2,1)} %get-tuple-element.15), channel_id=1, source_target_pairs={{1,0},{2,1},{3,2},{4,3},{5,4},{6,5},{7,6},{8,7},{9,8},{10,9},{11,1... | collective-permute-start | bytes 2555912 | tf_op jit(solution)/shard_map/ppermute | solution.py:21
  12.5 1.9 %collective-permute-start.2 = (bf16[48,64,128]{2,1,0:T(8,128)(2,1)}, bf16[48,64,128]{2,1,0:T(8,128)(2,1)S(1)}, u32[]{:S(2)}, u32[]{:S(2)}) collective-permute-start(bf16[48,64,128]{2,1,0:T(8,128)(2,1)} %get-tuple-element.16), channel_id=1, source_target_pairs={{0,2},{1,3},{2,4},{3,5},{4,6},{5,7},{6,8},{7,9},{8,10},{9,11},{10,... | collective-permute-start | bytes 2359304 | tf_op jit(solution)/shard_map/ppermute | solution.py:21
  14.4 5.7 %collective-permute-start.3 = (bf16[48,64,128]{2,1,0:T(8,128)(2,1)}, bf16[48,64,128]{2,1,0:T(8,128)(2,1)S(1)}, u32[]{:S(2)}, u32[]{:S(2)}) collective-permute-start(bf16[48,64,128]{2,1,0:T(8,128)(2,1)} %get-tuple-element.17), channel_id=1, source_target_pairs={{2,0},{3,1},{4,2},{5,3},{6,4},{7,5},{8,6},{9,7},{10,8},{11,9},{12,... | collective-permute-start | bytes 2359304 | tf_op jit(solution)/shard_map/ppermute | solution.py:21
  20.1 1.9 %collective-permute-start.4 = (bf16[48,64,128]{2,1,0:T(8,128)(2,1)}, bf16[48,64,128]{2,1,0:T(8,128)(2,1)}, u32[]{:S(2)}, u32[]{:S(2)}) collective-permute-start(bf16[48,64,128]{2,1,0:T(8,128)(2,1)} %get-tuple-element.18), channel_id=1, source_target_pairs={{0,3},{1,4},{2,5},{3,6},{4,7},{5,8},{6,9},{7,10},{8,11},{9,12},{10... | collective-permute-start | bytes 2359304 | tf_op jit(solution)/shard_map/ppermute | solution.py:21
  22.1 0.3 collective-permute-done.refs_1_.refs_0_
  22.3 0.0 copy-start
  22.3 28.6 %collective-permute-start.5 = (bf16[48,64,128]{2,1,0:T(8,128)(2,1)}, bf16[48,64,128]{2,1,0:T(8,128)(2,1)}, u32[]{:S(2)}, u32[]{:S(2)}) collective-permute-start(bf16[48,64,128]{2,1,0:T(8,128)(2,1)} %get-tuple-element.19), channel_id=1, source_target_pairs={{3,0},{4,1},{5,2},{6,3},{7,4},{8,5},{9,6},{10,7},{11,8},{12,9},{13... | collective-permute-start | bytes 2359304 | tf_op jit(solution)/shard_map/ppermute | solution.py:21
  50.9 2.3 %copy.13.refs_9_ = bf16[4096,64]{1,0:T(8,128)(2,1)} copy(bf16[4096,64]{0,1:T(8,128)(2,1)} %param.12) | data formatting | bytes 1048576 | tf_op args[1]
  53.3 2.4 %copy.12.refs_8_ = bf16[4096,64]{1,0:T(8,128)(2,1)} copy(bf16[4096,64]{0,1:T(8,128)(2,1)} %param.13) | data formatting | bytes 1048576 | tf_op args[2]
  55.6 0.0 collective-permute-done.1.refs_2_
  55.6 0.0 copy-done
  55.7 0.0 copy-start.1
  55.7 0.9 copy-done.1
  56.6 8.4 %shard_map.111.refs_10_ = f32[64,64,128]{2,1,0:T(8,128)} custom-call(s32[768]{0:T(1024)} %idx_ref.4, bf16[4096,768]{1,0:T(8,128)(2,1)} %mats_ref.4, bf16[52,64,128]{2,1,0:T(8,128)(2,1)} %copy-done, bf16[64,64,128]{2,1,0:T(8,128)(2,1)} %refs_1_.1, bf16[52,64,128]{2,1,0:T(8,128)(2,1)} %copy-done.1), custom_call_target="tpu_custom_call" | custom-call | flops 805306368 | bytes 9568256 | tf_op jit(solution)/shard_map/pallas_call | solution.py:101
  64.9 0.0 collective-permute-done.2.refs_3_
  64.9 0.0 copy-start.2
  64.9 15.9 %collective-permute-done.3.refs_4_ = bf16[48,64,128]{2,1,0:T(8,128)(2,1)S(1)} collective-permute-done((bf16[48,64,128]{2,1,0:T(8,128)(2,1)}, bf16[48,64,128]{2,1,0:T(8,128)(2,1)S(1)}, u32[]{:S(2)}, u32[]{:S(2)}) %collective-permute-start.3) | collective-permute-done | bytes 786464 | tf_op jit(solution)/shard_map/ppermute | solution.py:21
  80.8 0.0 copy-start.3
  80.8 0.0 collective-permute-done.4.refs_5_
  80.8 0.0 collective-permute-done.5.refs_6_
  80.8 0.0 copy-done.2
  80.8 0.9 copy-done.3
  81.7 6.6 %shard_map.110.refs_7_ = bf16[32,64,128]{2,1,0:T(8,128)(2,1)} custom-call(s32[512]{0:T(512)} %idx_ref.3, bf16[2048,1024]{1,0:T(8,128)(2,1)} %mats_ref.3, bf16[32,64,128]{2,1,0:T(8,128)(2,1)} %get-tuple-element.20.refs_0_, bf16[52,64,128]{2,1,0:T(8,128)(2,1)} %copy-done, bf16[52,64,128]{2,1,0:T(8,128)(2,1)} %copy-done.1, bf16[48,64,128]{2,1,0:T(8,128)(2,1)} %copy-done.2, ...), custom_call_target="tpu_custom_call" | custom-call | flops 536870912 | bytes 7340032 | tf_op jit(solution)/shard_map/pallas_call | solution.py:101
  88.4 11.8 %shard_map.112 = bf16[64,64,128]{2,1,0:T(8,128)(2,1)} custom-call(s32[1024]{0:T(1024)} %idx_ref.5, bf16[4096,1024]{1,0:T(8,128)(2,1)} %mats_ref.5, bf16[64,64,128]{2,1,0:T(8,128)(2,1)} %get-tuple-element.13.refs_0_, bf16[52,64,128]{2,1,0:T(8,128)(2,1)} %copy-done, bf16[52,64,128]{2,1,0:T(8,128)(2,1)} %copy-done.1, bf16[48,64,128]{2,1,0:T(8,128)(2,1)} %copy-done.2, ...), custom_call_target="tpu_custom_call" | custom-call | flops 1073741824 | bytes 14680064 | tf_op jit(solution)/shard_map/pallas_call | solution.py:101
Async XLA Ops:
  5.1 17.2 %collective-permute-start = (bf16[52,64,128]{2,1,0:T(8,128)(2,1)}, bf16[52,64,128]{2,1,0:T(8,128)(2,1)S(1)}, u32[]{:S(2)}, u32[]{:S(2)}) collective-permute-start(bf16[52,64,128]{2,1,0:T(8,128)(2,1)} %get-tuple-element.14), channel_id=1, source_target_pairs={{0,1},{1,2},{2,3},{3,4},{4,5},{5,6},{6,7},{7,8},{8,9},{9,10},{10,1... | collective-permute-start | bytes 2555912 | tf_op jit(solution)/shard_map/ppermute | solution.py:21
  7.0 48.6 %collective-permute-start.1 = (bf16[52,64,128]{2,1,0:T(8,128)(2,1)}, bf16[52,64,128]{2,1,0:T(8,128)(2,1)S(1)}, u32[]{:S(2)}, u32[]{:S(2)}) collective-permute-start(bf16[52,64,128]{2,1,0:T(8,128)(2,1)} %get-tuple-element.15), channel_id=1, source_target_pairs={{1,0},{2,1},{3,2},{4,3},{5,4},{6,5},{7,6},{8,7},{9,8},{10,9},{11,1... | collective-permute-start | bytes 2555912 | tf_op jit(solution)/shard_map/ppermute | solution.py:21
  12.5 52.4 %collective-permute-start.2 = (bf16[48,64,128]{2,1,0:T(8,128)(2,1)}, bf16[48,64,128]{2,1,0:T(8,128)(2,1)S(1)}, u32[]{:S(2)}, u32[]{:S(2)}) collective-permute-start(bf16[48,64,128]{2,1,0:T(8,128)(2,1)} %get-tuple-element.16), channel_id=1, source_target_pairs={{0,2},{1,3},{2,4},{3,5},{4,6},{5,7},{6,8},{7,9},{8,10},{9,11},{10,... | collective-permute-start | bytes 2359304 | tf_op jit(solution)/shard_map/ppermute | solution.py:21
  14.4 66.4 %collective-permute-start.3 = (bf16[48,64,128]{2,1,0:T(8,128)(2,1)}, bf16[48,64,128]{2,1,0:T(8,128)(2,1)S(1)}, u32[]{:S(2)}, u32[]{:S(2)}) collective-permute-start(bf16[48,64,128]{2,1,0:T(8,128)(2,1)} %get-tuple-element.17), channel_id=1, source_target_pairs={{2,0},{3,1},{4,2},{5,3},{6,4},{7,5},{8,6},{9,7},{10,8},{11,9},{12,... | collective-permute-start | bytes 2359304 | tf_op jit(solution)/shard_map/ppermute | solution.py:21
  20.1 60.7 %collective-permute-start.4 = (bf16[48,64,128]{2,1,0:T(8,128)(2,1)}, bf16[48,64,128]{2,1,0:T(8,128)(2,1)}, u32[]{:S(2)}, u32[]{:S(2)}) collective-permute-start(bf16[48,64,128]{2,1,0:T(8,128)(2,1)} %get-tuple-element.18), channel_id=1, source_target_pairs={{0,3},{1,4},{2,5},{3,6},{4,7},{5,8},{6,9},{7,10},{8,11},{9,12},{10... | collective-permute-start | bytes 2359304 | tf_op jit(solution)/shard_map/ppermute | solution.py:21
  22.3 33.3 %copy-start = (bf16[52,64,128]{2,1,0:T(8,128)(2,1)}, bf16[52,64,128]{2,1,0:T(8,128)(2,1)S(1)}, u32[]{:S(2)}) copy-start(bf16[52,64,128]{2,1,0:T(8,128)(2,1)S(1)} %collective-permute-done.refs_1_.refs_0_) | copy-start | bytes 2555908
  22.3 58.5 %collective-permute-start.5 = (bf16[48,64,128]{2,1,0:T(8,128)(2,1)}, bf16[48,64,128]{2,1,0:T(8,128)(2,1)}, u32[]{:S(2)}, u32[]{:S(2)}) collective-permute-start(bf16[48,64,128]{2,1,0:T(8,128)(2,1)} %get-tuple-element.19), channel_id=1, source_target_pairs={{3,0},{4,1},{5,2},{6,3},{7,4},{8,5},{9,6},{10,7},{11,8},{12,9},{13... | collective-permute-start | bytes 2359304 | tf_op jit(solution)/shard_map/ppermute | solution.py:21
  55.7 0.9 copy-start.1
  64.9 15.9 %copy-start.2 = (bf16[48,64,128]{2,1,0:T(8,128)(2,1)}, bf16[48,64,128]{2,1,0:T(8,128)(2,1)S(1)}, u32[]{:S(2)}) copy-start(bf16[48,64,128]{2,1,0:T(8,128)(2,1)S(1)} %collective-permute-done.2.refs_3_) | copy-start | bytes 2359300
  80.8 0.9 copy-start.3

commit v10 on v9

--- a/solution.py
+++ b/solution.py
@@ -75,7 +75,7 @@
 
         for tt in range(tb):
             base = (blk * tb + tt) * pairs
-            blocks = [pool_ref[jnp.clip(idx_ref[base + k], 0, total - 1)] for k in range(pairs)]
+            blocks = [pool_ref[idx_ref[base + k]] for k in range(pairs)]
             rhs = jnp.concatenate(blocks, axis=0)
             acc = jnp.dot(mats_ref[tt * LEAF:(tt + 1) * LEAF, :], rhs, preferred_element_type=jnp.float32)
             if epilogue is None:

time: 101 us -> 99.7 us (0.987)
  Pallas kernels: 31.9 us -> 30.6 us
    pallas_call x3, Pallas kernels: 26.8 us -> 25.5 us  [gather_dot(): pl.pallas_call(kernel, grid_spec=grid_spec, out_shape=jax.ShapeDtypeStruc...]
where the time goes in v10:
time: 99.7 us; the launch traced here: 99.1 us
  starting transfers between devices  45.5 us (46%)
  Pallas kernels  30.6 us (31%)
  waiting for transfers between devices  16.4 us (16%)
  local copies, waits for them, and re-layouts  6.51 us (7%)
    ppermute x6, starting transfers between devices, from_behind(): lax.ppermute(value, axis, [(source, source + steps) for source in range(f...  45.5 us
    pallas_call x3, Pallas kernels, gather_dot(): pl.pallas_call(kernel, grid_spec=grid_spec, out_shape=jax.ShapeDtypeStruc...  25.5 us
    ppermute x6, waiting for transfers between devices, from_behind(): lax.ppermute(value, axis, [(source, source + steps) for source in range(f...  16.4 us
    unnamed x10, local copies, waits for them, and re-layouts  6.51 us
    pallas_call x1, Pallas kernels, upward(): pl.pallas_call(kernel, in_specs=[smem, smem, vmem, vmem, vmem], out_specs...  5.1 us
  transfers between devices with their start and end apart: 6, of which 2 were waited for; matrix products, arithmetic and copies ran while one was open for 5% of the time, Pallas kernels for 8%

profile of v10, /device:TPU:24, one launch (start us, length us, event | category | flops | bytes accessed | tf_op | source)
XLA Modules:
  0.0 99.1 jit_solution(15778201166230697335)
XLA Ops:
  0.0 5.1 %shard_map.109 = (bf16[64,64,128]{2,1,0:T(8,128)(2,1)}, bf16[32,64,128]{2,1,0:T(8,128)(2,1)}, bf16[52,64,128]{2,1,0:T(8,128)(2,1)}, bf16[52,64,128]{2,1,0:T(8,12...) custom-call(s32[192]{0:T(256)} %bitcast.6, ...), custom_call_target="tpu_custom_call" | custom-call | flops 134217728 | bytes 16777216 | tf_op jit(solution)/shard_map/pallas_call | solution.py:158
  5.1 1.9 %collective-permute-start = (bf16[52,64,128]{2,1,0:T(8,128)(2,1)}, bf16[52,64,128]{2,1,0:T(8,128)(2,1)S(1)}, u32[]{:S(2)}, u32[]{:S(2)}) collective-permute-start(bf16[52,64,128]{2,1,0:T(8,128)(2,1)} %get-tuple-element.14), channel_id=1, source_target_pairs={{0,1},{1,2},{2,3},{3,4},{4,5},{5,6},{6,7},{7,8},{8,9},{9,10},{10,1... | collective-permute-start | bytes 2555912 | tf_op jit(solution)/shard_map/ppermute | solution.py:21
  7.0 5.4 %collective-permute-start.1 = (bf16[52,64,128]{2,1,0:T(8,128)(2,1)}, bf16[52,64,128]{2,1,0:T(8,128)(2,1)S(1)}, u32[]{:S(2)}, u32[]{:S(2)}) collective-permute-start(bf16[52,64,128]{2,1,0:T(8,128)(2,1)} %get-tuple-element.15), channel_id=1, source_target_pairs={{1,0},{2,1},{3,2},{4,3},{5,4},{6,5},{7,6},{8,7},{9,8},{10,9},{11,1... | collective-permute-start | bytes 2555912 | tf_op jit(solution)/shard_map/ppermute | solution.py:21
  12.5 1.9 %collective-permute-start.2 = (bf16[48,64,128]{2,1,0:T(8,128)(2,1)}, bf16[48,64,128]{2,1,0:T(8,128)(2,1)S(1)}, u32[]{:S(2)}, u32[]{:S(2)}) collective-permute-start(bf16[48,64,128]{2,1,0:T(8,128)(2,1)} %get-tuple-element.16), channel_id=1, source_target_pairs={{0,2},{1,3},{2,4},{3,5},{4,6},{5,7},{6,8},{7,9},{8,10},{9,11},{10,... | collective-permute-start | bytes 2359304 | tf_op jit(solution)/shard_map/ppermute | solution.py:21
  14.4 5.7 %collective-permute-start.3 = (bf16[48,64,128]{2,1,0:T(8,128)(2,1)}, bf16[48,64,128]{2,1,0:T(8,128)(2,1)S(1)}, u32[]{:S(2)}, u32[]{:S(2)}) collective-permute-start(bf16[48,64,128]{2,1,0:T(8,128)(2,1)} %get-tuple-element.17), channel_id=1, source_target_pairs={{2,0},{3,1},{4,2},{5,3},{6,4},{7,5},{8,6},{9,7},{10,8},{11,9},{12,... | collective-permute-start | bytes 2359304 | tf_op jit(solution)/shard_map/ppermute | solution.py:21
  20.1 1.9 %collective-permute-start.4 = (bf16[48,64,128]{2,1,0:T(8,128)(2,1)}, bf16[48,64,128]{2,1,0:T(8,128)(2,1)}, u32[]{:S(2)}, u32[]{:S(2)}) collective-permute-start(bf16[48,64,128]{2,1,0:T(8,128)(2,1)} %get-tuple-element.18), channel_id=1, source_target_pairs={{0,3},{1,4},{2,5},{3,6},{4,7},{5,8},{6,9},{7,10},{8,11},{9,12},{10... | collective-permute-start | bytes 2359304 | tf_op jit(solution)/shard_map/ppermute | solution.py:21
  22.1 0.3 collective-permute-done.refs_1_.refs_0_
  22.3 0.0 copy-start
  22.3 28.6 %collective-permute-start.5 = (bf16[48,64,128]{2,1,0:T(8,128)(2,1)}, bf16[48,64,128]{2,1,0:T(8,128)(2,1)}, u32[]{:S(2)}, u32[]{:S(2)}) collective-permute-start(bf16[48,64,128]{2,1,0:T(8,128)(2,1)} %get-tuple-element.19), channel_id=1, source_target_pairs={{3,0},{4,1},{5,2},{6,3},{7,4},{8,5},{9,6},{10,7},{11,8},{12,9},{13... | collective-permute-start | bytes 2359304 | tf_op jit(solution)/shard_map/ppermute | solution.py:21
  50.9 2.3 %copy.13.refs_9_ = bf16[4096,64]{1,0:T(8,128)(2,1)} copy(bf16[4096,64]{0,1:T(8,128)(2,1)} %param.12) | data formatting | bytes 1048576 | tf_op args[1]
  53.3 2.4 %copy.12.refs_8_ = bf16[4096,64]{1,0:T(8,128)(2,1)} copy(bf16[4096,64]{0,1:T(8,128)(2,1)} %param.13) | data formatting | bytes 1048576 | tf_op args[2]
  55.6 0.0 collective-permute-done.1.refs_2_
  55.6 0.0 copy-done
  55.7 0.0 copy-start.1
  55.7 0.9 copy-done.1
  56.6 8.1 %shard_map.111.refs_10_ = f32[64,64,128]{2,1,0:T(8,128)} custom-call(s32[768]{0:T(1024)} %idx_ref.4, bf16[4096,768]{1,0:T(8,128)(2,1)} %mats_ref.4, bf16[52,64,128]{2,1,0:T(8,128)(2,1)} %copy-done, bf16[64,64,128]{2,1,0:T(8,128)(2,1)} %refs_1_.1, bf16[52,64,128]{2,1,0:T(8,128)(2,1)} %copy-done.1), custom_call_target="tpu_custom_call" | custom-call | flops 805306368 | bytes 9568256 | tf_op jit(solution)/shard_map/pallas_call | solution.py:101
  64.6 0.0 collective-permute-done.2.refs_3_
  64.6 0.0 copy-start.2
  64.7 16.2 %collective-permute-done.3.refs_4_ = bf16[48,64,128]{2,1,0:T(8,128)(2,1)S(1)} collective-permute-done((bf16[48,64,128]{2,1,0:T(8,128)(2,1)}, bf16[48,64,128]{2,1,0:T(8,128)(2,1)S(1)}, u32[]{:S(2)}, u32[]{:S(2)}) %collective-permute-start.3) | collective-permute-done | bytes 786464 | tf_op jit(solution)/shard_map/ppermute | solution.py:21
  80.8 0.0 copy-start.3
  80.8 0.0 collective-permute-done.4.refs_5_
  80.8 0.0 collective-permute-done.5.refs_6_
  80.8 0.0 copy-done.2
  80.8 0.9 copy-done.3
  81.7 6.3 %shard_map.110.refs_7_ = bf16[32,64,128]{2,1,0:T(8,128)(2,1)} custom-call(s32[512]{0:T(512)} %idx_ref.3, bf16[2048,1024]{1,0:T(8,128)(2,1)} %mats_ref.3, bf16[32,64,128]{2,1,0:T(8,128)(2,1)} %get-tuple-element.20.refs_0_, bf16[52,64,128]{2,1,0:T(8,128)(2,1)} %copy-done, bf16[52,64,128]{2,1,0:T(8,128)(2,1)} %copy-done.1, bf16[48,64,128]{2,1,0:T(8,128)(2,1)} %copy-done.2, ...), custom_call_target="tpu_custom_call" | custom-call | flops 536870912 | bytes 7340032 | tf_op jit(solution)/shard_map/pallas_call | solution.py:101
  88.1 11.1 %shard_map.112 = bf16[64,64,128]{2,1,0:T(8,128)(2,1)} custom-call(s32[1024]{0:T(1024)} %idx_ref.5, bf16[4096,1024]{1,0:T(8,128)(2,1)} %mats_ref.5, bf16[64,64,128]{2,1,0:T(8,128)(2,1)} %get-tuple-element.13.refs_0_, bf16[52,64,128]{2,1,0:T(8,128)(2,1)} %copy-done, bf16[52,64,128]{2,1,0:T(8,128)(2,1)} %copy-done.1, bf16[48,64,128]{2,1,0:T(8,128)(2,1)} %copy-done.2, ...), custom_call_target="tpu_custom_call" | custom-call | flops 1073741824 | bytes 14680064 | tf_op jit(solution)/shard_map/pallas_call | solution.py:101
Async XLA Ops:
  5.1 17.2 %collective-permute-start = (bf16[52,64,128]{2,1,0:T(8,128)(2,1)}, bf16[52,64,128]{2,1,0:T(8,128)(2,1)S(1)}, u32[]{:S(2)}, u32[]{:S(2)}) collective-permute-start(bf16[52,64,128]{2,1,0:T(8,128)(2,1)} %get-tuple-element.14), channel_id=1, source_target_pairs={{0,1},{1,2},{2,3},{3,4},{4,5},{5,6},{6,7},{7,8},{8,9},{9,10},{10,1... | collective-permute-start | bytes 2555912 | tf_op jit(solution)/shard_map/ppermute | solution.py:21
  7.0 48.6 %collective-permute-start.1 = (bf16[52,64,128]{2,1,0:T(8,128)(2,1)}, bf16[52,64,128]{2,1,0:T(8,128)(2,1)S(1)}, u32[]{:S(2)}, u32[]{:S(2)}) collective-permute-start(bf16[52,64,128]{2,1,0:T(8,128)(2,1)} %get-tuple-element.15), channel_id=1, source_target_pairs={{1,0},{2,1},{3,2},{4,3},{5,4},{6,5},{7,6},{8,7},{9,8},{10,9},{11,1... | collective-permute-start | bytes 2555912 | tf_op jit(solution)/shard_map/ppermute | solution.py:21
  12.5 52.2 %collective-permute-start.2 = (bf16[48,64,128]{2,1,0:T(8,128)(2,1)}, bf16[48,64,128]{2,1,0:T(8,128)(2,1)S(1)}, u32[]{:S(2)}, u32[]{:S(2)}) collective-permute-start(bf16[48,64,128]{2,1,0:T(8,128)(2,1)} %get-tuple-element.16), channel_id=1, source_target_pairs={{0,2},{1,3},{2,4},{3,5},{4,6},{5,7},{6,8},{7,9},{8,10},{9,11},{10,... | collective-permute-start | bytes 2359304 | tf_op jit(solution)/shard_map/ppermute | solution.py:21
  14.4 66.4 %collective-permute-start.3 = (bf16[48,64,128]{2,1,0:T(8,128)(2,1)}, bf16[48,64,128]{2,1,0:T(8,128)(2,1)S(1)}, u32[]{:S(2)}, u32[]{:S(2)}) collective-permute-start(bf16[48,64,128]{2,1,0:T(8,128)(2,1)} %get-tuple-element.17), channel_id=1, source_target_pairs={{2,0},{3,1},{4,2},{5,3},{6,4},{7,5},{8,6},{9,7},{10,8},{11,9},{12,... | collective-permute-start | bytes 2359304 | tf_op jit(solution)/shard_map/ppermute | solution.py:21
  20.1 60.7 %collective-permute-start.4 = (bf16[48,64,128]{2,1,0:T(8,128)(2,1)}, bf16[48,64,128]{2,1,0:T(8,128)(2,1)}, u32[]{:S(2)}, u32[]{:S(2)}) collective-permute-start(bf16[48,64,128]{2,1,0:T(8,128)(2,1)} %get-tuple-element.18), channel_id=1, source_target_pairs={{0,3},{1,4},{2,5},{3,6},{4,7},{5,8},{6,9},{7,10},{8,11},{9,12},{10... | collective-permute-start | bytes 2359304 | tf_op jit(solution)/shard_map/ppermute | solution.py:21
  22.3 33.3 %copy-start = (bf16[52,64,128]{2,1,0:T(8,128)(2,1)}, bf16[52,64,128]{2,1,0:T(8,128)(2,1)S(1)}, u32[]{:S(2)}) copy-start(bf16[52,64,128]{2,1,0:T(8,128)(2,1)S(1)} %collective-permute-done.refs_1_.refs_0_) | copy-start | bytes 2555908
  22.3 58.5 %collective-permute-start.5 = (bf16[48,64,128]{2,1,0:T(8,128)(2,1)}, bf16[48,64,128]{2,1,0:T(8,128)(2,1)}, u32[]{:S(2)}, u32[]{:S(2)}) collective-permute-start(bf16[48,64,128]{2,1,0:T(8,128)(2,1)} %get-tuple-element.19), channel_id=1, source_target_pairs={{3,0},{4,1},{5,2},{6,3},{7,4},{8,5},{9,6},{10,7},{11,8},{12,9},{13... | collective-permute-start | bytes 2359304 | tf_op jit(solution)/shard_map/ppermute | solution.py:21
  55.7 0.9 copy-start.1
  64.6 16.2 %copy-start.2 = (bf16[48,64,128]{2,1,0:T(8,128)(2,1)}, bf16[48,64,128]{2,1,0:T(8,128)(2,1)S(1)}, u32[]{:S(2)}) copy-start(bf16[48,64,128]{2,1,0:T(8,128)(2,1)S(1)} %collective-permute-done.2.refs_3_) | copy-start | bytes 2359300
  80.8 0.9 copy-start.3

commit v11 on v10

--- a/solution.py
+++ b/solution.py
@@ -172,6 +172,105 @@
         ),
     )(send_fine, send_coarse, charges, basis_t, transfer_t)
     return outs[0], outs[1], outs[2:]
+
+
+def coupled_product(coarse_part, fine_part, transfer, leaf_basis, near_field):
+    c_idx, c_mats, c_segs, c_pairs = coarse_part
+    f_idx, f_mats, f_segs, f_pairs = fine_part
+    width = RANK
+    parents = c_mats.shape[0] // RANK
+    leaves = f_mats.shape[0] // LEAF
+    tb = min(BLOCK_TARGETS, leaves)
+    steps = leaves // tb
+    halves = 2 if parents % 2 == 0 else 1
+    c_rows = parents * RANK // halves
+    c_total = sum(s[2] for s in c_segs)
+    f_total = sum(s[2] for s in f_segs)
+    segs = c_segs + f_segs
+    n_c = len(c_segs)
+    n_seg = len(segs)
+
+    hbm = pl.BlockSpec(memory_space=pl.ANY)
+    in_specs = [hbm] + [pl.BlockSpec((tb * LEAF, f_pairs * width), lambda i, a, b: (i, 0))]
+    in_specs += [hbm] * n_seg
+    in_specs += [
+        pl.BlockSpec((tb * RANK, RANK), lambda i, a, b: (i, 0)),
+        pl.BlockSpec((tb * LEAF, RANK), lambda i, a, b: (i, 0)),
+        pl.BlockSpec((tb, LEAF, RHS), lambda i, a, b: (i, 0, 0)),
+    ]
+
+    def gather_sum(idx_ref, pool_ref, mats, base, pairs):
+        blocks = [pool_ref[idx_ref[base + k]] for k in range(pairs)]
+        return jnp.dot(mats, jnp.concatenate(blocks, axis=0), preferred_element_type=jnp.float32)
+
+    def kernel(ci_ref, fi_ref, cm_hbm, fm_ref, *refs):
+        seg_refs = refs[:n_seg]
+        e_ref, v_ref, near_ref, out_ref = refs[n_seg:n_seg + 4]
+        c_pool, f_pool, c_mats_v, cr_ref, acc_ref, sem = refs[n_seg + 4:]
+        blk = pl.program_id(0)
+
+        @pl.when(blk == 0)
+        def _():
+            seg_copies = []
+            for j, (ref, (_, lo, cnt, row)) in enumerate(zip(seg_refs, segs)):
+                pool = c_pool if j < n_c else f_pool
+                cp = pltpu.make_async_copy(ref.at[pl.ds(row, cnt)], pool.at[pl.ds(lo, cnt)], sem.at[j])
+                cp.start()
+                seg_copies.append(cp)
+            mat_copies = []
+            for h in range(halves):
+                cp = pltpu.make_async_copy(
+                    cm_hbm.at[pl.ds(h * c_rows, c_rows)], c_mats_v.at[pl.ds(h * c_rows, c_rows)], sem.at[n_seg + h]
+                )
+                cp.start()
+                mat_copies.append(cp)
+            for cp in seg_copies[:n_c]:
+                cp.wait()
+            per_half = parents // halves
+            for h in range(halves):
+                mat_copies[h].wait()
+                for p in range(h * per_half, (h + 1) * per_half):
+                    acc = gather_sum(ci_ref, c_pool, c_mats_v[p * RANK:(p + 1) * RANK, :], p * c_pairs, c_pairs)
+                    cr_ref[p] = acc.astype(jnp.bfloat16)
+            for cp in seg_copies[n_c:]:
+                cp.wait()
+
+        for tt in range(tb):
+            base = (blk * tb + tt) * f_pairs
+            acc_ref[tt] = gather_sum(fi_ref, f_pool, fm_ref[tt * LEAF:(tt + 1) * LEAF, :], base, f_pairs)
+        rounded = []
+        for tt in range(tb):
+            e = e_ref[tt * RANK:(tt + 1) * RANK, :]
+            down = jnp.dot(e, cr_ref[(blk * tb + tt) // 2], preferred_element_type=jnp.float32)
+            rounded.append((acc_ref[tt] + down).astype(jnp.bfloat16))
+        for tt in range(tb):
+            v = v_ref[tt * LEAF:(tt + 1) * LEAF, :]
+            far = jnp.dot(v, rounded[tt], preferred_element_type=jnp.float32)
+            out_ref[tt] = (far + near_ref[tt]).astype(jnp.bfloat16)
+
+    grid_spec = pltpu.PrefetchScalarGridSpec(
+        num_scalar_prefetch=2,
+        grid=(steps,),
+        in_specs=in_specs,
+        out_specs=pl.BlockSpec((tb, LEAF, RHS), lambda i, a, b: (i, 0, 0)),
+        scratch_shapes=[
+            pltpu.VMEM((c_total, width, RHS), jnp.bfloat16),
+            pltpu.VMEM((f_total, width, RHS), jnp.bfloat16),
+            pltpu.VMEM(c_mats.shape, jnp.bfloat16),
+            pltpu.VMEM((parents, RANK, RHS), jnp.bfloat16),
+            pltpu.VMEM((tb, LEAF, RHS), jnp.float32),
+            pltpu.SemaphoreType.DMA((n_seg + halves,)),
+        ],
+    )
+    flops = 2 * (c_mats.size + f_mats.size) * RHS
+    bytes_accessed = (c_mats.size + f_mats.size) * 2 + (c_total + f_total) * width * RHS * 2
+    return pl.pallas_call(
+        kernel,
+        grid_spec=grid_spec,
+        out_shape=jax.ShapeDtypeStruct((leaves, LEAF, RHS), jnp.bfloat16),
+        compiler_params=pltpu.CompilerParams(dimension_semantics=("arbitrary",)),
+        cost_estimate=pl.CostEstimate(flops=flops, transcendentals=0, bytes_accessed=bytes_accessed),
+    )(c_idx, f_idx, c_mats, f_mats, *[s[0] for s in segs], transfer, leaf_basis, near_field)
 
 
 def on_device(
@@ -212,42 +311,15 @@
     coarse_segments = [(coarse_coeffs, 0, parents, 0)]
     for slot in range(2 * REACH):
         coarse_segments.append((incoming[slot], parents + slot * coarse_each, coarse_each, fine_each))
-    coarse_round = gather_dot(
-        source_coarse, couple_coarse, coarse_segments, source_coarse.shape[0] // parents,
-        out_dtype=jnp.bfloat16,
-    )
-
     fine_segments = [(fine_coeffs, 0, leaves, 0)]
     for slot in range(2 * REACH):
         fine_segments.append((incoming[slot], leaves + slot * fine_each, fine_each, 0))
-
-    tb = min(BLOCK_TARGETS, leaves)
-
-    def finish(count, acc_ref, refs, out_ref):
-        cr_ref, e_ref, v_ref, near_ref = refs
-        rounded = []
-        for tt in range(count):
-            e = e_ref[tt * RANK:(tt + 1) * RANK, :]
-            down = jnp.dot(e, cr_ref[tt // 2], preferred_element_type=jnp.float32)
-            rounded.append((acc_ref[tt] + down).astype(jnp.bfloat16))
-        for tt in range(count):
-            v = v_ref[tt * LEAF:(tt + 1) * LEAF, :]
-            far = jnp.dot(v, rounded[tt], preferred_element_type=jnp.float32)
-            out_ref[tt] = (far + near_ref[tt]).astype(jnp.bfloat16)
-
-    epilogue = (
-        [coarse_round, transfer, leaf_basis, near_field],
-        [
-            pl.BlockSpec((tb // 2, RANK, RHS), lambda i, ix: (i, 0, 0)),
-            pl.BlockSpec((tb * RANK, RANK), lambda i, ix: (i, 0)),
-            pl.BlockSpec((tb * LEAF, RANK), lambda i, ix: (i, 0)),
-            pl.BlockSpec((tb, LEAF, RHS), lambda i, ix: (i, 0, 0)),
-        ],
-        finish,
-        jnp.bfloat16,
-    )
-    return gather_dot(
-        source_fine, couple_fine, fine_segments, source_fine.shape[0] // leaves, epilogue
+    return coupled_product(
+        (source_coarse, couple_coarse, coarse_segments, source_coarse.shape[0] // parents),
+        (source_fine, couple_fine, fine_segments, source_fine.shape[0] // leaves),
+        transfer,
+        leaf_basis,
+        near_field,
     )
 
 

time: 99.7 us -> 96.2 us (0.965)
  Pallas kernels: 30.6 us -> 27.1 us
    pallas_call x3 -> x1, Pallas kernels: 25.5 us -> 8.06 us  [gather_dot(): pl.pallas_call(kernel, grid_spec=grid_spec, out_shape=jax.ShapeDtypeStruc...]
    pallas_call x0 -> x1, Pallas kernels: none -> 13.9 us  [coupled_product(): pl.pallas_call(kernel, grid_spec=grid_spec, out_shape=jax.ShapeDtypeStruc...]
where the time goes in v11:
time: 96.2 us; the launch traced here: 95.7 us
  starting transfers between devices  45.5 us (47%)
  Pallas kernels  27.1 us (28%)
  waiting for transfers between devices  16.4 us (17%)
  local copies, waits for them, and re-layouts  6.51 us (7%)
    ppermute x6, starting transfers between devices, from_behind(): lax.ppermute(value, axis, [(source, source + steps) for source in range(f...  45.5 us
    ppermute x6, waiting for transfers between devices, from_behind(): lax.ppermute(value, axis, [(source, source + steps) for source in range(f...  16.4 us
    pallas_call x1, Pallas kernels, coupled_product(): pl.pallas_call(kernel, grid_spec=grid_spec, out_shape=jax.ShapeDtypeStruc...  13.9 us
    pallas_call x1, Pallas kernels, gather_dot(): pl.pallas_call(kernel, grid_spec=grid_spec, out_shape=jax.ShapeDtypeStruc...  8.06 us
    unnamed x10, local copies, waits for them, and re-layouts  6.51 us
    pallas_call x1, Pallas kernels, upward(): pl.pallas_call(kernel, in_specs=[smem, smem, vmem, vmem, vmem], out_specs...  5.16 us
  transfers between devices with their start and end apart: 6, of which 2 were waited for; matrix products, arithmetic and copies ran while one was open for 5% of the time, Pallas kernels for 8%

profile of v11, /device:TPU:24, one launch (start us, length us, event | category | flops | bytes accessed | tf_op | source)
XLA Modules:
  0.0 95.7 jit_solution(12485120796361401476)
XLA Ops:
  0.0 5.2 %shard_map.109 = (bf16[64,64,128]{2,1,0:T(8,128)(2,1)}, bf16[32,64,128]{2,1,0:T(8,128)(2,1)}, bf16[52,64,128]{2,1,0:T(8,128)(2,1)}, bf16[52,64,128]{2,1,0:T(8,12...) custom-call(s32[192]{0:T(256)} %bitcast.6, ...), custom_call_target="tpu_custom_call" | custom-call | flops 134217728 | bytes 16777216 | tf_op jit(solution)/shard_map/pallas_call | solution.py:158
  5.2 1.9 %collective-permute-start = (bf16[52,64,128]{2,1,0:T(8,128)(2,1)}, bf16[52,64,128]{2,1,0:T(8,128)(2,1)S(1)}, u32[]{:S(2)}, u32[]{:S(2)}) collective-permute-start(bf16[52,64,128]{2,1,0:T(8,128)(2,1)} %get-tuple-element.14), channel_id=1, source_target_pairs={{0,1},{1,2},{2,3},{3,4},{4,5},{5,6},{6,7},{7,8},{8,9},{9,10},{10,1... | collective-permute-start | bytes 2555912 | tf_op jit(solution)/shard_map/ppermute | solution.py:21
  7.1 5.4 %collective-permute-start.1 = (bf16[52,64,128]{2,1,0:T(8,128)(2,1)}, bf16[52,64,128]{2,1,0:T(8,128)(2,1)S(1)}, u32[]{:S(2)}, u32[]{:S(2)}) collective-permute-start(bf16[52,64,128]{2,1,0:T(8,128)(2,1)} %get-tuple-element.15), channel_id=1, source_target_pairs={{1,0},{2,1},{3,2},{4,3},{5,4},{6,5},{7,6},{8,7},{9,8},{10,9},{11,1... | collective-permute-start | bytes 2555912 | tf_op jit(solution)/shard_map/ppermute | solution.py:21
  12.5 1.9 %collective-permute-start.2 = (bf16[48,64,128]{2,1,0:T(8,128)(2,1)}, bf16[48,64,128]{2,1,0:T(8,128)(2,1)S(1)}, u32[]{:S(2)}, u32[]{:S(2)}) collective-permute-start(bf16[48,64,128]{2,1,0:T(8,128)(2,1)} %get-tuple-element.16), channel_id=1, source_target_pairs={{0,2},{1,3},{2,4},{3,5},{4,6},{5,7},{6,8},{7,9},{8,10},{9,11},{10,... | collective-permute-start | bytes 2359304 | tf_op jit(solution)/shard_map/ppermute | solution.py:21
  14.5 5.7 %collective-permute-start.3 = (bf16[48,64,128]{2,1,0:T(8,128)(2,1)}, bf16[48,64,128]{2,1,0:T(8,128)(2,1)S(1)}, u32[]{:S(2)}, u32[]{:S(2)}) collective-permute-start(bf16[48,64,128]{2,1,0:T(8,128)(2,1)} %get-tuple-element.17), channel_id=1, source_target_pairs={{2,0},{3,1},{4,2},{5,3},{6,4},{7,5},{8,6},{9,7},{10,8},{11,9},{12,... | collective-permute-start | bytes 2359304 | tf_op jit(solution)/shard_map/ppermute | solution.py:21
  20.2 1.9 %collective-permute-start.4 = (bf16[48,64,128]{2,1,0:T(8,128)(2,1)}, bf16[48,64,128]{2,1,0:T(8,128)(2,1)}, u32[]{:S(2)}, u32[]{:S(2)}) collective-permute-start(bf16[48,64,128]{2,1,0:T(8,128)(2,1)} %get-tuple-element.18), channel_id=1, source_target_pairs={{0,3},{1,4},{2,5},{3,6},{4,7},{5,8},{6,9},{7,10},{8,11},{9,12},{10... | collective-permute-start | bytes 2359304 | tf_op jit(solution)/shard_map/ppermute | solution.py:21
  22.1 0.3 collective-permute-done.refs_0_.refs_1_.refs_8_
  22.4 0.0 copy-start
  22.4 28.6 %collective-permute-start.5 = (bf16[48,64,128]{2,1,0:T(8,128)(2,1)}, bf16[48,64,128]{2,1,0:T(8,128)(2,1)}, u32[]{:S(2)}, u32[]{:S(2)}) collective-permute-start(bf16[48,64,128]{2,1,0:T(8,128)(2,1)} %get-tuple-element.19), channel_id=1, source_target_pairs={{3,0},{4,1},{5,2},{6,3},{7,4},{8,5},{9,6},{10,7},{11,8},{12,9},{13... | collective-permute-start | bytes 2359304 | tf_op jit(solution)/shard_map/ppermute | solution.py:21
  51.0 2.3 %copy.13.refs_15_ = bf16[4096,64]{1,0:T(8,128)(2,1)} copy(bf16[4096,64]{0,1:T(8,128)(2,1)} %param.12) | data formatting | bytes 1048576 | tf_op args[1]
  53.3 2.4 %copy.12.refs_14_ = bf16[4096,64]{1,0:T(8,128)(2,1)} copy(bf16[4096,64]{0,1:T(8,128)(2,1)} %param.13) | data formatting | bytes 1048576 | tf_op args[2]
  55.7 0.0 collective-permute-done.1.refs_2_.refs_9_
  55.7 0.0 copy-done
  55.7 0.0 copy-start.1
  55.7 0.9 copy-done.1
  56.6 8.1 %shard_map.110.refs_16_ = f32[64,64,128]{2,1,0:T(8,128)} custom-call(s32[768]{0:T(1024)} %idx_ref.1, bf16[4096,768]{1,0:T(8,128)(2,1)} %mats_ref.1, bf16[52,64,128]{2,1,0:T(8,128)(2,1)} %copy-done, bf16[64,64,128]{2,1,0:T(8,128)(2,1)} %refs_1_.1, bf16[52,64,128]{2,1,0:T(8,128)(2,1)} %copy-done.1), custom_call_target="tpu_custom_call" | custom-call | flops 805306368 | bytes 9568256 | tf_op jit(solution)/shard_map/pallas_call | solution.py:101
  64.7 0.0 collective-permute-done.2.refs_3_.refs_10_
  64.7 0.0 copy-start.2
  64.7 16.2 %collective-permute-done.3.refs_4_.refs_11_ = bf16[48,64,128]{2,1,0:T(8,128)(2,1)S(1)} collective-permute-done((bf16[48,64,128]{2,1,0:T(8,128)(2,1)}, bf16[48,64,128]{2,1,0:T(8,128)(2,1)S(1)}, u32[]{:S(2)}, u32[]{:S(2)}) %collective-permute-start.3) | collective-permute-done | bytes 786464 | tf_op jit(solution)/shard_map/ppermute | solution.py:21
  80.9 0.0 copy-start.3
  80.9 0.0 collective-permute-done.4.refs_5_.refs_12_
  80.9 0.0 collective-permute-done.5.refs_6_.refs_13_
  80.9 0.0 copy-done.2
  80.9 0.9 copy-done.3
  81.8 13.9 %shard_map.111 = bf16[64,64,128]{2,1,0:T(8,128)(2,1)} custom-call(s32[512]{0:T(512)} %ci_ref.1, s32[1024]{0:T(1024)} %fi_ref.1, bf16[2048,1024]{1,0:T(8,128)(2,1)} %cm_hbm.1, bf16[4096,1024]{1,0:T(8,128)(2,1)} %fm_ref.1, bf16[32,64,128]{2,1,0:T(8,128)(2,1)} %get-tuple-element.13.refs_0_, bf16[52,64,128]{2,1,0:T(8,128)(2,1)} %copy-done, ...), custom_call_target="tpu_custom_call" | custom-call | flops 1610612736 | bytes 18874368 | tf_op jit(solution)/shard_map/pallas_call | solution.py:267
Async XLA Ops:
  5.2 17.2 %collective-permute-start = (bf16[52,64,128]{2,1,0:T(8,128)(2,1)}, bf16[52,64,128]{2,1,0:T(8,128)(2,1)S(1)}, u32[]{:S(2)}, u32[]{:S(2)}) collective-permute-start(bf16[52,64,128]{2,1,0:T(8,128)(2,1)} %get-tuple-element.14), channel_id=1, source_target_pairs={{0,1},{1,2},{2,3},{3,4},{4,5},{5,6},{6,7},{7,8},{8,9},{9,10},{10,1... | collective-permute-start | bytes 2555912 | tf_op jit(solution)/shard_map/ppermute | solution.py:21
  7.1 48.6 %collective-permute-start.1 = (bf16[52,64,128]{2,1,0:T(8,128)(2,1)}, bf16[52,64,128]{2,1,0:T(8,128)(2,1)S(1)}, u32[]{:S(2)}, u32[]{:S(2)}) collective-permute-start(bf16[52,64,128]{2,1,0:T(8,128)(2,1)} %get-tuple-element.15), channel_id=1, source_target_pairs={{1,0},{2,1},{3,2},{4,3},{5,4},{6,5},{7,6},{8,7},{9,8},{10,9},{11,1... | collective-permute-start | bytes 2555912 | tf_op jit(solution)/shard_map/ppermute | solution.py:21
  12.5 52.1 %collective-permute-start.2 = (bf16[48,64,128]{2,1,0:T(8,128)(2,1)}, bf16[48,64,128]{2,1,0:T(8,128)(2,1)S(1)}, u32[]{:S(2)}, u32[]{:S(2)}) collective-permute-start(bf16[48,64,128]{2,1,0:T(8,128)(2,1)} %get-tuple-element.16), channel_id=1, source_target_pairs={{0,2},{1,3},{2,4},{3,5},{4,6},{5,7},{6,8},{7,9},{8,10},{9,11},{10,... | collective-permute-start | bytes 2359304 | tf_op jit(solution)/shard_map/ppermute | solution.py:21
  14.5 66.4 %collective-permute-start.3 = (bf16[48,64,128]{2,1,0:T(8,128)(2,1)}, bf16[48,64,128]{2,1,0:T(8,128)(2,1)S(1)}, u32[]{:S(2)}, u32[]{:S(2)}) collective-permute-start(bf16[48,64,128]{2,1,0:T(8,128)(2,1)} %get-tuple-element.17), channel_id=1, source_target_pairs={{2,0},{3,1},{4,2},{5,3},{6,4},{7,5},{8,6},{9,7},{10,8},{11,9},{12,... | collective-permute-start | bytes 2359304 | tf_op jit(solution)/shard_map/ppermute | solution.py:21
  20.2 60.7 %collective-permute-start.4 = (bf16[48,64,128]{2,1,0:T(8,128)(2,1)}, bf16[48,64,128]{2,1,0:T(8,128)(2,1)}, u32[]{:S(2)}, u32[]{:S(2)}) collective-permute-start(bf16[48,64,128]{2,1,0:T(8,128)(2,1)} %get-tuple-element.18), channel_id=1, source_target_pairs={{0,3},{1,4},{2,5},{3,6},{4,7},{5,8},{6,9},{7,10},{8,11},{9,12},{10... | collective-permute-start | bytes 2359304 | tf_op jit(solution)/shard_map/ppermute | solution.py:21
  22.4 33.3 %copy-start = (bf16[52,64,128]{2,1,0:T(8,128)(2,1)}, bf16[52,64,128]{2,1,0:T(8,128)(2,1)S(1)}, u32[]{:S(2)}) copy-start(bf16[52,64,128]{2,1,0:T(8,128)(2,1)S(1)} %collective-permute-done.refs_0_.refs_1_.refs_8_) | copy-start | bytes 2555908
  22.4 58.5 %collective-permute-start.5 = (bf16[48,64,128]{2,1,0:T(8,128)(2,1)}, bf16[48,64,128]{2,1,0:T(8,128)(2,1)}, u32[]{:S(2)}, u32[]{:S(2)}) collective-permute-start(bf16[48,64,128]{2,1,0:T(8,128)(2,1)} %get-tuple-element.19), channel_id=1, source_target_pairs={{3,0},{4,1},{5,2},{6,3},{7,4},{8,5},{9,6},{10,7},{11,8},{12,9},{13... | collective-permute-start | bytes 2359304 | tf_op jit(solution)/shard_map/ppermute | solution.py:21
  55.7 0.9 copy-start.1
  64.7 16.2 %copy-start.2 = (bf16[48,64,128]{2,1,0:T(8,128)(2,1)}, bf16[48,64,128]{2,1,0:T(8,128)(2,1)S(1)}, u32[]{:S(2)}) copy-start(bf16[48,64,128]{2,1,0:T(8,128)(2,1)S(1)} %collective-permute-done.2.refs_3_.refs_10_) | copy-start | bytes 2359300
  80.9 0.9 copy-start.3

commit v12 on v11

--- a/solution.py
+++ b/solution.py
@@ -182,7 +182,7 @@
     leaves = f_mats.shape[0] // LEAF
     tb = min(BLOCK_TARGETS, leaves)
     steps = leaves // tb
-    halves = 2 if parents % 2 == 0 else 1
+    halves = 4 if parents % 4 == 0 else 1
     c_rows = parents * RANK // halves
     c_total = sum(s[2] for s in c_segs)
     f_total = sum(s[2] for s in f_segs)
@@ -214,9 +214,11 @@
             seg_copies = []
             for j, (ref, (_, lo, cnt, row)) in enumerate(zip(seg_refs, segs)):
                 pool = c_pool if j < n_c else f_pool
-                cp = pltpu.make_async_copy(ref.at[pl.ds(row, cnt)], pool.at[pl.ds(lo, cnt)], sem.at[j])
+                seg_copies.append(
+                    pltpu.make_async_copy(ref.at[pl.ds(row, cnt)], pool.at[pl.ds(lo, cnt)], sem.at[j])
+                )
+            for cp in seg_copies[:n_c]:
                 cp.start()
-                seg_copies.append(cp)
             mat_copies = []
             for h in range(halves):
                 cp = pltpu.make_async_copy(
@@ -229,6 +231,9 @@
             per_half = parents // halves
             for h in range(halves):
                 mat_copies[h].wait()
+                if h == 0:
+                    for cp in seg_copies[n_c:]:
+                        cp.start()
                 for p in range(h * per_half, (h + 1) * per_half):
                     acc = gather_sum(ci_ref, c_pool, c_mats_v[p * RANK:(p + 1) * RANK, :], p * c_pairs, c_pairs)
                     cr_ref[p] = acc.astype(jnp.bfloat16)

time: 96.2 us -> 95.7 us (level)
  no operation moved by 1% of the time
where the time goes in v12:
time: 95.7 us; the launch traced here: 95.1 us
  starting transfers between devices  45.5 us (48%)
  Pallas kernels  26.6 us (28%)
  waiting for transfers between devices  16.4 us (17%)
  local copies, waits for them, and re-layouts  6.51 us (7%)
    ppermute x6, starting transfers between devices, from_behind(): lax.ppermute(value, axis, [(source, source + steps) for source in range(f...  45.5 us
    ppermute x6, waiting for transfers between devices, from_behind(): lax.ppermute(value, axis, [(source, source + steps) for source in range(f...  16.4 us
    pallas_call x1, Pallas kernels, coupled_product(): pl.pallas_call(kernel, grid_spec=grid_spec, out_shape=jax.ShapeDtypeStruc...  13.4 us
    pallas_call x1, Pallas kernels, gather_dot(): pl.pallas_call(kernel, grid_spec=grid_spec, out_shape=jax.ShapeDtypeStruc...  8.06 us
    unnamed x10, local copies, waits for them, and re-layouts  6.51 us
    pallas_call x1, Pallas kernels, upward(): pl.pallas_call(kernel, in_specs=[smem, smem, vmem, vmem, vmem], out_specs...  5.16 us
  transfers between devices with their start and end apart: 6, of which 2 were waited for; matrix products, arithmetic and copies ran while one was open for 5% of the time, Pallas kernels for 8%

profile of v12, /device:TPU:24, one launch (start us, length us, event | category | flops | bytes accessed | tf_op | source)
XLA Modules:
  0.0 95.1 jit_solution(14488468411008243572)
XLA Ops:
  0.0 5.2 %shard_map.109 = (bf16[64,64,128]{2,1,0:T(8,128)(2,1)}, bf16[32,64,128]{2,1,0:T(8,128)(2,1)}, bf16[52,64,128]{2,1,0:T(8,128)(2,1)}, bf16[52,64,128]{2,1,0:T(8,12...) custom-call(s32[192]{0:T(256)} %bitcast.6, ...), custom_call_target="tpu_custom_call" | custom-call | flops 134217728 | bytes 16777216 | tf_op jit(solution)/shard_map/pallas_call | solution.py:158
  5.2 1.9 %collective-permute-start = (bf16[52,64,128]{2,1,0:T(8,128)(2,1)}, bf16[52,64,128]{2,1,0:T(8,128)(2,1)S(1)}, u32[]{:S(2)}, u32[]{:S(2)}) collective-permute-start(bf16[52,64,128]{2,1,0:T(8,128)(2,1)} %get-tuple-element.14), channel_id=1, source_target_pairs={{0,1},{1,2},{2,3},{3,4},{4,5},{5,6},{6,7},{7,8},{8,9},{9,10},{10,1... | collective-permute-start | bytes 2555912 | tf_op jit(solution)/shard_map/ppermute | solution.py:21
  7.1 5.4 %collective-permute-start.1 = (bf16[52,64,128]{2,1,0:T(8,128)(2,1)}, bf16[52,64,128]{2,1,0:T(8,128)(2,1)S(1)}, u32[]{:S(2)}, u32[]{:S(2)}) collective-permute-start(bf16[52,64,128]{2,1,0:T(8,128)(2,1)} %get-tuple-element.15), channel_id=1, source_target_pairs={{1,0},{2,1},{3,2},{4,3},{5,4},{6,5},{7,6},{8,7},{9,8},{10,9},{11,1... | collective-permute-start | bytes 2555912 | tf_op jit(solution)/shard_map/ppermute | solution.py:21
  12.5 1.9 %collective-permute-start.2 = (bf16[48,64,128]{2,1,0:T(8,128)(2,1)}, bf16[48,64,128]{2,1,0:T(8,128)(2,1)S(1)}, u32[]{:S(2)}, u32[]{:S(2)}) collective-permute-start(bf16[48,64,128]{2,1,0:T(8,128)(2,1)} %get-tuple-element.16), channel_id=1, source_target_pairs={{0,2},{1,3},{2,4},{3,5},{4,6},{5,7},{6,8},{7,9},{8,10},{9,11},{10,... | collective-permute-start | bytes 2359304 | tf_op jit(solution)/shard_map/ppermute | solution.py:21
  14.5 5.7 %collective-permute-start.3 = (bf16[48,64,128]{2,1,0:T(8,128)(2,1)}, bf16[48,64,128]{2,1,0:T(8,128)(2,1)S(1)}, u32[]{:S(2)}, u32[]{:S(2)}) collective-permute-start(bf16[48,64,128]{2,1,0:T(8,128)(2,1)} %get-tuple-element.17), channel_id=1, source_target_pairs={{2,0},{3,1},{4,2},{5,3},{6,4},{7,5},{8,6},{9,7},{10,8},{11,9},{12,... | collective-permute-start | bytes 2359304 | tf_op jit(solution)/shard_map/ppermute | solution.py:21
  20.2 1.9 %collective-permute-start.4 = (bf16[48,64,128]{2,1,0:T(8,128)(2,1)}, bf16[48,64,128]{2,1,0:T(8,128)(2,1)}, u32[]{:S(2)}, u32[]{:S(2)}) collective-permute-start(bf16[48,64,128]{2,1,0:T(8,128)(2,1)} %get-tuple-element.18), channel_id=1, source_target_pairs={{0,3},{1,4},{2,5},{3,6},{4,7},{5,8},{6,9},{7,10},{8,11},{9,12},{10... | collective-permute-start | bytes 2359304 | tf_op jit(solution)/shard_map/ppermute | solution.py:21
  22.1 0.3 collective-permute-done.refs_0_.refs_1_.refs_8_
  22.4 0.0 copy-start
  22.4 28.6 %collective-permute-start.5 = (bf16[48,64,128]{2,1,0:T(8,128)(2,1)}, bf16[48,64,128]{2,1,0:T(8,128)(2,1)}, u32[]{:S(2)}, u32[]{:S(2)}) collective-permute-start(bf16[48,64,128]{2,1,0:T(8,128)(2,1)} %get-tuple-element.19), channel_id=1, source_target_pairs={{3,0},{4,1},{5,2},{6,3},{7,4},{8,5},{9,6},{10,7},{11,8},{12,9},{13... | collective-permute-start | bytes 2359304 | tf_op jit(solution)/shard_map/ppermute | solution.py:21
  51.0 2.3 %copy.13.refs_15_ = bf16[4096,64]{1,0:T(8,128)(2,1)} copy(bf16[4096,64]{0,1:T(8,128)(2,1)} %param.12) | data formatting | bytes 1048576 | tf_op args[1]
  53.3 2.4 %copy.12.refs_14_ = bf16[4096,64]{1,0:T(8,128)(2,1)} copy(bf16[4096,64]{0,1:T(8,128)(2,1)} %param.13) | data formatting | bytes 1048576 | tf_op args[2]
  55.7 0.0 collective-permute-done.1.refs_2_.refs_9_
  55.7 0.0 copy-done
  55.7 0.0 copy-start.1
  55.7 0.9 copy-done.1
  56.6 8.1 %shard_map.110.refs_16_ = f32[64,64,128]{2,1,0:T(8,128)} custom-call(s32[768]{0:T(1024)} %idx_ref.1, bf16[4096,768]{1,0:T(8,128)(2,1)} %mats_ref.1, bf16[52,64,128]{2,1,0:T(8,128)(2,1)} %copy-done, bf16[64,64,128]{2,1,0:T(8,128)(2,1)} %refs_1_.1, bf16[52,64,128]{2,1,0:T(8,128)(2,1)} %copy-done.1), custom_call_target="tpu_custom_call" | custom-call | flops 805306368 | bytes 9568256 | tf_op jit(solution)/shard_map/pallas_call | solution.py:101
  64.7 0.0 collective-permute-done.2.refs_3_.refs_10_
  64.7 0.0 copy-start.2
  64.7 16.2 %collective-permute-done.3.refs_4_.refs_11_ = bf16[48,64,128]{2,1,0:T(8,128)(2,1)S(1)} collective-permute-done((bf16[48,64,128]{2,1,0:T(8,128)(2,1)}, bf16[48,64,128]{2,1,0:T(8,128)(2,1)S(1)}, u32[]{:S(2)}, u32[]{:S(2)}) %collective-permute-start.3) | collective-permute-done | bytes 786464 | tf_op jit(solution)/shard_map/ppermute | solution.py:21
  80.9 0.0 copy-start.3
  80.9 0.0 collective-permute-done.4.refs_5_.refs_12_
  80.9 0.0 collective-permute-done.5.refs_6_.refs_13_
  80.9 0.0 copy-done.2
  80.9 0.9 copy-done.3
  81.8 13.4 %shard_map.111 = bf16[64,64,128]{2,1,0:T(8,128)(2,1)} custom-call(s32[512]{0:T(512)} %ci_ref.1, s32[1024]{0:T(1024)} %fi_ref.1, bf16[2048,1024]{1,0:T(8,128)(2,1)} %cm_hbm.1, bf16[4096,1024]{1,0:T(8,128)(2,1)} %fm_ref.1, bf16[32,64,128]{2,1,0:T(8,128)(2,1)} %get-tuple-element.13.refs_0_, bf16[52,64,128]{2,1,0:T(8,128)(2,1)} %copy-done, ...), custom_call_target="tpu_custom_call" | custom-call | flops 1610612736 | bytes 18874368 | tf_op jit(solution)/shard_map/pallas_call | solution.py:272
Async XLA Ops:
  5.2 17.2 %collective-permute-start = (bf16[52,64,128]{2,1,0:T(8,128)(2,1)}, bf16[52,64,128]{2,1,0:T(8,128)(2,1)S(1)}, u32[]{:S(2)}, u32[]{:S(2)}) collective-permute-start(bf16[52,64,128]{2,1,0:T(8,128)(2,1)} %get-tuple-element.14), channel_id=1, source_target_pairs={{0,1},{1,2},{2,3},{3,4},{4,5},{5,6},{6,7},{7,8},{8,9},{9,10},{10,1... | collective-permute-start | bytes 2555912 | tf_op jit(solution)/shard_map/ppermute | solution.py:21
  7.1 48.6 %collective-permute-start.1 = (bf16[52,64,128]{2,1,0:T(8,128)(2,1)}, bf16[52,64,128]{2,1,0:T(8,128)(2,1)S(1)}, u32[]{:S(2)}, u32[]{:S(2)}) collective-permute-start(bf16[52,64,128]{2,1,0:T(8,128)(2,1)} %get-tuple-element.15), channel_id=1, source_target_pairs={{1,0},{2,1},{3,2},{4,3},{5,4},{6,5},{7,6},{8,7},{9,8},{10,9},{11,1... | collective-permute-start | bytes 2555912 | tf_op jit(solution)/shard_map/ppermute | solution.py:21
  12.5 52.1 %collective-permute-start.2 = (bf16[48,64,128]{2,1,0:T(8,128)(2,1)}, bf16[48,64,128]{2,1,0:T(8,128)(2,1)S(1)}, u32[]{:S(2)}, u32[]{:S(2)}) collective-permute-start(bf16[48,64,128]{2,1,0:T(8,128)(2,1)} %get-tuple-element.16), channel_id=1, source_target_pairs={{0,2},{1,3},{2,4},{3,5},{4,6},{5,7},{6,8},{7,9},{8,10},{9,11},{10,... | collective-permute-start | bytes 2359304 | tf_op jit(solution)/shard_map/ppermute | solution.py:21
  14.5 66.4 %collective-permute-start.3 = (bf16[48,64,128]{2,1,0:T(8,128)(2,1)}, bf16[48,64,128]{2,1,0:T(8,128)(2,1)S(1)}, u32[]{:S(2)}, u32[]{:S(2)}) collective-permute-start(bf16[48,64,128]{2,1,0:T(8,128)(2,1)} %get-tuple-element.17), channel_id=1, source_target_pairs={{2,0},{3,1},{4,2},{5,3},{6,4},{7,5},{8,6},{9,7},{10,8},{11,9},{12,... | collective-permute-start | bytes 2359304 | tf_op jit(solution)/shard_map/ppermute | solution.py:21
  20.2 60.7 %collective-permute-start.4 = (bf16[48,64,128]{2,1,0:T(8,128)(2,1)}, bf16[48,64,128]{2,1,0:T(8,128)(2,1)}, u32[]{:S(2)}, u32[]{:S(2)}) collective-permute-start(bf16[48,64,128]{2,1,0:T(8,128)(2,1)} %get-tuple-element.18), channel_id=1, source_target_pairs={{0,3},{1,4},{2,5},{3,6},{4,7},{5,8},{6,9},{7,10},{8,11},{9,12},{10... | collective-permute-start | bytes 2359304 | tf_op jit(solution)/shard_map/ppermute | solution.py:21
  22.4 33.3 %copy-start = (bf16[52,64,128]{2,1,0:T(8,128)(2,1)}, bf16[52,64,128]{2,1,0:T(8,128)(2,1)S(1)}, u32[]{:S(2)}) copy-start(bf16[52,64,128]{2,1,0:T(8,128)(2,1)S(1)} %collective-permute-done.refs_0_.refs_1_.refs_8_) | copy-start | bytes 2555908
  22.4 58.5 %collective-permute-start.5 = (bf16[48,64,128]{2,1,0:T(8,128)(2,1)}, bf16[48,64,128]{2,1,0:T(8,128)(2,1)}, u32[]{:S(2)}, u32[]{:S(2)}) collective-permute-start(bf16[48,64,128]{2,1,0:T(8,128)(2,1)} %get-tuple-element.19), channel_id=1, source_target_pairs={{3,0},{4,1},{5,2},{6,3},{7,4},{8,5},{9,6},{10,7},{11,8},{12,9},{13... | collective-permute-start | bytes 2359304 | tf_op jit(solution)/shard_map/ppermute | solution.py:21
  55.7 0.9 copy-start.1
  64.7 16.2 %copy-start.2 = (bf16[48,64,128]{2,1,0:T(8,128)(2,1)}, bf16[48,64,128]{2,1,0:T(8,128)(2,1)S(1)}, u32[]{:S(2)}) copy-start(bf16[48,64,128]{2,1,0:T(8,128)(2,1)S(1)} %collective-permute-done.2.refs_3_.refs_10_) | copy-start | bytes 2359300
  80.9 0.9 copy-start.3

commit v13 on v12

--- a/solution.py
+++ b/solution.py
@@ -107,71 +107,98 @@
     )(idx, mats, *seg_arrays, *extra)
 
 
-def upward(charges, basis_t, transfer_t, send_fine, send_coarse, fine_each, coarse_each):
+def upward(charges, basis_t, transfer_t, send_fine, send_coarse, fine_each, coarse_each, packets):
     leaves = charges.shape[0]
     parents = leaves // 2
     slots = 2 * REACH
     each = fine_each + coarse_each
     sizes = [each + (HALO if q < 2 else 0) for q in range(slots)]
-
-    def kernel(sf_ref, sc_ref, x_ref, v_ref, e_ref, fine_out, coarse_out, *rest):
-        packet_refs = rest[:slots]
-        fine_v, coarse_v = rest[slots:slots + 2]
-        bufs = rest[slots + 2:2 * slots + 2]
-        sem = rest[2 * slots + 2]
-        for j in range(parents):
-            col = j * 2 * RANK
-            f0 = jnp.dot(v_ref[:, col:col + RANK], x_ref[2 * j], preferred_element_type=jnp.float32)
-            f1 = jnp.dot(v_ref[:, col + RANK:col + 2 * RANK], x_ref[2 * j + 1], preferred_element_type=jnp.float32)
-            pair = jnp.concatenate([f0.astype(jnp.bfloat16), f1.astype(jnp.bfloat16)], axis=0)
-            fine_v[2 * j] = pair[:RANK]
-            fine_v[2 * j + 1] = pair[RANK:]
-            e = e_ref[:, col:col + 2 * RANK]
-            coarse_v[j] = jnp.dot(e, pair, preferred_element_type=jnp.float32).astype(jnp.bfloat16)
-
-        copies = [
-            pltpu.make_async_copy(fine_v, fine_out, sem.at[0]),
-            pltpu.make_async_copy(coarse_v, coarse_out, sem.at[1]),
-        ]
-        for cp in copies:
-            cp.start()
-        for q in range(slots):
-            buf = bufs[q]
-            for m in range(fine_each):
-                buf[m] = fine_v[jnp.clip(sf_ref[q * fine_each + m], 0, leaves - 1)]
-            for m in range(coarse_each):
-                buf[fine_each + m] = coarse_v[jnp.clip(sc_ref[q * coarse_each + m], 0, parents - 1)]
-            if q == 0:
-                buf[each:each + HALO] = x_ref[leaves - HALO:leaves]
-            elif q == 1:
-                buf[each:each + HALO] = x_ref[0:HALO]
-            cp = pltpu.make_async_copy(buf, packet_refs[q], sem.at[2 + q])
-            cp.start()
-            copies.append(cp)
+    chunks = 4 if parents % 4 == 0 else 1
+    per = parents // chunks
+
+    def kernel(sf_ref, sc_ref, x_hbm, v_hbm, e_hbm, *rest):
+        n_out = slots if packets else 2
+        outs = rest[:n_out]
+        x_ref, v_ref, e_ref, fine_v, coarse_v = rest[n_out:n_out + 5]
+        bufs = rest[n_out + 5:len(rest) - 2]
+        in_sem, sem = rest[len(rest) - 2:]
+        loads = []
+        for c in range(chunks):
+            lo, cols = 2 * c * per, 2 * c * per * RANK
+            span = pl.ds(cols, 2 * per * RANK)
+            trio = [
+                pltpu.make_async_copy(x_hbm.at[pl.ds(lo, 2 * per)], x_ref.at[pl.ds(lo, 2 * per)], in_sem.at[3 * c]),
+                pltpu.make_async_copy(v_hbm.at[:, span], v_ref.at[:, span], in_sem.at[3 * c + 1]),
+                pltpu.make_async_copy(e_hbm.at[:, span], e_ref.at[:, span], in_sem.at[3 * c + 2]),
+            ]
+            for cp in trio:
+                cp.start()
+            loads.append(trio)
+        for c in range(chunks):
+            for cp in loads[c]:
+                cp.wait()
+            for j in range(c * per, (c + 1) * per):
+                col = j * 2 * RANK
+                f0 = jnp.dot(v_ref[:, col:col + RANK], x_ref[2 * j], preferred_element_type=jnp.float32)
+                f1 = jnp.dot(v_ref[:, col + RANK:col + 2 * RANK], x_ref[2 * j + 1], preferred_element_type=jnp.float32)
+                pair = jnp.concatenate([f0.astype(jnp.bfloat16), f1.astype(jnp.bfloat16)], axis=0)
+                fine_v[2 * j] = pair[:RANK]
+                fine_v[2 * j + 1] = pair[RANK:]
+                e = e_ref[:, col:col + 2 * RANK]
+                coarse_v[j] = jnp.dot(e, pair, preferred_element_type=jnp.float32).astype(jnp.bfloat16)
+
+        copies = []
+        if not packets:
+            copies = [
+                pltpu.make_async_copy(fine_v, outs[0], sem.at[0]),
+                pltpu.make_async_copy(coarse_v, outs[1], sem.at[1]),
+            ]
+            for cp in copies:
+                cp.start()
+        else:
+            for q in range(slots):
+                buf = bufs[q]
+                for m in range(fine_each):
+                    buf[m] = fine_v[sf_ref[q * fine_each + m]]
+                for m in range(coarse_each):
+                    buf[fine_each + m] = coarse_v[sc_ref[q * coarse_each + m]]
+                if q == 0:
+                    buf[each:each + HALO] = x_ref[leaves - HALO:leaves]
+                elif q == 1:
+                    buf[each:each + HALO] = x_ref[0:HALO]
+                cp = pltpu.make_async_copy(buf, outs[q], sem.at[q])
+                cp.start()
+                copies.append(cp)
         for cp in copies:
             cp.wait()
 
     smem = pl.BlockSpec(memory_space=pltpu.SMEM)
-    vmem = pl.BlockSpec(memory_space=pltpu.VMEM)
     hbm = pl.BlockSpec(memory_space=pl.ANY)
     block = jax.ShapeDtypeStruct
-    outs = pl.pallas_call(
+    if packets:
+        out_shape = [block((n, RANK, RHS), jnp.bfloat16) for n in sizes]
+        bufs = [pltpu.VMEM((n, RANK, RHS), jnp.bfloat16) for n in sizes]
+    else:
+        out_shape = [block((leaves, RANK, RHS), jnp.bfloat16), block((parents, RANK, RHS), jnp.bfloat16)]
+        bufs = []
+    return pl.pallas_call(
         kernel,
-        in_specs=[smem, smem, vmem, vmem, vmem],
-        out_specs=[hbm] * (2 + slots),
-        out_shape=[block((leaves, RANK, RHS), jnp.bfloat16), block((parents, RANK, RHS), jnp.bfloat16)]
-        + [block((n, RANK, RHS), jnp.bfloat16) for n in sizes],
+        in_specs=[smem, smem, hbm, hbm, hbm],
+        out_specs=[hbm] * len(out_shape),
+        out_shape=out_shape,
         scratch_shapes=[
+            pltpu.VMEM(charges.shape, jnp.bfloat16),
+            pltpu.VMEM(basis_t.shape, jnp.bfloat16),
+            pltpu.VMEM(transfer_t.shape, jnp.bfloat16),
             pltpu.VMEM((leaves, RANK, RHS), jnp.bfloat16),
             pltpu.VMEM((parents, RANK, RHS), jnp.bfloat16),
         ]
-        + [pltpu.VMEM((n, RANK, RHS), jnp.bfloat16) for n in sizes]
-        + [pltpu.SemaphoreType.DMA((2 + slots,))],
+        + bufs
+        + [pltpu.SemaphoreType.DMA((3 * chunks,)), pltpu.SemaphoreType.DMA((len(out_shape),))],
         cost_estimate=pl.CostEstimate(
-            flops=2 * leaves * LEAF * RANK * RHS * 2, transcendentals=0, bytes_accessed=16 * 2 ** 20
+            flops=2 * leaves * LEAF * RANK * RHS * 2, transcendentals=0, bytes_accessed=8 * 2 ** 20
         ),
     )(send_fine, send_coarse, charges, basis_t, transfer_t)
-    return outs[0], outs[1], outs[2:]
 
 
 def coupled_product(coarse_part, fine_part, transfer, leaf_basis, near_field):
@@ -298,8 +325,11 @@
     axis = ("leaf", "couple")
     basis_t = leaf_basis.T
     transfer_t = transfer.T
-    fine_coeffs, coarse_coeffs, packets = upward(
-        charges, basis_t, transfer_t, send_fine[0], send_coarse[0], fine_each, coarse_each
+    packets = upward(
+        charges, basis_t, transfer_t, send_fine[0], send_coarse[0], fine_each, coarse_each, True
+    )
+    fine_coeffs, coarse_coeffs = upward(
+        charges, basis_t, transfer_t, send_fine[0], send_coarse[0], fine_each, coarse_each, False
     )
     incoming = []
     for slot, offset in enumerate(offset_list()):

time: 95.7 us -> 96.6 us (level)
  Pallas kernels: 26.6 us -> 32.1 us
  waiting for transfers between devices: 16.4 us -> 11.8 us
    pallas_call x1 -> x2, Pallas kernels: 5.16 us -> 10.7 us  [upward(): pl.pallas_call(kernel, in_specs=[smem, smem, hbm, hbm, hbm], out_specs=[h...]
    ppermute x6, waiting for transfers between devices: 16.4 us -> 11.8 us  [from_behind(): lax.ppermute(value, axis, [(source, source + steps) for source in range(f...]
  transfers between devices with their start and end apart: 6 -> 6, of which waited for: 2 -> 2; matrix products, arithmetic and copies ran while one was open for 5% -> 5% of each run, Pallas kernels for 8% -> 13%
where the time goes in v13:
time: 96.6 us; the launch traced here: 96 us
  starting transfers between devices  45.5 us (47%)
  Pallas kernels  32.1 us (33%)
  waiting for transfers between devices  11.8 us (12%)
  local copies, waits for them, and re-layouts  6.52 us (7%)
    ppermute x6, starting transfers between devices, from_behind(): lax.ppermute(value, axis, [(source, source + steps) for source in range(f...  45.5 us
    pallas_call x1, Pallas kernels, coupled_product(): pl.pallas_call(kernel, grid_spec=grid_spec, out_shape=jax.ShapeDtypeStruc...  13.4 us
    ppermute x6, waiting for transfers between devices, from_behind(): lax.ppermute(value, axis, [(source, source + steps) for source in range(f...  11.8 us
    pallas_call x2, Pallas kernels, upward(): pl.pallas_call(kernel, in_specs=[smem, smem, hbm, hbm, hbm], out_specs=[h...  10.7 us
    pallas_call x1, Pallas kernels, gather_dot(): pl.pallas_call(kernel, grid_spec=grid_spec, out_shape=jax.ShapeDtypeStruc...  8.06 us
    unnamed x10, local copies, waits for them, and re-layouts  6.52 us
  transfers between devices with their start and end apart: 6, of which 2 were waited for; matrix products, arithmetic and copies ran while one was open for 5% of the time, Pallas kernels for 13%

profile of v13, /device:TPU:24, one launch (start us, length us, event | category | flops | bytes accessed | tf_op | source)
XLA Modules:
  0.0 96.0 jit_solution(7191316698368263257)
XLA Ops:
  0.0 6.0 %shard_map.110 = (bf16[52,64,128]{2,1,0:T(8,128)(2,1)}, bf16[52,64,128]{2,1,0:T(8,128)(2,1)}, bf16[48,64,128]{2,1,0:T(8,128)(2,1)}, bf16[48,64,128]{2,1,0:T(8,12...) custom-call(s32[192]{0:T(256)} %bitcast.8, s32[96]{0:T(128)} %bitcast.10, ...), custom_call_target="tpu_custom_call" | custom-call | flops 134217728 | bytes 8388608 | tf_op jit(solution)/shard_map/pallas_call | solution.py:184
  6.0 1.9 %collective-permute-start = (bf16[52,64,128]{2,1,0:T(8,128)(2,1)}, bf16[52,64,128]{2,1,0:T(8,128)(2,1)S(1)}, u32[]{:S(2)}, u32[]{:S(2)}) collective-permute-start(bf16[52,64,128]{2,1,0:T(8,128)(2,1)} %get-tuple-element.14), channel_id=1, source_target_pairs={{0,1},{1,2},{2,3},{3,4},{4,5},{5,6},{6,7},{7,8},{8,9},{9,10},{10,1... | collective-permute-start | bytes 2555912 | tf_op jit(solution)/shard_map/ppermute | solution.py:21
  8.0 5.4 %collective-permute-start.1 = (bf16[52,64,128]{2,1,0:T(8,128)(2,1)}, bf16[52,64,128]{2,1,0:T(8,128)(2,1)S(1)}, u32[]{:S(2)}, u32[]{:S(2)}) collective-permute-start(bf16[52,64,128]{2,1,0:T(8,128)(2,1)} %get-tuple-element.15), channel_id=1, source_target_pairs={{1,0},{2,1},{3,2},{4,3},{5,4},{6,5},{7,6},{8,7},{9,8},{10,9},{11,1... | collective-permute-start | bytes 2555912 | tf_op jit(solution)/shard_map/ppermute | solution.py:21
  13.4 1.9 %collective-permute-start.2 = (bf16[48,64,128]{2,1,0:T(8,128)(2,1)}, bf16[48,64,128]{2,1,0:T(8,128)(2,1)S(1)}, u32[]{:S(2)}, u32[]{:S(2)}) collective-permute-start(bf16[48,64,128]{2,1,0:T(8,128)(2,1)} %get-tuple-element.16), channel_id=1, source_target_pairs={{0,2},{1,3},{2,4},{3,5},{4,6},{5,7},{6,8},{7,9},{8,10},{9,11},{10,... | collective-permute-start | bytes 2359304 | tf_op jit(solution)/shard_map/ppermute | solution.py:21
  15.3 5.7 %collective-permute-start.3 = (bf16[48,64,128]{2,1,0:T(8,128)(2,1)}, bf16[48,64,128]{2,1,0:T(8,128)(2,1)S(1)}, u32[]{:S(2)}, u32[]{:S(2)}) collective-permute-start(bf16[48,64,128]{2,1,0:T(8,128)(2,1)} %get-tuple-element.17), channel_id=1, source_target_pairs={{2,0},{3,1},{4,2},{5,3},{6,4},{7,5},{8,6},{9,7},{10,8},{11,9},{12,... | collective-permute-start | bytes 2359304 | tf_op jit(solution)/shard_map/ppermute | solution.py:21
  21.1 1.9 %collective-permute-start.4 = (bf16[48,64,128]{2,1,0:T(8,128)(2,1)}, bf16[48,64,128]{2,1,0:T(8,128)(2,1)}, u32[]{:S(2)}, u32[]{:S(2)}) collective-permute-start(bf16[48,64,128]{2,1,0:T(8,128)(2,1)} %get-tuple-element.18), channel_id=1, source_target_pairs={{0,3},{1,4},{2,5},{3,6},{4,7},{5,8},{6,9},{7,10},{8,11},{9,12},{10... | collective-permute-start | bytes 2359304 | tf_op jit(solution)/shard_map/ppermute | solution.py:21
  23.0 0.3 collective-permute-done.refs_0_.refs_1_.refs_8_
  23.3 0.0 copy-start
  23.3 28.6 %collective-permute-start.5 = (bf16[48,64,128]{2,1,0:T(8,128)(2,1)}, bf16[48,64,128]{2,1,0:T(8,128)(2,1)}, u32[]{:S(2)}, u32[]{:S(2)}) collective-permute-start(bf16[48,64,128]{2,1,0:T(8,128)(2,1)} %get-tuple-element.19), channel_id=1, source_target_pairs={{3,0},{4,1},{5,2},{6,3},{7,4},{8,5},{9,6},{10,7},{11,8},{12,9},{13... | collective-permute-start | bytes 2359304 | tf_op jit(solution)/shard_map/ppermute | solution.py:21
  51.9 2.4 %copy.13.refs_15_ = bf16[4096,64]{1,0:T(8,128)(2,1)} copy(bf16[4096,64]{0,1:T(8,128)(2,1)} %param.12) | data formatting | bytes 1048576 | tf_op args[1]
  54.2 2.4 %copy.12.refs_14_ = bf16[4096,64]{1,0:T(8,128)(2,1)} copy(bf16[4096,64]{0,1:T(8,128)(2,1)} %param.13) | data formatting | bytes 1048576 | tf_op args[2]
  56.6 4.6 %shard_map.109 = (bf16[64,64,128]{2,1,0:T(8,128)(2,1)}, bf16[32,64,128]{2,1,0:T(8,128)(2,1)}) custom-call(s32[192]{0:T(256)} %bitcast.9, s32[96]{0:T(128)} %bitcast.11, bf16[64,64,128]{2,1,0:T(8,128)(2,1)} %refs_1_.1, bf16[64,4096]{1,0:T(8,128)(2,1)} %bitcast.5, bf16[64,4096]{1,0:T(8,128)(2,1)} %bitcast.7), custom_call_target="tpu_custom_call" | custom-call | flops 134217728 | bytes 8388608 | tf_op jit(solution)/shard_map/pallas_call | solution.py:184
  61.2 0.0 collective-permute-done.1.refs_2_.refs_9_
  61.2 0.0 copy-done
  61.3 0.0 copy-start.1
  61.3 0.9 copy-done.1
  62.2 8.1 %shard_map.111.refs_16_ = f32[64,64,128]{2,1,0:T(8,128)} custom-call(s32[768]{0:T(1024)} %idx_ref.1, bf16[4096,768]{1,0:T(8,128)(2,1)} %mats_ref.1, bf16[52,64,128]{2,1,0:T(8,128)(2,1)} %copy-done, bf16[64,64,128]{2,1,0:T(8,128)(2,1)} %refs_1_.1, bf16[52,64,128]{2,1,0:T(8,128)(2,1)} %copy-done.1), custom_call_target="tpu_custom_call" | custom-call | flops 805306368 | bytes 9568256 | tf_op jit(solution)/shard_map/pallas_call | solution.py:101
  70.2 0.0 collective-permute-done.2.refs_3_.refs_10_
  70.2 0.0 copy-start.2
  70.2 11.5 %collective-permute-done.3.refs_4_.refs_11_ = bf16[48,64,128]{2,1,0:T(8,128)(2,1)S(1)} collective-permute-done((bf16[48,64,128]{2,1,0:T(8,128)(2,1)}, bf16[48,64,128]{2,1,0:T(8,128)(2,1)S(1)}, u32[]{:S(2)}, u32[]{:S(2)}) %collective-permute-start.3) | collective-permute-done | bytes 786464 | tf_op jit(solution)/shard_map/ppermute | solution.py:21
  81.7 0.0 copy-start.3
  81.7 0.0 collective-permute-done.4.refs_5_.refs_12_
  81.8 0.0 collective-permute-done.5.refs_6_.refs_13_
  81.8 0.0 copy-done.2
  81.8 0.9 copy-done.3
  82.6 13.4 %shard_map.112 = bf16[64,64,128]{2,1,0:T(8,128)(2,1)} custom-call(s32[512]{0:T(512)} %ci_ref.1, s32[1024]{0:T(1024)} %fi_ref.1, bf16[2048,1024]{1,0:T(8,128)(2,1)} %cm_hbm.1, bf16[4096,1024]{1,0:T(8,128)(2,1)} %fm_ref.1, bf16[32,64,128]{2,1,0:T(8,128)(2,1)} %get-tuple-element.13.refs_0_, bf16[52,64,128]{2,1,0:T(8,128)(2,1)} %copy-done, ...), custom_call_target="tpu_custom_call" | custom-call | flops 1610612736 | bytes 18874368 | tf_op jit(solution)/shard_map/pallas_call | solution.py:299
Async XLA Ops:
  6.0 17.2 %collective-permute-start = (bf16[52,64,128]{2,1,0:T(8,128)(2,1)}, bf16[52,64,128]{2,1,0:T(8,128)(2,1)S(1)}, u32[]{:S(2)}, u32[]{:S(2)}) collective-permute-start(bf16[52,64,128]{2,1,0:T(8,128)(2,1)} %get-tuple-element.14), channel_id=1, source_target_pairs={{0,1},{1,2},{2,3},{3,4},{4,5},{5,6},{6,7},{7,8},{8,9},{9,10},{10,1... | collective-permute-start | bytes 2555912 | tf_op jit(solution)/shard_map/ppermute | solution.py:21
  8.0 53.3 %collective-permute-start.1 = (bf16[52,64,128]{2,1,0:T(8,128)(2,1)}, bf16[52,64,128]{2,1,0:T(8,128)(2,1)S(1)}, u32[]{:S(2)}, u32[]{:S(2)}) collective-permute-start(bf16[52,64,128]{2,1,0:T(8,128)(2,1)} %get-tuple-element.15), channel_id=1, source_target_pairs={{1,0},{2,1},{3,2},{4,3},{5,4},{6,5},{7,6},{8,7},{9,8},{10,9},{11,1... | collective-permute-start | bytes 2555912 | tf_op jit(solution)/shard_map/ppermute | solution.py:21
  13.4 56.8 %collective-permute-start.2 = (bf16[48,64,128]{2,1,0:T(8,128)(2,1)}, bf16[48,64,128]{2,1,0:T(8,128)(2,1)S(1)}, u32[]{:S(2)}, u32[]{:S(2)}) collective-permute-start(bf16[48,64,128]{2,1,0:T(8,128)(2,1)} %get-tuple-element.16), channel_id=1, source_target_pairs={{0,2},{1,3},{2,4},{3,5},{4,6},{5,7},{6,8},{7,9},{8,10},{9,11},{10,... | collective-permute-start | bytes 2359304 | tf_op jit(solution)/shard_map/ppermute | solution.py:21
  15.3 66.4 %collective-permute-start.3 = (bf16[48,64,128]{2,1,0:T(8,128)(2,1)}, bf16[48,64,128]{2,1,0:T(8,128)(2,1)S(1)}, u32[]{:S(2)}, u32[]{:S(2)}) collective-permute-start(bf16[48,64,128]{2,1,0:T(8,128)(2,1)} %get-tuple-element.17), channel_id=1, source_target_pairs={{2,0},{3,1},{4,2},{5,3},{6,4},{7,5},{8,6},{9,7},{10,8},{11,9},{12,... | collective-permute-start | bytes 2359304 | tf_op jit(solution)/shard_map/ppermute | solution.py:21
  21.1 60.7 %collective-permute-start.4 = (bf16[48,64,128]{2,1,0:T(8,128)(2,1)}, bf16[48,64,128]{2,1,0:T(8,128)(2,1)}, u32[]{:S(2)}, u32[]{:S(2)}) collective-permute-start(bf16[48,64,128]{2,1,0:T(8,128)(2,1)} %get-tuple-element.18), channel_id=1, source_target_pairs={{0,3},{1,4},{2,5},{3,6},{4,7},{5,8},{6,9},{7,10},{8,11},{9,12},{10... | collective-permute-start | bytes 2359304 | tf_op jit(solution)/shard_map/ppermute | solution.py:21
  23.3 38.0 %copy-start = (bf16[52,64,128]{2,1,0:T(8,128)(2,1)}, bf16[52,64,128]{2,1,0:T(8,128)(2,1)S(1)}, u32[]{:S(2)}) copy-start(bf16[52,64,128]{2,1,0:T(8,128)(2,1)S(1)} %collective-permute-done.refs_0_.refs_1_.refs_8_) | copy-start | bytes 2555908
  23.3 58.5 %collective-permute-start.5 = (bf16[48,64,128]{2,1,0:T(8,128)(2,1)}, bf16[48,64,128]{2,1,0:T(8,128)(2,1)}, u32[]{:S(2)}, u32[]{:S(2)}) collective-permute-start(bf16[48,64,128]{2,1,0:T(8,128)(2,1)} %get-tuple-element.19), channel_id=1, source_target_pairs={{3,0},{4,1},{5,2},{6,3},{7,4},{8,5},{9,6},{10,7},{11,8},{12,9},{13... | collective-permute-start | bytes 2359304 | tf_op jit(solution)/shard_map/ppermute | solution.py:21
  61.3 0.9 copy-start.1
  70.2 11.5 %copy-start.2 = (bf16[48,64,128]{2,1,0:T(8,128)(2,1)}, bf16[48,64,128]{2,1,0:T(8,128)(2,1)S(1)}, u32[]{:S(2)}) copy-start(bf16[48,64,128]{2,1,0:T(8,128)(2,1)S(1)} %collective-permute-done.2.refs_3_.refs_10_) | copy-start | bytes 2359300
  81.7 0.9 copy-start.3

commit v14 on v13

--- a/solution.py
+++ b/solution.py
@@ -116,27 +116,13 @@
     chunks = 4 if parents % 4 == 0 else 1
     per = parents // chunks
 
-    def kernel(sf_ref, sc_ref, x_hbm, v_hbm, e_hbm, *rest):
+    def kernel(sf_ref, sc_ref, x_ref, v_ref, e_ref, *rest):
         n_out = slots if packets else 2
         outs = rest[:n_out]
-        x_ref, v_ref, e_ref, fine_v, coarse_v = rest[n_out:n_out + 5]
-        bufs = rest[n_out + 5:len(rest) - 2]
-        in_sem, sem = rest[len(rest) - 2:]
-        loads = []
+        fine_v, coarse_v = rest[n_out:n_out + 2]
+        bufs = rest[n_out + 2:len(rest) - 1]
+        sem = rest[len(rest) - 1]
         for c in range(chunks):
-            lo, cols = 2 * c * per, 2 * c * per * RANK
-            span = pl.ds(cols, 2 * per * RANK)
-            trio = [
-                pltpu.make_async_copy(x_hbm.at[pl.ds(lo, 2 * per)], x_ref.at[pl.ds(lo, 2 * per)], in_sem.at[3 * c]),
-                pltpu.make_async_copy(v_hbm.at[:, span], v_ref.at[:, span], in_sem.at[3 * c + 1]),
-                pltpu.make_async_copy(e_hbm.at[:, span], e_ref.at[:, span], in_sem.at[3 * c + 2]),
-            ]
-            for cp in trio:
-                cp.start()
-            loads.append(trio)
-        for c in range(chunks):
-            for cp in loads[c]:
-                cp.wait()
             for j in range(c * per, (c + 1) * per):
                 col = j * 2 * RANK
                 f0 = jnp.dot(v_ref[:, col:col + RANK], x_ref[2 * j], preferred_element_type=jnp.float32)
@@ -173,6 +159,7 @@
             cp.wait()
 
     smem = pl.BlockSpec(memory_space=pltpu.SMEM)
+    vmem = pl.BlockSpec(memory_space=pltpu.VMEM)
     hbm = pl.BlockSpec(memory_space=pl.ANY)
     block = jax.ShapeDtypeStruct
     if packets:
@@ -183,18 +170,15 @@
         bufs = []
     return pl.pallas_call(
         kernel,
-        in_specs=[smem, smem, hbm, hbm, hbm],
+        in_specs=[smem, smem, vmem, vmem, vmem],
         out_specs=[hbm] * len(out_shape),
         out_shape=out_shape,
         scratch_shapes=[
-            pltpu.VMEM(charges.shape, jnp.bfloat16),
-            pltpu.VMEM(basis_t.shape, jnp.bfloat16),
-            pltpu.VMEM(transfer_t.shape, jnp.bfloat16),
             pltpu.VMEM((leaves, RANK, RHS), jnp.bfloat16),
             pltpu.VMEM((parents, RANK, RHS), jnp.bfloat16),
         ]
         + bufs
-        + [pltpu.SemaphoreType.DMA((3 * chunks,)), pltpu.SemaphoreType.DMA((len(out_shape),))],
+        + [pltpu.SemaphoreType.DMA((len(out_shape),))],
         cost_estimate=pl.CostEstimate(
             flops=2 * leaves * LEAF * RANK * RHS * 2, transcendentals=0, bytes_accessed=8 * 2 ** 20
         ),

time: 96.6 us -> 95.3 us (0.987)
  Pallas kernels: 32.1 us -> 29.6 us
  waiting for transfers between devices: 11.8 us -> 13 us
    pallas_call x2, Pallas kernels: 10.7 us -> 8.2 us  [upward(): pl.pallas_call(kernel, in_specs=[smem, smem, vmem, vmem, vmem], out_specs...]
    ppermute x6, waiting for transfers between devices: 11.8 us -> 13 us  [from_behind(): lax.ppermute(value, axis, [(source, source + steps) for source in range(f...]
  transfers between devices with their start and end apart: 6 -> 6, of which waited for: 2 -> 2; matrix products, arithmetic and copies ran while one was open for 5% -> 5% of each run, Pallas kernels for 13% -> 12%
where the time goes in v14:
time: 95.3 us; the launch traced here: 94.8 us
  starting transfers between devices  45.5 us (48%)
  Pallas kernels  29.6 us (31%)
  waiting for transfers between devices  13 us (14%)
  local copies, waits for them, and re-layouts  6.52 us (7%)
    ppermute x6, starting transfers between devices, from_behind(): lax.ppermute(value, axis, [(source, source + steps) for source in range(f...  45.5 us
    pallas_call x1, Pallas kernels, coupled_product(): pl.pallas_call(kernel, grid_spec=grid_spec, out_shape=jax.ShapeDtypeStruc...  13.3 us
    ppermute x6, waiting for transfers between devices, from_behind(): lax.ppermute(value, axis, [(source, source + steps) for source in range(f...  13 us
    pallas_call x2, Pallas kernels, upward(): pl.pallas_call(kernel, in_specs=[smem, smem, vmem, vmem, vmem], out_specs...  8.2 us
    pallas_call x1, Pallas kernels, gather_dot(): pl.pallas_call(kernel, grid_spec=grid_spec, out_shape=jax.ShapeDtypeStruc...  8.05 us
    unnamed x10, local copies, waits for them, and re-layouts  6.52 us
  transfers between devices with their start and end apart: 6, of which 2 were waited for; matrix products, arithmetic and copies ran while one was open for 5% of the time, Pallas kernels for 12%

profile of v14, /device:TPU:24, one launch (start us, length us, event | category | flops | bytes accessed | tf_op | source)
XLA Modules:
  0.0 94.8 jit_solution(16005553867015738537)
XLA Ops:
  0.0 4.8 %shard_map.110 = (bf16[52,64,128]{2,1,0:T(8,128)(2,1)}, bf16[52,64,128]{2,1,0:T(8,128)(2,1)}, bf16[48,64,128]{2,1,0:T(8,128)(2,1)}, bf16[48,64,128]{2,1,0:T(8,12...) custom-call(s32[192]{0:T(256)} %bitcast.8, s32[96]{0:T(128)} %bitcast.10, ...), custom_call_target="tpu_custom_call" | custom-call | flops 134217728 | bytes 8388608 | tf_op jit(solution)/shard_map/pallas_call | solution.py:171
  4.8 1.9 %collective-permute-start = (bf16[52,64,128]{2,1,0:T(8,128)(2,1)}, bf16[52,64,128]{2,1,0:T(8,128)(2,1)S(1)}, u32[]{:S(2)}, u32[]{:S(2)}) collective-permute-start(bf16[52,64,128]{2,1,0:T(8,128)(2,1)} %get-tuple-element.14), channel_id=1, source_target_pairs={{0,1},{1,2},{2,3},{3,4},{4,5},{5,6},{6,7},{7,8},{8,9},{9,10},{10,1... | collective-permute-start | bytes 2555912 | tf_op jit(solution)/shard_map/ppermute | solution.py:21
  6.7 5.4 %collective-permute-start.1 = (bf16[52,64,128]{2,1,0:T(8,128)(2,1)}, bf16[52,64,128]{2,1,0:T(8,128)(2,1)S(1)}, u32[]{:S(2)}, u32[]{:S(2)}) collective-permute-start(bf16[52,64,128]{2,1,0:T(8,128)(2,1)} %get-tuple-element.15), channel_id=1, source_target_pairs={{1,0},{2,1},{3,2},{4,3},{5,4},{6,5},{7,6},{8,7},{9,8},{10,9},{11,1... | collective-permute-start | bytes 2555912 | tf_op jit(solution)/shard_map/ppermute | solution.py:21
  12.2 1.9 %collective-permute-start.2 = (bf16[48,64,128]{2,1,0:T(8,128)(2,1)}, bf16[48,64,128]{2,1,0:T(8,128)(2,1)S(1)}, u32[]{:S(2)}, u32[]{:S(2)}) collective-permute-start(bf16[48,64,128]{2,1,0:T(8,128)(2,1)} %get-tuple-element.16), channel_id=1, source_target_pairs={{0,2},{1,3},{2,4},{3,5},{4,6},{5,7},{6,8},{7,9},{8,10},{9,11},{10,... | collective-permute-start | bytes 2359304 | tf_op jit(solution)/shard_map/ppermute | solution.py:21
  14.1 5.7 %collective-permute-start.3 = (bf16[48,64,128]{2,1,0:T(8,128)(2,1)}, bf16[48,64,128]{2,1,0:T(8,128)(2,1)S(1)}, u32[]{:S(2)}, u32[]{:S(2)}) collective-permute-start(bf16[48,64,128]{2,1,0:T(8,128)(2,1)} %get-tuple-element.17), channel_id=1, source_target_pairs={{2,0},{3,1},{4,2},{5,3},{6,4},{7,5},{8,6},{9,7},{10,8},{11,9},{12,... | collective-permute-start | bytes 2359304 | tf_op jit(solution)/shard_map/ppermute | solution.py:21
  19.8 1.9 %collective-permute-start.4 = (bf16[48,64,128]{2,1,0:T(8,128)(2,1)}, bf16[48,64,128]{2,1,0:T(8,128)(2,1)}, u32[]{:S(2)}, u32[]{:S(2)}) collective-permute-start(bf16[48,64,128]{2,1,0:T(8,128)(2,1)} %get-tuple-element.18), channel_id=1, source_target_pairs={{0,3},{1,4},{2,5},{3,6},{4,7},{5,8},{6,9},{7,10},{8,11},{9,12},{10... | collective-permute-start | bytes 2359304 | tf_op jit(solution)/shard_map/ppermute | solution.py:21
  21.8 0.3 collective-permute-done.refs_0_.refs_1_.refs_8_
  22.0 0.0 copy-start
  22.0 28.6 %collective-permute-start.5 = (bf16[48,64,128]{2,1,0:T(8,128)(2,1)}, bf16[48,64,128]{2,1,0:T(8,128)(2,1)}, u32[]{:S(2)}, u32[]{:S(2)}) collective-permute-start(bf16[48,64,128]{2,1,0:T(8,128)(2,1)} %get-tuple-element.19), channel_id=1, source_target_pairs={{3,0},{4,1},{5,2},{6,3},{7,4},{8,5},{9,6},{10,7},{11,8},{12,9},{13... | collective-permute-start | bytes 2359304 | tf_op jit(solution)/shard_map/ppermute | solution.py:21
  50.6 2.4 %copy.13.refs_15_ = bf16[4096,64]{1,0:T(8,128)(2,1)} copy(bf16[4096,64]{0,1:T(8,128)(2,1)} %param.12) | data formatting | bytes 1048576 | tf_op args[1]
  53.0 2.4 %copy.12.refs_14_ = bf16[4096,64]{1,0:T(8,128)(2,1)} copy(bf16[4096,64]{0,1:T(8,128)(2,1)} %param.13) | data formatting | bytes 1048576 | tf_op args[2]
  55.4 3.4 %shard_map.109 = (bf16[64,64,128]{2,1,0:T(8,128)(2,1)}, bf16[32,64,128]{2,1,0:T(8,128)(2,1)}) custom-call(s32[192]{0:T(256)} %bitcast.9, s32[96]{0:T(128)} %bitcast.11, bf16[64,64,128]{2,1,0:T(8,128)(2,1)} %refs_1_.1, bf16[64,4096]{1,0:T(8,128)(2,1)} %bitcast.5, bf16[64,4096]{1,0:T(8,128)(2,1)} %bitcast.7), custom_call_target="tpu_custom_call" | custom-call | flops 134217728 | bytes 8388608 | tf_op jit(solution)/shard_map/pallas_call | solution.py:171
  58.8 0.0 collective-permute-done.1.refs_2_.refs_9_
  58.8 0.0 copy-done
  58.8 0.0 copy-start.1
  58.8 0.9 copy-done.1
  59.7 8.0 %shard_map.111.refs_16_ = f32[64,64,128]{2,1,0:T(8,128)} custom-call(s32[768]{0:T(1024)} %idx_ref.1, bf16[4096,768]{1,0:T(8,128)(2,1)} %mats_ref.1, bf16[52,64,128]{2,1,0:T(8,128)(2,1)} %copy-done, bf16[64,64,128]{2,1,0:T(8,128)(2,1)} %refs_1_.1, bf16[52,64,128]{2,1,0:T(8,128)(2,1)} %copy-done.1), custom_call_target="tpu_custom_call" | custom-call | flops 805306368 | bytes 9568256 | tf_op jit(solution)/shard_map/pallas_call | solution.py:101
  67.7 0.0 collective-permute-done.2.refs_3_.refs_10_
  67.8 0.0 copy-start.2
  67.8 12.7 %collective-permute-done.3.refs_4_.refs_11_ = bf16[48,64,128]{2,1,0:T(8,128)(2,1)S(1)} collective-permute-done((bf16[48,64,128]{2,1,0:T(8,128)(2,1)}, bf16[48,64,128]{2,1,0:T(8,128)(2,1)S(1)}, u32[]{:S(2)}, u32[]{:S(2)}) %collective-permute-start.3) | collective-permute-done | bytes 786464 | tf_op jit(solution)/shard_map/ppermute | solution.py:21
  80.5 0.0 copy-start.3
  80.5 0.0 collective-permute-done.4.refs_5_.refs_12_
  80.5 0.0 collective-permute-done.5.refs_6_.refs_13_
  80.5 0.0 copy-done.2
  80.5 0.9 copy-done.3
  81.4 13.3 %shard_map.112 = bf16[64,64,128]{2,1,0:T(8,128)(2,1)} custom-call(s32[512]{0:T(512)} %ci_ref.1, s32[1024]{0:T(1024)} %fi_ref.1, bf16[2048,1024]{1,0:T(8,128)(2,1)} %cm_hbm.1, bf16[4096,1024]{1,0:T(8,128)(2,1)} %fm_ref.1, bf16[32,64,128]{2,1,0:T(8,128)(2,1)} %get-tuple-element.13.refs_0_, bf16[52,64,128]{2,1,0:T(8,128)(2,1)} %copy-done, ...), custom_call_target="tpu_custom_call" | custom-call | flops 1610612736 | bytes 18874368 | tf_op jit(solution)/shard_map/pallas_call | solution.py:283
Async XLA Ops:
  4.8 17.2 %collective-permute-start = (bf16[52,64,128]{2,1,0:T(8,128)(2,1)}, bf16[52,64,128]{2,1,0:T(8,128)(2,1)S(1)}, u32[]{:S(2)}, u32[]{:S(2)}) collective-permute-start(bf16[52,64,128]{2,1,0:T(8,128)(2,1)} %get-tuple-element.14), channel_id=1, source_target_pairs={{0,1},{1,2},{2,3},{3,4},{4,5},{5,6},{6,7},{7,8},{8,9},{9,10},{10,1... | collective-permute-start | bytes 2555912 | tf_op jit(solution)/shard_map/ppermute | solution.py:21
  6.7 52.0 %collective-permute-start.1 = (bf16[52,64,128]{2,1,0:T(8,128)(2,1)}, bf16[52,64,128]{2,1,0:T(8,128)(2,1)S(1)}, u32[]{:S(2)}, u32[]{:S(2)}) collective-permute-start(bf16[52,64,128]{2,1,0:T(8,128)(2,1)} %get-tuple-element.15), channel_id=1, source_target_pairs={{1,0},{2,1},{3,2},{4,3},{5,4},{6,5},{7,6},{8,7},{9,8},{10,9},{11,1... | collective-permute-start | bytes 2555912 | tf_op jit(solution)/shard_map/ppermute | solution.py:21
  12.2 55.6 %collective-permute-start.2 = (bf16[48,64,128]{2,1,0:T(8,128)(2,1)}, bf16[48,64,128]{2,1,0:T(8,128)(2,1)S(1)}, u32[]{:S(2)}, u32[]{:S(2)}) collective-permute-start(bf16[48,64,128]{2,1,0:T(8,128)(2,1)} %get-tuple-element.16), channel_id=1, source_target_pairs={{0,2},{1,3},{2,4},{3,5},{4,6},{5,7},{6,8},{7,9},{8,10},{9,11},{10,... | collective-permute-start | bytes 2359304 | tf_op jit(solution)/shard_map/ppermute | solution.py:21
  14.1 66.4 %collective-permute-start.3 = (bf16[48,64,128]{2,1,0:T(8,128)(2,1)}, bf16[48,64,128]{2,1,0:T(8,128)(2,1)S(1)}, u32[]{:S(2)}, u32[]{:S(2)}) collective-permute-start(bf16[48,64,128]{2,1,0:T(8,128)(2,1)} %get-tuple-element.17), channel_id=1, source_target_pairs={{2,0},{3,1},{4,2},{5,3},{6,4},{7,5},{8,6},{9,7},{10,8},{11,9},{12,... | collective-permute-start | bytes 2359304 | tf_op jit(solution)/shard_map/ppermute | solution.py:21
  19.8 60.7 %collective-permute-start.4 = (bf16[48,64,128]{2,1,0:T(8,128)(2,1)}, bf16[48,64,128]{2,1,0:T(8,128)(2,1)}, u32[]{:S(2)}, u32[]{:S(2)}) collective-permute-start(bf16[48,64,128]{2,1,0:T(8,128)(2,1)} %get-tuple-element.18), channel_id=1, source_target_pairs={{0,3},{1,4},{2,5},{3,6},{4,7},{5,8},{6,9},{7,10},{8,11},{9,12},{10... | collective-permute-start | bytes 2359304 | tf_op jit(solution)/shard_map/ppermute | solution.py:21
  22.0 36.8 %copy-start = (bf16[52,64,128]{2,1,0:T(8,128)(2,1)}, bf16[52,64,128]{2,1,0:T(8,128)(2,1)S(1)}, u32[]{:S(2)}) copy-start(bf16[52,64,128]{2,1,0:T(8,128)(2,1)S(1)} %collective-permute-done.refs_0_.refs_1_.refs_8_) | copy-start | bytes 2555908
  22.0 58.5 %collective-permute-start.5 = (bf16[48,64,128]{2,1,0:T(8,128)(2,1)}, bf16[48,64,128]{2,1,0:T(8,128)(2,1)}, u32[]{:S(2)}, u32[]{:S(2)}) collective-permute-start(bf16[48,64,128]{2,1,0:T(8,128)(2,1)} %get-tuple-element.19), channel_id=1, source_target_pairs={{3,0},{4,1},{5,2},{6,3},{7,4},{8,5},{9,6},{10,7},{11,8},{12,9},{13... | collective-permute-start | bytes 2359304 | tf_op jit(solution)/shard_map/ppermute | solution.py:21
  58.8 0.9 copy-start.1
  67.8 12.8 %copy-start.2 = (bf16[48,64,128]{2,1,0:T(8,128)(2,1)}, bf16[48,64,128]{2,1,0:T(8,128)(2,1)S(1)}, u32[]{:S(2)}) copy-start(bf16[48,64,128]{2,1,0:T(8,128)(2,1)S(1)} %collective-permute-done.2.refs_3_.refs_10_) | copy-start | bytes 2359300
  80.5 0.9 copy-start.3

commit v15 on v14

--- a/solution.py
+++ b/solution.py
@@ -12,7 +12,7 @@
 RHS = 128
 HALO = 4
 REACH = 3
-BLOCK_TARGETS = 16
+BLOCK_TARGETS = 32
 
 
 def from_behind(value, axis, steps):

time: 95.3 us -> 95.4 us (level)
  transfers between devices with their start and end apart: 6 -> 6, of which waited for: 2 -> 2; matrix products, arithmetic and copies ran while one was open for 5% -> 5% of each run, Pallas kernels for 12% -> 11%
where the time goes in v15:
time: 95.4 us; the launch traced here: 94.9 us
  starting transfers between devices  45.5 us (48%)
  Pallas kernels  29.1 us (31%)
  waiting for transfers between devices  13.6 us (14%)
  local copies, waits for them, and re-layouts  6.52 us (7%)
    ppermute x6, starting transfers between devices, from_behind(): lax.ppermute(value, axis, [(source, source + steps) for source in range(f...  45.5 us
    ppermute x6, waiting for transfers between devices, from_behind(): lax.ppermute(value, axis, [(source, source + steps) for source in range(f...  13.6 us
    pallas_call x1, Pallas kernels, coupled_product(): pl.pallas_call(kernel, grid_spec=grid_spec, out_shape=jax.ShapeDtypeStruc...  13.5 us
    pallas_call x2, Pallas kernels, upward(): pl.pallas_call(kernel, in_specs=[smem, smem, vmem, vmem, vmem], out_specs...  8.2 us
    pallas_call x1, Pallas kernels, gather_dot(): pl.pallas_call(kernel, grid_spec=grid_spec, out_shape=jax.ShapeDtypeStruc...  7.44 us
    unnamed x10, local copies, waits for them, and re-layouts  6.52 us
  transfers between devices with their start and end apart: 6, of which 2 were waited for; matrix products, arithmetic and copies ran while one was open for 5% of the time, Pallas kernels for 11%

profile of v15, /device:TPU:24, one launch (start us, length us, event | category | flops | bytes accessed | tf_op | source)
XLA Modules:
  0.0 94.9 jit_solution(11604173740250162656)
XLA Ops:
  0.0 4.8 %shard_map.110 = (bf16[52,64,128]{2,1,0:T(8,128)(2,1)}, bf16[52,64,128]{2,1,0:T(8,128)(2,1)}, bf16[48,64,128]{2,1,0:T(8,128)(2,1)}, bf16[48,64,128]{2,1,0:T(8,12...) custom-call(s32[192]{0:T(256)} %bitcast.8, s32[96]{0:T(128)} %bitcast.10, ...), custom_call_target="tpu_custom_call" | custom-call | flops 134217728 | bytes 8388608 | tf_op jit(solution)/shard_map/pallas_call | solution.py:171
  4.8 1.9 %collective-permute-start = (bf16[52,64,128]{2,1,0:T(8,128)(2,1)}, bf16[52,64,128]{2,1,0:T(8,128)(2,1)S(1)}, u32[]{:S(2)}, u32[]{:S(2)}) collective-permute-start(bf16[52,64,128]{2,1,0:T(8,128)(2,1)} %get-tuple-element.14), channel_id=1, source_target_pairs={{0,1},{1,2},{2,3},{3,4},{4,5},{5,6},{6,7},{7,8},{8,9},{9,10},{10,1... | collective-permute-start | bytes 2555912 | tf_op jit(solution)/shard_map/ppermute | solution.py:21
  6.7 5.4 %collective-permute-start.1 = (bf16[52,64,128]{2,1,0:T(8,128)(2,1)}, bf16[52,64,128]{2,1,0:T(8,128)(2,1)S(1)}, u32[]{:S(2)}, u32[]{:S(2)}) collective-permute-start(bf16[52,64,128]{2,1,0:T(8,128)(2,1)} %get-tuple-element.15), channel_id=1, source_target_pairs={{1,0},{2,1},{3,2},{4,3},{5,4},{6,5},{7,6},{8,7},{9,8},{10,9},{11,1... | collective-permute-start | bytes 2555912 | tf_op jit(solution)/shard_map/ppermute | solution.py:21
  12.2 1.9 %collective-permute-start.2 = (bf16[48,64,128]{2,1,0:T(8,128)(2,1)}, bf16[48,64,128]{2,1,0:T(8,128)(2,1)S(1)}, u32[]{:S(2)}, u32[]{:S(2)}) collective-permute-start(bf16[48,64,128]{2,1,0:T(8,128)(2,1)} %get-tuple-element.16), channel_id=1, source_target_pairs={{0,2},{1,3},{2,4},{3,5},{4,6},{5,7},{6,8},{7,9},{8,10},{9,11},{10,... | collective-permute-start | bytes 2359304 | tf_op jit(solution)/shard_map/ppermute | solution.py:21
  14.1 5.7 %collective-permute-start.3 = (bf16[48,64,128]{2,1,0:T(8,128)(2,1)}, bf16[48,64,128]{2,1,0:T(8,128)(2,1)S(1)}, u32[]{:S(2)}, u32[]{:S(2)}) collective-permute-start(bf16[48,64,128]{2,1,0:T(8,128)(2,1)} %get-tuple-element.17), channel_id=1, source_target_pairs={{2,0},{3,1},{4,2},{5,3},{6,4},{7,5},{8,6},{9,7},{10,8},{11,9},{12,... | collective-permute-start | bytes 2359304 | tf_op jit(solution)/shard_map/ppermute | solution.py:21
  19.8 1.9 %collective-permute-start.4 = (bf16[48,64,128]{2,1,0:T(8,128)(2,1)}, bf16[48,64,128]{2,1,0:T(8,128)(2,1)}, u32[]{:S(2)}, u32[]{:S(2)}) collective-permute-start(bf16[48,64,128]{2,1,0:T(8,128)(2,1)} %get-tuple-element.18), channel_id=1, source_target_pairs={{0,3},{1,4},{2,5},{3,6},{4,7},{5,8},{6,9},{7,10},{8,11},{9,12},{10... | collective-permute-start | bytes 2359304 | tf_op jit(solution)/shard_map/ppermute | solution.py:21
  21.8 0.3 collective-permute-done.refs_0_.refs_1_.refs_8_
  22.0 0.0 copy-start
  22.0 28.6 %collective-permute-start.5 = (bf16[48,64,128]{2,1,0:T(8,128)(2,1)}, bf16[48,64,128]{2,1,0:T(8,128)(2,1)}, u32[]{:S(2)}, u32[]{:S(2)}) collective-permute-start(bf16[48,64,128]{2,1,0:T(8,128)(2,1)} %get-tuple-element.19), channel_id=1, source_target_pairs={{3,0},{4,1},{5,2},{6,3},{7,4},{8,5},{9,6},{10,7},{11,8},{12,9},{13... | collective-permute-start | bytes 2359304 | tf_op jit(solution)/shard_map/ppermute | solution.py:21
  50.6 2.4 %copy.13.refs_15_ = bf16[4096,64]{1,0:T(8,128)(2,1)} copy(bf16[4096,64]{0,1:T(8,128)(2,1)} %param.12) | data formatting | bytes 1048576 | tf_op args[1]
  53.0 2.4 %copy.12.refs_14_ = bf16[4096,64]{1,0:T(8,128)(2,1)} copy(bf16[4096,64]{0,1:T(8,128)(2,1)} %param.13) | data formatting | bytes 1048576 | tf_op args[2]
  55.4 3.4 %shard_map.109 = (bf16[64,64,128]{2,1,0:T(8,128)(2,1)}, bf16[32,64,128]{2,1,0:T(8,128)(2,1)}) custom-call(s32[192]{0:T(256)} %bitcast.9, s32[96]{0:T(128)} %bitcast.11, bf16[64,64,128]{2,1,0:T(8,128)(2,1)} %refs_1_.1, bf16[64,4096]{1,0:T(8,128)(2,1)} %bitcast.5, bf16[64,4096]{1,0:T(8,128)(2,1)} %bitcast.7), custom_call_target="tpu_custom_call" | custom-call | flops 134217728 | bytes 8388608 | tf_op jit(solution)/shard_map/pallas_call | solution.py:171
  58.8 0.0 collective-permute-done.1.refs_2_.refs_9_
  58.8 0.0 copy-done
  58.8 0.0 copy-start.1
  58.8 0.9 copy-done.1
  59.7 7.4 %shard_map.111.refs_16_ = f32[64,64,128]{2,1,0:T(8,128)} custom-call(s32[768]{0:T(1024)} %idx_ref.1, bf16[4096,768]{1,0:T(8,128)(2,1)} %mats_ref.1, bf16[52,64,128]{2,1,0:T(8,128)(2,1)} %copy-done, bf16[64,64,128]{2,1,0:T(8,128)(2,1)} %refs_1_.1, bf16[52,64,128]{2,1,0:T(8,128)(2,1)} %copy-done.1), custom_call_target="tpu_custom_call" | custom-call | flops 805306368 | bytes 9568256 | tf_op jit(solution)/shard_map/pallas_call | solution.py:101
  67.1 0.0 collective-permute-done.2.refs_3_.refs_10_
  67.2 0.0 copy-start.2
  67.2 13.3 %collective-permute-done.3.refs_4_.refs_11_ = bf16[48,64,128]{2,1,0:T(8,128)(2,1)S(1)} collective-permute-done((bf16[48,64,128]{2,1,0:T(8,128)(2,1)}, bf16[48,64,128]{2,1,0:T(8,128)(2,1)S(1)}, u32[]{:S(2)}, u32[]{:S(2)}) %collective-permute-start.3) | collective-permute-done | bytes 786464 | tf_op jit(solution)/shard_map/ppermute | solution.py:21
  80.5 0.0 copy-start.3
  80.5 0.0 collective-permute-done.4.refs_5_.refs_12_
  80.5 0.0 collective-permute-done.5.refs_6_.refs_13_
  80.5 0.0 copy-done.2
  80.5 0.9 copy-done.3
  81.4 13.5 %shard_map.112 = bf16[64,64,128]{2,1,0:T(8,128)(2,1)} custom-call(s32[512]{0:T(512)} %ci_ref.1, s32[1024]{0:T(1024)} %fi_ref.1, bf16[2048,1024]{1,0:T(8,128)(2,1)} %cm_hbm.1, bf16[4096,1024]{1,0:T(8,128)(2,1)} %fm_ref.1, bf16[32,64,128]{2,1,0:T(8,128)(2,1)} %get-tuple-element.13.refs_0_, bf16[52,64,128]{2,1,0:T(8,128)(2,1)} %copy-done, ...), custom_call_target="tpu_custom_call" | custom-call | flops 1610612736 | bytes 18874368 | tf_op jit(solution)/shard_map/pallas_call | solution.py:283
Async XLA Ops:
  4.8 17.2 %collective-permute-start = (bf16[52,64,128]{2,1,0:T(8,128)(2,1)}, bf16[52,64,128]{2,1,0:T(8,128)(2,1)S(1)}, u32[]{:S(2)}, u32[]{:S(2)}) collective-permute-start(bf16[52,64,128]{2,1,0:T(8,128)(2,1)} %get-tuple-element.14), channel_id=1, source_target_pairs={{0,1},{1,2},{2,3},{3,4},{4,5},{5,6},{6,7},{7,8},{8,9},{9,10},{10,1... | collective-permute-start | bytes 2555912 | tf_op jit(solution)/shard_map/ppermute | solution.py:21
  6.7 52.0 %collective-permute-start.1 = (bf16[52,64,128]{2,1,0:T(8,128)(2,1)}, bf16[52,64,128]{2,1,0:T(8,128)(2,1)S(1)}, u32[]{:S(2)}, u32[]{:S(2)}) collective-permute-start(bf16[52,64,128]{2,1,0:T(8,128)(2,1)} %get-tuple-element.15), channel_id=1, source_target_pairs={{1,0},{2,1},{3,2},{4,3},{5,4},{6,5},{7,6},{8,7},{9,8},{10,9},{11,1... | collective-permute-start | bytes 2555912 | tf_op jit(solution)/shard_map/ppermute | solution.py:21
  12.2 55.0 %collective-permute-start.2 = (bf16[48,64,128]{2,1,0:T(8,128)(2,1)}, bf16[48,64,128]{2,1,0:T(8,128)(2,1)S(1)}, u32[]{:S(2)}, u32[]{:S(2)}) collective-permute-start(bf16[48,64,128]{2,1,0:T(8,128)(2,1)} %get-tuple-element.16), channel_id=1, source_target_pairs={{0,2},{1,3},{2,4},{3,5},{4,6},{5,7},{6,8},{7,9},{8,10},{9,11},{10,... | collective-permute-start | bytes 2359304 | tf_op jit(solution)/shard_map/ppermute | solution.py:21
  14.1 66.4 %collective-permute-start.3 = (bf16[48,64,128]{2,1,0:T(8,128)(2,1)}, bf16[48,64,128]{2,1,0:T(8,128)(2,1)S(1)}, u32[]{:S(2)}, u32[]{:S(2)}) collective-permute-start(bf16[48,64,128]{2,1,0:T(8,128)(2,1)} %get-tuple-element.17), channel_id=1, source_target_pairs={{2,0},{3,1},{4,2},{5,3},{6,4},{7,5},{8,6},{9,7},{10,8},{11,9},{12,... | collective-permute-start | bytes 2359304 | tf_op jit(solution)/shard_map/ppermute | solution.py:21
  19.8 60.7 %collective-permute-start.4 = (bf16[48,64,128]{2,1,0:T(8,128)(2,1)}, bf16[48,64,128]{2,1,0:T(8,128)(2,1)}, u32[]{:S(2)}, u32[]{:S(2)}) collective-permute-start(bf16[48,64,128]{2,1,0:T(8,128)(2,1)} %get-tuple-element.18), channel_id=1, source_target_pairs={{0,3},{1,4},{2,5},{3,6},{4,7},{5,8},{6,9},{7,10},{8,11},{9,12},{10... | collective-permute-start | bytes 2359304 | tf_op jit(solution)/shard_map/ppermute | solution.py:21
  22.0 36.8 %copy-start = (bf16[52,64,128]{2,1,0:T(8,128)(2,1)}, bf16[52,64,128]{2,1,0:T(8,128)(2,1)S(1)}, u32[]{:S(2)}) copy-start(bf16[52,64,128]{2,1,0:T(8,128)(2,1)S(1)} %collective-permute-done.refs_0_.refs_1_.refs_8_) | copy-start | bytes 2555908
  22.0 58.5 %collective-permute-start.5 = (bf16[48,64,128]{2,1,0:T(8,128)(2,1)}, bf16[48,64,128]{2,1,0:T(8,128)(2,1)}, u32[]{:S(2)}, u32[]{:S(2)}) collective-permute-start(bf16[48,64,128]{2,1,0:T(8,128)(2,1)} %get-tuple-element.19), channel_id=1, source_target_pairs={{3,0},{4,1},{5,2},{6,3},{7,4},{8,5},{9,6},{10,7},{11,8},{12,9},{13... | collective-permute-start | bytes 2359304 | tf_op jit(solution)/shard_map/ppermute | solution.py:21
  58.8 0.9 copy-start.1
  67.2 13.4 %copy-start.2 = (bf16[48,64,128]{2,1,0:T(8,128)(2,1)}, bf16[48,64,128]{2,1,0:T(8,128)(2,1)S(1)}, u32[]{:S(2)}) copy-start(bf16[48,64,128]{2,1,0:T(8,128)(2,1)S(1)} %collective-permute-done.2.refs_3_.refs_10_) | copy-start | bytes 2359300
  80.5 0.9 copy-start.3

commit v16 on v14

--- a/solution.py
+++ b/solution.py
@@ -202,7 +202,7 @@
     n_seg = len(segs)
 
     hbm = pl.BlockSpec(memory_space=pl.ANY)
-    in_specs = [hbm] + [pl.BlockSpec((tb * LEAF, f_pairs * width), lambda i, a, b: (i, 0))]
+    in_specs = [hbm, hbm]
     in_specs += [hbm] * n_seg
     in_specs += [
         pl.BlockSpec((tb * RANK, RANK), lambda i, a, b: (i, 0)),
@@ -214,11 +214,15 @@
         blocks = [pool_ref[idx_ref[base + k]] for k in range(pairs)]
         return jnp.dot(mats, jnp.concatenate(blocks, axis=0), preferred_element_type=jnp.float32)
 
-    def kernel(ci_ref, fi_ref, cm_hbm, fm_ref, *refs):
+    def kernel(ci_ref, fi_ref, cm_hbm, fm_hbm, *refs):
         seg_refs = refs[:n_seg]
         e_ref, v_ref, near_ref, out_ref = refs[n_seg:n_seg + 4]
-        c_pool, f_pool, c_mats_v, cr_ref, acc_ref, sem = refs[n_seg + 4:]
+        c_pool, f_pool, c_mats_v, cr_ref, acc_ref, sem, fm_v, fm_sem = refs[n_seg + 4:]
         blk = pl.program_id(0)
+        rows = tb * LEAF
+
+        def fine_block(step, slot):
+            return pltpu.make_async_copy(fm_hbm.at[pl.ds(step * rows, rows)], fm_v.at[slot], fm_sem.at[slot])
 
         @pl.when(blk == 0)
         def _():
@@ -245,12 +249,21 @@
                 if h == 0:
                     for cp in seg_copies[n_c:]:
                         cp.start()
+                    fine_block(0, 0).start()
                 for p in range(h * per_half, (h + 1) * per_half):
                     acc = gather_sum(ci_ref, c_pool, c_mats_v[p * RANK:(p + 1) * RANK, :], p * c_pairs, c_pairs)
                     cr_ref[p] = acc.astype(jnp.bfloat16)
             for cp in seg_copies[n_c:]:
                 cp.wait()
 
+        slot = blk % 2
+        fine_block(blk, slot).wait()
+
+        @pl.when(blk + 1 < steps)
+        def _():
+            fine_block(blk + 1, 1 - slot).start()
+
+        fm_ref = fm_v.at[slot]
         for tt in range(tb):
             base = (blk * tb + tt) * f_pairs
             acc_ref[tt] = gather_sum(fi_ref, f_pool, fm_ref[tt * LEAF:(tt + 1) * LEAF, :], base, f_pairs)
@@ -276,6 +289,8 @@
             pltpu.VMEM((parents, RANK, RHS), jnp.bfloat16),
             pltpu.VMEM((tb, LEAF, RHS), jnp.float32),
             pltpu.SemaphoreType.DMA((n_seg + halves,)),
+            pltpu.VMEM((2, tb * LEAF, f_pairs * width), jnp.bfloat16),
+            pltpu.SemaphoreType.DMA((2,)),
         ],
     )
     flops = 2 * (c_mats.size + f_mats.size) * RHS

time: 95.3 us -> 96 us (level)
  no operation moved by 1% of the time
where the time goes in v16:
time: 96 us; the launch traced here: 95.4 us
  starting transfers between devices  45.5 us (47%)
  Pallas kernels  30.3 us (32%)
  waiting for transfers between devices  13 us (14%)
  local copies, waits for them, and re-layouts  6.52 us (7%)
    ppermute x6, starting transfers between devices, from_behind(): lax.ppermute(value, axis, [(source, source + steps) for source in range(f...  45.5 us
    pallas_call x1, Pallas kernels, coupled_product(): pl.pallas_call(kernel, grid_spec=grid_spec, out_shape=jax.ShapeDtypeStruc...  14 us
    ppermute x6, waiting for transfers between devices, from_behind(): lax.ppermute(value, axis, [(source, source + steps) for source in range(f...  13 us
    pallas_call x2, Pallas kernels, upward(): pl.pallas_call(kernel, in_specs=[smem, smem, vmem, vmem, vmem], out_specs...  8.2 us
    pallas_call x1, Pallas kernels, gather_dot(): pl.pallas_call(kernel, grid_spec=grid_spec, out_shape=jax.ShapeDtypeStruc...  8.05 us
    unnamed x10, local copies, waits for them, and re-layouts  6.52 us
  transfers between devices with their start and end apart: 6, of which 2 were waited for; matrix products, arithmetic and copies ran while one was open for 5% of the time, Pallas kernels for 12%

profile of v16, /device:TPU:24, one launch (start us, length us, event | category | flops | bytes accessed | tf_op | source)
XLA Modules:
  0.0 95.4 jit_solution(8160471972160841375)
XLA Ops:
  0.0 4.8 %shard_map.110 = (bf16[52,64,128]{2,1,0:T(8,128)(2,1)}, bf16[52,64,128]{2,1,0:T(8,128)(2,1)}, bf16[48,64,128]{2,1,0:T(8,128)(2,1)}, bf16[48,64,128]{2,1,0:T(8,12...) custom-call(s32[192]{0:T(256)} %bitcast.8, s32[96]{0:T(128)} %bitcast.10, ...), custom_call_target="tpu_custom_call" | custom-call | flops 134217728 | bytes 8388608 | tf_op jit(solution)/shard_map/pallas_call | solution.py:171
  4.8 1.9 %collective-permute-start = (bf16[52,64,128]{2,1,0:T(8,128)(2,1)}, bf16[52,64,128]{2,1,0:T(8,128)(2,1)S(1)}, u32[]{:S(2)}, u32[]{:S(2)}) collective-permute-start(bf16[52,64,128]{2,1,0:T(8,128)(2,1)} %get-tuple-element.14), channel_id=1, source_target_pairs={{0,1},{1,2},{2,3},{3,4},{4,5},{5,6},{6,7},{7,8},{8,9},{9,10},{10,1... | collective-permute-start | bytes 2555912 | tf_op jit(solution)/shard_map/ppermute | solution.py:21
  6.7 5.4 %collective-permute-start.1 = (bf16[52,64,128]{2,1,0:T(8,128)(2,1)}, bf16[52,64,128]{2,1,0:T(8,128)(2,1)S(1)}, u32[]{:S(2)}, u32[]{:S(2)}) collective-permute-start(bf16[52,64,128]{2,1,0:T(8,128)(2,1)} %get-tuple-element.15), channel_id=1, source_target_pairs={{1,0},{2,1},{3,2},{4,3},{5,4},{6,5},{7,6},{8,7},{9,8},{10,9},{11,1... | collective-permute-start | bytes 2555912 | tf_op jit(solution)/shard_map/ppermute | solution.py:21
  12.2 1.9 %collective-permute-start.2 = (bf16[48,64,128]{2,1,0:T(8,128)(2,1)}, bf16[48,64,128]{2,1,0:T(8,128)(2,1)S(1)}, u32[]{:S(2)}, u32[]{:S(2)}) collective-permute-start(bf16[48,64,128]{2,1,0:T(8,128)(2,1)} %get-tuple-element.16), channel_id=1, source_target_pairs={{0,2},{1,3},{2,4},{3,5},{4,6},{5,7},{6,8},{7,9},{8,10},{9,11},{10,... | collective-permute-start | bytes 2359304 | tf_op jit(solution)/shard_map/ppermute | solution.py:21
  14.1 5.7 %collective-permute-start.3 = (bf16[48,64,128]{2,1,0:T(8,128)(2,1)}, bf16[48,64,128]{2,1,0:T(8,128)(2,1)S(1)}, u32[]{:S(2)}, u32[]{:S(2)}) collective-permute-start(bf16[48,64,128]{2,1,0:T(8,128)(2,1)} %get-tuple-element.17), channel_id=1, source_target_pairs={{2,0},{3,1},{4,2},{5,3},{6,4},{7,5},{8,6},{9,7},{10,8},{11,9},{12,... | collective-permute-start | bytes 2359304 | tf_op jit(solution)/shard_map/ppermute | solution.py:21
  19.8 1.9 %collective-permute-start.4 = (bf16[48,64,128]{2,1,0:T(8,128)(2,1)}, bf16[48,64,128]{2,1,0:T(8,128)(2,1)}, u32[]{:S(2)}, u32[]{:S(2)}) collective-permute-start(bf16[48,64,128]{2,1,0:T(8,128)(2,1)} %get-tuple-element.18), channel_id=1, source_target_pairs={{0,3},{1,4},{2,5},{3,6},{4,7},{5,8},{6,9},{7,10},{8,11},{9,12},{10... | collective-permute-start | bytes 2359304 | tf_op jit(solution)/shard_map/ppermute | solution.py:21
  21.8 0.3 collective-permute-done.refs_0_.refs_1_.refs_8_
  22.0 0.0 copy-start
  22.0 28.6 %collective-permute-start.5 = (bf16[48,64,128]{2,1,0:T(8,128)(2,1)}, bf16[48,64,128]{2,1,0:T(8,128)(2,1)}, u32[]{:S(2)}, u32[]{:S(2)}) collective-permute-start(bf16[48,64,128]{2,1,0:T(8,128)(2,1)} %get-tuple-element.19), channel_id=1, source_target_pairs={{3,0},{4,1},{5,2},{6,3},{7,4},{8,5},{9,6},{10,7},{11,8},{12,9},{13... | collective-permute-start | bytes 2359304 | tf_op jit(solution)/shard_map/ppermute | solution.py:21
  50.6 2.4 %copy.13.refs_15_ = bf16[4096,64]{1,0:T(8,128)(2,1)} copy(bf16[4096,64]{0,1:T(8,128)(2,1)} %param.12) | data formatting | bytes 1048576 | tf_op args[1]
  53.0 2.4 %copy.12.refs_14_ = bf16[4096,64]{1,0:T(8,128)(2,1)} copy(bf16[4096,64]{0,1:T(8,128)(2,1)} %param.13) | data formatting | bytes 1048576 | tf_op args[2]
  55.4 3.4 %shard_map.109 = (bf16[64,64,128]{2,1,0:T(8,128)(2,1)}, bf16[32,64,128]{2,1,0:T(8,128)(2,1)}) custom-call(s32[192]{0:T(256)} %bitcast.9, s32[96]{0:T(128)} %bitcast.11, bf16[64,64,128]{2,1,0:T(8,128)(2,1)} %refs_1_.1, bf16[64,4096]{1,0:T(8,128)(2,1)} %bitcast.5, bf16[64,4096]{1,0:T(8,128)(2,1)} %bitcast.7), custom_call_target="tpu_custom_call" | custom-call | flops 134217728 | bytes 8388608 | tf_op jit(solution)/shard_map/pallas_call | solution.py:171
  58.8 0.0 collective-permute-done.1.refs_2_.refs_9_
  58.8 0.0 copy-done
  58.8 0.0 copy-start.1
  58.8 0.9 copy-done.1
  59.7 8.0 %shard_map.111.refs_16_ = f32[64,64,128]{2,1,0:T(8,128)} custom-call(s32[768]{0:T(1024)} %idx_ref.1, bf16[4096,768]{1,0:T(8,128)(2,1)} %mats_ref.1, bf16[52,64,128]{2,1,0:T(8,128)(2,1)} %copy-done, bf16[64,64,128]{2,1,0:T(8,128)(2,1)} %refs_1_.1, bf16[52,64,128]{2,1,0:T(8,128)(2,1)} %copy-done.1), custom_call_target="tpu_custom_call" | custom-call | flops 805306368 | bytes 9568256 | tf_op jit(solution)/shard_map/pallas_call | solution.py:101
  67.7 0.0 collective-permute-done.2.refs_3_.refs_10_
  67.8 0.0 copy-start.2
  67.8 12.7 %collective-permute-done.3.refs_4_.refs_11_ = bf16[48,64,128]{2,1,0:T(8,128)(2,1)S(1)} collective-permute-done((bf16[48,64,128]{2,1,0:T(8,128)(2,1)}, bf16[48,64,128]{2,1,0:T(8,128)(2,1)S(1)}, u32[]{:S(2)}, u32[]{:S(2)}) %collective-permute-start.3) | collective-permute-done | bytes 786464 | tf_op jit(solution)/shard_map/ppermute | solution.py:21
  80.5 0.0 copy-start.3
  80.5 0.0 collective-permute-done.4.refs_5_.refs_12_
  80.5 0.0 collective-permute-done.5.refs_6_.refs_13_
  80.5 0.0 copy-done.2
  80.5 0.9 copy-done.3
  81.4 14.0 %shard_map.112 = bf16[64,64,128]{2,1,0:T(8,128)(2,1)} custom-call(s32[512]{0:T(512)} %ci_ref.1, s32[1024]{0:T(1024)} %fi_ref.1, bf16[2048,1024]{1,0:T(8,128)(2,1)} %cm_hbm.1, bf16[4096,1024]{1,0:T(8,128)(2,1)} %fm_hbm.1, bf16[32,64,128]{2,1,0:T(8,128)(2,1)} %get-tuple-element.13.refs_0_, bf16[52,64,128]{2,1,0:T(8,128)(2,1)} %copy-done, ...), custom_call_target="tpu_custom_call" | custom-call | flops 1610612736 | bytes 18874368 | tf_op jit(solution)/shard_map/pallas_call | solution.py:298
Async XLA Ops:
  4.8 17.2 %collective-permute-start = (bf16[52,64,128]{2,1,0:T(8,128)(2,1)}, bf16[52,64,128]{2,1,0:T(8,128)(2,1)S(1)}, u32[]{:S(2)}, u32[]{:S(2)}) collective-permute-start(bf16[52,64,128]{2,1,0:T(8,128)(2,1)} %get-tuple-element.14), channel_id=1, source_target_pairs={{0,1},{1,2},{2,3},{3,4},{4,5},{5,6},{6,7},{7,8},{8,9},{9,10},{10,1... | collective-permute-start | bytes 2555912 | tf_op jit(solution)/shard_map/ppermute | solution.py:21
  6.7 52.0 %collective-permute-start.1 = (bf16[52,64,128]{2,1,0:T(8,128)(2,1)}, bf16[52,64,128]{2,1,0:T(8,128)(2,1)S(1)}, u32[]{:S(2)}, u32[]{:S(2)}) collective-permute-start(bf16[52,64,128]{2,1,0:T(8,128)(2,1)} %get-tuple-element.15), channel_id=1, source_target_pairs={{1,0},{2,1},{3,2},{4,3},{5,4},{6,5},{7,6},{8,7},{9,8},{10,9},{11,1... | collective-permute-start | bytes 2555912 | tf_op jit(solution)/shard_map/ppermute | solution.py:21
  12.2 55.6 %collective-permute-start.2 = (bf16[48,64,128]{2,1,0:T(8,128)(2,1)}, bf16[48,64,128]{2,1,0:T(8,128)(2,1)S(1)}, u32[]{:S(2)}, u32[]{:S(2)}) collective-permute-start(bf16[48,64,128]{2,1,0:T(8,128)(2,1)} %get-tuple-element.16), channel_id=1, source_target_pairs={{0,2},{1,3},{2,4},{3,5},{4,6},{5,7},{6,8},{7,9},{8,10},{9,11},{10,... | collective-permute-start | bytes 2359304 | tf_op jit(solution)/shard_map/ppermute | solution.py:21
  14.1 66.4 %collective-permute-start.3 = (bf16[48,64,128]{2,1,0:T(8,128)(2,1)}, bf16[48,64,128]{2,1,0:T(8,128)(2,1)S(1)}, u32[]{:S(2)}, u32[]{:S(2)}) collective-permute-start(bf16[48,64,128]{2,1,0:T(8,128)(2,1)} %get-tuple-element.17), channel_id=1, source_target_pairs={{2,0},{3,1},{4,2},{5,3},{6,4},{7,5},{8,6},{9,7},{10,8},{11,9},{12,... | collective-permute-start | bytes 2359304 | tf_op jit(solution)/shard_map/ppermute | solution.py:21
  19.8 60.7 %collective-permute-start.4 = (bf16[48,64,128]{2,1,0:T(8,128)(2,1)}, bf16[48,64,128]{2,1,0:T(8,128)(2,1)}, u32[]{:S(2)}, u32[]{:S(2)}) collective-permute-start(bf16[48,64,128]{2,1,0:T(8,128)(2,1)} %get-tuple-element.18), channel_id=1, source_target_pairs={{0,3},{1,4},{2,5},{3,6},{4,7},{5,8},{6,9},{7,10},{8,11},{9,12},{10... | collective-permute-start | bytes 2359304 | tf_op jit(solution)/shard_map/ppermute | solution.py:21
  22.0 36.8 %copy-start = (bf16[52,64,128]{2,1,0:T(8,128)(2,1)}, bf16[52,64,128]{2,1,0:T(8,128)(2,1)S(1)}, u32[]{:S(2)}) copy-start(bf16[52,64,128]{2,1,0:T(8,128)(2,1)S(1)} %collective-permute-done.refs_0_.refs_1_.refs_8_) | copy-start | bytes 2555908
  22.0 58.5 %collective-permute-start.5 = (bf16[48,64,128]{2,1,0:T(8,128)(2,1)}, bf16[48,64,128]{2,1,0:T(8,128)(2,1)}, u32[]{:S(2)}, u32[]{:S(2)}) collective-permute-start(bf16[48,64,128]{2,1,0:T(8,128)(2,1)} %get-tuple-element.19), channel_id=1, source_target_pairs={{3,0},{4,1},{5,2},{6,3},{7,4},{8,5},{9,6},{10,7},{11,8},{12,9},{13... | collective-permute-start | bytes 2359304 | tf_op jit(solution)/shard_map/ppermute | solution.py:21
  58.8 0.9 copy-start.1
  67.8 12.8 %copy-start.2 = (bf16[48,64,128]{2,1,0:T(8,128)(2,1)}, bf16[48,64,128]{2,1,0:T(8,128)(2,1)S(1)}, u32[]{:S(2)}) copy-start(bf16[48,64,128]{2,1,0:T(8,128)(2,1)S(1)} %collective-permute-done.2.refs_3_.refs_10_) | copy-start | bytes 2359300
  80.5 0.9 copy-start.3

commit v17 on v14

--- a/solution.py
+++ b/solution.py
@@ -255,10 +255,11 @@
             base = (blk * tb + tt) * f_pairs
             acc_ref[tt] = gather_sum(fi_ref, f_pool, fm_ref[tt * LEAF:(tt + 1) * LEAF, :], base, f_pairs)
         rounded = []
-        for tt in range(tb):
-            e = e_ref[tt * RANK:(tt + 1) * RANK, :]
-            down = jnp.dot(e, cr_ref[(blk * tb + tt) // 2], preferred_element_type=jnp.float32)
-            rounded.append((acc_ref[tt] + down).astype(jnp.bfloat16))
+        for j in range(tb // 2):
+            e = e_ref[2 * j * RANK:(2 * j + 2) * RANK, :]
+            down = jnp.dot(e, cr_ref[blk * (tb // 2) + j], preferred_element_type=jnp.float32)
+            for h in range(2):
+                rounded.append((acc_ref[2 * j + h] + down[h * RANK:(h + 1) * RANK]).astype(jnp.bfloat16))
         for tt in range(tb):
             v = v_ref[tt * LEAF:(tt + 1) * LEAF, :]
             far = jnp.dot(v, rounded[tt], preferred_element_type=jnp.float32)

time: 95.3 us -> 95.3 us (level)
  no operation moved by 1% of the time
where the time goes in v17:
time: 95.3 us; the launch traced here: 94.8 us
  starting transfers between devices  45.5 us (48%)
  Pallas kernels  29.6 us (31%)
  waiting for transfers between devices  13 us (14%)
  local copies, waits for them, and re-layouts  6.52 us (7%)
    ppermute x6, starting transfers between devices, from_behind(): lax.ppermute(value, axis, [(source, source + steps) for source in range(f...  45.5 us
    pallas_call x1, Pallas kernels, coupled_product(): pl.pallas_call(kernel, grid_spec=grid_spec, out_shape=jax.ShapeDtypeStruc...  13.4 us
    ppermute x6, waiting for transfers between devices, from_behind(): lax.ppermute(value, axis, [(source, source + steps) for source in range(f...  13 us
    pallas_call x2, Pallas kernels, upward(): pl.pallas_call(kernel, in_specs=[smem, smem, vmem, vmem, vmem], out_specs...  8.2 us
    pallas_call x1, Pallas kernels, gather_dot(): pl.pallas_call(kernel, grid_spec=grid_spec, out_shape=jax.ShapeDtypeStruc...  8.05 us
    unnamed x10, local copies, waits for them, and re-layouts  6.52 us
  transfers between devices with their start and end apart: 6, of which 2 were waited for; matrix products, arithmetic and copies ran while one was open for 5% of the time, Pallas kernels for 12%

profile of v17, /device:TPU:24, one launch (start us, length us, event | category | flops | bytes accessed | tf_op | source)
XLA Modules:
  0.0 94.8 jit_solution(10752363153566427889)
XLA Ops:
  0.0 4.8 %shard_map.110 = (bf16[52,64,128]{2,1,0:T(8,128)(2,1)}, bf16[52,64,128]{2,1,0:T(8,128)(2,1)}, bf16[48,64,128]{2,1,0:T(8,128)(2,1)}, bf16[48,64,128]{2,1,0:T(8,12...) custom-call(s32[192]{0:T(256)} %bitcast.8, s32[96]{0:T(128)} %bitcast.10, ...), custom_call_target="tpu_custom_call" | custom-call | flops 134217728 | bytes 8388608 | tf_op jit(solution)/shard_map/pallas_call | solution.py:171
  4.8 1.9 %collective-permute-start = (bf16[52,64,128]{2,1,0:T(8,128)(2,1)}, bf16[52,64,128]{2,1,0:T(8,128)(2,1)S(1)}, u32[]{:S(2)}, u32[]{:S(2)}) collective-permute-start(bf16[52,64,128]{2,1,0:T(8,128)(2,1)} %get-tuple-element.14), channel_id=1, source_target_pairs={{0,1},{1,2},{2,3},{3,4},{4,5},{5,6},{6,7},{7,8},{8,9},{9,10},{10,1... | collective-permute-start | bytes 2555912 | tf_op jit(solution)/shard_map/ppermute | solution.py:21
  6.7 5.4 %collective-permute-start.1 = (bf16[52,64,128]{2,1,0:T(8,128)(2,1)}, bf16[52,64,128]{2,1,0:T(8,128)(2,1)S(1)}, u32[]{:S(2)}, u32[]{:S(2)}) collective-permute-start(bf16[52,64,128]{2,1,0:T(8,128)(2,1)} %get-tuple-element.15), channel_id=1, source_target_pairs={{1,0},{2,1},{3,2},{4,3},{5,4},{6,5},{7,6},{8,7},{9,8},{10,9},{11,1... | collective-permute-start | bytes 2555912 | tf_op jit(solution)/shard_map/ppermute | solution.py:21
  12.2 1.9 %collective-permute-start.2 = (bf16[48,64,128]{2,1,0:T(8,128)(2,1)}, bf16[48,64,128]{2,1,0:T(8,128)(2,1)S(1)}, u32[]{:S(2)}, u32[]{:S(2)}) collective-permute-start(bf16[48,64,128]{2,1,0:T(8,128)(2,1)} %get-tuple-element.16), channel_id=1, source_target_pairs={{0,2},{1,3},{2,4},{3,5},{4,6},{5,7},{6,8},{7,9},{8,10},{9,11},{10,... | collective-permute-start | bytes 2359304 | tf_op jit(solution)/shard_map/ppermute | solution.py:21
  14.1 5.7 %collective-permute-start.3 = (bf16[48,64,128]{2,1,0:T(8,128)(2,1)}, bf16[48,64,128]{2,1,0:T(8,128)(2,1)S(1)}, u32[]{:S(2)}, u32[]{:S(2)}) collective-permute-start(bf16[48,64,128]{2,1,0:T(8,128)(2,1)} %get-tuple-element.17), channel_id=1, source_target_pairs={{2,0},{3,1},{4,2},{5,3},{6,4},{7,5},{8,6},{9,7},{10,8},{11,9},{12,... | collective-permute-start | bytes 2359304 | tf_op jit(solution)/shard_map/ppermute | solution.py:21
  19.8 1.9 %collective-permute-start.4 = (bf16[48,64,128]{2,1,0:T(8,128)(2,1)}, bf16[48,64,128]{2,1,0:T(8,128)(2,1)}, u32[]{:S(2)}, u32[]{:S(2)}) collective-permute-start(bf16[48,64,128]{2,1,0:T(8,128)(2,1)} %get-tuple-element.18), channel_id=1, source_target_pairs={{0,3},{1,4},{2,5},{3,6},{4,7},{5,8},{6,9},{7,10},{8,11},{9,12},{10... | collective-permute-start | bytes 2359304 | tf_op jit(solution)/shard_map/ppermute | solution.py:21
  21.8 0.3 collective-permute-done.refs_0_.refs_1_.refs_8_
  22.0 0.0 copy-start
  22.0 28.6 %collective-permute-start.5 = (bf16[48,64,128]{2,1,0:T(8,128)(2,1)}, bf16[48,64,128]{2,1,0:T(8,128)(2,1)}, u32[]{:S(2)}, u32[]{:S(2)}) collective-permute-start(bf16[48,64,128]{2,1,0:T(8,128)(2,1)} %get-tuple-element.19), channel_id=1, source_target_pairs={{3,0},{4,1},{5,2},{6,3},{7,4},{8,5},{9,6},{10,7},{11,8},{12,9},{13... | collective-permute-start | bytes 2359304 | tf_op jit(solution)/shard_map/ppermute | solution.py:21
  50.6 2.4 %copy.13.refs_15_ = bf16[4096,64]{1,0:T(8,128)(2,1)} copy(bf16[4096,64]{0,1:T(8,128)(2,1)} %param.12) | data formatting | bytes 1048576 | tf_op args[1]
  53.0 2.4 %copy.12.refs_14_ = bf16[4096,64]{1,0:T(8,128)(2,1)} copy(bf16[4096,64]{0,1:T(8,128)(2,1)} %param.13) | data formatting | bytes 1048576 | tf_op args[2]
  55.4 3.4 %shard_map.109 = (bf16[64,64,128]{2,1,0:T(8,128)(2,1)}, bf16[32,64,128]{2,1,0:T(8,128)(2,1)}) custom-call(s32[192]{0:T(256)} %bitcast.9, s32[96]{0:T(128)} %bitcast.11, bf16[64,64,128]{2,1,0:T(8,128)(2,1)} %refs_1_.1, bf16[64,4096]{1,0:T(8,128)(2,1)} %bitcast.5, bf16[64,4096]{1,0:T(8,128)(2,1)} %bitcast.7), custom_call_target="tpu_custom_call" | custom-call | flops 134217728 | bytes 8388608 | tf_op jit(solution)/shard_map/pallas_call | solution.py:171
  58.8 0.0 collective-permute-done.1.refs_2_.refs_9_
  58.8 0.0 copy-done
  58.8 0.0 copy-start.1
  58.8 0.9 copy-done.1
  59.7 8.0 %shard_map.111.refs_16_ = f32[64,64,128]{2,1,0:T(8,128)} custom-call(s32[768]{0:T(1024)} %idx_ref.1, bf16[4096,768]{1,0:T(8,128)(2,1)} %mats_ref.1, bf16[52,64,128]{2,1,0:T(8,128)(2,1)} %copy-done, bf16[64,64,128]{2,1,0:T(8,128)(2,1)} %refs_1_.1, bf16[52,64,128]{2,1,0:T(8,128)(2,1)} %copy-done.1), custom_call_target="tpu_custom_call" | custom-call | flops 805306368 | bytes 9568256 | tf_op jit(solution)/shard_map/pallas_call | solution.py:101
  67.7 0.0 collective-permute-done.2.refs_3_.refs_10_
  67.8 0.0 copy-start.2
  67.8 12.7 %collective-permute-done.3.refs_4_.refs_11_ = bf16[48,64,128]{2,1,0:T(8,128)(2,1)S(1)} collective-permute-done((bf16[48,64,128]{2,1,0:T(8,128)(2,1)}, bf16[48,64,128]{2,1,0:T(8,128)(2,1)S(1)}, u32[]{:S(2)}, u32[]{:S(2)}) %collective-permute-start.3) | collective-permute-done | bytes 786464 | tf_op jit(solution)/shard_map/ppermute | solution.py:21
  80.5 0.0 copy-start.3
  80.5 0.0 collective-permute-done.4.refs_5_.refs_12_
  80.5 0.0 collective-permute-done.5.refs_6_.refs_13_
  80.5 0.0 copy-done.2
  80.5 0.9 copy-done.3
  81.4 13.4 %shard_map.112 = bf16[64,64,128]{2,1,0:T(8,128)(2,1)} custom-call(s32[512]{0:T(512)} %ci_ref.1, s32[1024]{0:T(1024)} %fi_ref.1, bf16[2048,1024]{1,0:T(8,128)(2,1)} %cm_hbm.1, bf16[4096,1024]{1,0:T(8,128)(2,1)} %fm_ref.1, bf16[32,64,128]{2,1,0:T(8,128)(2,1)} %get-tuple-element.13.refs_0_, bf16[52,64,128]{2,1,0:T(8,128)(2,1)} %copy-done, ...), custom_call_target="tpu_custom_call" | custom-call | flops 1610612736 | bytes 18874368 | tf_op jit(solution)/shard_map/pallas_call | solution.py:284
Async XLA Ops:
  4.8 17.2 %collective-permute-start = (bf16[52,64,128]{2,1,0:T(8,128)(2,1)}, bf16[52,64,128]{2,1,0:T(8,128)(2,1)S(1)}, u32[]{:S(2)}, u32[]{:S(2)}) collective-permute-start(bf16[52,64,128]{2,1,0:T(8,128)(2,1)} %get-tuple-element.14), channel_id=1, source_target_pairs={{0,1},{1,2},{2,3},{3,4},{4,5},{5,6},{6,7},{7,8},{8,9},{9,10},{10,1... | collective-permute-start | bytes 2555912 | tf_op jit(solution)/shard_map/ppermute | solution.py:21
  6.7 52.0 %collective-permute-start.1 = (bf16[52,64,128]{2,1,0:T(8,128)(2,1)}, bf16[52,64,128]{2,1,0:T(8,128)(2,1)S(1)}, u32[]{:S(2)}, u32[]{:S(2)}) collective-permute-start(bf16[52,64,128]{2,1,0:T(8,128)(2,1)} %get-tuple-element.15), channel_id=1, source_target_pairs={{1,0},{2,1},{3,2},{4,3},{5,4},{6,5},{7,6},{8,7},{9,8},{10,9},{11,1... | collective-permute-start | bytes 2555912 | tf_op jit(solution)/shard_map/ppermute | solution.py:21
  12.2 55.6 %collective-permute-start.2 = (bf16[48,64,128]{2,1,0:T(8,128)(2,1)}, bf16[48,64,128]{2,1,0:T(8,128)(2,1)S(1)}, u32[]{:S(2)}, u32[]{:S(2)}) collective-permute-start(bf16[48,64,128]{2,1,0:T(8,128)(2,1)} %get-tuple-element.16), channel_id=1, source_target_pairs={{0,2},{1,3},{2,4},{3,5},{4,6},{5,7},{6,8},{7,9},{8,10},{9,11},{10,... | collective-permute-start | bytes 2359304 | tf_op jit(solution)/shard_map/ppermute | solution.py:21
  14.1 66.4 %collective-permute-start.3 = (bf16[48,64,128]{2,1,0:T(8,128)(2,1)}, bf16[48,64,128]{2,1,0:T(8,128)(2,1)S(1)}, u32[]{:S(2)}, u32[]{:S(2)}) collective-permute-start(bf16[48,64,128]{2,1,0:T(8,128)(2,1)} %get-tuple-element.17), channel_id=1, source_target_pairs={{2,0},{3,1},{4,2},{5,3},{6,4},{7,5},{8,6},{9,7},{10,8},{11,9},{12,... | collective-permute-start | bytes 2359304 | tf_op jit(solution)/shard_map/ppermute | solution.py:21
  19.8 60.7 %collective-permute-start.4 = (bf16[48,64,128]{2,1,0:T(8,128)(2,1)}, bf16[48,64,128]{2,1,0:T(8,128)(2,1)}, u32[]{:S(2)}, u32[]{:S(2)}) collective-permute-start(bf16[48,64,128]{2,1,0:T(8,128)(2,1)} %get-tuple-element.18), channel_id=1, source_target_pairs={{0,3},{1,4},{2,5},{3,6},{4,7},{5,8},{6,9},{7,10},{8,11},{9,12},{10... | collective-permute-start | bytes 2359304 | tf_op jit(solution)/shard_map/ppermute | solution.py:21
  22.0 36.8 %copy-start = (bf16[52,64,128]{2,1,0:T(8,128)(2,1)}, bf16[52,64,128]{2,1,0:T(8,128)(2,1)S(1)}, u32[]{:S(2)}) copy-start(bf16[52,64,128]{2,1,0:T(8,128)(2,1)S(1)} %collective-permute-done.refs_0_.refs_1_.refs_8_) | copy-start | bytes 2555908
  22.0 58.5 %collective-permute-start.5 = (bf16[48,64,128]{2,1,0:T(8,128)(2,1)}, bf16[48,64,128]{2,1,0:T(8,128)(2,1)}, u32[]{:S(2)}, u32[]{:S(2)}) collective-permute-start(bf16[48,64,128]{2,1,0:T(8,128)(2,1)} %get-tuple-element.19), channel_id=1, source_target_pairs={{3,0},{4,1},{5,2},{6,3},{7,4},{8,5},{9,6},{10,7},{11,8},{12,9},{13... | collective-permute-start | bytes 2359304 | tf_op jit(solution)/shard_map/ppermute | solution.py:21
  58.8 0.9 copy-start.1
  67.8 12.8 %copy-start.2 = (bf16[48,64,128]{2,1,0:T(8,128)(2,1)}, bf16[48,64,128]{2,1,0:T(8,128)(2,1)S(1)}, u32[]{:S(2)}) copy-start(bf16[48,64,128]{2,1,0:T(8,128)(2,1)S(1)} %collective-permute-done.2.refs_3_.refs_10_) | copy-start | bytes 2359300
  80.5 0.9 copy-start.3

commit v18 on v17

--- a/solution.py
+++ b/solution.py
@@ -116,13 +116,23 @@
     chunks = 4 if parents % 4 == 0 else 1
     per = parents // chunks
 
-    def kernel(sf_ref, sc_ref, x_ref, v_ref, e_ref, *rest):
+    def kernel(sf_ref, sc_ref, x_hbm, v_ref, e_hbm, *rest):
         n_out = slots if packets else 2
         outs = rest[:n_out]
-        fine_v, coarse_v = rest[n_out:n_out + 2]
-        bufs = rest[n_out + 2:len(rest) - 1]
-        sem = rest[len(rest) - 1]
+        fine_v, coarse_v, x_ref, e_ref = rest[n_out:n_out + 4]
+        bufs = rest[n_out + 4:len(rest) - 2]
+        sem, in_sem = rest[len(rest) - 2:]
+        loads = []
         for c in range(chunks):
+            rows = pl.ds(2 * c * per, 2 * per)
+            cp = pltpu.make_async_copy(x_hbm.at[rows], x_ref.at[rows], in_sem.at[c])
+            cp.start()
+            loads.append(cp)
+        e_load = pltpu.make_async_copy(e_hbm, e_ref, in_sem.at[chunks])
+        e_load.start()
+        pairs_v = []
+        for c in range(chunks):
+            loads[c].wait()
             for j in range(c * per, (c + 1) * per):
                 col = j * 2 * RANK
                 f0 = jnp.dot(v_ref[:, col:col + RANK], x_ref[2 * j], preferred_element_type=jnp.float32)
@@ -130,8 +140,12 @@
                 pair = jnp.concatenate([f0.astype(jnp.bfloat16), f1.astype(jnp.bfloat16)], axis=0)
                 fine_v[2 * j] = pair[:RANK]
                 fine_v[2 * j + 1] = pair[RANK:]
-                e = e_ref[:, col:col + 2 * RANK]
-                coarse_v[j] = jnp.dot(e, pair, preferred_element_type=jnp.float32).astype(jnp.bfloat16)
+        e_load.wait()
+        for j in range(parents):
+            col = j * 2 * RANK
+            pair = jnp.concatenate([fine_v[2 * j], fine_v[2 * j + 1]], axis=0)
+            e = e_ref[:, col:col + 2 * RANK]
+            coarse_v[j] = jnp.dot(e, pair, preferred_element_type=jnp.float32).astype(jnp.bfloat16)
 
         copies = []
         if not packets:
@@ -170,15 +184,17 @@
         bufs = []
     return pl.pallas_call(
         kernel,
-        in_specs=[smem, smem, vmem, vmem, vmem],
+        in_specs=[smem, smem, hbm, vmem, hbm],
         out_specs=[hbm] * len(out_shape),
         out_shape=out_shape,
         scratch_shapes=[
             pltpu.VMEM((leaves, RANK, RHS), jnp.bfloat16),
             pltpu.VMEM((parents, RANK, RHS), jnp.bfloat16),
+            pltpu.VMEM(charges.shape, jnp.bfloat16),
+            pltpu.VMEM(transfer_t.shape, jnp.bfloat16),
         ]
         + bufs
-        + [pltpu.SemaphoreType.DMA((len(out_shape),))],
+        + [pltpu.SemaphoreType.DMA((len(out_shape),)), pltpu.SemaphoreType.DMA((chunks + 1,))],
         cost_estimate=pl.CostEstimate(
             flops=2 * leaves * LEAF * RANK * RHS * 2, transcendentals=0, bytes_accessed=8 * 2 ** 20
         ),

time: 95.3 us -> 96.4 us (1.012)
  Pallas kernels: 29.6 us -> 31.5 us
    pallas_call x2, Pallas kernels: 8.2 us -> 10.1 us  [upward(): pl.pallas_call(kernel, in_specs=[smem, smem, hbm, vmem, hbm], out_specs=[...]
  transfers between devices with their start and end apart: 6 -> 6, of which waited for: 2 -> 2; matrix products, arithmetic and copies ran while one was open for 5% -> 5% of each run, Pallas kernels for 12% -> 13%
where the time goes in v18:
time: 96.4 us; the launch traced here: 95.8 us
  starting transfers between devices  45.5 us (47%)
  Pallas kernels  31.5 us (33%)
  waiting for transfers between devices  12.1 us (13%)
  local copies, waits for them, and re-layouts  6.52 us (7%)
    ppermute x6, starting transfers between devices, from_behind(): lax.ppermute(value, axis, [(source, source + steps) for source in range(f...  45.5 us
    pallas_call x1, Pallas kernels, coupled_product(): pl.pallas_call(kernel, grid_spec=grid_spec, out_shape=jax.ShapeDtypeStruc...  13.3 us
    ppermute x6, waiting for transfers between devices, from_behind(): lax.ppermute(value, axis, [(source, source + steps) for source in range(f...  12.1 us
    pallas_call x2, Pallas kernels, upward(): pl.pallas_call(kernel, in_specs=[smem, smem, hbm, vmem, hbm], out_specs=[...  10.1 us
    pallas_call x1, Pallas kernels, gather_dot(): pl.pallas_call(kernel, grid_spec=grid_spec, out_shape=jax.ShapeDtypeStruc...  8.06 us
    unnamed x10, local copies, waits for them, and re-layouts  6.52 us
  transfers between devices with their start and end apart: 6, of which 2 were waited for; matrix products, arithmetic and copies ran while one was open for 5% of the time, Pallas kernels for 13%

profile of v18, /device:TPU:24, one launch (start us, length us, event | category | flops | bytes accessed | tf_op | source)
XLA Modules:
  0.0 95.8 jit_solution(6413062058899766068)
XLA Ops:
  0.0 5.8 %shard_map.110 = (bf16[52,64,128]{2,1,0:T(8,128)(2,1)}, bf16[52,64,128]{2,1,0:T(8,128)(2,1)}, bf16[48,64,128]{2,1,0:T(8,128)(2,1)}, bf16[48,64,128]{2,1,0:T(8,12...) custom-call(s32[192]{0:T(256)} %bitcast.8, s32[96]{0:T(128)} %bitcast.10, ...), custom_call_target="tpu_custom_call" | custom-call | flops 134217728 | bytes 8388608 | tf_op jit(solution)/shard_map/pallas_call | solution.py:185
  5.9 1.9 %collective-permute-start = (bf16[52,64,128]{2,1,0:T(8,128)(2,1)}, bf16[52,64,128]{2,1,0:T(8,128)(2,1)S(1)}, u32[]{:S(2)}, u32[]{:S(2)}) collective-permute-start(bf16[52,64,128]{2,1,0:T(8,128)(2,1)} %get-tuple-element.14), channel_id=1, source_target_pairs={{0,1},{1,2},{2,3},{3,4},{4,5},{5,6},{6,7},{7,8},{8,9},{9,10},{10,1... | collective-permute-start | bytes 2555912 | tf_op jit(solution)/shard_map/ppermute | solution.py:21
  7.8 5.4 %collective-permute-start.1 = (bf16[52,64,128]{2,1,0:T(8,128)(2,1)}, bf16[52,64,128]{2,1,0:T(8,128)(2,1)S(1)}, u32[]{:S(2)}, u32[]{:S(2)}) collective-permute-start(bf16[52,64,128]{2,1,0:T(8,128)(2,1)} %get-tuple-element.15), channel_id=1, source_target_pairs={{1,0},{2,1},{3,2},{4,3},{5,4},{6,5},{7,6},{8,7},{9,8},{10,9},{11,1... | collective-permute-start | bytes 2555912 | tf_op jit(solution)/shard_map/ppermute | solution.py:21
  13.2 1.9 %collective-permute-start.2 = (bf16[48,64,128]{2,1,0:T(8,128)(2,1)}, bf16[48,64,128]{2,1,0:T(8,128)(2,1)S(1)}, u32[]{:S(2)}, u32[]{:S(2)}) collective-permute-start(bf16[48,64,128]{2,1,0:T(8,128)(2,1)} %get-tuple-element.16), channel_id=1, source_target_pairs={{0,2},{1,3},{2,4},{3,5},{4,6},{5,7},{6,8},{7,9},{8,10},{9,11},{10,... | collective-permute-start | bytes 2359304 | tf_op jit(solution)/shard_map/ppermute | solution.py:21
  15.2 5.7 %collective-permute-start.3 = (bf16[48,64,128]{2,1,0:T(8,128)(2,1)}, bf16[48,64,128]{2,1,0:T(8,128)(2,1)S(1)}, u32[]{:S(2)}, u32[]{:S(2)}) collective-permute-start(bf16[48,64,128]{2,1,0:T(8,128)(2,1)} %get-tuple-element.17), channel_id=1, source_target_pairs={{2,0},{3,1},{4,2},{5,3},{6,4},{7,5},{8,6},{9,7},{10,8},{11,9},{12,... | collective-permute-start | bytes 2359304 | tf_op jit(solution)/shard_map/ppermute | solution.py:21
  20.9 1.9 %collective-permute-start.4 = (bf16[48,64,128]{2,1,0:T(8,128)(2,1)}, bf16[48,64,128]{2,1,0:T(8,128)(2,1)}, u32[]{:S(2)}, u32[]{:S(2)}) collective-permute-start(bf16[48,64,128]{2,1,0:T(8,128)(2,1)} %get-tuple-element.18), channel_id=1, source_target_pairs={{0,3},{1,4},{2,5},{3,6},{4,7},{5,8},{6,9},{7,10},{8,11},{9,12},{10... | collective-permute-start | bytes 2359304 | tf_op jit(solution)/shard_map/ppermute | solution.py:21
  22.8 0.3 collective-permute-done.refs_0_.refs_1_.refs_8_
  23.1 0.0 copy-start
  23.1 28.6 %collective-permute-start.5 = (bf16[48,64,128]{2,1,0:T(8,128)(2,1)}, bf16[48,64,128]{2,1,0:T(8,128)(2,1)}, u32[]{:S(2)}, u32[]{:S(2)}) collective-permute-start(bf16[48,64,128]{2,1,0:T(8,128)(2,1)} %get-tuple-element.19), channel_id=1, source_target_pairs={{3,0},{4,1},{5,2},{6,3},{7,4},{8,5},{9,6},{10,7},{11,8},{12,9},{13... | collective-permute-start | bytes 2359304 | tf_op jit(solution)/shard_map/ppermute | solution.py:21
  51.7 2.4 %copy.13.refs_15_ = bf16[4096,64]{1,0:T(8,128)(2,1)} copy(bf16[4096,64]{0,1:T(8,128)(2,1)} %param.12) | data formatting | bytes 1048576 | tf_op args[1]
  54.0 2.4 %copy.12.refs_14_ = bf16[4096,64]{1,0:T(8,128)(2,1)} copy(bf16[4096,64]{0,1:T(8,128)(2,1)} %param.13) | data formatting | bytes 1048576 | tf_op args[2]
  56.4 4.3 %shard_map.109 = (bf16[64,64,128]{2,1,0:T(8,128)(2,1)}, bf16[32,64,128]{2,1,0:T(8,128)(2,1)}) custom-call(s32[192]{0:T(256)} %bitcast.9, s32[96]{0:T(128)} %bitcast.11, bf16[64,64,128]{2,1,0:T(8,128)(2,1)} %refs_1_.1, bf16[64,4096]{1,0:T(8,128)(2,1)} %bitcast.5, bf16[64,4096]{1,0:T(8,128)(2,1)} %bitcast.7), custom_call_target="tpu_custom_call" | custom-call | flops 134217728 | bytes 8388608 | tf_op jit(solution)/shard_map/pallas_call | solution.py:185
  60.7 0.0 collective-permute-done.1.refs_2_.refs_9_
  60.7 0.0 copy-done
  60.7 0.0 copy-start.1
  60.8 0.9 copy-done.1
  61.6 8.1 %shard_map.111.refs_16_ = f32[64,64,128]{2,1,0:T(8,128)} custom-call(s32[768]{0:T(1024)} %idx_ref.1, bf16[4096,768]{1,0:T(8,128)(2,1)} %mats_ref.1, bf16[52,64,128]{2,1,0:T(8,128)(2,1)} %copy-done, bf16[64,64,128]{2,1,0:T(8,128)(2,1)} %refs_1_.1, bf16[52,64,128]{2,1,0:T(8,128)(2,1)} %copy-done.1), custom_call_target="tpu_custom_call" | custom-call | flops 805306368 | bytes 9568256 | tf_op jit(solution)/shard_map/pallas_call | solution.py:101
  69.7 0.0 collective-permute-done.2.refs_3_.refs_10_
  69.7 0.0 copy-start.2
  69.7 11.8 %collective-permute-done.3.refs_4_.refs_11_ = bf16[48,64,128]{2,1,0:T(8,128)(2,1)S(1)} collective-permute-done((bf16[48,64,128]{2,1,0:T(8,128)(2,1)}, bf16[48,64,128]{2,1,0:T(8,128)(2,1)S(1)}, u32[]{:S(2)}, u32[]{:S(2)}) %collective-permute-start.3) | collective-permute-done | bytes 786464 | tf_op jit(solution)/shard_map/ppermute | solution.py:21
  81.6 0.0 copy-start.3
  81.6 0.0 collective-permute-done.4.refs_5_.refs_12_
  81.6 0.0 collective-permute-done.5.refs_6_.refs_13_
  81.6 0.0 copy-done.2
  81.6 0.9 copy-done.3
  82.5 13.3 %shard_map.112 = bf16[64,64,128]{2,1,0:T(8,128)(2,1)} custom-call(s32[512]{0:T(512)} %ci_ref.1, s32[1024]{0:T(1024)} %fi_ref.1, bf16[2048,1024]{1,0:T(8,128)(2,1)} %cm_hbm.1, bf16[4096,1024]{1,0:T(8,128)(2,1)} %fm_ref.1, bf16[32,64,128]{2,1,0:T(8,128)(2,1)} %get-tuple-element.13.refs_0_, bf16[52,64,128]{2,1,0:T(8,128)(2,1)} %copy-done, ...), custom_call_target="tpu_custom_call" | custom-call | flops 1610612736 | bytes 18874368 | tf_op jit(solution)/shard_map/pallas_call | solution.py:300
Async XLA Ops:
  5.9 17.2 %collective-permute-start = (bf16[52,64,128]{2,1,0:T(8,128)(2,1)}, bf16[52,64,128]{2,1,0:T(8,128)(2,1)S(1)}, u32[]{:S(2)}, u32[]{:S(2)}) collective-permute-start(bf16[52,64,128]{2,1,0:T(8,128)(2,1)} %get-tuple-element.14), channel_id=1, source_target_pairs={{0,1},{1,2},{2,3},{3,4},{4,5},{5,6},{6,7},{7,8},{8,9},{9,10},{10,1... | collective-permute-start | bytes 2555912 | tf_op jit(solution)/shard_map/ppermute | solution.py:21
  7.8 52.9 %collective-permute-start.1 = (bf16[52,64,128]{2,1,0:T(8,128)(2,1)}, bf16[52,64,128]{2,1,0:T(8,128)(2,1)S(1)}, u32[]{:S(2)}, u32[]{:S(2)}) collective-permute-start(bf16[52,64,128]{2,1,0:T(8,128)(2,1)} %get-tuple-element.15), channel_id=1, source_target_pairs={{1,0},{2,1},{3,2},{4,3},{5,4},{6,5},{7,6},{8,7},{9,8},{10,9},{11,1... | collective-permute-start | bytes 2555912 | tf_op jit(solution)/shard_map/ppermute | solution.py:21
  13.2 56.5 %collective-permute-start.2 = (bf16[48,64,128]{2,1,0:T(8,128)(2,1)}, bf16[48,64,128]{2,1,0:T(8,128)(2,1)S(1)}, u32[]{:S(2)}, u32[]{:S(2)}) collective-permute-start(bf16[48,64,128]{2,1,0:T(8,128)(2,1)} %get-tuple-element.16), channel_id=1, source_target_pairs={{0,2},{1,3},{2,4},{3,5},{4,6},{5,7},{6,8},{7,9},{8,10},{9,11},{10,... | collective-permute-start | bytes 2359304 | tf_op jit(solution)/shard_map/ppermute | solution.py:21
  15.2 66.4 %collective-permute-start.3 = (bf16[48,64,128]{2,1,0:T(8,128)(2,1)}, bf16[48,64,128]{2,1,0:T(8,128)(2,1)S(1)}, u32[]{:S(2)}, u32[]{:S(2)}) collective-permute-start(bf16[48,64,128]{2,1,0:T(8,128)(2,1)} %get-tuple-element.17), channel_id=1, source_target_pairs={{2,0},{3,1},{4,2},{5,3},{6,4},{7,5},{8,6},{9,7},{10,8},{11,9},{12,... | collective-permute-start | bytes 2359304 | tf_op jit(solution)/shard_map/ppermute | solution.py:21
  20.9 60.7 %collective-permute-start.4 = (bf16[48,64,128]{2,1,0:T(8,128)(2,1)}, bf16[48,64,128]{2,1,0:T(8,128)(2,1)}, u32[]{:S(2)}, u32[]{:S(2)}) collective-permute-start(bf16[48,64,128]{2,1,0:T(8,128)(2,1)} %get-tuple-element.18), channel_id=1, source_target_pairs={{0,3},{1,4},{2,5},{3,6},{4,7},{5,8},{6,9},{7,10},{8,11},{9,12},{10... | collective-permute-start | bytes 2359304 | tf_op jit(solution)/shard_map/ppermute | solution.py:21
  23.1 37.7 %copy-start = (bf16[52,64,128]{2,1,0:T(8,128)(2,1)}, bf16[52,64,128]{2,1,0:T(8,128)(2,1)S(1)}, u32[]{:S(2)}) copy-start(bf16[52,64,128]{2,1,0:T(8,128)(2,1)S(1)} %collective-permute-done.refs_0_.refs_1_.refs_8_) | copy-start | bytes 2555908
  23.1 58.5 %collective-permute-start.5 = (bf16[48,64,128]{2,1,0:T(8,128)(2,1)}, bf16[48,64,128]{2,1,0:T(8,128)(2,1)}, u32[]{:S(2)}, u32[]{:S(2)}) collective-permute-start(bf16[48,64,128]{2,1,0:T(8,128)(2,1)} %get-tuple-element.19), channel_id=1, source_target_pairs={{3,0},{4,1},{5,2},{6,3},{7,4},{8,5},{9,6},{10,7},{11,8},{12,9},{13... | collective-permute-start | bytes 2359304 | tf_op jit(solution)/shard_map/ppermute | solution.py:21
  60.7 0.9 copy-start.1
  69.7 11.9 %copy-start.2 = (bf16[48,64,128]{2,1,0:T(8,128)(2,1)}, bf16[48,64,128]{2,1,0:T(8,128)(2,1)S(1)}, u32[]{:S(2)}) copy-start(bf16[48,64,128]{2,1,0:T(8,128)(2,1)S(1)} %collective-permute-done.2.refs_3_.refs_10_) | copy-start | bytes 2359300
  81.6 0.9 copy-start.3

commit v19 on v17

--- a/solution.py
+++ b/solution.py
@@ -242,7 +242,7 @@
             per_half = parents // halves
             for h in range(halves):
                 mat_copies[h].wait()
-                if h == 0:
+                if h == min(1, halves - 1):
                     for cp in seg_copies[n_c:]:
                         cp.start()
                 for p in range(h * per_half, (h + 1) * per_half):

time: 95.3 us -> 95.7 us (level)
  no operation moved by 1% of the time
where the time goes in v19:
time: 95.7 us; the launch traced here: 95.1 us
  starting transfers between devices  45.5 us (48%)
  Pallas kernels  29.9 us (31%)
  waiting for transfers between devices  13 us (14%)
  local copies, waits for them, and re-layouts  6.52 us (7%)
    ppermute x6, starting transfers between devices, from_behind(): lax.ppermute(value, axis, [(source, source + steps) for source in range(f...  45.5 us
    pallas_call x1, Pallas kernels, coupled_product(): pl.pallas_call(kernel, grid_spec=grid_spec, out_shape=jax.ShapeDtypeStruc...  13.7 us
    ppermute x6, waiting for transfers between devices, from_behind(): lax.ppermute(value, axis, [(source, source + steps) for source in range(f...  13 us
    pallas_call x2, Pallas kernels, upward(): pl.pallas_call(kernel, in_specs=[smem, smem, vmem, vmem, vmem], out_specs...  8.2 us
    pallas_call x1, Pallas kernels, gather_dot(): pl.pallas_call(kernel, grid_spec=grid_spec, out_shape=jax.ShapeDtypeStruc...  8.05 us
    unnamed x10, local copies, waits for them, and re-layouts  6.52 us
  transfers between devices with their start and end apart: 6, of which 2 were waited for; matrix products, arithmetic and copies ran while one was open for 5% of the time, Pallas kernels for 12%

profile of v19, /device:TPU:24, one launch (start us, length us, event | category | flops | bytes accessed | tf_op | source)
XLA Modules:
  0.0 95.1 jit_solution(14774998702563811749)
XLA Ops:
  0.0 4.8 %shard_map.110 = (bf16[52,64,128]{2,1,0:T(8,128)(2,1)}, bf16[52,64,128]{2,1,0:T(8,128)(2,1)}, bf16[48,64,128]{2,1,0:T(8,128)(2,1)}, bf16[48,64,128]{2,1,0:T(8,12...) custom-call(s32[192]{0:T(256)} %bitcast.8, s32[96]{0:T(128)} %bitcast.10, ...), custom_call_target="tpu_custom_call" | custom-call | flops 134217728 | bytes 8388608 | tf_op jit(solution)/shard_map/pallas_call | solution.py:171
  4.8 1.9 %collective-permute-start = (bf16[52,64,128]{2,1,0:T(8,128)(2,1)}, bf16[52,64,128]{2,1,0:T(8,128)(2,1)S(1)}, u32[]{:S(2)}, u32[]{:S(2)}) collective-permute-start(bf16[52,64,128]{2,1,0:T(8,128)(2,1)} %get-tuple-element.14), channel_id=1, source_target_pairs={{0,1},{1,2},{2,3},{3,4},{4,5},{5,6},{6,7},{7,8},{8,9},{9,10},{10,1... | collective-permute-start | bytes 2555912 | tf_op jit(solution)/shard_map/ppermute | solution.py:21
  6.7 5.4 %collective-permute-start.1 = (bf16[52,64,128]{2,1,0:T(8,128)(2,1)}, bf16[52,64,128]{2,1,0:T(8,128)(2,1)S(1)}, u32[]{:S(2)}, u32[]{:S(2)}) collective-permute-start(bf16[52,64,128]{2,1,0:T(8,128)(2,1)} %get-tuple-element.15), channel_id=1, source_target_pairs={{1,0},{2,1},{3,2},{4,3},{5,4},{6,5},{7,6},{8,7},{9,8},{10,9},{11,1... | collective-permute-start | bytes 2555912 | tf_op jit(solution)/shard_map/ppermute | solution.py:21
  12.2 1.9 %collective-permute-start.2 = (bf16[48,64,128]{2,1,0:T(8,128)(2,1)}, bf16[48,64,128]{2,1,0:T(8,128)(2,1)S(1)}, u32[]{:S(2)}, u32[]{:S(2)}) collective-permute-start(bf16[48,64,128]{2,1,0:T(8,128)(2,1)} %get-tuple-element.16), channel_id=1, source_target_pairs={{0,2},{1,3},{2,4},{3,5},{4,6},{5,7},{6,8},{7,9},{8,10},{9,11},{10,... | collective-permute-start | bytes 2359304 | tf_op jit(solution)/shard_map/ppermute | solution.py:21
  14.1 5.7 %collective-permute-start.3 = (bf16[48,64,128]{2,1,0:T(8,128)(2,1)}, bf16[48,64,128]{2,1,0:T(8,128)(2,1)S(1)}, u32[]{:S(2)}, u32[]{:S(2)}) collective-permute-start(bf16[48,64,128]{2,1,0:T(8,128)(2,1)} %get-tuple-element.17), channel_id=1, source_target_pairs={{2,0},{3,1},{4,2},{5,3},{6,4},{7,5},{8,6},{9,7},{10,8},{11,9},{12,... | collective-permute-start | bytes 2359304 | tf_op jit(solution)/shard_map/ppermute | solution.py:21
  19.8 1.9 %collective-permute-start.4 = (bf16[48,64,128]{2,1,0:T(8,128)(2,1)}, bf16[48,64,128]{2,1,0:T(8,128)(2,1)}, u32[]{:S(2)}, u32[]{:S(2)}) collective-permute-start(bf16[48,64,128]{2,1,0:T(8,128)(2,1)} %get-tuple-element.18), channel_id=1, source_target_pairs={{0,3},{1,4},{2,5},{3,6},{4,7},{5,8},{6,9},{7,10},{8,11},{9,12},{10... | collective-permute-start | bytes 2359304 | tf_op jit(solution)/shard_map/ppermute | solution.py:21
  21.8 0.3 collective-permute-done.refs_0_.refs_1_.refs_8_
  22.0 0.0 copy-start
  22.0 28.6 %collective-permute-start.5 = (bf16[48,64,128]{2,1,0:T(8,128)(2,1)}, bf16[48,64,128]{2,1,0:T(8,128)(2,1)}, u32[]{:S(2)}, u32[]{:S(2)}) collective-permute-start(bf16[48,64,128]{2,1,0:T(8,128)(2,1)} %get-tuple-element.19), channel_id=1, source_target_pairs={{3,0},{4,1},{5,2},{6,3},{7,4},{8,5},{9,6},{10,7},{11,8},{12,9},{13... | collective-permute-start | bytes 2359304 | tf_op jit(solution)/shard_map/ppermute | solution.py:21
  50.6 2.4 %copy.13.refs_15_ = bf16[4096,64]{1,0:T(8,128)(2,1)} copy(bf16[4096,64]{0,1:T(8,128)(2,1)} %param.12) | data formatting | bytes 1048576 | tf_op args[1]
  53.0 2.4 %copy.12.refs_14_ = bf16[4096,64]{1,0:T(8,128)(2,1)} copy(bf16[4096,64]{0,1:T(8,128)(2,1)} %param.13) | data formatting | bytes 1048576 | tf_op args[2]
  55.4 3.4 %shard_map.109 = (bf16[64,64,128]{2,1,0:T(8,128)(2,1)}, bf16[32,64,128]{2,1,0:T(8,128)(2,1)}) custom-call(s32[192]{0:T(256)} %bitcast.9, s32[96]{0:T(128)} %bitcast.11, bf16[64,64,128]{2,1,0:T(8,128)(2,1)} %refs_1_.1, bf16[64,4096]{1,0:T(8,128)(2,1)} %bitcast.5, bf16[64,4096]{1,0:T(8,128)(2,1)} %bitcast.7), custom_call_target="tpu_custom_call" | custom-call | flops 134217728 | bytes 8388608 | tf_op jit(solution)/shard_map/pallas_call | solution.py:171
  58.8 0.0 collective-permute-done.1.refs_2_.refs_9_
  58.8 0.0 copy-done
  58.8 0.0 copy-start.1
  58.8 0.9 copy-done.1
  59.7 8.0 %shard_map.111.refs_16_ = f32[64,64,128]{2,1,0:T(8,128)} custom-call(s32[768]{0:T(1024)} %idx_ref.1, bf16[4096,768]{1,0:T(8,128)(2,1)} %mats_ref.1, bf16[52,64,128]{2,1,0:T(8,128)(2,1)} %copy-done, bf16[64,64,128]{2,1,0:T(8,128)(2,1)} %refs_1_.1, bf16[52,64,128]{2,1,0:T(8,128)(2,1)} %copy-done.1), custom_call_target="tpu_custom_call" | custom-call | flops 805306368 | bytes 9568256 | tf_op jit(solution)/shard_map/pallas_call | solution.py:101
  67.7 0.0 collective-permute-done.2.refs_3_.refs_10_
  67.8 0.0 copy-start.2
  67.8 12.7 %collective-permute-done.3.refs_4_.refs_11_ = bf16[48,64,128]{2,1,0:T(8,128)(2,1)S(1)} collective-permute-done((bf16[48,64,128]{2,1,0:T(8,128)(2,1)}, bf16[48,64,128]{2,1,0:T(8,128)(2,1)S(1)}, u32[]{:S(2)}, u32[]{:S(2)}) %collective-permute-start.3) | collective-permute-done | bytes 786464 | tf_op jit(solution)/shard_map/ppermute | solution.py:21
  80.5 0.0 copy-start.3
  80.5 0.0 collective-permute-done.4.refs_5_.refs_12_
  80.5 0.0 collective-permute-done.5.refs_6_.refs_13_
  80.5 0.0 copy-done.2
  80.5 0.9 copy-done.3
  81.4 13.7 %shard_map.112 = bf16[64,64,128]{2,1,0:T(8,128)(2,1)} custom-call(s32[512]{0:T(512)} %ci_ref.1, s32[1024]{0:T(1024)} %fi_ref.1, bf16[2048,1024]{1,0:T(8,128)(2,1)} %cm_hbm.1, bf16[4096,1024]{1,0:T(8,128)(2,1)} %fm_ref.1, bf16[32,64,128]{2,1,0:T(8,128)(2,1)} %get-tuple-element.13.refs_0_, bf16[52,64,128]{2,1,0:T(8,128)(2,1)} %copy-done, ...), custom_call_target="tpu_custom_call" | custom-call | flops 1610612736 | bytes 18874368 | tf_op jit(solution)/shard_map/pallas_call | solution.py:284
Async XLA Ops:
  4.8 17.2 %collective-permute-start = (bf16[52,64,128]{2,1,0:T(8,128)(2,1)}, bf16[52,64,128]{2,1,0:T(8,128)(2,1)S(1)}, u32[]{:S(2)}, u32[]{:S(2)}) collective-permute-start(bf16[52,64,128]{2,1,0:T(8,128)(2,1)} %get-tuple-element.14), channel_id=1, source_target_pairs={{0,1},{1,2},{2,3},{3,4},{4,5},{5,6},{6,7},{7,8},{8,9},{9,10},{10,1... | collective-permute-start | bytes 2555912 | tf_op jit(solution)/shard_map/ppermute | solution.py:21
  6.7 52.0 %collective-permute-start.1 = (bf16[52,64,128]{2,1,0:T(8,128)(2,1)}, bf16[52,64,128]{2,1,0:T(8,128)(2,1)S(1)}, u32[]{:S(2)}, u32[]{:S(2)}) collective-permute-start(bf16[52,64,128]{2,1,0:T(8,128)(2,1)} %get-tuple-element.15), channel_id=1, source_target_pairs={{1,0},{2,1},{3,2},{4,3},{5,4},{6,5},{7,6},{8,7},{9,8},{10,9},{11,1... | collective-permute-start | bytes 2555912 | tf_op jit(solution)/shard_map/ppermute | solution.py:21
  12.2 55.6 %collective-permute-start.2 = (bf16[48,64,128]{2,1,0:T(8,128)(2,1)}, bf16[48,64,128]{2,1,0:T(8,128)(2,1)S(1)}, u32[]{:S(2)}, u32[]{:S(2)}) collective-permute-start(bf16[48,64,128]{2,1,0:T(8,128)(2,1)} %get-tuple-element.16), channel_id=1, source_target_pairs={{0,2},{1,3},{2,4},{3,5},{4,6},{5,7},{6,8},{7,9},{8,10},{9,11},{10,... | collective-permute-start | bytes 2359304 | tf_op jit(solution)/shard_map/ppermute | solution.py:21
  14.1 66.4 %collective-permute-start.3 = (bf16[48,64,128]{2,1,0:T(8,128)(2,1)}, bf16[48,64,128]{2,1,0:T(8,128)(2,1)S(1)}, u32[]{:S(2)}, u32[]{:S(2)}) collective-permute-start(bf16[48,64,128]{2,1,0:T(8,128)(2,1)} %get-tuple-element.17), channel_id=1, source_target_pairs={{2,0},{3,1},{4,2},{5,3},{6,4},{7,5},{8,6},{9,7},{10,8},{11,9},{12,... | collective-permute-start | bytes 2359304 | tf_op jit(solution)/shard_map/ppermute | solution.py:21
  19.8 60.7 %collective-permute-start.4 = (bf16[48,64,128]{2,1,0:T(8,128)(2,1)}, bf16[48,64,128]{2,1,0:T(8,128)(2,1)}, u32[]{:S(2)}, u32[]{:S(2)}) collective-permute-start(bf16[48,64,128]{2,1,0:T(8,128)(2,1)} %get-tuple-element.18), channel_id=1, source_target_pairs={{0,3},{1,4},{2,5},{3,6},{4,7},{5,8},{6,9},{7,10},{8,11},{9,12},{10... | collective-permute-start | bytes 2359304 | tf_op jit(solution)/shard_map/ppermute | solution.py:21
  22.0 36.8 %copy-start = (bf16[52,64,128]{2,1,0:T(8,128)(2,1)}, bf16[52,64,128]{2,1,0:T(8,128)(2,1)S(1)}, u32[]{:S(2)}) copy-start(bf16[52,64,128]{2,1,0:T(8,128)(2,1)S(1)} %collective-permute-done.refs_0_.refs_1_.refs_8_) | copy-start | bytes 2555908
  22.0 58.5 %collective-permute-start.5 = (bf16[48,64,128]{2,1,0:T(8,128)(2,1)}, bf16[48,64,128]{2,1,0:T(8,128)(2,1)}, u32[]{:S(2)}, u32[]{:S(2)}) collective-permute-start(bf16[48,64,128]{2,1,0:T(8,128)(2,1)} %get-tuple-element.19), channel_id=1, source_target_pairs={{3,0},{4,1},{5,2},{6,3},{7,4},{8,5},{9,6},{10,7},{11,8},{12,9},{13... | collective-permute-start | bytes 2359304 | tf_op jit(solution)/shard_map/ppermute | solution.py:21
  58.8 0.9 copy-start.1
  67.8 12.8 %copy-start.2 = (bf16[48,64,128]{2,1,0:T(8,128)(2,1)}, bf16[48,64,128]{2,1,0:T(8,128)(2,1)S(1)}, u32[]{:S(2)}) copy-start(bf16[48,64,128]{2,1,0:T(8,128)(2,1)S(1)} %collective-permute-done.2.refs_3_.refs_10_) | copy-start | bytes 2359300
  80.5 0.9 copy-start.3
